TPU v7x, 32 devices: a whole 2x2x4 slice. The times are simulated.
32 devices in a mesh: ctx: 8 (over z, x), tp: 4 (over y, core).
Axes of the slice: x: 2, y: 2, z: 4, core: 2. Of those that a mesh axis runs over, the one named last changes fastest.
Arguments:
- queries: bfloat16 [8192, 5120], P('ctx', 'tp'), may hold values from -6 to 6
- keys: bfloat16 [8192, 5120], P('ctx', 'tp'), may hold values from -6 to 6
- values: bfloat16 [8192, 5120], P('ctx', 'tp'), may hold values from -6 to 6
- gates: bfloat16 [8192, 5120], P('ctx', 'tp'), may hold values from -6 to 6
- gain: float32 [5120], P('tp'), may hold values from 0.1 to 1.9
- out_weight: bfloat16 [5120, 6144], P('tp'), may hold values from -0.078125 to 0.078125
Outputs:
- layer_out: bfloat16 [8192, 6144], P(('ctx', 'tp'))
All inputs are finite; a program needn't handle non-finite values.
Results may differ from a plain program's by a relative error of at most 0.014.
Values may be sent and summed in bfloat16 or wider, within the bound.
No kernel may reach another device: no remote copies, remote signals or barrier semaphores. Data moves between devices by JAX's collectives and lax.ppermute only.
A program may use at most 128 MiB of HBM per device.

v0:
```python
import jax
import jax.numpy as jnp
from jax import lax
from jax.sharding import PartitionSpec as P

HD = 128


epsilon = 1e-05


def from_behind(block, axis, distance):
    devices = range(lax.axis_size(axis))
    route = [(i - distance, i) for i in devices if i - distance in devices]
    return lax.ppermute(block, axis, route)


def on_device(queries, keys, values, gates, gain, out_weight):
    tokens = queries.shape[0]
    columns = queries.shape[1]
    head_count = columns // HD
    highest = lax.Precision.HIGHEST
    query_act = (
        jax.nn.silu(queries.astype(jnp.float32))
        .astype(jnp.bfloat16)
        .reshape(tokens, head_count, HD)
    )
    key_act = (
        jax.nn.silu(keys.astype(jnp.float32)).astype(jnp.bfloat16).reshape(tokens, head_count, HD)
    )
    value_rows = values.reshape(tokens, head_count, HD)
    own_state = jnp.einsum("thd,the->hde", key_act, value_rows, preferred_element_type=jnp.float32)
    zero_state = jnp.zeros_like(own_state)

    def hand_off(hop_index, prefix):
        return from_behind((prefix + own_state).astype(jnp.bfloat16), "ctx", 1).astype(jnp.float32)

    prefix = lax.fori_loop(0, lax.axis_size("ctx") - 1, hand_off, zero_state)
    scores = jnp.einsum("thd,shd->hts", query_act, key_act, preferred_element_type=jnp.float32)
    causal = jnp.tril(jnp.ones((tokens, tokens), dtype=bool))
    scores = jnp.where(causal[None], scores, jnp.float32(0.0)).astype(jnp.bfloat16)
    local_part = jnp.einsum("hts,she->the", scores, value_rows, preferred_element_type=jnp.float32)
    remote_part = jnp.einsum(
        "thd,hde->the", query_act.astype(jnp.float32), prefix, precision=highest
    )
    attention = remote_part + local_part
    mean_sq = jnp.mean(attention * attention, axis=-1, keepdims=True)
    normed = attention * lax.rsqrt(mean_sq + epsilon) * gain.reshape(head_count, HD)
    gate_open = jax.nn.sigmoid(gates.astype(jnp.float32)).reshape(tokens, head_count, HD)
    mixed_rows = (normed * gate_open).astype(jnp.bfloat16).reshape(tokens, columns)
    return lax.psum_scatter(
        jnp.dot(mixed_rows, out_weight, preferred_element_type=jnp.float32).astype(jnp.bfloat16),
        "tp",
        scatter_dimension=0,
        tiled=True,
    )


def solution(mesh):
    return jax.shard_map(
        on_device,
        mesh=mesh,
        in_specs=(
            P("ctx", "tp"),
            P("ctx", "tp"),
            P("ctx", "tp"),
            P("ctx", "tp"),
            P("tp"),
            P("tp", None),
        ),
        out_specs=P(("ctx", "tp"), None),
        check_vma=False,
    )
```

profile of v0, /device:TPU:24, one launch (start us, length us, event | category | flops | bytes accessed | tf_op | source)
XLA Modules:
  0.0 267.8 jit_solution(3341780787993774739)
XLA Ops:
  7.8 3.0 %copy.13 = bf16[1024,1280]{0,1:T(8,128)(2,1)S(1)} copy(bf16[1024,1280]{1,0:T(8,128)(2,1)} %param.8) | data formatting | bytes 5242880 | tf_op args[0]
  10.8 3.0 %fusion.13 = bf16[1024,1280]{0,1:T(8,128)(2,1)} fusion(bf16[1024,1280]{0,1:T(8,128)(2,1)S(1)} %copy.13), kind=kLoop, calls=%fused_computation.19 | loop fusion | flops 7864320 | bytes 5242880 | tf_op jit(solution)/shard_map/convert_element_type | solution.py:25
  13.8 3.0 %copy.11 = bf16[1024,1280]{0,1:T(8,128)(2,1)S(1)} copy(bf16[1024,1280]{1,0:T(8,128)(2,1)} %param.9) | data formatting | bytes 5242880 | tf_op args[1]
  16.8 3.1 %fusion.9 = bf16[1024,1280]{0,1:T(8,128)(2,1)} fusion(bf16[1024,1280]{0,1:T(8,128)(2,1)S(1)} %copy.11), kind=kLoop, calls=%fused_computation.15 | loop fusion | flops 7864320 | bytes 5242880 | tf_op jit(solution)/shard_map/convert_element_type | solution.py:29
  19.9 4.5 %copy.12 = bf16[1024,1280]{0,1:T(8,128)(2,1)} copy(bf16[1024,1280]{1,0:T(8,128)(2,1)} %param.10) | data formatting | bytes 5242880 | tf_op args[2]
  24.4 3.4 %fusion.15 = f32[10,128,128]{2,1,0:T(8,128)S(1)} fusion(bf16[1024,10,128]{0,2,1:T(8,128)(2,1)} %bitcast.22, bf16[1024,10,128]{0,2,1:T(8,128)(2,1)} %bitcast.24), kind=kOutput, calls=%fused_computation.27 | convolution fusion | flops 335544320 | bytes 5898240 | tf_op jit(solution)/shard_map/thd,the->hde/dot_general | solution.py:32
  27.8 16.3 %fusion.1 = f32[10,1024,128]{1,2,0:T(8,128)} fusion(bf16[1024,10,128]{0,2,1:T(8,128)(2,1)} %bitcast.25, pred[1024,1024]{1,0:T(8,128)(4,1)S(1)} %copy-done, bf16[1024,10,128]{0,2,1:T(8,128)(2,1)} %bitcast.26, bf16[1024,10,128]{0,2,1:T(8,128)(2,1)} %bitcast.23), kind=kOutput, calls=%fused_computation.3 | convolution fusion | flops 5389680640 | bytes 14155776 | tf_op jit(solution)/shard_map/hts,she->the/dot_general | solution.py:42
  44.0 75.5 %while.11 = (s32[]{:T(128)}, f32[10,128,128]{2,1,0:T(8,128)S(1)}, f32[10,128,128]{2,1,0:T(8,128)S(1)}, s32[]{:T(128)}, s32[]{:T(128)}) while((s32[]{:T(128)}, f32[10,128,128]{2,1,0:T(8,128)S(1)}, f32[10,128,128]{2,1,0:T(8,128)S(1)}, s32[]{:T(128)}, s32[]{:T(128)}) %tuple.23), condition=%wide.region_1.2_spmd.clone, body=%wide.region_0.1_spmd.clone.sunk | while | flops 655363 | bytes 3932271 | solution.py:38
  44.1 3.4 %collective-permute-start = (bf16[10,128,128]{2,1,0:T(8,128)(2,1)S(1)}, bf16[10,128,128]{2,1,0:T(8,128)(2,1)S(1)}, u32[]{:S(2)}, u32[]{:S(2)}) collective-permute-start(bf16[10,128,128]{2,1,0:T(8,128)(2,1)S(1)} %fusion.26), channel_id=1, source_target_pairs={{0,4},{4,8},{8,12},{12,16},{16,20},{20,24},{24,28},{1,5},{5,9},{9,... | collective-permute-start | bytes 983048 | tf_op jit(solution)/shard_map/while/body/eval_jaxpr/ppermute | solution.py:15
  47.5 8.8 %collective-permute-done = bf16[10,128,128]{2,1,0:T(8,128)(2,1)S(1)} collective-permute-done((bf16[10,128,128]{2,1,0:T(8,128)(2,1)S(1)}, bf16[10,128,128]{2,1,0:T(8,128)(2,1)S(1)}, u32[]{:S(2)}, u32[]{:S(2)}) %collective-permute-start) | collective-permute-done | bytes 327712 | tf_op jit(solution)/shard_map/while/body/eval_jaxpr/ppermute | solution.py:15
  56.5 2.5 collective-permute-start
  59.0 8.9 %collective-permute-done = bf16[10,128,128]{2,1,0:T(8,128)(2,1)S(1)} collective-permute-done((bf16[10,128,128]{2,1,0:T(8,128)(2,1)S(1)}, bf16[10,128,128]{2,1,0:T(8,128)(2,1)S(1)}, u32[]{:S(2)}, u32[]{:S(2)}) %collective-permute-start) | collective-permute-done | bytes 327712 | tf_op jit(solution)/shard_map/while/body/eval_jaxpr/ppermute | solution.py:15
  68.1 1.9 collective-permute-start
  70.0 8.6 %collective-permute-done = bf16[10,128,128]{2,1,0:T(8,128)(2,1)S(1)} collective-permute-done((bf16[10,128,128]{2,1,0:T(8,128)(2,1)S(1)}, bf16[10,128,128]{2,1,0:T(8,128)(2,1)S(1)}, u32[]{:S(2)}, u32[]{:S(2)}) %collective-permute-start) | collective-permute-done | bytes 327712 | tf_op jit(solution)/shard_map/while/body/eval_jaxpr/ppermute | solution.py:15
  80.7 7.9 %collective-permute-done = bf16[10,128,128]{2,1,0:T(8,128)(2,1)S(1)} collective-permute-done((bf16[10,128,128]{2,1,0:T(8,128)(2,1)S(1)}, bf16[10,128,128]{2,1,0:T(8,128)(2,1)S(1)}, u32[]{:S(2)}, u32[]{:S(2)}) %collective-permute-start) | collective-permute-done | bytes 327712 | tf_op jit(solution)/shard_map/while/body/eval_jaxpr/ppermute | solution.py:15
  90.7 7.9 %collective-permute-done = bf16[10,128,128]{2,1,0:T(8,128)(2,1)S(1)} collective-permute-done((bf16[10,128,128]{2,1,0:T(8,128)(2,1)S(1)}, bf16[10,128,128]{2,1,0:T(8,128)(2,1)S(1)}, u32[]{:S(2)}, u32[]{:S(2)}) %collective-permute-start) | collective-permute-done | bytes 327712 | tf_op jit(solution)/shard_map/while/body/eval_jaxpr/ppermute | solution.py:15
  98.8 1.9 collective-permute-start
  100.8 8.6 %collective-permute-done = bf16[10,128,128]{2,1,0:T(8,128)(2,1)S(1)} collective-permute-done((bf16[10,128,128]{2,1,0:T(8,128)(2,1)S(1)}, bf16[10,128,128]{2,1,0:T(8,128)(2,1)S(1)}, u32[]{:S(2)}, u32[]{:S(2)}) %collective-permute-start) | collective-permute-done | bytes 327712 | tf_op jit(solution)/shard_map/while/body/eval_jaxpr/ppermute | solution.py:15
  111.4 7.9 %collective-permute-done = bf16[10,128,128]{2,1,0:T(8,128)(2,1)S(1)} collective-permute-done((bf16[10,128,128]{2,1,0:T(8,128)(2,1)S(1)}, bf16[10,128,128]{2,1,0:T(8,128)(2,1)S(1)}, u32[]{:S(2)}, u32[]{:S(2)}) %collective-permute-start) | collective-permute-done | bytes 327712 | tf_op jit(solution)/shard_map/while/body/eval_jaxpr/ppermute | solution.py:15
  119.6 8.2 %multiply_reduce_fusion = (f32[1024,10]{0,1:T(8,128)S(1)}, f32[1024,10,128]{0,2,1:T(8,128)}) fusion(f32[10,1024,128]{1,2,0:T(8,128)} %fusion.1, f32[10,128,128]{2,1,0:T(8,128)S(1)} %get-tuple-element.22, bf16[1024,10,128]{0,2,1:T(8,128)(2,1)} %bitcast.27), kind=kOutput, calls=%fused_computation.23 | convolution fusion | flops 2017187840 | bytes 13803520 | tf_op jit(solution)/shard_map/thd,hde->the/dot_general | solution.py:43
  127.9 4.5 %copy.16 = bf16[1024,1280]{0,1:T(8,128)(2,1)} copy(bf16[1024,1280]{1,0:T(8,128)(2,1)} %param.11) | data formatting | bytes 5242880 | tf_op args[3]
  132.3 3.2 %add_divide_fusion = f32[1024,1280]{0,1:T(8,128)S(1)} fusion(bf16[1024,1280]{0,1:T(8,128)(2,1)} %copy.16), kind=kLoop, calls=%fused_computation.22 | loop fusion | flops 5242880 | bytes 7864320 | tf_op jit(solution)/shard_map/div | solution.py:49
  136.6 24.6 %convolution_convert_fusion = bf16[1024,6144]{1,0:T(8,128)(2,1)} fusion(bf16[1024,1280]{0,1:T(8,128)(2,1)S(1)} %bitcast.28, bf16[1280,6144]{1,0:T(8,128)(2,1)} %param.13), kind=kOutput, calls=%fused_computation.7 | convolution fusion | flops 16112418816 | bytes 30932992 | tf_op jit(solution)/shard_map/dot_general | solution.py:52
  161.2 99.8 %reduce-scatter.2.cloned.1.call-done = bf16[256,6144]{1,0:T(8,128)(2,1)} async-done(((bf16[1024,6144]{1,0:T(8,128)(2,1)}), bf16[256,6144]{1,0:T(8,128)(2,1)}) %reduce-scatter.2.cloned.1.call-update) | async-done | bytes 3145744 | tf_op jit(solution)/shard_map/reduce_scatter | solution.py:51
  (32 shorter events, 9.0 us)
Async XLA Ops:
  6.5 254.5 %reduce-scatter.2.cloned.1.call-start = ((), (), s32[]{:S(2)}) async-start(), calls=%async_computation.1 | async-start | bytes 15728640 | tf_op jit(solution)/shard_map/reduce_scatter | solution.py:51
  19.9 7.9 %copy-start = (pred[1024,1024]{1,0:T(8,128)(4,1)S(1)}, pred[1024,1024]{1,0:T(8,128)(4,1)}, u32[]{:S(2)}) copy-start(pred[1024,1024]{1,0:T(8,128)(4,1)} %iota_compare_fusion) | copy-start | bytes 3145732
  44.1 12.2 %collective-permute-start = (bf16[10,128,128]{2,1,0:T(8,128)(2,1)S(1)}, bf16[10,128,128]{2,1,0:T(8,128)(2,1)S(1)}, u32[]{:S(2)}, u32[]{:S(2)}) collective-permute-start(bf16[10,128,128]{2,1,0:T(8,128)(2,1)S(1)} %fusion.26), channel_id=1, source_target_pairs={{0,4},{4,8},{8,12},{12,16},{16,20},{20,24},{24,28},{1,5},{5,9},{9,... | collective-permute-start | bytes 983048 | tf_op jit(solution)/shard_map/while/body/eval_jaxpr/ppermute | solution.py:15
  56.5 11.4 %collective-permute-start = (bf16[10,128,128]{2,1,0:T(8,128)(2,1)S(1)}, bf16[10,128,128]{2,1,0:T(8,128)(2,1)S(1)}, u32[]{:S(2)}, u32[]{:S(2)}) collective-permute-start(bf16[10,128,128]{2,1,0:T(8,128)(2,1)S(1)} %fusion.26), channel_id=1, source_target_pairs={{0,4},{4,8},{8,12},{12,16},{16,20},{20,24},{24,28},{1,5},{5,9},{9,... | collective-permute-start | bytes 983048 | tf_op jit(solution)/shard_map/while/body/eval_jaxpr/ppermute | solution.py:15
  68.1 10.5 %collective-permute-start = (bf16[10,128,128]{2,1,0:T(8,128)(2,1)S(1)}, bf16[10,128,128]{2,1,0:T(8,128)(2,1)S(1)}, u32[]{:S(2)}, u32[]{:S(2)}) collective-permute-start(bf16[10,128,128]{2,1,0:T(8,128)(2,1)S(1)} %fusion.26), channel_id=1, source_target_pairs={{0,4},{4,8},{8,12},{12,16},{16,20},{20,24},{24,28},{1,5},{5,9},{9,... | collective-permute-start | bytes 983048 | tf_op jit(solution)/shard_map/while/body/eval_jaxpr/ppermute | solution.py:15
  78.8 9.9 %collective-permute-start = (bf16[10,128,128]{2,1,0:T(8,128)(2,1)S(1)}, bf16[10,128,128]{2,1,0:T(8,128)(2,1)S(1)}, u32[]{:S(2)}, u32[]{:S(2)}) collective-permute-start(bf16[10,128,128]{2,1,0:T(8,128)(2,1)S(1)} %fusion.26), channel_id=1, source_target_pairs={{0,4},{4,8},{8,12},{12,16},{16,20},{20,24},{24,28},{1,5},{5,9},{9,... | collective-permute-start | bytes 983048 | tf_op jit(solution)/shard_map/while/body/eval_jaxpr/ppermute | solution.py:15
  88.8 9.9 %collective-permute-start = (bf16[10,128,128]{2,1,0:T(8,128)(2,1)S(1)}, bf16[10,128,128]{2,1,0:T(8,128)(2,1)S(1)}, u32[]{:S(2)}, u32[]{:S(2)}) collective-permute-start(bf16[10,128,128]{2,1,0:T(8,128)(2,1)S(1)} %fusion.26), channel_id=1, source_target_pairs={{0,4},{4,8},{8,12},{12,16},{16,20},{20,24},{24,28},{1,5},{5,9},{9,... | collective-permute-start | bytes 983048 | tf_op jit(solution)/shard_map/while/body/eval_jaxpr/ppermute | solution.py:15
  98.8 10.5 %collective-permute-start = (bf16[10,128,128]{2,1,0:T(8,128)(2,1)S(1)}, bf16[10,128,128]{2,1,0:T(8,128)(2,1)S(1)}, u32[]{:S(2)}, u32[]{:S(2)}) collective-permute-start(bf16[10,128,128]{2,1,0:T(8,128)(2,1)S(1)} %fusion.26), channel_id=1, source_target_pairs={{0,4},{4,8},{8,12},{12,16},{16,20},{20,24},{24,28},{1,5},{5,9},{9,... | collective-permute-start | bytes 983048 | tf_op jit(solution)/shard_map/while/body/eval_jaxpr/ppermute | solution.py:15
  109.5 9.9 %collective-permute-start = (bf16[10,128,128]{2,1,0:T(8,128)(2,1)S(1)}, bf16[10,128,128]{2,1,0:T(8,128)(2,1)S(1)}, u32[]{:S(2)}, u32[]{:S(2)}) collective-permute-start(bf16[10,128,128]{2,1,0:T(8,128)(2,1)S(1)} %fusion.26), channel_id=1, source_target_pairs={{0,4},{4,8},{8,12},{12,16},{16,20},{20,24},{24,28},{1,5},{5,9},{9,... | collective-permute-start | bytes 983048 | tf_op jit(solution)/shard_map/while/body/eval_jaxpr/ppermute | solution.py:15
  127.8 7.7 %slice-start = ((s8[5242880]{0:T(1024)(128)(4,1)}), s8[1048576]{0:T(1024)(128)(4,1)S(1)}, s32[]{:S(2)}) async-start(s8[5242880]{0:T(1024)(128)(4,1)} %bitcast.19), calls=%async_computation.2 | async-start | bytes 2097152
  132.3 3.3 %slice-start.1 = ((s8[5242880]{0:T(1024)(128)(4,1)}), s8[4194304]{0:T(1024)(128)(4,1)S(1)}, s32[]{:S(2)}) async-start(s8[5242880]{0:T(1024)(128)(4,1)} %bitcast.19), calls=%async_computation.3 | async-start | bytes 8388608
  132.3 3.3 %copy-start.1 = (f32[1280]{0:T(1024)S(1)}, f32[1280]{0:T(1024)}, u32[]{:S(2)}) copy-start(f32[1280]{0:T(1024)} %param.12) | copy-start | bytes 15364
Sparse Core Ops, SparseCore 0:
  161.3 99.6 reduce-scatter.1
where the time goes:
time: 270 us; the launch traced here: 268 us
  waiting for transfers between devices  159 us (59%)
  matrix products  52.4 us (19%)
  starting transfers between devices  15.5 us (6%)
  local copies, waits for them, and re-layouts  14.9 us (6%)
  between operations  13.5 us (5%)
  other arithmetic  12.5 us (5%)
    reduce_scatter x1, waiting for transfers between devices, on_device(): lax.psum_scatter(jnp.dot(mixed_rows, out_weight, preferred_element_type=j...  99.8 us
    ppermute x7, waiting for transfers between devices, from_behind(): return lax.ppermute(block, axis, route)  58.7 us
    dot_general x1, matrix products, on_device(): jnp.dot(mixed_rows, out_weight, preferred_element_type=jnp.float32)  24.6 us
    dot_general x1, matrix products, on_device(): jnp.einsum('hts,she->the', scores, value_rows, preferred_element_type=jnp...  16.3 us
    ppermute x7, starting transfers between devices, from_behind(): return lax.ppermute(block, axis, route)  15.5 us
    unnamed x12, local copies, waits for them, and re-layouts  14.9 us
    dot_general x1, matrix products, on_device(): jnp.einsum('thd,hde->the', query_act.astype(jnp.float32), prefix, precisi...  8.23 us
  transfers between devices with their start and end apart: 8, of which 8 were waited for; matrix products, arithmetic and copies ran while one was open for 0% of the time, Pallas kernels for 0%

commit v1 on v0

v1 whole, which is shorter than its diff:
```python
import jax
import jax.numpy as jnp
import numpy as np
from jax import lax
from jax.sharding import Mesh
from jax.sharding import PartitionSpec as P

HD = 128
COLUMN_CHUNKS = 3


epsilon = 1e-05


def split_bf16(x):
    hi = x.astype(jnp.bfloat16)
    lo = (x - hi.astype(jnp.float32)).astype(jnp.bfloat16)
    return hi, lo


def on_device(queries, keys, values, gates, gain, out_weight):
    tokens = queries.shape[0]
    columns = queries.shape[1]
    head_count = columns // HD
    ctx_size = lax.axis_size("ctx")
    ty_size = lax.axis_size("ty")
    tc_size = lax.axis_size("tc")
    query_act = (
        jax.nn.silu(queries.astype(jnp.float32))
        .astype(jnp.bfloat16)
        .reshape(tokens, head_count, HD)
    )
    key_act = (
        jax.nn.silu(keys.astype(jnp.float32)).astype(jnp.bfloat16).reshape(tokens, head_count, HD)
    )
    value_rows = values.reshape(tokens, head_count, HD)
    own_state = jnp.einsum("thd,the->hde", key_act, value_rows, preferred_element_type=jnp.float32)

    states = lax.all_gather(own_state.astype(jnp.bfloat16), "ctx", axis=0, tiled=False)
    earlier = jnp.arange(ctx_size) < lax.axis_index("ctx")
    prefix = jnp.sum(
        jnp.where(earlier[:, None, None, None], states.astype(jnp.float32), 0.0), axis=0
    )

    scores = jnp.einsum("thd,shd->hts", query_act, key_act, preferred_element_type=jnp.float32)
    causal = jnp.tril(jnp.ones((tokens, tokens), dtype=bool))
    scores = jnp.where(causal[None], scores, jnp.float32(0.0)).astype(jnp.bfloat16)
    local_part = jnp.einsum("hts,she->the", scores, value_rows, preferred_element_type=jnp.float32)
    prefix_hi, prefix_lo = split_bf16(prefix)
    remote_part = jnp.einsum(
        "thd,hde->the", query_act, prefix_hi, preferred_element_type=jnp.float32
    ) + jnp.einsum("thd,hde->the", query_act, prefix_lo, preferred_element_type=jnp.float32)
    attention = remote_part + local_part
    mean_sq = jnp.mean(attention * attention, axis=-1, keepdims=True)
    normed = attention * lax.rsqrt(mean_sq + epsilon) * gain.reshape(head_count, HD)
    gate_open = jax.nn.sigmoid(gates.astype(jnp.float32)).reshape(tokens, head_count, HD)
    mixed_rows = (normed * gate_open).astype(jnp.bfloat16).reshape(tokens, columns)

    block = tokens // (ty_size * tc_size)
    mixed_rows = (
        mixed_rows.reshape(ty_size, tc_size, block, columns)
        .transpose(1, 0, 2, 3)
        .reshape(tokens, columns)
    )
    width = out_weight.shape[1]
    chunk = width // COLUMN_CHUNKS
    pieces = []
    for c in range(COLUMN_CHUNKS):
        part = jnp.dot(
            mixed_rows, out_weight[:, c * chunk:(c + 1) * chunk], preferred_element_type=jnp.float32
        ).astype(jnp.bfloat16)
        part = lax.psum_scatter(part, "tc", scatter_dimension=0, tiled=True)
        part = lax.psum_scatter(part, "ty", scatter_dimension=0, tiled=True)
        pieces.append(part)
    return jnp.concatenate(pieces, axis=1)


def solution(mesh):
    ctx_size, tp_size = mesh.devices.shape
    split = Mesh(
        np.asarray(mesh.devices).reshape(ctx_size, tp_size // 2, 2), ("ctx", "ty", "tc")
    )
    tp = ("ty", "tc")
    return jax.shard_map(
        on_device,
        mesh=split,
        in_specs=(
            P("ctx", tp),
            P("ctx", tp),
            P("ctx", tp),
            P("ctx", tp),
            P(tp),
            P(tp, None),
        ),
        out_specs=P(("ctx",) + tp, None),
        check_vma=False,
    )
```

time: 270 us -> 263 us (0.974)
  starting transfers between devices: 15.5 us -> 0.43 us
  local copies, waits for them, and re-layouts: 14.9 us -> 28 us
  waiting for transfers between devices: 159 us -> 149 us
  other arithmetic: 12.5 us -> 17.9 us
    ppermute x7 -> x0, waiting for transfers between devices: 58.7 us -> none  [from_behind(): return lax.ppermute(block, axis, route)]
    reduce_scatter x1 -> x6, waiting for transfers between devices: 99.8 us -> 125 us  [the longest x3 103 us: on_device(): part = lax.psum_scatter(part, 'ty', scatter_dimension=0, tiled=True)]
    all_gather x0 -> x1, waiting for transfers between devices: none -> 23.6 us  [on_device(): lax.all_gather(own_state.astype(jnp.bfloat16), 'ctx', axis=0, tiled=False)]
    ppermute x7 -> x0, starting transfers between devices: 15.5 us -> none  [from_behind(): return lax.ppermute(block, axis, route)]
    another operation x0 -> x2, local copies, waits for them, and re-layouts: none -> 9.33 us  [on_device(): mixed_rows.reshape(ty_size, tc_size, block, columns).transpose(1, 0, 2, 3)]
    unnamed x12 -> x18, local copies, waits for them, and re-layouts: 14.9 us -> 18.7 us
    concatenate x0 -> x1, other arithmetic: none -> 3.17 us  [on_device(): return jnp.concatenate(pieces, axis=1)]
    dot_general x2 -> x5, matrix products: 32.8 us -> 31.6 us  [the longest x3 29.3 us: on_device(): jnp.dot(mixed_rows, out_weight[:, c * chunk:(c + 1) * chunk], preferred_e...]
  transfers between devices with their start and end apart: 8 -> 7, of which waited for: 8 -> 6; matrix products, arithmetic and copies ran while one was open for 0% -> 19% of each run, Pallas kernels for 0% -> 0%
where the time goes in v1:
time: 263 us; the launch traced here: 260 us
  waiting for transfers between devices  149 us (57%)
  matrix products  51.2 us (19%)
  local copies, waits for them, and re-layouts  28 us (11%)
  other arithmetic  17.9 us (7%)
  between operations  13.6 us (5%)
    reduce_scatter x3, waiting for transfers between devices, on_device(): part = lax.psum_scatter(part, 'ty', scatter_dimension=0, tiled=True)  103 us
    dot_general x3, matrix products, on_device(): jnp.dot(mixed_rows, out_weight[:, c * chunk:(c + 1) * chunk], preferred_e...  29.3 us
    all_gather x1, waiting for transfers between devices, on_device(): lax.all_gather(own_state.astype(jnp.bfloat16), 'ctx', axis=0, tiled=False)  23.6 us
    reduce_scatter x3, waiting for transfers between devices, on_device(): part = lax.psum_scatter(part, 'tc', scatter_dimension=0, tiled=True)  21.9 us
    unnamed x18, local copies, waits for them, and re-layouts  18.7 us
    dot_general x1, matrix products, on_device(): jnp.einsum('hts,she->the', scores, value_rows, preferred_element_type=jnp...  16.3 us
    another operation x2, local copies, waits for them, and re-layouts, on_device(): mixed_rows.reshape(ty_size, tc_size, block, columns).transpose(1, 0, 2, 3)  9.33 us
  transfers between devices with their start and end apart: 7, of which 6 were waited for; matrix products, arithmetic and copies ran while one was open for 19% of the time, Pallas kernels for 0%

profile of v1, /device:TPU:24, one launch (start us, length us, event | category | flops | bytes accessed | tf_op | source)
XLA Modules:
  0.0 260.4 jit_solution(15461320034258896576)
XLA Ops:
  6.5 4.4 %copy.21 = bf16[1024,1280]{0,1:T(8,128)(2,1)} copy(bf16[1024,1280]{1,0:T(8,128)(2,1)} %param.7) | data formatting | bytes 5242880 | tf_op args[1]
  10.9 3.3 %fusion.8 = bf16[1024,1280]{0,1:T(8,128)(2,1)S(1)} fusion(bf16[1024,1280]{0,1:T(8,128)(2,1)} %copy.21), kind=kLoop, calls=%fused_computation.12 | loop fusion | flops 7864320 | bytes 5242880 | tf_op jit(solution)/shard_map/convert_element_type | solution.py:34
  14.2 4.9 %copy.22 = bf16[1024,1280]{0,1:T(8,128)(2,1)} copy(bf16[1024,1280]{1,0:T(8,128)(2,1)} %param.8) | data formatting | bytes 5242880 | tf_op args[2]
  19.1 3.3 %convolution_convert_fusion = bf16[10,128,128]{2,1,0:T(8,128)(2,1)} fusion(bf16[1024,10,128]{0,2,1:T(8,128)(2,1)S(1)} %bitcast.32, bf16[1024,10,128]{0,2,1:T(8,128)(2,1)} %bitcast.34), kind=kOutput, calls=%fused_computation.34 | convolution fusion | flops 335708160 | bytes 5570560 | tf_op jit(solution)/shard_map/thd,the->hde/dot_general | solution.py:37
  22.7 4.5 %copy.24 = bf16[1024,1280]{0,1:T(8,128)(2,1)} copy(bf16[1024,1280]{1,0:T(8,128)(2,1)} %param.6) | data formatting | bytes 5242880 | tf_op args[0]
  27.2 3.0 %copy.31 = bf16[1024,1280]{0,1:T(8,128)(2,1)S(1)} copy(bf16[1024,1280]{1,0:T(8,128)(2,1)} %param.9) | data formatting | bytes 5242880 | tf_op args[3]
  31.5 3.7 %add_divide_fusion = f32[1024,1280]{0,1:T(8,128)} fusion(bf16[1024,1280]{0,1:T(8,128)(2,1)S(1)} %copy.31), kind=kLoop, calls=%fused_computation.27 | loop fusion | flops 5242880 | bytes 7864320 | tf_op jit(solution)/shard_map/div | solution.py:56
  35.2 1.6 fusion.12
  36.7 16.3 %fusion = f32[10,1024,128]{1,2,0:T(8,128)} fusion(bf16[1024,10,128]{0,2,1:T(8,128)(2,1)} %bitcast.35, pred[1024,1024]{1,0:T(8,128)(4,1)} %iota_compare_fusion, bf16[1024,10,128]{0,2,1:T(8,128)(2,1)S(1)} %bitcast.26, bf16[1024,10,128]{0,2,1:T(8,128)(2,1)} %bitcast.33), kind=kOutput, calls=%fused_computation.1 | convolution fusion | flops 5389680640 | bytes 14155776 | tf_op jit(solution)/shard_map/hts,she->the/dot_general | solution.py:48
  53.0 23.6 %all-gather.3.cloned.1.call-done = bf16[80,128,128]{2,1,0:T(8,128)(2,1)} async-done(((bf16[10,128,128]{2,1,0:T(8,128)(2,1)}), bf16[80,128,128]{2,1,0:T(8,128)(2,1)}) %all-gather.3.cloned.1.call-update) | async-done | bytes 2621456 | tf_op jit(solution)/shard_map/all_gather | solution.py:39
  76.6 2.6 fusion.13
  81.8 2.4 multiply_convert_fusion
  84.2 4.3 %reshape_reshape.3 = bf16[2,2,256,1280]{2,1,0,3:T(2,128)(2,1)S(1)} reshape(bf16[1024,10,128]{0,2,1:T(8,128)(2,1)} %multiply_convert_fusion) | data formatting | bytes 5242880 | tf_op jit(solution)/shard_map/reshape;reshape | solution.py:61
  88.5 5.0 %copy.32 = bf16[2,2,256,1280]{3,2,0,1:T(8,128)(2,1)} copy(bf16[2,2,256,1280]{2,1,0,3:T(2,128)(2,1)S(1)} %reshape_reshape.3) | data formatting | bytes 5242880 | tf_op jit(solution)/shard_map/reshape;reshape | solution.py:61
  93.5 10.0 %fusion.26 = bf16[1024,2048]{1,0:T(8,128)(2,1)} fusion(bf16[1024,1280]{1,0:T(8,128)(2,1)} %bitcast.37, bf16[1280,6144]{1,0:T(8,128)(2,1)} %param.11), kind=kOutput, calls=%fused_computation.32 | convolution fusion | flops 5370806272 | bytes 12058624 | tf_op jit(solution)/shard_map/dot_general | solution.py:69
  103.5 1.7 copy-done.3
  105.2 9.6 %fusion.23 = bf16[1024,2048]{1,0:T(8,128)(2,1)} fusion(bf16[1024,1280]{1,0:T(8,128)(2,1)S(1)} %bitcast.38, bf16[1280,6144]{1,0:T(8,128)(2,1)} %param.11), kind=kOutput, calls=%fused_computation.31 | convolution fusion | flops 5370806272 | bytes 12058624 | tf_op jit(solution)/shard_map/dot_general | solution.py:69
  114.9 9.7 %fusion.20 = bf16[1024,2048]{1,0:T(8,128)(2,1)} fusion(bf16[1024,1280]{1,0:T(8,128)(2,1)S(1)} %bitcast.39, bf16[1280,6144]{1,0:T(8,128)(2,1)} %param.11), kind=kOutput, calls=%fused_computation.30 | convolution fusion | flops 5370806272 | bytes 12058624 | tf_op jit(solution)/shard_map/dot_general | solution.py:69
  125.3 6.4 %reduce-scatter.11.cloned.1.call-done = bf16[512,2048]{1,0:T(8,128)(2,1)} async-done(((bf16[1024,2048]{1,0:T(8,128)(2,1)}), bf16[512,2048]{1,0:T(8,128)(2,1)}) %reduce-scatter.11.cloned.1.call-update) | async-done | bytes 2097168 | tf_op jit(solution)/shard_map/reduce_scatter | solution.py:72
  131.8 15.4 %reduce-scatter.7.cloned.1.call-done = bf16[512,2048]{1,0:T(8,128)(2,1)} async-done(((bf16[1024,2048]{1,0:T(8,128)(2,1)}), bf16[512,2048]{1,0:T(8,128)(2,1)}) %reduce-scatter.7.cloned.1.call-update) | async-done | bytes 2097168 | tf_op jit(solution)/shard_map/reduce_scatter | solution.py:72
  147.3 34.9 %reduce-scatter.17.cloned.1.call-done = bf16[256,2048]{1,0:T(8,128)(2,1)} async-done(((bf16[512,2048]{1,0:T(8,128)(2,1)}), bf16[256,2048]{1,0:T(8,128)(2,1)}) %reduce-scatter.17.cloned.1.call-update) | async-done | bytes 1048592 | tf_op jit(solution)/shard_map/reduce_scatter | solution.py:73
  182.2 34.0 %reduce-scatter.13.cloned.1.call-done = bf16[256,2048]{1,0:T(8,128)(2,1)} async-done(((bf16[512,2048]{1,0:T(8,128)(2,1)}), bf16[256,2048]{1,0:T(8,128)(2,1)}) %reduce-scatter.13.cloned.1.call-update) | async-done | bytes 1048592 | tf_op jit(solution)/shard_map/reduce_scatter | solution.py:73
  216.2 34.2 %reduce-scatter.9.cloned.1.call-done = bf16[256,2048]{1,0:T(8,128)(2,1)} async-done(((bf16[512,2048]{1,0:T(8,128)(2,1)}), bf16[256,2048]{1,0:T(8,128)(2,1)}) %reduce-scatter.9.cloned.1.call-update) | async-done | bytes 1048592 | tf_op jit(solution)/shard_map/reduce_scatter | solution.py:73
  250.4 3.2 %pad_maximum_fusion = bf16[256,6144]{1,0:T(8,128)(2,1)} fusion(bf16[256,2048]{1,0:T(8,128)(2,1)} %reduce-scatter.17.cloned.1.call-done, bf16[256,2048]{1,0:T(8,128)(2,1)} %reduce-scatter.13.cloned.1.call-done, bf16[256,2048]{1,0:T(8,128)(2,1)} %reduce-scatter.9.cloned.1.call-done), kind=kLoop, calls=%fused_computation.33 | loop fusion | flops 9437184 | bytes 6291456 | tf_op jit(solution)/shard_map/concatenate | solution.py:75
  (34 shorter events, 4.9 us)
Async XLA Ops:
  6.5 70.1 %all-gather.3.cloned.1.call-start = ((), (), s32[]{:S(2)}) async-start(), calls=%async_computation.12 | async-start | bytes 2949120 | tf_op jit(solution)/shard_map/all_gather | solution.py:39
  14.2 8.3 %copy-start = (bf16[1024,1280]{0,1:T(8,128)(2,1)}, bf16[1024,1280]{0,1:T(8,128)(2,1)S(1)}, u32[]{:S(2)}) copy-start(bf16[1024,1280]{0,1:T(8,128)(2,1)S(1)} %fusion.8) | copy-start | bytes 7864324
  22.5 102.2 %reduce-scatter.15.cloned.1.call-start = ((), (), s32[]{:S(2)}) async-start(), calls=%async_computation.10 | async-start | bytes 6291456 | tf_op jit(solution)/shard_map/reduce_scatter | solution.py:72
  30.2 5.0 %copy-start.1 = (bf16[1024,1280]{0,1:T(8,128)(2,1)S(1)}, bf16[1024,1280]{0,1:T(8,128)(2,1)}, u32[]{:S(2)}) copy-start(bf16[1024,1280]{0,1:T(8,128)(2,1)} %copy.24) | copy-start | bytes 7864324
  76.6 3.5 %copy-start.2 = (f32[10,1024,128]{1,2,0:T(8,128)S(1)}, f32[10,1024,128]{1,2,0:T(8,128)}, u32[]{:S(2)}) copy-start(f32[10,1024,128]{1,2,0:T(8,128)} %fusion) | copy-start | bytes 15728644
  79.2 2.4 slice-start
  80.1 1.7 slice-start.1
  80.1 1.7 copy-start.4
  103.5 1.7 copy-start.3
  103.5 28.2 %reduce-scatter.11.cloned.1.call-start = ((), (), s32[]{:S(2)}) async-start(), calls=%async_computation.8 | async-start | bytes 6291456 | tf_op jit(solution)/shard_map/reduce_scatter | solution.py:72
  114.8 32.4 %reduce-scatter.7.cloned.1.call-start = ((), (), s32[]{:S(2)}) async-start(), calls=%async_computation.6 | async-start | bytes 6291456 | tf_op jit(solution)/shard_map/reduce_scatter | solution.py:72
  124.7 57.5 %reduce-scatter.17.cloned.1.call-start = ((), (), s32[]{:S(2)}) async-start(), calls=%async_computation.11 | async-start | bytes 3145728 | tf_op jit(solution)/shard_map/reduce_scatter | solution.py:73
  125.2 91.0 %reduce-scatter.13.cloned.1.call-start = ((), (), s32[]{:S(2)}) async-start(), calls=%async_computation.9 | async-start | bytes 3145728 | tf_op jit(solution)/shard_map/reduce_scatter | solution.py:73
  131.7 118.7 %reduce-scatter.9.cloned.1.call-start = ((), (), s32[]{:S(2)}) async-start(), calls=%async_computation.7 | async-start | bytes 3145728 | tf_op jit(solution)/shard_map/reduce_scatter | solution.py:73
Sparse Core Ops, SparseCore 0:
  22.6 53.9 all-gather.2
  103.6 12.4 reduce-scatter.14
  118.4 13.2 reduce-scatter.10
  133.9 13.3 reduce-scatter.6
  149.3 32.8 reduce-scatter.16
  184.3 31.8 reduce-scatter.12
  218.5 31.8 reduce-scatter.8

commit v2 on v1

v2 whole, which is shorter than its diff:
```python
import jax
import jax.numpy as jnp
import numpy as np
from jax import lax
from jax.sharding import Mesh
from jax.sharding import PartitionSpec as P

HD = 128
COLUMN_CHUNKS = 3


epsilon = 1e-05


def split_bf16(x):
    hi = x.astype(jnp.bfloat16)
    lo = (x - hi.astype(jnp.float32)).astype(jnp.bfloat16)
    return hi, lo


def shift(block, axis, distance):
    size = lax.axis_size(axis)
    return lax.ppermute(block, axis, [(i, i + distance) for i in range(size) if i + distance < size])


def swap(block, axis):
    return lax.ppermute(block, axis, [(0, 1), (1, 0)])


def exclusive_prefix(state, axis):
    inclusive = state
    exclusive = jnp.zeros_like(state)
    distance = 1
    while distance < lax.axis_size(axis):
        arrived = shift(inclusive.astype(jnp.bfloat16), axis, distance).astype(jnp.float32)
        exclusive = exclusive + arrived
        inclusive = inclusive + arrived
        distance *= 2
    return exclusive


def project_and_reduce(mixed_rows, out_weight):
    tokens, columns = mixed_rows.shape
    ty_size = lax.axis_size("ty")
    tc_size = lax.axis_size("tc")
    block = tokens // (ty_size * tc_size)
    width = out_weight.shape[1]

    def product(rows):
        return jnp.dot(rows, out_weight, preferred_element_type=jnp.float32).astype(jnp.bfloat16)

    if ty_size != 2 or tc_size != 2:
        ordered = (
            mixed_rows.reshape(ty_size, tc_size, block, columns)
            .transpose(1, 0, 2, 3)
            .reshape(tokens, columns)
        )
        part = product(ordered)
        part = lax.psum_scatter(part, "tc", scatter_dimension=0, tiled=True)
        return lax.psum_scatter(part, "ty", scatter_dimension=0, tiled=True)

    ty = lax.axis_index("ty")
    tc = lax.axis_index("tc")

    def rows_of(owner_ty, owner_tc):
        start = (owner_ty * tc_size + owner_tc) * block
        return lax.dynamic_slice_in_dim(mixed_rows, start, block, axis=0)

    chunk = width // COLUMN_CHUNKS
    across = []
    for c in range(COLUMN_CHUNKS):
        weight = out_weight[:, c * chunk:(c + 1) * chunk]
        partner_part = jnp.dot(
            rows_of(1 - ty, 1 - tc), weight, preferred_element_type=jnp.float32
        ).astype(jnp.bfloat16)
        from_partner = swap(partner_part, "tc")
        own_part = jnp.dot(rows_of(1 - ty, tc), weight, preferred_element_type=jnp.float32)
        chip_sum = (own_part.astype(jnp.bfloat16).astype(jnp.float32) + from_partner.astype(jnp.float32))
        across.append(swap(chip_sum.astype(jnp.bfloat16), "ty"))
    near = swap(product(rows_of(ty, 1 - tc)), "tc")
    mine = product(rows_of(ty, tc))
    far = jnp.concatenate(across, axis=1)
    total = mine.astype(jnp.float32) + near.astype(jnp.float32) + far.astype(jnp.float32)
    return total.astype(jnp.bfloat16)


def on_device(queries, keys, values, gates, gain, out_weight):
    tokens = queries.shape[0]
    columns = queries.shape[1]
    head_count = columns // HD
    key_act = (
        jax.nn.silu(keys.astype(jnp.float32)).astype(jnp.bfloat16).reshape(tokens, head_count, HD)
    )
    value_rows = values.reshape(tokens, head_count, HD)
    own_state = jnp.einsum("thd,the->hde", key_act, value_rows, preferred_element_type=jnp.float32)
    prefix = exclusive_prefix(own_state, "ctx")

    query_act = (
        jax.nn.silu(queries.astype(jnp.float32))
        .astype(jnp.bfloat16)
        .reshape(tokens, head_count, HD)
    )
    scores = jnp.einsum("thd,shd->hts", query_act, key_act, preferred_element_type=jnp.float32)
    causal = jnp.tril(jnp.ones((tokens, tokens), dtype=bool))
    scores = jnp.where(causal[None], scores, jnp.float32(0.0)).astype(jnp.bfloat16)
    local_part = jnp.einsum("hts,she->the", scores, value_rows, preferred_element_type=jnp.float32)
    prefix_hi, prefix_lo = split_bf16(prefix)
    remote_part = jnp.einsum(
        "thd,hde->the", query_act, prefix_hi, preferred_element_type=jnp.float32
    ) + jnp.einsum("thd,hde->the", query_act, prefix_lo, preferred_element_type=jnp.float32)
    attention = remote_part + local_part
    mean_sq = jnp.mean(attention * attention, axis=-1, keepdims=True)
    normed = attention * lax.rsqrt(mean_sq + epsilon) * gain.reshape(head_count, HD)
    gate_open = jax.nn.sigmoid(gates.astype(jnp.float32)).reshape(tokens, head_count, HD)
    mixed_rows = (normed * gate_open).astype(jnp.bfloat16).reshape(tokens, columns)
    return project_and_reduce(mixed_rows, out_weight)


def solution(mesh):
    ctx_size, tp_size = mesh.devices.shape
    split = Mesh(
        np.asarray(mesh.devices).reshape(ctx_size, tp_size // 2, 2), ("ctx", "ty", "tc")
    )
    tp = ("ty", "tc")
    return jax.shard_map(
        on_device,
        mesh=split,
        in_specs=(
            P("ctx", tp),
            P("ctx", tp),
            P("ctx", tp),
            P("ctx", tp),
            P(tp),
            P(tp, None),
        ),
        out_specs=P(("ctx",) + tp, None),
        check_vma=False,
    )
```

time: 263 us -> 183 us (0.70)
  waiting for transfers between devices: 149 us -> 73.8 us
  between operations: 13.6 us -> 0.2 us
  local copies, waits for them, and re-layouts: 28 us -> 17.1 us
  starting transfers between devices: 0.43 us -> 10.9 us
  matrix products: 51.2 us -> 58.6 us
  other arithmetic: 17.9 us -> 22.2 us
    reduce_scatter x6 -> x0, waiting for transfers between devices: 125 us -> none  [the longest x3 103 us: on_device(): part = lax.psum_scatter(part, 'ty', scatter_dimension=0, tiled=True)]
    ppermute x0 -> x10, waiting for transfers between devices: none -> 73.8 us  [the longest x7 61.5 us: swap(): return lax.ppermute(block, axis, [(0, 1), (1, 0)])]
    all_gather x1 -> x0, waiting for transfers between devices: 23.6 us -> none  [on_device(): lax.all_gather(own_state.astype(jnp.bfloat16), 'ctx', axis=0, tiled=False)]
    ppermute x0 -> x10, starting transfers between devices: none -> 10.9 us  [the longest x3 6.13 us: shift(): lax.ppermute(block, axis, [(i, i + distance) for i in range(size) if i +...]
    another operation x2 -> x0, local copies, waits for them, and re-layouts: 9.33 us -> none  [on_device(): mixed_rows.reshape(ty_size, tc_size, block, columns).transpose(1, 0, 2, 3)]
    dot_general x1, matrix products: 0.88 us -> 7 us  [on_device(): jnp.einsum('thd,hde->the', query_act, prefix_hi, preferred_element_type=j...]
    convert_element_type x0 -> x2, other arithmetic: none -> 3.71 us  [exclusive_prefix(): inclusive.astype(jnp.bfloat16)]
    concatenate x1 -> x0, other arithmetic: 3.17 us -> none  [on_device(): return jnp.concatenate(pieces, axis=1)]
  transfers between devices with their start and end apart: 7 -> 10, of which waited for: 6 -> 4; matrix products, arithmetic and copies ran while one was open for 19% -> 28% of each run, Pallas kernels for 0% -> 0%
where the time goes in v2:
time: 183 us
  waiting for transfers between devices  73.8 us (40%)
  matrix products  58.6 us (32%)
  other arithmetic  22.2 us (12%)
  local copies, waits for them, and re-layouts  17.1 us (9%)
  starting transfers between devices  10.9 us (6%)
    ppermute x7, waiting for transfers between devices, swap(): return lax.ppermute(block, axis, [(0, 1), (1, 0)])  61.5 us
    dot_general x2, matrix products, product(): jnp.dot(rows, out_weight, preferred_element_type=jnp.float32)  19.1 us
    unnamed x18, local copies, waits for them, and re-layouts  17.1 us
    dot_general x1, matrix products, on_device(): jnp.einsum('hts,she->the', scores, value_rows, preferred_element_type=jnp...  16.2 us
    ppermute x3, waiting for transfers between devices, shift(): lax.ppermute(block, axis, [(i, i + distance) for i in range(size) if i +...  12.3 us
    dot_general x3, matrix products, project_and_reduce(): jnp.dot(rows_of(1 - ty, tc), weight, preferred_element_type=jnp.float32)  7.8 us
    dot_general x1, matrix products, on_device(): jnp.einsum('thd,hde->the', query_act, prefix_hi, preferred_element_type=j...  7 us
    ppermute x3, starting transfers between devices, shift(): lax.ppermute(block, axis, [(i, i + distance) for i in range(size) if i +...  6.13 us
  transfers between devices with their start and end apart: 10, of which 4 were waited for; matrix products, arithmetic and copies ran while one was open for 28% of the time, Pallas kernels for 0%

profile of v2, /device:TPU:24, one launch (start us, length us, event | category | flops | bytes accessed | tf_op | source)
XLA Modules:
  0.0 182.8 jit_solution(14788778249031153325)
XLA Ops:
  0.0 3.0 %copy.16 = bf16[1024,1280]{0,1:T(8,128)(2,1)S(1)} copy(bf16[1024,1280]{1,0:T(8,128)(2,1)} %param.8) | data formatting | bytes 5242880 | tf_op args[2]
  3.0 5.0 %copy.15 = bf16[1024,1280]{0,1:T(8,128)(2,1)} copy(bf16[1024,1280]{1,0:T(8,128)(2,1)} %param.7) | data formatting | bytes 5242880 | tf_op args[1]
  8.0 3.3 %fusion.9 = bf16[1024,1280]{0,1:T(8,128)(2,1)S(1)} fusion(bf16[1024,1280]{0,1:T(8,128)(2,1)} %copy.15), kind=kLoop, calls=%fused_computation.16 | loop fusion | flops 7864320 | bytes 5242880 | tf_op jit(solution)/shard_map/convert_element_type | solution.py:92
  11.3 1.8 %fusion.90 = (bf16[10,128,128]{2,1,0:T(8,128)(2,1)}, f32[10,128,128]{2,1,0:T(8,128)S(1)}) fusion(bf16[1024,10,128]{0,2,1:T(8,128)(2,1)S(1)} %bitcast.27, bf16[1024,10,128]{0,2,1:T(8,128)(2,1)S(1)} %bitcast.25), kind=kOutput, calls=%fused_computation.77 | convolution fusion | flops 335708160 | bytes 6225920 | tf_op jit(solution)/shard_map/thd,the->hde/dot_general | solution.py:95
  13.2 3.4 %collective-permute-start = (bf16[10,128,128]{2,1,0:T(8,128)(2,1)}, bf16[10,128,128]{2,1,0:T(8,128)(2,1)}, u32[]{:S(2)}, u32[]{:S(2)}) collective-permute-start(bf16[10,128,128]{2,1,0:T(8,128)(2,1)} %get-tuple-element.5), channel_id=1, source_target_pairs={{0,4},{4,8},{8,12},{12,16},{16,20},{20,24},{24,28},{1,5},{5,9},{9,... | collective-permute-start | bytes 983048 | tf_op jit(solution)/shard_map/ppermute | solution.py:23
  16.6 4.5 %copy.18 = bf16[1024,1280]{0,1:T(8,128)(2,1)} copy(bf16[1024,1280]{1,0:T(8,128)(2,1)} %param.6) | data formatting | bytes 5242880 | tf_op args[0]
  21.1 3.3 %fusion.13 = bf16[1024,1280]{0,1:T(8,128)(2,1)S(1)} fusion(bf16[1024,1280]{0,1:T(8,128)(2,1)} %copy.18), kind=kLoop, calls=%fused_computation.20 | loop fusion | flops 7864320 | bytes 5242880 | tf_op jit(solution)/shard_map/convert_element_type | solution.py:100
  25.7 1.8 fusion.77
  28.8 16.2 %fusion = f32[10,1024,128]{1,2,0:T(8,128)} fusion(bf16[1024,10,128]{0,2,1:T(8,128)(2,1)} %bitcast.26, pred[1024,1024]{1,0:T(8,128)(4,1)} %iota_compare_fusion, bf16[1024,10,128]{0,2,1:T(8,128)(2,1)S(1)} %bitcast.19, bf16[1024,10,128]{0,2,1:T(8,128)(2,1)} %bitcast.28), kind=kOutput, calls=%fused_computation.1 | convolution fusion | flops 5389680640 | bytes 14155776 | tf_op jit(solution)/shard_map/hts,she->the/dot_general | solution.py:106
  45.0 4.4 %copy.23 = bf16[1024,1280]{0,1:T(8,128)(2,1)} copy(bf16[1024,1280]{1,0:T(8,128)(2,1)} %param.9) | data formatting | bytes 5242880 | tf_op args[3]
  49.4 1.9 %fusion.54 = bf16[10,128,128]{2,1,0:T(8,128)(2,1)} fusion(bf16[10,128,128]{2,1,0:T(8,128)(2,1)} %collective-permute-done.1, f32[10,128,128]{2,1,0:T(8,128)S(1)} %get-tuple-element.6, bf16[10,128,128]{2,1,0:T(8,128)(2,1)} %collective-permute-done), kind=kLoop, calls=%fused_computation.54 | loop fusion | flops 819200 | bytes 1638400 | tf_op jit(solution)/shard_map/convert_element_type | solution.py:35
  52.8 5.5 %add_divide_fusion = f32[1024,1280]{0,1:T(8,128)} fusion(bf16[1024,1280]{0,1:T(8,128)(2,1)} %copy.23), kind=kLoop, calls=%fused_computation.23 | loop fusion | flops 5242880 | bytes 7864320 | tf_op jit(solution)/shard_map/div | solution.py:114
  58.2 12.3 %collective-permute-done.2 = bf16[10,128,128]{2,1,0:T(8,128)(2,1)S(1)} collective-permute-done((bf16[10,128,128]{2,1,0:T(8,128)(2,1)}, bf16[10,128,128]{2,1,0:T(8,128)(2,1)S(1)}, u32[]{:S(2)}, u32[]{:S(2)}) %collective-permute-start.2) | collective-permute-done | bytes 327712 | tf_op jit(solution)/shard_map/ppermute | solution.py:23
  70.5 2.0 %fusion.80 = f32[10,128,1024]{2,1,0:T(8,128)S(1)} fusion(bf16[1024,10,128]{0,2,1:T(8,128)(2,1)S(1)} %bitcast.20, bf16[10,128,128]{2,1,0:T(8,128)(2,1)S(1)} %collective-permute-done.2, bf16[10,128,128]{2,1,0:T(8,128)(2,1)} %collective-permute-done.1, bf16[10,128,128]{2,1,0:T(8,128)(2,1)} %collective-permute-done), kind=kOutput, calls=%fused_computation.66 | convolution fusion | flops 337018880 | bytes 8847360 | tf_op jit(solution)/shard_map/thd,hde->the/dot_general | solution.py:110
  72.5 7.0 %multiply_reduce_fusion = (f32[1024,10]{0,1:T(8,128)S(1)}, f32[1024,10,128]{0,2,1:T(8,128)}) fusion(f32[10,1024,128]{1,2,0:T(8,128)} %fusion, f32[10,128,1024]{2,1,0:T(8,128)S(1)} %fusion.80, bf16[1024,10,128]{0,2,1:T(8,128)(2,1)S(1)} %bitcast.21, bf16[10,128,128]{2,1,0:T(8,128)(2,1)S(1)} %collective-permute-done.2, ...), kind=kOutput, calls=%fused_computation.24 | convolution fusion | flops 341760000 | bytes 19374080 | tf_op jit(solution)/shard_map/thd,hde->the/dot_general | solution.py:108
  79.5 5.2 %multiply_convert_fusion = bf16[1024,10,128]{0,2,1:T(8,128)(2,1)S(1)} fusion(f32[1024,10,128]{0,2,1:T(8,128)} %bitcast.24, f32[1024,10,128]{0,2,1:T(8,128)} %get-tuple-element.8, f32[10,128]{1,0:T(8,128)S(1)} %bitcast.37, f32[1024,10]{0,1:T(8,128)S(1)} %add_rsqrt_fusion), kind=kLoop, calls=%fused_computation.22 | loop fusion | flops 5242880 | bytes 13153280 | tf_op jit(solution)/shard_map/convert_element_type | solution.py:115
  86.5 5.9 %convolution_convert_fusion = bf16[256,6144]{1,0:T(8,128)(2,1)} fusion(bf16[1280,6144]{1,0:T(8,128)(2,1)S(1)} %bitcast.23, bf16[1024,1280]{0,1:T(8,128)(2,1)S(1)} %bitcast.30, s32[]{:T(128)S(6)} %select_n.24), kind=kOutput, calls=%fused_computation.5 | convolution fusion | flops 4028104704 | bytes 19529732 | tf_op jit(solution)/shard_map/dot_general | solution.py:50
  96.7 2.5 %add_convert_fusion.1 = bf16[256,2048]{1,0:T(8,128)(2,1)} fusion(bf16[256,2048]{1,0:T(8,128)(2,1)S(1)} %collective-permute-done.8, bf16[1280,6144]{1,0:T(8,128)(2,1)S(1)} %bitcast.23, bf16[1024,1280]{0,1:T(8,128)(2,1)S(1)} %bitcast.33, s32[]{:T(128)S(6)} %select_n.25), kind=kOutput, calls=%fused_computation.47 | convolution fusion | flops 1344798720 | bytes 7995396 | tf_op jit(solution)/shard_map/dot_general | solution.py:77
  100.8 2.6 %add_convert_fusion.2 = bf16[256,2048]{1,0:T(8,128)(2,1)} fusion(bf16[256,2048]{1,0:T(8,128)(2,1)S(1)} %collective-permute-done.6, bf16[1280,6144]{1,0:T(8,128)(2,1)S(1)} %bitcast.23, bf16[1024,1280]{0,1:T(8,128)(2,1)S(1)} %bitcast.34, s32[]{:T(128)S(6)} %select_n.25), kind=kOutput, calls=%fused_computation.48 | convolution fusion | flops 1344798720 | bytes 7995396 | tf_op jit(solution)/shard_map/dot_general | solution.py:77
  104.1 2.6 %add_convert_fusion.3 = bf16[256,2048]{1,0:T(8,128)(2,1)} fusion(bf16[256,2048]{1,0:T(8,128)(2,1)S(1)} %collective-permute-done.4, bf16[1280,6144]{1,0:T(8,128)(2,1)S(1)} %bitcast.23, bf16[1024,1280]{0,1:T(8,128)(2,1)S(1)} %bitcast.35, s32[]{:T(128)S(6)} %select_n.25), kind=kOutput, calls=%fused_computation.49 | convolution fusion | flops 1344798720 | bytes 7995396 | tf_op jit(solution)/shard_map/dot_general | solution.py:77
  108.1 17.5 %collective-permute-done.9 = bf16[256,2048]{1,0:T(8,128)(2,1)} collective-permute-done((bf16[256,2048]{1,0:T(8,128)(2,1)}, bf16[256,2048]{1,0:T(8,128)(2,1)}, u32[]{:S(2)}, u32[]{:S(2)}) %collective-permute-start.9) | collective-permute-done | bytes 1048608 | tf_op jit(solution)/shard_map/ppermute | solution.py:27
  125.6 22.5 %collective-permute-done.7 = bf16[256,2048]{1,0:T(8,128)(2,1)} collective-permute-done((bf16[256,2048]{1,0:T(8,128)(2,1)}, bf16[256,2048]{1,0:T(8,128)(2,1)}, u32[]{:S(2)}, u32[]{:S(2)}) %collective-permute-start.7) | collective-permute-done | bytes 1048608 | tf_op jit(solution)/shard_map/ppermute | solution.py:27
  148.0 21.6 %collective-permute-done.5 = bf16[256,2048]{1,0:T(8,128)(2,1)} collective-permute-done((bf16[256,2048]{1,0:T(8,128)(2,1)}, bf16[256,2048]{1,0:T(8,128)(2,1)}, u32[]{:S(2)}, u32[]{:S(2)}) %collective-permute-start.5) | collective-permute-done | bytes 1048608 | tf_op jit(solution)/shard_map/ppermute | solution.py:27
  169.6 13.2 %add_convert_fusion = bf16[256,6144]{1,0:T(8,128)(2,1)} fusion(bf16[256,6144]{1,0:T(8,128)(2,1)} %collective-permute-done.3, bf16[256,2048]{1,0:T(8,128)(2,1)} %collective-permute-done.9, bf16[256,2048]{1,0:T(8,128)(2,1)} %collective-permute-done.7, bf16[256,2048]{1,0:T(8,128)(2,1)} %collective-permute-done.5, bf16[1280,6144]{1,0:T(8,128)(2,1)} %param.11, ...), kind=kOutput, calls=%fused_computation.12 | convolution fusion | flops 4045406208 | bytes 25821188 | tf_op jit(solution)/shard_map/dot_general | solution.py:50
  (35 shorter events, 13.8 us)
Async XLA Ops:
  3.0 8.3 %copy-start = (bf16[1024,1280]{0,1:T(8,128)(2,1)}, bf16[1024,1280]{0,1:T(8,128)(2,1)S(1)}, u32[]{:S(2)}) copy-start(bf16[1024,1280]{0,1:T(8,128)(2,1)S(1)} %copy.16) | copy-start | bytes 7864324
  11.3 1.9 %copy-start.1 = (bf16[1024,1280]{0,1:T(8,128)(2,1)}, bf16[1024,1280]{0,1:T(8,128)(2,1)S(1)}, u32[]{:S(2)}) copy-start(bf16[1024,1280]{0,1:T(8,128)(2,1)S(1)} %fusion.9) | copy-start | bytes 7864324
  13.2 12.5 %collective-permute-start = (bf16[10,128,128]{2,1,0:T(8,128)(2,1)}, bf16[10,128,128]{2,1,0:T(8,128)(2,1)}, u32[]{:S(2)}, u32[]{:S(2)}) collective-permute-start(bf16[10,128,128]{2,1,0:T(8,128)(2,1)} %get-tuple-element.5), channel_id=1, source_target_pairs={{0,4},{4,8},{8,12},{12,16},{16,20},{20,24},{24,28},{1,5},{5,9},{9,... | collective-permute-start | bytes 983048 | tf_op jit(solution)/shard_map/ppermute | solution.py:23
  27.5 21.9 %collective-permute-start.1 = (bf16[10,128,128]{2,1,0:T(8,128)(2,1)}, bf16[10,128,128]{2,1,0:T(8,128)(2,1)}, u32[]{:S(2)}, u32[]{:S(2)}) collective-permute-start(bf16[10,128,128]{2,1,0:T(8,128)(2,1)} %fusion.77), channel_id=1, source_target_pairs={{0,8},{4,12},{8,16},{12,20},{16,24},{20,28},{1,9},{5,13},{9,17},{1... | collective-permute-start | bytes 983048 | tf_op jit(solution)/shard_map/ppermute | solution.py:23
  51.3 19.2 %collective-permute-start.2 = (bf16[10,128,128]{2,1,0:T(8,128)(2,1)}, bf16[10,128,128]{2,1,0:T(8,128)(2,1)S(1)}, u32[]{:S(2)}, u32[]{:S(2)}) collective-permute-start(bf16[10,128,128]{2,1,0:T(8,128)(2,1)} %fusion.54), channel_id=1, source_target_pairs={{0,16},{4,20},{8,24},{12,28},{1,17},{5,21},{9,25},{13,29},{2,18},{... | collective-permute-start | bytes 983048 | tf_op jit(solution)/shard_map/ppermute | solution.py:23
  72.4 7.1 %copy-start.2 = (f32[1280]{0:T(1024)S(1)}, f32[1280]{0:T(1024)}, u32[]{:S(2)}) copy-start(f32[1280]{0:T(1024)} %param.10) | copy-start | bytes 15364
  72.5 12.2 %slice-start = ((s8[15728640]{0:T(1024)(128)(4,1)}), s8[4194304]{0:T(1024)(128)(4,1)S(1)}, s32[]{:S(2)}) async-start(s8[15728640]{0:T(1024)(128)(4,1)} %bitcast.22), calls=%async_computation | async-start | bytes 8388608
  72.5 12.2 %slice-start.1 = ((s8[15728640]{0:T(1024)(128)(4,1)}), s8[4194304]{0:T(1024)(128)(4,1)S(1)}, s32[]{:S(2)}) async-start(s8[15728640]{0:T(1024)(128)(4,1)} %bitcast.22), calls=%async_computation.1 | async-start | bytes 8388608
  72.5 12.2 %slice-start.2 = ((s8[15728640]{0:T(1024)(128)(4,1)}), s8[4194304]{0:T(1024)(128)(4,1)S(1)}, s32[]{:S(2)}) async-start(s8[15728640]{0:T(1024)(128)(4,1)} %bitcast.22), calls=%async_computation.2 | async-start | bytes 8388608
  79.5 5.4 %slice-start.3 = ((s8[15728640]{0:T(1024)(128)(4,1)}), s8[3145728]{0:T(1024)(128)(4,1)S(1)}, s32[]{:S(2)}) async-start(s8[15728640]{0:T(1024)(128)(4,1)} %bitcast.22), calls=%async_computation.3 | async-start | bytes 6291456
  86.5 10.2 %collective-permute-start.8 = (bf16[256,2048]{1,0:T(8,128)(2,1)S(1)}, bf16[256,2048]{1,0:T(8,128)(2,1)S(1)}, u32[]{:S(2)}, u32[]{:S(2)}) collective-permute-start(bf16[256,2048]{1,0:T(8,128)(2,1)S(1)} %fusion.50), channel_id=1, source_target_pairs={{0,1},{1,0},{2,3},{3,2},{4,5},{5,4},{6,7},{7,6},{8,9},{9,8},{10,11... | collective-permute-start | bytes 3145736 | tf_op jit(solution)/shard_map/ppermute | solution.py:27
  92.5 77.1 %collective-permute-start.3 = (bf16[256,6144]{1,0:T(8,128)(2,1)}, bf16[256,6144]{1,0:T(8,128)(2,1)}, u32[]{:S(2)}, u32[]{:S(2)}) collective-permute-start(bf16[256,6144]{1,0:T(8,128)(2,1)} %convolution_convert_fusion), channel_id=1, source_target_pairs={{0,1},{1,0},{2,3},{3,2},{4,5},{5,4},{6,7},{7,6},{8,9},{9,8},{10,11... | collective-permute-start | bytes 9437192 | tf_op jit(solution)/shard_map/ppermute | solution.py:27
  94.5 6.3 %collective-permute-start.6 = (bf16[256,2048]{1,0:T(8,128)(2,1)S(1)}, bf16[256,2048]{1,0:T(8,128)(2,1)S(1)}, u32[]{:S(2)}, u32[]{:S(2)}) collective-permute-start(bf16[256,2048]{1,0:T(8,128)(2,1)S(1)} %fusion.41), channel_id=1, source_target_pairs={{0,1},{1,0},{2,3},{3,2},{4,5},{5,4},{6,7},{7,6},{8,9},{9,8},{10,11... | collective-permute-start | bytes 3145736 | tf_op jit(solution)/shard_map/ppermute | solution.py:27
  96.2 7.9 %collective-permute-start.4 = (bf16[256,2048]{1,0:T(8,128)(2,1)S(1)}, bf16[256,2048]{1,0:T(8,128)(2,1)S(1)}, u32[]{:S(2)}, u32[]{:S(2)}) collective-permute-start(bf16[256,2048]{1,0:T(8,128)(2,1)S(1)} %fusion.32), channel_id=1, source_target_pairs={{0,1},{1,0},{2,3},{3,2},{4,5},{5,4},{6,7},{7,6},{8,9},{9,8},{10,11... | collective-permute-start | bytes 3145736 | tf_op jit(solution)/shard_map/ppermute | solution.py:27
  99.2 26.3 %collective-permute-start.9 = (bf16[256,2048]{1,0:T(8,128)(2,1)}, bf16[256,2048]{1,0:T(8,128)(2,1)}, u32[]{:S(2)}, u32[]{:S(2)}) collective-permute-start(bf16[256,2048]{1,0:T(8,128)(2,1)} %add_convert_fusion.1), channel_id=1, source_target_pairs={{0,2},{2,0},{1,3},{3,1},{4,6},{6,4},{5,7},{7,5},{8,10},{10,8},{9,1... | collective-permute-start | bytes 3145736 | tf_op jit(solution)/shard_map/ppermute | solution.py:27
  103.4 44.6 %collective-permute-start.7 = (bf16[256,2048]{1,0:T(8,128)(2,1)}, bf16[256,2048]{1,0:T(8,128)(2,1)}, u32[]{:S(2)}, u32[]{:S(2)}) collective-permute-start(bf16[256,2048]{1,0:T(8,128)(2,1)} %add_convert_fusion.2), channel_id=1, source_target_pairs={{0,2},{2,0},{1,3},{3,1},{4,6},{6,4},{5,7},{7,5},{8,10},{10,8},{9,1... | collective-permute-start | bytes 3145736 | tf_op jit(solution)/shard_map/ppermute | solution.py:27
  106.7 62.9 %collective-permute-start.5 = (bf16[256,2048]{1,0:T(8,128)(2,1)}, bf16[256,2048]{1,0:T(8,128)(2,1)}, u32[]{:S(2)}, u32[]{:S(2)}) collective-permute-start(bf16[256,2048]{1,0:T(8,128)(2,1)} %add_convert_fusion.3), channel_id=1, source_target_pairs={{0,2},{2,0},{1,3},{3,1},{4,6},{6,4},{5,7},{7,5},{8,10},{10,8},{9,1... | collective-permute-start | bytes 3145736 | tf_op jit(solution)/shard_map/ppermute | solution.py:27

commit v3 on v2

--- a/solution.py
+++ b/solution.py
@@ -78,7 +78,7 @@
         chip_sum = (own_part.astype(jnp.bfloat16).astype(jnp.float32) + from_partner.astype(jnp.float32))
         across.append(swap(chip_sum.astype(jnp.bfloat16), "ty"))
     near = swap(product(rows_of(ty, 1 - tc)), "tc")
-    mine = product(rows_of(ty, tc))
+    mine = lax.optimization_barrier(product(rows_of(ty, tc)))
     far = jnp.concatenate(across, axis=1)
     total = mine.astype(jnp.float32) + near.astype(jnp.float32) + far.astype(jnp.float32)
     return total.astype(jnp.bfloat16)

time: 183 us -> 174 us (0.951)
  matrix products: 58.6 us -> 50 us
  waiting for transfers between devices: 73.8 us -> 69.1 us
  other arithmetic: 22.2 us -> 26.2 us
    dot_general x2, matrix products: 19.1 us -> 10.6 us  [product(): jnp.dot(rows, out_weight, preferred_element_type=jnp.float32)]
    ppermute x7, waiting for transfers between devices: 61.5 us -> 56.9 us  [swap(): return lax.ppermute(block, axis, [(0, 1), (1, 0)])]
    convert_element_type x0 -> x1, other arithmetic: none -> 4.03 us  [project_and_reduce(): return total.astype(jnp.bfloat16)]
  transfers between devices with their start and end apart: 10 -> 10, of which waited for: 4 -> 4; matrix products, arithmetic and copies ran while one was open for 28% -> 33% of each run, Pallas kernels for 0% -> 0%
where the time goes in v3:
time: 174 us
  waiting for transfers between devices  69.1 us (40%)
  matrix products  50 us (29%)
  other arithmetic  26.2 us (15%)
  local copies, waits for them, and re-layouts  17.1 us (10%)
  starting transfers between devices  10.8 us (6%)
    ppermute x7, waiting for transfers between devices, swap(): return lax.ppermute(block, axis, [(0, 1), (1, 0)])  56.9 us
    unnamed x18, local copies, waits for them, and re-layouts  17.1 us
    dot_general x1, matrix products, on_device(): jnp.einsum('hts,she->the', scores, value_rows, preferred_element_type=jnp...  16.2 us
    ppermute x3, waiting for transfers between devices, shift(): lax.ppermute(block, axis, [(i, i + distance) for i in range(size) if i +...  12.3 us
    dot_general x2, matrix products, product(): jnp.dot(rows, out_weight, preferred_element_type=jnp.float32)  10.6 us
    dot_general x3, matrix products, project_and_reduce(): jnp.dot(rows_of(1 - ty, tc), weight, preferred_element_type=jnp.float32)  7.7 us
    dot_general x1, matrix products, on_device(): jnp.einsum('thd,hde->the', query_act, prefix_hi, preferred_element_type=j...  7 us
    ppermute x3, starting transfers between devices, shift(): lax.ppermute(block, axis, [(i, i + distance) for i in range(size) if i +...  6.13 us
  transfers between devices with their start and end apart: 10, of which 4 were waited for; matrix products, arithmetic and copies ran while one was open for 33% of the time, Pallas kernels for 0%

profile of v3, /device:TPU:24, one launch (start us, length us, event | category | flops | bytes accessed | tf_op | source)
XLA Modules:
  0.0 173.6 jit_solution(392669743070459751)
XLA Ops:
  0.0 3.0 %copy.16 = bf16[1024,1280]{0,1:T(8,128)(2,1)S(1)} copy(bf16[1024,1280]{1,0:T(8,128)(2,1)} %param.8) | data formatting | bytes 5242880 | tf_op args[2]
  3.0 5.0 %copy.15 = bf16[1024,1280]{0,1:T(8,128)(2,1)} copy(bf16[1024,1280]{1,0:T(8,128)(2,1)} %param.7) | data formatting | bytes 5242880 | tf_op args[1]
  8.0 3.3 %fusion.8 = bf16[1024,1280]{0,1:T(8,128)(2,1)S(1)} fusion(bf16[1024,1280]{0,1:T(8,128)(2,1)} %copy.15), kind=kLoop, calls=%fused_computation.15 | loop fusion | flops 7864320 | bytes 5242880 | tf_op jit(solution)/shard_map/convert_element_type | solution.py:92
  11.3 1.8 %fusion.87 = (bf16[10,128,128]{2,1,0:T(8,128)(2,1)}, f32[10,128,128]{2,1,0:T(8,128)S(1)}) fusion(bf16[1024,10,128]{0,2,1:T(8,128)(2,1)S(1)} %bitcast.27, bf16[1024,10,128]{0,2,1:T(8,128)(2,1)S(1)} %bitcast.25), kind=kOutput, calls=%fused_computation.76 | convolution fusion | flops 335708160 | bytes 6225920 | tf_op jit(solution)/shard_map/thd,the->hde/dot_general | solution.py:95
  13.2 3.4 %collective-permute-start = (bf16[10,128,128]{2,1,0:T(8,128)(2,1)}, bf16[10,128,128]{2,1,0:T(8,128)(2,1)}, u32[]{:S(2)}, u32[]{:S(2)}) collective-permute-start(bf16[10,128,128]{2,1,0:T(8,128)(2,1)} %get-tuple-element.5), channel_id=1, source_target_pairs={{0,4},{4,8},{8,12},{12,16},{16,20},{20,24},{24,28},{1,5},{5,9},{9,... | collective-permute-start | bytes 983048 | tf_op jit(solution)/shard_map/ppermute | solution.py:23
  16.6 4.5 %copy.18 = bf16[1024,1280]{0,1:T(8,128)(2,1)} copy(bf16[1024,1280]{1,0:T(8,128)(2,1)} %param.6) | data formatting | bytes 5242880 | tf_op args[0]
  21.1 3.3 %fusion.12 = bf16[1024,1280]{0,1:T(8,128)(2,1)S(1)} fusion(bf16[1024,1280]{0,1:T(8,128)(2,1)} %copy.18), kind=kLoop, calls=%fused_computation.19 | loop fusion | flops 7864320 | bytes 5242880 | tf_op jit(solution)/shard_map/convert_element_type | solution.py:100
  28.8 16.2 %fusion = f32[10,1024,128]{1,2,0:T(8,128)} fusion(bf16[1024,10,128]{0,2,1:T(8,128)(2,1)} %bitcast.26, pred[1024,1024]{1,0:T(8,128)(4,1)} %iota_compare_fusion, bf16[1024,10,128]{0,2,1:T(8,128)(2,1)S(1)} %bitcast.21, bf16[1024,10,128]{0,2,1:T(8,128)(2,1)} %bitcast.28), kind=kOutput, calls=%fused_computation.1 | convolution fusion | flops 5389680640 | bytes 14155776 | tf_op jit(solution)/shard_map/hts,she->the/dot_general | solution.py:106
  45.0 4.4 %copy.23 = bf16[1024,1280]{0,1:T(8,128)(2,1)} copy(bf16[1024,1280]{1,0:T(8,128)(2,1)} %param.9) | data formatting | bytes 5242880 | tf_op args[3]
  49.4 1.9 %fusion.53 = bf16[10,128,128]{2,1,0:T(8,128)(2,1)} fusion(bf16[10,128,128]{2,1,0:T(8,128)(2,1)} %collective-permute-done.1, f32[10,128,128]{2,1,0:T(8,128)S(1)} %get-tuple-element.6, bf16[10,128,128]{2,1,0:T(8,128)(2,1)} %collective-permute-done), kind=kLoop, calls=%fused_computation.53 | loop fusion | flops 819200 | bytes 1638400 | tf_op jit(solution)/shard_map/convert_element_type | solution.py:35
  52.8 5.5 %add_divide_fusion = f32[1024,1280]{0,1:T(8,128)} fusion(bf16[1024,1280]{0,1:T(8,128)(2,1)} %copy.23), kind=kLoop, calls=%fused_computation.22 | loop fusion | flops 5242880 | bytes 7864320 | tf_op jit(solution)/shard_map/div | solution.py:114
  58.2 12.3 %collective-permute-done.2 = bf16[10,128,128]{2,1,0:T(8,128)(2,1)S(1)} collective-permute-done((bf16[10,128,128]{2,1,0:T(8,128)(2,1)}, bf16[10,128,128]{2,1,0:T(8,128)(2,1)S(1)}, u32[]{:S(2)}, u32[]{:S(2)}) %collective-permute-start.2) | collective-permute-done | bytes 327712 | tf_op jit(solution)/shard_map/ppermute | solution.py:23
  70.5 2.0 %fusion.77 = f32[10,128,1024]{2,1,0:T(8,128)S(1)} fusion(bf16[1024,10,128]{0,2,1:T(8,128)(2,1)S(1)} %bitcast.22, bf16[10,128,128]{2,1,0:T(8,128)(2,1)S(1)} %collective-permute-done.2, bf16[10,128,128]{2,1,0:T(8,128)(2,1)} %collective-permute-done.1, bf16[10,128,128]{2,1,0:T(8,128)(2,1)} %collective-permute-done), kind=kOutput, calls=%fused_computation.65 | convolution fusion | flops 337018880 | bytes 8847360 | tf_op jit(solution)/shard_map/thd,hde->the/dot_general | solution.py:110
  72.5 7.0 %multiply_reduce_fusion = (f32[1024,10]{0,1:T(8,128)S(1)}, f32[1024,10,128]{0,2,1:T(8,128)}) fusion(f32[10,1024,128]{1,2,0:T(8,128)} %fusion, f32[10,128,1024]{2,1,0:T(8,128)S(1)} %fusion.77, bf16[1024,10,128]{0,2,1:T(8,128)(2,1)S(1)} %bitcast.23, bf16[10,128,128]{2,1,0:T(8,128)(2,1)S(1)} %collective-permute-done.2, ...), kind=kOutput, calls=%fused_computation.23 | convolution fusion | flops 341760000 | bytes 19374080 | tf_op jit(solution)/shard_map/thd,hde->the/dot_general | solution.py:108
  79.5 5.2 %multiply_convert_fusion = bf16[1024,10,128]{0,2,1:T(8,128)(2,1)S(1)} fusion(f32[1024,10,128]{0,2,1:T(8,128)} %bitcast.24, f32[1024,10,128]{0,2,1:T(8,128)} %get-tuple-element.8, f32[10,128]{1,0:T(8,128)S(1)} %bitcast.37, f32[1024,10]{0,1:T(8,128)S(1)} %add_rsqrt_fusion), kind=kLoop, calls=%fused_computation.21 | loop fusion | flops 5242880 | bytes 13153280 | tf_op jit(solution)/shard_map/convert_element_type | solution.py:115
  86.6 5.9 %convolution_convert_fusion = bf16[256,6144]{1,0:T(8,128)(2,1)} fusion(bf16[1280,6144]{1,0:T(8,128)(2,1)S(1)} %bitcast.20, bf16[1024,1280]{0,1:T(8,128)(2,1)S(1)} %bitcast.30, s32[]{:T(128)S(6)} %select_n.24), kind=kOutput, calls=%fused_computation.5 | convolution fusion | flops 4028104704 | bytes 19529732 | tf_op jit(solution)/shard_map/dot_general | solution.py:50
  96.7 2.6 %add_convert_fusion.1 = bf16[256,2048]{1,0:T(8,128)(2,1)} fusion(bf16[256,2048]{1,0:T(8,128)(2,1)S(1)} %collective-permute-done.8, bf16[1280,6144]{1,0:T(8,128)(2,1)S(1)} %bitcast.20, bf16[1024,1280]{0,1:T(8,128)(2,1)S(1)} %bitcast.33, s32[]{:T(128)S(6)} %select_n.25), kind=kOutput, calls=%fused_computation.46 | convolution fusion | flops 1344798720 | bytes 7995396 | tf_op jit(solution)/shard_map/dot_general | solution.py:77
  100.8 2.6 %add_convert_fusion.2 = bf16[256,2048]{1,0:T(8,128)(2,1)} fusion(bf16[256,2048]{1,0:T(8,128)(2,1)S(1)} %collective-permute-done.6, bf16[1280,6144]{1,0:T(8,128)(2,1)S(1)} %bitcast.20, bf16[1024,1280]{0,1:T(8,128)(2,1)S(1)} %bitcast.34, s32[]{:T(128)S(6)} %select_n.25), kind=kOutput, calls=%fused_computation.47 | convolution fusion | flops 1344798720 | bytes 7995396 | tf_op jit(solution)/shard_map/dot_general | solution.py:77
  104.0 2.6 %add_convert_fusion.3 = bf16[256,2048]{1,0:T(8,128)(2,1)} fusion(bf16[256,2048]{1,0:T(8,128)(2,1)S(1)} %collective-permute-done.4, bf16[1280,6144]{1,0:T(8,128)(2,1)S(1)} %bitcast.20, bf16[1024,1280]{0,1:T(8,128)(2,1)S(1)} %bitcast.35, s32[]{:T(128)S(6)} %select_n.25), kind=kOutput, calls=%fused_computation.48 | convolution fusion | flops 1344798720 | bytes 7995396 | tf_op jit(solution)/shard_map/dot_general | solution.py:77
  107.9 4.7 %convolution_convert_fusion.1 = bf16[256,6144]{1,0:T(8,128)(2,1)S(1)} fusion(bf16[1280,6144]{1,0:T(8,128)(2,1)S(1)} %bitcast.20, bf16[1024,1280]{0,1:T(8,128)(2,1)S(1)} %bitcast.36, s32[]{:T(128)S(6)} %select_n.23), kind=kOutput, calls=%fused_computation.6 | convolution fusion | flops 4028104704 | bytes 19529732 | tf_op jit(solution)/shard_map/dot_general | solution.py:50
  112.7 12.9 %collective-permute-done.9 = bf16[256,2048]{1,0:T(8,128)(2,1)S(1)} collective-permute-done((bf16[256,2048]{1,0:T(8,128)(2,1)}, bf16[256,2048]{1,0:T(8,128)(2,1)S(1)}, u32[]{:S(2)}, u32[]{:S(2)}) %collective-permute-start.9) | collective-permute-done | bytes 1048608 | tf_op jit(solution)/shard_map/ppermute | solution.py:27
  125.5 22.5 %collective-permute-done.7 = bf16[256,2048]{1,0:T(8,128)(2,1)S(1)} collective-permute-done((bf16[256,2048]{1,0:T(8,128)(2,1)}, bf16[256,2048]{1,0:T(8,128)(2,1)S(1)}, u32[]{:S(2)}, u32[]{:S(2)}) %collective-permute-start.7) | collective-permute-done | bytes 1048608 | tf_op jit(solution)/shard_map/ppermute | solution.py:27
  148.0 21.5 %collective-permute-done.5 = bf16[256,2048]{1,0:T(8,128)(2,1)S(1)} collective-permute-done((bf16[256,2048]{1,0:T(8,128)(2,1)}, bf16[256,2048]{1,0:T(8,128)(2,1)S(1)}, u32[]{:S(2)}, u32[]{:S(2)}) %collective-permute-start.5) | collective-permute-done | bytes 1048608 | tf_op jit(solution)/shard_map/ppermute | solution.py:27
  169.5 4.0 %add_convert_fusion = bf16[256,6144]{1,0:T(8,128)(2,1)} fusion(bf16[256,6144]{1,0:T(8,128)(2,1)} %collective-permute-done.3, bf16[256,6144]{1,0:T(8,128)(2,1)S(1)} %convolution_convert_fusion.1, bf16[256,2048]{1,0:T(8,128)(2,1)S(1)} %collective-permute-done.9, bf16[256,2048]{1,0:T(8,128)(2,1)S(1)} %collective-permute-done.7, ...), kind=kLoop, calls=%fused_computation.11 | loop fusion | flops 17301504 | bytes 12582912 | tf_op jit(solution)/shard_map/convert_element_type | solution.py:84
  (36 shorter events, 15.5 us)
Async XLA Ops:
  3.0 8.3 %copy-start = (bf16[1024,1280]{0,1:T(8,128)(2,1)}, bf16[1024,1280]{0,1:T(8,128)(2,1)S(1)}, u32[]{:S(2)}) copy-start(bf16[1024,1280]{0,1:T(8,128)(2,1)S(1)} %copy.16) | copy-start | bytes 7864324
  11.3 1.9 %copy-start.1 = (bf16[1024,1280]{0,1:T(8,128)(2,1)}, bf16[1024,1280]{0,1:T(8,128)(2,1)S(1)}, u32[]{:S(2)}) copy-start(bf16[1024,1280]{0,1:T(8,128)(2,1)S(1)} %fusion.8) | copy-start | bytes 7864324
  13.2 12.5 %collective-permute-start = (bf16[10,128,128]{2,1,0:T(8,128)(2,1)}, bf16[10,128,128]{2,1,0:T(8,128)(2,1)}, u32[]{:S(2)}, u32[]{:S(2)}) collective-permute-start(bf16[10,128,128]{2,1,0:T(8,128)(2,1)} %get-tuple-element.5), channel_id=1, source_target_pairs={{0,4},{4,8},{8,12},{12,16},{16,20},{20,24},{24,28},{1,5},{5,9},{9,... | collective-permute-start | bytes 983048 | tf_op jit(solution)/shard_map/ppermute | solution.py:23
  27.5 21.9 %collective-permute-start.1 = (bf16[10,128,128]{2,1,0:T(8,128)(2,1)}, bf16[10,128,128]{2,1,0:T(8,128)(2,1)}, u32[]{:S(2)}, u32[]{:S(2)}) collective-permute-start(bf16[10,128,128]{2,1,0:T(8,128)(2,1)} %fusion.74), channel_id=1, source_target_pairs={{0,8},{4,12},{8,16},{12,20},{16,24},{20,28},{1,9},{5,13},{9,17},{1... | collective-permute-start | bytes 983048 | tf_op jit(solution)/shard_map/ppermute | solution.py:23
  51.3 19.2 %collective-permute-start.2 = (bf16[10,128,128]{2,1,0:T(8,128)(2,1)}, bf16[10,128,128]{2,1,0:T(8,128)(2,1)S(1)}, u32[]{:S(2)}, u32[]{:S(2)}) collective-permute-start(bf16[10,128,128]{2,1,0:T(8,128)(2,1)} %fusion.53), channel_id=1, source_target_pairs={{0,16},{4,20},{8,24},{12,28},{1,17},{5,21},{9,25},{13,29},{2,18},{... | collective-permute-start | bytes 983048 | tf_op jit(solution)/shard_map/ppermute | solution.py:23
  72.4 7.1 %copy-start.2 = (f32[1280]{0:T(1024)S(1)}, f32[1280]{0:T(1024)}, u32[]{:S(2)}) copy-start(f32[1280]{0:T(1024)} %param.10) | copy-start | bytes 15364
  72.5 12.2 %slice-start = ((s8[15728640]{0:T(1024)(128)(4,1)}), s8[4194304]{0:T(1024)(128)(4,1)S(1)}, s32[]{:S(2)}) async-start(s8[15728640]{0:T(1024)(128)(4,1)} %bitcast.19), calls=%async_computation | async-start | bytes 8388608
  72.5 12.2 %slice-start.1 = ((s8[15728640]{0:T(1024)(128)(4,1)}), s8[4194304]{0:T(1024)(128)(4,1)S(1)}, s32[]{:S(2)}) async-start(s8[15728640]{0:T(1024)(128)(4,1)} %bitcast.19), calls=%async_computation.1 | async-start | bytes 8388608
  72.5 12.2 %slice-start.2 = ((s8[15728640]{0:T(1024)(128)(4,1)}), s8[4194304]{0:T(1024)(128)(4,1)S(1)}, s32[]{:S(2)}) async-start(s8[15728640]{0:T(1024)(128)(4,1)} %bitcast.19), calls=%async_computation.2 | async-start | bytes 8388608
  79.5 5.4 %slice-start.3 = ((s8[15728640]{0:T(1024)(128)(4,1)}), s8[3145728]{0:T(1024)(128)(4,1)S(1)}, s32[]{:S(2)}) async-start(s8[15728640]{0:T(1024)(128)(4,1)} %bitcast.19), calls=%async_computation.3 | async-start | bytes 6291456
  86.5 10.2 %collective-permute-start.8 = (bf16[256,2048]{1,0:T(8,128)(2,1)S(1)}, bf16[256,2048]{1,0:T(8,128)(2,1)S(1)}, u32[]{:S(2)}, u32[]{:S(2)}) collective-permute-start(bf16[256,2048]{1,0:T(8,128)(2,1)S(1)} %fusion.49), channel_id=1, source_target_pairs={{0,1},{1,0},{2,3},{3,2},{4,5},{5,4},{6,7},{7,6},{8,9},{9,8},{10,11... | collective-permute-start | bytes 3145736 | tf_op jit(solution)/shard_map/ppermute | solution.py:27
  92.5 77.1 %collective-permute-start.3 = (bf16[256,6144]{1,0:T(8,128)(2,1)}, bf16[256,6144]{1,0:T(8,128)(2,1)}, u32[]{:S(2)}, u32[]{:S(2)}) collective-permute-start(bf16[256,6144]{1,0:T(8,128)(2,1)} %convolution_convert_fusion), channel_id=1, source_target_pairs={{0,1},{1,0},{2,3},{3,2},{4,5},{5,4},{6,7},{7,6},{8,9},{9,8},{10,11... | collective-permute-start | bytes 9437192 | tf_op jit(solution)/shard_map/ppermute | solution.py:27
  94.5 6.3 %collective-permute-start.6 = (bf16[256,2048]{1,0:T(8,128)(2,1)S(1)}, bf16[256,2048]{1,0:T(8,128)(2,1)S(1)}, u32[]{:S(2)}, u32[]{:S(2)}) collective-permute-start(bf16[256,2048]{1,0:T(8,128)(2,1)S(1)} %fusion.40), channel_id=1, source_target_pairs={{0,1},{1,0},{2,3},{3,2},{4,5},{5,4},{6,7},{7,6},{8,9},{9,8},{10,11... | collective-permute-start | bytes 3145736 | tf_op jit(solution)/shard_map/ppermute | solution.py:27
  96.2 7.8 %collective-permute-start.4 = (bf16[256,2048]{1,0:T(8,128)(2,1)S(1)}, bf16[256,2048]{1,0:T(8,128)(2,1)S(1)}, u32[]{:S(2)}, u32[]{:S(2)}) collective-permute-start(bf16[256,2048]{1,0:T(8,128)(2,1)S(1)} %fusion.31), channel_id=1, source_target_pairs={{0,1},{1,0},{2,3},{3,2},{4,5},{5,4},{6,7},{7,6},{8,9},{9,8},{10,11... | collective-permute-start | bytes 3145736 | tf_op jit(solution)/shard_map/ppermute | solution.py:27
  99.3 26.2 %collective-permute-start.9 = (bf16[256,2048]{1,0:T(8,128)(2,1)}, bf16[256,2048]{1,0:T(8,128)(2,1)S(1)}, u32[]{:S(2)}, u32[]{:S(2)}) collective-permute-start(bf16[256,2048]{1,0:T(8,128)(2,1)} %add_convert_fusion.1), channel_id=1, source_target_pairs={{0,2},{2,0},{1,3},{3,1},{4,6},{6,4},{5,7},{7,5},{8,10},{10,8},{9,1... | collective-permute-start | bytes 3145736 | tf_op jit(solution)/shard_map/ppermute | solution.py:27
  103.3 44.6 %collective-permute-start.7 = (bf16[256,2048]{1,0:T(8,128)(2,1)}, bf16[256,2048]{1,0:T(8,128)(2,1)S(1)}, u32[]{:S(2)}, u32[]{:S(2)}) collective-permute-start(bf16[256,2048]{1,0:T(8,128)(2,1)} %add_convert_fusion.2), channel_id=1, source_target_pairs={{0,2},{2,0},{1,3},{3,1},{4,6},{6,4},{5,7},{7,5},{8,10},{10,8},{9,1... | collective-permute-start | bytes 3145736 | tf_op jit(solution)/shard_map/ppermute | solution.py:27
  106.6 63.0 %collective-permute-start.5 = (bf16[256,2048]{1,0:T(8,128)(2,1)}, bf16[256,2048]{1,0:T(8,128)(2,1)S(1)}, u32[]{:S(2)}, u32[]{:S(2)}) collective-permute-start(bf16[256,2048]{1,0:T(8,128)(2,1)} %add_convert_fusion.3), channel_id=1, source_target_pairs={{0,2},{2,0},{1,3},{3,1},{4,6},{6,4},{5,7},{7,5},{8,10},{10,8},{9,1... | collective-permute-start | bytes 3145736 | tf_op jit(solution)/shard_map/ppermute | solution.py:27

commit v4 on v3

--- a/solution.py
+++ b/solution.py
@@ -2,14 +2,128 @@
 import jax.numpy as jnp
 import numpy as np
 from jax import lax
+from jax.experimental import pallas as pl
+from jax.experimental.pallas import tpu as pltpu
 from jax.sharding import Mesh
 from jax.sharding import PartitionSpec as P
 
 HD = 128
 COLUMN_CHUNKS = 3
+QUERY_TILE = 256
 
 
 epsilon = 1e-05
+
+
+def silu(x):
+    x = x.astype(jnp.float32)
+    return (x / (1.0 + jnp.exp(-x))).astype(jnp.bfloat16)
+
+
+def head_block(tokens):
+    return pl.BlockSpec((tokens, HD), lambda h: (0, h))
+
+
+def state_kernel(k_ref, v_ref, state_ref):
+    key_act = silu(k_ref[...])
+    state_ref[0] = lax.dot_general(
+        key_act, v_ref[...], (((0,), (0,)), ((), ())), preferred_element_type=jnp.float32
+    )
+
+
+def key_value_states(keys, values):
+    tokens, columns = keys.shape
+    heads = columns // HD
+    return pl.pallas_call(
+        state_kernel,
+        grid=(heads,),
+        in_specs=[head_block(tokens), head_block(tokens)],
+        out_specs=pl.BlockSpec((1, HD, HD), lambda h: (h, 0, 0)),
+        out_shape=jax.ShapeDtypeStruct((heads, HD, HD), jnp.float32),
+        cost_estimate=pl.CostEstimate(
+            flops=2 * tokens * HD * HD * heads,
+            transcendentals=tokens * columns,
+            bytes_accessed=4 * tokens * columns + 4 * heads * HD * HD,
+        ),
+    )(keys, values)
+
+
+def local_kernel(q_ref, k_ref, v_ref, out_ref):
+    tokens = q_ref.shape[0]
+    query_act = silu(q_ref[...])
+    key_act = silu(k_ref[...])
+    value_rows = v_ref[...]
+    for tile in range(tokens // QUERY_TILE):
+        seen = (tile + 1) * QUERY_TILE
+        scores = lax.dot_general(
+            query_act[tile * QUERY_TILE:seen],
+            key_act[:seen],
+            (((1,), (1,)), ((), ())),
+            preferred_element_type=jnp.float32,
+        )
+        row = lax.broadcasted_iota(jnp.int32, scores.shape, 0) + tile * QUERY_TILE
+        col = lax.broadcasted_iota(jnp.int32, scores.shape, 1)
+        scores = jnp.where(row >= col, scores, 0.0).astype(jnp.bfloat16)
+        out_ref[tile * QUERY_TILE:seen, :] = jnp.dot(
+            scores, value_rows[:seen], preferred_element_type=jnp.float32
+        )
+
+
+def local_attention(queries, keys, values):
+    tokens, columns = queries.shape
+    heads = columns // HD
+    tiles = tokens // QUERY_TILE
+    pairs = QUERY_TILE * QUERY_TILE * tiles * (tiles + 1) // 2
+    return pl.pallas_call(
+        local_kernel,
+        grid=(heads,),
+        in_specs=[head_block(tokens)] * 3,
+        out_specs=head_block(tokens),
+        out_shape=jax.ShapeDtypeStruct((tokens, columns), jnp.float32),
+        cost_estimate=pl.CostEstimate(
+            flops=4 * pairs * HD * heads,
+            transcendentals=2 * tokens * columns,
+            bytes_accessed=10 * tokens * columns,
+        ),
+    )(queries, keys, values)
+
+
+def mix_kernel(local_ref, q_ref, g_ref, hi_ref, lo_ref, gain_ref, out_ref):
+    query_act = silu(q_ref[...])
+    remote = jnp.dot(query_act, hi_ref[0], preferred_element_type=jnp.float32) + jnp.dot(
+        query_act, lo_ref[0], preferred_element_type=jnp.float32
+    )
+    attention = local_ref[...] + remote
+    mean_sq = jnp.mean(attention * attention, axis=-1, keepdims=True)
+    normed = attention * lax.rsqrt(mean_sq + epsilon) * gain_ref[...]
+    gates = g_ref[...].astype(jnp.float32)
+    gate_open = 1.0 / (1.0 + jnp.exp(-gates))
+    out_ref[...] = (normed * gate_open).astype(out_ref.dtype)
+
+
+def mix(local_part, queries, gates, prefix_hi, prefix_lo, gain):
+    tokens, columns = queries.shape
+    heads = columns // HD
+    state_block = pl.BlockSpec((1, HD, HD), lambda h: (h, 0, 0))
+    return pl.pallas_call(
+        mix_kernel,
+        grid=(heads,),
+        in_specs=[
+            head_block(tokens),
+            head_block(tokens),
+            head_block(tokens),
+            state_block,
+            state_block,
+            pl.BlockSpec((1, HD), lambda h: (0, h)),
+        ],
+        out_specs=head_block(tokens),
+        out_shape=jax.ShapeDtypeStruct((tokens, columns), jnp.bfloat16),
+        cost_estimate=pl.CostEstimate(
+            flops=4 * tokens * HD * HD * heads,
+            transcendentals=2 * tokens * columns,
+            bytes_accessed=10 * tokens * columns,
+        ),
+    )(local_part, queries, gates, prefix_hi, prefix_lo, gain.reshape(1, columns))
 
 
 def split_bf16(x):
@@ -85,34 +199,11 @@
 
 
 def on_device(queries, keys, values, gates, gain, out_weight):
-    tokens = queries.shape[0]
-    columns = queries.shape[1]
-    head_count = columns // HD
-    key_act = (
-        jax.nn.silu(keys.astype(jnp.float32)).astype(jnp.bfloat16).reshape(tokens, head_count, HD)
-    )
-    value_rows = values.reshape(tokens, head_count, HD)
-    own_state = jnp.einsum("thd,the->hde", key_act, value_rows, preferred_element_type=jnp.float32)
+    own_state = key_value_states(keys, values)
     prefix = exclusive_prefix(own_state, "ctx")
-
-    query_act = (
-        jax.nn.silu(queries.astype(jnp.float32))
-        .astype(jnp.bfloat16)
-        .reshape(tokens, head_count, HD)
-    )
-    scores = jnp.einsum("thd,shd->hts", query_act, key_act, preferred_element_type=jnp.float32)
-    causal = jnp.tril(jnp.ones((tokens, tokens), dtype=bool))
-    scores = jnp.where(causal[None], scores, jnp.float32(0.0)).astype(jnp.bfloat16)
-    local_part = jnp.einsum("hts,she->the", scores, value_rows, preferred_element_type=jnp.float32)
+    local_part = local_attention(queries, keys, values)
     prefix_hi, prefix_lo = split_bf16(prefix)
-    remote_part = jnp.einsum(
-        "thd,hde->the", query_act, prefix_hi, preferred_element_type=jnp.float32
-    ) + jnp.einsum("thd,hde->the", query_act, prefix_lo, preferred_element_type=jnp.float32)
-    attention = remote_part + local_part
-    mean_sq = jnp.mean(attention * attention, axis=-1, keepdims=True)
-    normed = attention * lax.rsqrt(mean_sq + epsilon) * gain.reshape(head_count, HD)
-    gate_open = jax.nn.sigmoid(gates.astype(jnp.float32)).reshape(tokens, head_count, HD)
-    mixed_rows = (normed * gate_open).astype(jnp.bfloat16).reshape(tokens, columns)
+    mixed_rows = mix(local_part, queries, gates, prefix_hi, prefix_lo, gain)
     return project_and_reduce(mixed_rows, out_weight)
 
 

time: 174 us -> 166 us (0.954)
  the two profiles are of different devices: /device:TPU:24 before, /device:TPU:0 now
where the time goes in v4:
time: 166 us; the launch traced here: 165 us
  waiting for transfers between devices  65.5 us (39%)
  matrix products  38 us (23%)
  Pallas kernels  32.9 us (20%)
  starting transfers between devices  20.5 us (12%)
  other arithmetic  7.15 us (4%)
    ppermute x7, waiting for transfers between devices, swap(): return lax.ppermute(block, axis, [(0, 1), (1, 0)])  52.4 us
    dot_general x2, matrix products, product(): jnp.dot(rows, out_weight, preferred_element_type=jnp.float32)  21.2 us
    ppermute x3, starting transfers between devices, shift(): lax.ppermute(block, axis, [(i, i + distance) for i in range(size) if i +...  15.7 us
    pallas_call x1, Pallas kernels, local_attention(): pl.pallas_call(local_kernel, grid=(heads,), in_specs=[head_block(tokens)]...  14 us
    ppermute x3, waiting for transfers between devices, shift(): lax.ppermute(block, axis, [(i, i + distance) for i in range(size) if i +...  13 us
    pallas_call x1, Pallas kernels, mix(): pl.pallas_call(mix_kernel, grid=(heads,), in_specs=[head_block(tokens), h...  10.5 us
    dot_general x3, matrix products, project_and_reduce(): jnp.dot(rows_of(1 - ty, 1 - tc), weight, preferred_element_type=jnp.float32)  10 us
    pallas_call x1, Pallas kernels, key_value_states(): pl.pallas_call(state_kernel, grid=(heads,), in_specs=[head_block(tokens),...  8.37 us
  transfers between devices with their start and end apart: 10, of which 5 were waited for; matrix products, arithmetic and copies ran while one was open for 18% of the time, Pallas kernels for 8%

profile of v4, /device:TPU:0, one launch (start us, length us, event | category | flops | bytes accessed | tf_op | source)
XLA Modules:
  0.0 164.9 jit_solution(17717784083246705923)
XLA Ops:
  0.0 8.4 %shard_map.65 = f32[10,128,128]{2,1,0:T(8,128)} custom-call(bf16[1024,1280]{1,0:T(8,128)(2,1)} %k_ref.3, bf16[1024,1280]{1,0:T(8,128)(2,1)} %v_ref.3), custom_call_target="tpu_custom_call" | custom-call | flops 335544320 | bytes 5898240 | tf_op jit(solution)/shard_map/pallas_call | solution.py:37
  9.5 4.9 %collective-permute-start = (bf16[10,128,128]{2,1,0:T(8,128)(2,1)S(1)}, bf16[10,128,128]{2,1,0:T(8,128)(2,1)S(1)}, u32[]{:S(2)}, u32[]{:S(2)}) collective-permute-start(bf16[10,128,128]{2,1,0:T(8,128)(2,1)S(1)} %convert_element_type.90), channel_id=1, source_target_pairs={{0,4},{4,8},{8,12},{12,16},{16,20},{20,24},{24,28},{1,5},{5,9},{9,... | collective-permute-start | bytes 983048 | tf_op jit(solution)/shard_map/ppermute | solution.py:137
  14.4 6.9 %collective-permute-done = bf16[10,128,128]{2,1,0:T(8,128)(2,1)S(1)} collective-permute-done((bf16[10,128,128]{2,1,0:T(8,128)(2,1)S(1)}, bf16[10,128,128]{2,1,0:T(8,128)(2,1)S(1)}, u32[]{:S(2)}, u32[]{:S(2)}) %collective-permute-start) | collective-permute-done | bytes 327712 | tf_op jit(solution)/shard_map/ppermute | solution.py:137
  21.4 1.2 fusion.61
  22.5 5.4 %collective-permute-start.1 = (bf16[10,128,128]{2,1,0:T(8,128)(2,1)S(1)}, bf16[10,128,128]{2,1,0:T(8,128)(2,1)S(1)}, u32[]{:S(2)}, u32[]{:S(2)}) collective-permute-start(bf16[10,128,128]{2,1,0:T(8,128)(2,1)S(1)} %fusion.61), channel_id=1, source_target_pairs={{0,8},{4,12},{8,16},{12,20},{16,24},{20,28},{1,9},{5,13},{9,17},{1... | collective-permute-start | bytes 983048 | tf_op jit(solution)/shard_map/ppermute | solution.py:137
  27.9 6.1 %collective-permute-done.1 = bf16[10,128,128]{2,1,0:T(8,128)(2,1)S(1)} collective-permute-done((bf16[10,128,128]{2,1,0:T(8,128)(2,1)S(1)}, bf16[10,128,128]{2,1,0:T(8,128)(2,1)S(1)}, u32[]{:S(2)}, u32[]{:S(2)}) %collective-permute-start.1) | collective-permute-done | bytes 327712 | tf_op jit(solution)/shard_map/ppermute | solution.py:137
  34.0 1.2 fusion.40
  35.2 5.4 %collective-permute-start.2 = (bf16[10,128,128]{2,1,0:T(8,128)(2,1)S(1)}, bf16[10,128,128]{2,1,0:T(8,128)(2,1)S(1)}, u32[]{:S(2)}, u32[]{:S(2)}) collective-permute-start(bf16[10,128,128]{2,1,0:T(8,128)(2,1)S(1)} %fusion.40), channel_id=1, source_target_pairs={{0,16},{4,20},{8,24},{12,28},{1,17},{5,21},{9,25},{13,29},{2,18},{... | collective-permute-start | bytes 983048 | tf_op jit(solution)/shard_map/ppermute | solution.py:137
  41.2 14.0 %shard_map.64.local_ref = f32[1024,1280]{1,0:T(8,128)} custom-call(bf16[1024,1280]{1,0:T(8,128)(2,1)} %q_ref.3, bf16[1024,1280]{1,0:T(8,128)(2,1)} %k_ref.3, bf16[1024,1280]{1,0:T(8,128)(2,1)} %v_ref.3), custom_call_target="tpu_custom_call" | custom-call | flops 3355443200 | bytes 13107200 | tf_op jit(solution)/shard_map/pallas_call | solution.py:77
  56.3 10.5 %shard_map.66 = bf16[1024,1280]{1,0:T(8,128)(2,1)} custom-call(f32[1024,1280]{1,0:T(8,128)} %shard_map.64.local_ref, bf16[1024,1280]{1,0:T(8,128)(2,1)} %q_ref.3, bf16[1024,1280]{1,0:T(8,128)(2,1)} %g_ref.1, bf16[10,128,128]{2,1,0:T(8,128)(2,1)} %get-tuple-element.6.hi_ref, bf16[10,128,128]{2,1,0:T(8,128)(2,1)} %get-tuple-element.5.lo_ref, ...), custom_call_target="tpu_custom_call" | custom-call | flops 671088640 | bytes 13107200 | tf_op jit(solution)/shard_map/pallas_call | solution.py:108
  66.8 4.4 %fusion.18 = bf16[256,2048]{1,0:T(8,128)(2,1)S(1)} fusion(bf16[1280,6144]{1,0:T(8,128)(2,1)} %param.11, bf16[1024,1280]{1,0:T(8,128)(2,1)} %shard_map.66, s32[]{:T(128)S(6)} %select_n.19), kind=kOutput, calls=%fused_computation.17 | convolution fusion | flops 1342701568 | bytes 6946820 | tf_op jit(solution)/shard_map/dot_general | solution.py:187
  71.2 4.2 %fusion.27 = bf16[256,2048]{1,0:T(8,128)(2,1)S(1)} fusion(bf16[1280,6144]{1,0:T(8,128)(2,1)} %param.11, bf16[1024,1280]{1,0:T(8,128)(2,1)S(1)} %copy-done, s32[]{:T(128)S(6)} %select_n.19), kind=kOutput, calls=%fused_computation.20 | convolution fusion | flops 1342701568 | bytes 6946820 | tf_op jit(solution)/shard_map/dot_general | solution.py:187
  76.0 11.3 %convolution_convert_fusion = bf16[256,6144]{1,0:T(8,128)(2,1)} fusion(bf16[1280,6144]{1,0:T(8,128)(2,1)} %param.11, bf16[1024,1280]{1,0:T(8,128)(2,1)S(1)} %copy-done, s32[]{:T(128)S(6)} %select_n.17), kind=kOutput, calls=%fused_computation | convolution fusion | flops 4028104704 | bytes 19529732 | tf_op jit(solution)/shard_map/dot_general | solution.py:164
  87.3 1.5 fusion.36
  89.4 2.7 %add_convert_fusion.3 = bf16[256,2048]{1,0:T(8,128)(2,1)S(1)} fusion(bf16[256,2048]{1,0:T(8,128)(2,1)} %collective-permute-done.4, bf16[1280,6144]{1,0:T(8,128)(2,1)S(1)} %bitcast.3, bf16[1024,1280]{1,0:T(8,128)(2,1)S(1)} %copy-done, s32[]{:T(128)S(6)} %select_n.18), kind=kOutput, calls=%fused_computation.26 | convolution fusion | flops 1344798720 | bytes 7995396 | tf_op jit(solution)/shard_map/dot_general | solution.py:191
  92.2 1.6 collective-permute-start.5
  93.8 2.5 %add_convert_fusion.2 = bf16[256,2048]{1,0:T(8,128)(2,1)} fusion(bf16[256,2048]{1,0:T(8,128)(2,1)S(1)} %collective-permute-done.6, bf16[1280,6144]{1,0:T(8,128)(2,1)S(1)} %bitcast.3, bf16[1024,1280]{1,0:T(8,128)(2,1)S(1)} %copy-done, s32[]{:T(128)S(6)} %select_n.18), kind=kOutput, calls=%fused_computation.25 | convolution fusion | flops 1344798720 | bytes 7995396 | tf_op jit(solution)/shard_map/dot_general | solution.py:191
  96.8 1.5 add_convert_fusion.1
  98.3 1.6 collective-permute-start.9
  99.9 9.9 %convolution_convert_fusion.1 = bf16[256,6144]{1,0:T(8,128)(2,1)S(1)} fusion(bf16[1280,6144]{1,0:T(8,128)(2,1)} %param.11, bf16[1024,1280]{1,0:T(8,128)(2,1)S(1)} %copy-done, s32[]{:T(128)S(6)} %select_n.16), kind=kOutput, calls=%fused_computation.1 | convolution fusion | flops 4028104704 | bytes 19529732 | tf_op jit(solution)/shard_map/dot_general | solution.py:164
  109.8 8.4 %collective-permute-done.5 = bf16[256,2048]{1,0:T(8,128)(2,1)S(1)} collective-permute-done((bf16[256,2048]{1,0:T(8,128)(2,1)S(1)}, bf16[256,2048]{1,0:T(8,128)(2,1)S(1)}, u32[]{:S(2)}, u32[]{:S(2)}) %collective-permute-start.5) | collective-permute-done | bytes 1048608 | tf_op jit(solution)/shard_map/ppermute | solution.py:141
  118.3 22.5 %collective-permute-done.7 = bf16[256,2048]{1,0:T(8,128)(2,1)S(1)} collective-permute-done((bf16[256,2048]{1,0:T(8,128)(2,1)}, bf16[256,2048]{1,0:T(8,128)(2,1)S(1)}, u32[]{:S(2)}, u32[]{:S(2)}) %collective-permute-start.7) | collective-permute-done | bytes 1048608 | tf_op jit(solution)/shard_map/ppermute | solution.py:141
  140.7 21.5 %collective-permute-done.9 = bf16[256,2048]{1,0:T(8,128)(2,1)S(1)} collective-permute-done((bf16[256,2048]{1,0:T(8,128)(2,1)S(1)}, bf16[256,2048]{1,0:T(8,128)(2,1)S(1)}, u32[]{:S(2)}, u32[]{:S(2)}) %collective-permute-start.9) | collective-permute-done | bytes 1048608 | tf_op jit(solution)/shard_map/ppermute | solution.py:141
  162.3 2.6 %add_convert_fusion = bf16[256,6144]{1,0:T(8,128)(2,1)} fusion(bf16[256,6144]{1,0:T(8,128)(2,1)S(1)} %collective-permute-done.3, bf16[256,6144]{1,0:T(8,128)(2,1)S(1)} %convolution_convert_fusion.1, bf16[256,2048]{1,0:T(8,128)(2,1)S(1)} %collective-permute-done.9, bf16[256,2048]{1,0:T(8,128)(2,1)S(1)} %collective-permute-done.7, ...), kind=kLoop, calls=%fused_computation.2 | loop fusion | flops 17301504 | bytes 12582912 | tf_op jit(solution)/shard_map/convert_element_type | solution.py:198
  (26 shorter events, 4.5 us)
Async XLA Ops:
  8.4 32.3 %copy-start.1 = (f32[1280]{0:T(1024)S(1)}, f32[1280]{0:T(1024)}, u32[]{:S(2)}) copy-start(f32[1280]{0:T(1024)} %param.10) | copy-start | bytes 15364
  9.5 11.8 %collective-permute-start = (bf16[10,128,128]{2,1,0:T(8,128)(2,1)S(1)}, bf16[10,128,128]{2,1,0:T(8,128)(2,1)S(1)}, u32[]{:S(2)}, u32[]{:S(2)}) collective-permute-start(bf16[10,128,128]{2,1,0:T(8,128)(2,1)S(1)} %convert_element_type.90), channel_id=1, source_target_pairs={{0,4},{4,8},{8,12},{12,16},{16,20},{20,24},{24,28},{1,5},{5,9},{9,... | collective-permute-start | bytes 983048 | tf_op jit(solution)/shard_map/ppermute | solution.py:137
  22.5 11.5 %collective-permute-start.1 = (bf16[10,128,128]{2,1,0:T(8,128)(2,1)S(1)}, bf16[10,128,128]{2,1,0:T(8,128)(2,1)S(1)}, u32[]{:S(2)}, u32[]{:S(2)}) collective-permute-start(bf16[10,128,128]{2,1,0:T(8,128)(2,1)S(1)} %fusion.61), channel_id=1, source_target_pairs={{0,8},{4,12},{8,16},{12,20},{16,24},{20,28},{1,9},{5,13},{9,17},{1... | collective-permute-start | bytes 983048 | tf_op jit(solution)/shard_map/ppermute | solution.py:137
  35.2 20.0 %collective-permute-start.2 = (bf16[10,128,128]{2,1,0:T(8,128)(2,1)S(1)}, bf16[10,128,128]{2,1,0:T(8,128)(2,1)S(1)}, u32[]{:S(2)}, u32[]{:S(2)}) collective-permute-start(bf16[10,128,128]{2,1,0:T(8,128)(2,1)S(1)} %fusion.40), channel_id=1, source_target_pairs={{0,16},{4,20},{8,24},{12,28},{1,17},{5,21},{9,25},{13,29},{2,18},{... | collective-permute-start | bytes 983048 | tf_op jit(solution)/shard_map/ppermute | solution.py:137
  66.8 4.4 %copy-start = (bf16[1024,1280]{1,0:T(8,128)(2,1)S(1)}, bf16[1024,1280]{1,0:T(8,128)(2,1)}, u32[]{:S(2)}) copy-start(bf16[1024,1280]{1,0:T(8,128)(2,1)} %shard_map.66) | copy-start | bytes 7864324
  71.2 16.1 %slice-start = ((s8[15728640]{0:T(1024)(128)(4,1)}), s8[4194304]{0:T(1024)(128)(4,1)S(1)}, s32[]{:S(2)}) async-start(s8[15728640]{0:T(1024)(128)(4,1)} %bitcast.2), calls=%async_computation | async-start | bytes 8388608
  71.2 16.1 %slice-start.1 = ((s8[15728640]{0:T(1024)(128)(4,1)}), s8[4194304]{0:T(1024)(128)(4,1)S(1)}, s32[]{:S(2)}) async-start(s8[15728640]{0:T(1024)(128)(4,1)} %bitcast.2), calls=%async_computation.1 | async-start | bytes 8388608
  75.4 11.9 %slice-start.2 = ((s8[15728640]{0:T(1024)(128)(4,1)}), s8[4194304]{0:T(1024)(128)(4,1)S(1)}, s32[]{:S(2)}) async-start(s8[15728640]{0:T(1024)(128)(4,1)} %bitcast.2), calls=%async_computation.2 | async-start | bytes 8388608
  75.4 11.9 %slice-start.3 = ((s8[15728640]{0:T(1024)(128)(4,1)}), s8[3145728]{0:T(1024)(128)(4,1)S(1)}, s32[]{:S(2)}) async-start(s8[15728640]{0:T(1024)(128)(4,1)} %bitcast.2), calls=%async_computation.3 | async-start | bytes 6291456
  75.4 14.0 %collective-permute-start.4 = (bf16[256,2048]{1,0:T(8,128)(2,1)S(1)}, bf16[256,2048]{1,0:T(8,128)(2,1)}, u32[]{:S(2)}, u32[]{:S(2)}) collective-permute-start(bf16[256,2048]{1,0:T(8,128)(2,1)S(1)} %fusion.18), channel_id=1, source_target_pairs={{0,1},{1,0},{2,3},{3,2},{4,5},{5,4},{6,7},{7,6},{8,9},{9,8},{10,11... | collective-permute-start | bytes 3145736 | tf_op jit(solution)/shard_map/ppermute | solution.py:141
  75.5 18.3 %collective-permute-start.6 = (bf16[256,2048]{1,0:T(8,128)(2,1)S(1)}, bf16[256,2048]{1,0:T(8,128)(2,1)S(1)}, u32[]{:S(2)}, u32[]{:S(2)}) collective-permute-start(bf16[256,2048]{1,0:T(8,128)(2,1)S(1)} %fusion.27), channel_id=1, source_target_pairs={{0,1},{1,0},{2,3},{3,2},{4,5},{5,4},{6,7},{7,6},{8,9},{9,8},{10,11... | collective-permute-start | bytes 3145736 | tf_op jit(solution)/shard_map/ppermute | solution.py:141
  87.3 75.0 %collective-permute-start.3 = (bf16[256,6144]{1,0:T(8,128)(2,1)}, bf16[256,6144]{1,0:T(8,128)(2,1)S(1)}, u32[]{:S(2)}, u32[]{:S(2)}) collective-permute-start(bf16[256,6144]{1,0:T(8,128)(2,1)} %convolution_convert_fusion), channel_id=1, source_target_pairs={{0,1},{1,0},{2,3},{3,2},{4,5},{5,4},{6,7},{7,6},{8,9},{9,8},{10,11... | collective-permute-start | bytes 9437192 | tf_op jit(solution)/shard_map/ppermute | solution.py:141
  88.9 7.9 %collective-permute-start.8 = (bf16[256,2048]{1,0:T(8,128)(2,1)S(1)}, bf16[256,2048]{1,0:T(8,128)(2,1)S(1)}, u32[]{:S(2)}, u32[]{:S(2)}) collective-permute-start(bf16[256,2048]{1,0:T(8,128)(2,1)S(1)} %fusion.36), channel_id=1, source_target_pairs={{0,1},{1,0},{2,3},{3,2},{4,5},{5,4},{6,7},{7,6},{8,9},{9,8},{10,11... | collective-permute-start | bytes 3145736 | tf_op jit(solution)/shard_map/ppermute | solution.py:141
  92.2 26.1 %collective-permute-start.5 = (bf16[256,2048]{1,0:T(8,128)(2,1)S(1)}, bf16[256,2048]{1,0:T(8,128)(2,1)S(1)}, u32[]{:S(2)}, u32[]{:S(2)}) collective-permute-start(bf16[256,2048]{1,0:T(8,128)(2,1)S(1)} %add_convert_fusion.3), channel_id=1, source_target_pairs={{0,2},{2,0},{1,3},{3,1},{4,6},{6,4},{5,7},{7,5},{8,10},{10,8},{9,1... | collective-permute-start | bytes 3145736 | tf_op jit(solution)/shard_map/ppermute | solution.py:141
  96.3 44.5 %collective-permute-start.7 = (bf16[256,2048]{1,0:T(8,128)(2,1)}, bf16[256,2048]{1,0:T(8,128)(2,1)S(1)}, u32[]{:S(2)}, u32[]{:S(2)}) collective-permute-start(bf16[256,2048]{1,0:T(8,128)(2,1)} %add_convert_fusion.2), channel_id=1, source_target_pairs={{0,2},{2,0},{1,3},{3,1},{4,6},{6,4},{5,7},{7,5},{8,10},{10,8},{9,1... | collective-permute-start | bytes 3145736 | tf_op jit(solution)/shard_map/ppermute | solution.py:141
  98.3 64.0 %collective-permute-start.9 = (bf16[256,2048]{1,0:T(8,128)(2,1)S(1)}, bf16[256,2048]{1,0:T(8,128)(2,1)S(1)}, u32[]{:S(2)}, u32[]{:S(2)}) collective-permute-start(bf16[256,2048]{1,0:T(8,128)(2,1)S(1)} %add_convert_fusion.1), channel_id=1, source_target_pairs={{0,2},{2,0},{1,3},{3,1},{4,6},{6,4},{5,7},{7,5},{8,10},{10,8},{9,1... | collective-permute-start | bytes 3145736 | tf_op jit(solution)/shard_map/ppermute | solution.py:141

commit v5 on v4

--- a/solution.py
+++ b/solution.py
@@ -10,6 +10,7 @@
 HD = 128
 COLUMN_CHUNKS = 3
 QUERY_TILE = 256
+ROW_TILE = 256
 
 
 epsilon = 1e-05
@@ -25,10 +26,22 @@
 
 
 def state_kernel(k_ref, v_ref, state_ref):
+    @pl.when(pl.program_id(0) == 0)
+    def _():
+        state_ref[...] = jnp.zeros_like(state_ref)
+
     key_act = silu(k_ref[...])
-    state_ref[0] = lax.dot_general(
-        key_act, v_ref[...], (((0,), (0,)), ((), ())), preferred_element_type=jnp.float32
-    )
+    value_rows = v_ref[...]
+    for h in range(state_ref.shape[0]):
+        heads = slice(h * HD, (h + 1) * HD)
+        state_ref[h] += lax.dot_general(
+            key_act[:, heads], value_rows[:, heads], (((0,), (0,)), ((), ())),
+            preferred_element_type=jnp.float32,
+        )
+
+
+def row_block(columns):
+    return pl.BlockSpec((ROW_TILE, columns), lambda i: (i, 0))
 
 
 def key_value_states(keys, values):
@@ -36,9 +49,9 @@
     heads = columns // HD
     return pl.pallas_call(
         state_kernel,
-        grid=(heads,),
-        in_specs=[head_block(tokens), head_block(tokens)],
-        out_specs=pl.BlockSpec((1, HD, HD), lambda h: (h, 0, 0)),
+        grid=(tokens // ROW_TILE,),
+        in_specs=[row_block(columns), row_block(columns)],
+        out_specs=pl.BlockSpec((heads, HD, HD), lambda i: (0, 0, 0)),
         out_shape=jax.ShapeDtypeStruct((heads, HD, HD), jnp.float32),
         cost_estimate=pl.CostEstimate(
             flops=2 * tokens * HD * HD * heads,
@@ -90,33 +103,35 @@
 
 def mix_kernel(local_ref, q_ref, g_ref, hi_ref, lo_ref, gain_ref, out_ref):
     query_act = silu(q_ref[...])
-    remote = jnp.dot(query_act, hi_ref[0], preferred_element_type=jnp.float32) + jnp.dot(
-        query_act, lo_ref[0], preferred_element_type=jnp.float32
-    )
-    attention = local_ref[...] + remote
-    mean_sq = jnp.mean(attention * attention, axis=-1, keepdims=True)
-    normed = attention * lax.rsqrt(mean_sq + epsilon) * gain_ref[...]
     gates = g_ref[...].astype(jnp.float32)
     gate_open = 1.0 / (1.0 + jnp.exp(-gates))
-    out_ref[...] = (normed * gate_open).astype(out_ref.dtype)
+    for h in range(hi_ref.shape[0]):
+        heads = slice(h * HD, (h + 1) * HD)
+        remote = jnp.dot(query_act[:, heads], hi_ref[h], preferred_element_type=jnp.float32) + jnp.dot(
+            query_act[:, heads], lo_ref[h], preferred_element_type=jnp.float32
+        )
+        attention = local_ref[:, heads] + remote
+        mean_sq = jnp.mean(attention * attention, axis=-1, keepdims=True)
+        normed = attention * lax.rsqrt(mean_sq + epsilon) * gain_ref[:, heads]
+        out_ref[:, heads] = (normed * gate_open[:, heads]).astype(out_ref.dtype)
 
 
 def mix(local_part, queries, gates, prefix_hi, prefix_lo, gain):
     tokens, columns = queries.shape
     heads = columns // HD
-    state_block = pl.BlockSpec((1, HD, HD), lambda h: (h, 0, 0))
+    whole_state = pl.BlockSpec((heads, HD, HD), lambda i: (0, 0, 0))
     return pl.pallas_call(
         mix_kernel,
-        grid=(heads,),
+        grid=(tokens // ROW_TILE,),
         in_specs=[
-            head_block(tokens),
-            head_block(tokens),
-            head_block(tokens),
-            state_block,
-            state_block,
-            pl.BlockSpec((1, HD), lambda h: (0, h)),
+            row_block(columns),
+            row_block(columns),
+            row_block(columns),
+            whole_state,
+            whole_state,
+            pl.BlockSpec((1, columns), lambda i: (0, 0)),
         ],
-        out_specs=head_block(tokens),
+        out_specs=row_block(columns),
         out_shape=jax.ShapeDtypeStruct((tokens, columns), jnp.bfloat16),
         cost_estimate=pl.CostEstimate(
             flops=4 * tokens * HD * HD * heads,
@@ -181,7 +196,8 @@
         return lax.dynamic_slice_in_dim(mixed_rows, start, block, axis=0)
 
     chunk = width // COLUMN_CHUNKS
-    across = []
+    chip_sums = []
+    near_parts = []
     for c in range(COLUMN_CHUNKS):
         weight = out_weight[:, c * chunk:(c + 1) * chunk]
         partner_part = jnp.dot(
@@ -190,10 +206,16 @@
         from_partner = swap(partner_part, "tc")
         own_part = jnp.dot(rows_of(1 - ty, tc), weight, preferred_element_type=jnp.float32)
         chip_sum = (own_part.astype(jnp.bfloat16).astype(jnp.float32) + from_partner.astype(jnp.float32))
-        across.append(swap(chip_sum.astype(jnp.bfloat16), "ty"))
-    near = swap(product(rows_of(ty, 1 - tc)), "tc")
+        chip_sums.append(chip_sum.astype(jnp.bfloat16))
+        near_parts.append(jnp.dot(
+            rows_of(ty, 1 - tc), weight, preferred_element_type=jnp.float32
+        ).astype(jnp.bfloat16))
+    chip_sums, near_parts, mixed_rows = lax.optimization_barrier((chip_sums, near_parts, mixed_rows))
+    across = [swap(chip_sum, "ty") for chip_sum in chip_sums]
+    near = [swap(part, "tc") for part in near_parts]
     mine = lax.optimization_barrier(product(rows_of(ty, tc)))
     far = jnp.concatenate(across, axis=1)
+    near = jnp.concatenate(near, axis=1)
     total = mine.astype(jnp.float32) + near.astype(jnp.float32) + far.astype(jnp.float32)
     return total.astype(jnp.bfloat16)
 

time: 166 us -> 168 us (1.012)
  Pallas kernels: 32.9 us -> 27.8 us
  waiting for transfers between devices: 65.5 us -> 69.9 us
  matrix products: 38 us -> 40.3 us
    dot_general x2 -> x1, matrix products: 21.2 us -> 9.92 us  [product(): jnp.dot(rows, out_weight, preferred_element_type=jnp.float32)]
    dot_general x0 -> x3, matrix products: none -> 10.2 us  [project_and_reduce(): jnp.dot(rows_of(ty, 1 - tc), weight, preferred_element_type=jnp.float32)]
    pallas_call x2, Pallas kernels: 18.9 us -> 13.8 us  [the longest x1 8.3 us: mix(): pl.pallas_call(mix_kernel, grid=(tokens // ROW_TILE,), in_specs=[row_bloc...]
    ppermute x7 -> x9, waiting for transfers between devices: 52.4 us -> 56.9 us  [swap(): return lax.ppermute(block, axis, [(0, 1), (1, 0)])]
    dot_general x3, matrix products: 10 us -> 12.7 us  [project_and_reduce(): jnp.dot(rows_of(1 - ty, 1 - tc), weight, preferred_element_type=jnp.float32)]
    ppermute x7 -> x9, starting transfers between devices: 4.8 us -> 4.99 us  [swap(): return lax.ppermute(block, axis, [(0, 1), (1, 0)])]
  transfers between devices with their start and end apart: 10 -> 12, of which waited for: 5 -> 6; matrix products, arithmetic and copies ran while one was open for 18% -> 15% of each run, Pallas kernels for 8% -> 8%
where the time goes in v5:
time: 168 us
  waiting for transfers between devices  69.9 us (42%)
  matrix products  40.3 us (24%)
  Pallas kernels  27.8 us (17%)
  starting transfers between devices  20.7 us (12%)
  other arithmetic  8.16 us (5%)
    ppermute x9, waiting for transfers between devices, swap(): return lax.ppermute(block, axis, [(0, 1), (1, 0)])  56.9 us
    ppermute x3, starting transfers between devices, shift(): lax.ppermute(block, axis, [(i, i + distance) for i in range(size) if i +...  15.7 us
    pallas_call x1, Pallas kernels, local_attention(): pl.pallas_call(local_kernel, grid=(heads,), in_specs=[head_block(tokens)]...  14 us
    ppermute x3, waiting for transfers between devices, shift(): lax.ppermute(block, axis, [(i, i + distance) for i in range(size) if i +...  13 us
    dot_general x3, matrix products, project_and_reduce(): jnp.dot(rows_of(1 - ty, 1 - tc), weight, preferred_element_type=jnp.float32)  12.7 us
    dot_general x3, matrix products, project_and_reduce(): jnp.dot(rows_of(ty, 1 - tc), weight, preferred_element_type=jnp.float32)  10.2 us
    dot_general x1, matrix products, product(): jnp.dot(rows, out_weight, preferred_element_type=jnp.float32)  9.92 us
    pallas_call x1, Pallas kernels, mix(): pl.pallas_call(mix_kernel, grid=(tokens // ROW_TILE,), in_specs=[row_bloc...  8.3 us
  transfers between devices with their start and end apart: 12, of which 6 were waited for; matrix products, arithmetic and copies ran while one was open for 15% of the time, Pallas kernels for 8%

profile of v5, /device:TPU:0, one launch (start us, length us, event | category | flops | bytes accessed | tf_op | source)
XLA Modules:
  0.0 167.7 jit_solution(18356383553879361537)
XLA Ops:
  0.0 5.5 %shard_map.65 = f32[10,128,128]{2,1,0:T(8,128)} custom-call(bf16[1024,1280]{1,0:T(8,128)(2,1)} %k_ref.3, bf16[1024,1280]{1,0:T(8,128)(2,1)} %v_ref.3), custom_call_target="tpu_custom_call" | custom-call | flops 335544320 | bytes 5898240 | tf_op jit(solution)/shard_map/pallas_call | solution.py:50
  6.7 4.9 %collective-permute-start = (bf16[10,128,128]{2,1,0:T(8,128)(2,1)S(1)}, bf16[10,128,128]{2,1,0:T(8,128)(2,1)S(1)}, u32[]{:S(2)}, u32[]{:S(2)}) collective-permute-start(bf16[10,128,128]{2,1,0:T(8,128)(2,1)S(1)} %convert_element_type.96), channel_id=1, source_target_pairs={{0,4},{4,8},{8,12},{12,16},{16,20},{20,24},{24,28},{1,5},{5,9},{9,... | collective-permute-start | bytes 983048 | tf_op jit(solution)/shard_map/ppermute | solution.py:152
  11.6 6.9 %collective-permute-done = bf16[10,128,128]{2,1,0:T(8,128)(2,1)S(1)} collective-permute-done((bf16[10,128,128]{2,1,0:T(8,128)(2,1)S(1)}, bf16[10,128,128]{2,1,0:T(8,128)(2,1)S(1)}, u32[]{:S(2)}, u32[]{:S(2)}) %collective-permute-start) | collective-permute-done | bytes 327712 | tf_op jit(solution)/shard_map/ppermute | solution.py:152
  19.7 5.4 %collective-permute-start.1 = (bf16[10,128,128]{2,1,0:T(8,128)(2,1)S(1)}, bf16[10,128,128]{2,1,0:T(8,128)(2,1)S(1)}, u32[]{:S(2)}, u32[]{:S(2)}) collective-permute-start(bf16[10,128,128]{2,1,0:T(8,128)(2,1)S(1)} %fusion.78), channel_id=1, source_target_pairs={{0,8},{4,12},{8,16},{12,20},{16,24},{20,28},{1,9},{5,13},{9,17},{1... | collective-permute-start | bytes 983048 | tf_op jit(solution)/shard_map/ppermute | solution.py:152
  25.1 6.1 %collective-permute-done.1 = bf16[10,128,128]{2,1,0:T(8,128)(2,1)S(1)} collective-permute-done((bf16[10,128,128]{2,1,0:T(8,128)(2,1)S(1)}, bf16[10,128,128]{2,1,0:T(8,128)(2,1)S(1)}, u32[]{:S(2)}, u32[]{:S(2)}) %collective-permute-start.1) | collective-permute-done | bytes 327712 | tf_op jit(solution)/shard_map/ppermute | solution.py:152
  32.4 5.4 %collective-permute-start.2 = (bf16[10,128,128]{2,1,0:T(8,128)(2,1)S(1)}, bf16[10,128,128]{2,1,0:T(8,128)(2,1)S(1)}, u32[]{:S(2)}, u32[]{:S(2)}) collective-permute-start(bf16[10,128,128]{2,1,0:T(8,128)(2,1)S(1)} %fusion.55), channel_id=1, source_target_pairs={{0,16},{4,20},{8,24},{12,28},{1,17},{5,21},{9,25},{13,29},{2,18},{... | collective-permute-start | bytes 983048 | tf_op jit(solution)/shard_map/ppermute | solution.py:152
  38.4 14.0 %shard_map.64.local_ref = f32[1024,1280]{1,0:T(8,128)} custom-call(bf16[1024,1280]{1,0:T(8,128)(2,1)} %q_ref.3, bf16[1024,1280]{1,0:T(8,128)(2,1)} %k_ref.3, bf16[1024,1280]{1,0:T(8,128)(2,1)} %v_ref.3), custom_call_target="tpu_custom_call" | custom-call | flops 3355443200 | bytes 13107200 | tf_op jit(solution)/shard_map/pallas_call | solution.py:90
  53.4 8.3 %shard_map.66 = bf16[1024,1280]{1,0:T(8,128)(2,1)} custom-call(f32[1024,1280]{1,0:T(8,128)} %shard_map.64.local_ref, bf16[1024,1280]{1,0:T(8,128)(2,1)} %q_ref.3, bf16[1024,1280]{1,0:T(8,128)(2,1)} %g_ref.1, bf16[10,128,128]{2,1,0:T(8,128)(2,1)} %get-tuple-element.20.hi_ref, bf16[10,128,128]{2,1,0:T(8,128)(2,1)} %get-tuple-element.19.lo_ref, ...), custom_call_target="tpu_custom_call" | custom-call | flops 671088640 | bytes 13107200 | tf_op jit(solution)/shard_map/pallas_call | solution.py:123
  61.7 4.4 %fusion.36 = bf16[256,2048]{1,0:T(8,128)(2,1)S(1)} fusion(bf16[1280,6144]{1,0:T(8,128)(2,1)} %param.11, bf16[1024,1280]{1,0:T(8,128)(2,1)} %shard_map.66, s32[]{:T(128)S(6)} %select_n.9), kind=kOutput, calls=%fused_computation.26 | convolution fusion | flops 1342701568 | bytes 6946820 | tf_op jit(solution)/shard_map/dot_general | solution.py:203
  66.1 4.2 %fusion.48 = bf16[256,2048]{1,0:T(8,128)(2,1)S(1)} fusion(bf16[1280,6144]{1,0:T(8,128)(2,1)} %param.11, bf16[1024,1280]{1,0:T(8,128)(2,1)S(1)} %copy-done, s32[]{:T(128)S(6)} %select_n.9), kind=kOutput, calls=%fused_computation.30 | convolution fusion | flops 1342701568 | bytes 6946820 | tf_op jit(solution)/shard_map/dot_general | solution.py:203
  70.3 4.2 %fusion.24 = bf16[256,2048]{1,0:T(8,128)(2,1)S(1)} fusion(bf16[1280,6144]{1,0:T(8,128)(2,1)} %param.11, bf16[1024,1280]{1,0:T(8,128)(2,1)S(1)} %copy-done, s32[]{:T(128)S(6)} %select_n.9), kind=kOutput, calls=%fused_computation.22 | convolution fusion | flops 1342701568 | bytes 6946820 | tf_op jit(solution)/shard_map/dot_general | solution.py:203
  74.6 5.2 %fusion.39 = bf16[256,2048]{1,0:T(8,128)(2,1)} fusion(bf16[1280,6144]{1,0:T(8,128)(2,1)} %param.11, bf16[1024,1280]{1,0:T(8,128)(2,1)S(1)} %copy-done, s32[]{:T(128)S(6)} %select_n.20), kind=kOutput, calls=%fused_computation.27 | convolution fusion | flops 1342701568 | bytes 6946820 | tf_op jit(solution)/shard_map/dot_general | solution.py:210
  80.3 2.5 %fusion.51 = bf16[256,2048]{1,0:T(8,128)(2,1)} fusion(bf16[1280,6144]{1,0:T(8,128)(2,1)S(1)} %bitcast.2, bf16[1024,1280]{1,0:T(8,128)(2,1)S(1)} %copy-done, s32[]{:T(128)S(6)} %select_n.20), kind=kOutput, calls=%fused_computation.31 | convolution fusion | flops 1342701568 | bytes 6946820 | tf_op jit(solution)/shard_map/dot_general | solution.py:210
  82.8 2.5 %fusion.27 = bf16[256,2048]{1,0:T(8,128)(2,1)} fusion(bf16[1280,6144]{1,0:T(8,128)(2,1)S(1)} %bitcast.2, bf16[1024,1280]{1,0:T(8,128)(2,1)S(1)} %copy-done, s32[]{:T(128)S(6)} %select_n.20), kind=kOutput, calls=%fused_computation.23 | convolution fusion | flops 1342701568 | bytes 6946820 | tf_op jit(solution)/shard_map/dot_general | solution.py:210
  85.3 2.5 %add_convert_fusion.3 = bf16[256,2048]{1,0:T(8,128)(2,1)} fusion(bf16[256,2048]{1,0:T(8,128)(2,1)S(1)} %collective-permute-done.3, bf16[1280,6144]{1,0:T(8,128)(2,1)S(1)} %bitcast.2, bf16[1024,1280]{1,0:T(8,128)(2,1)S(1)} %copy-done, s32[]{:T(128)S(6)} %select_n.8), kind=kOutput, calls=%fused_computation.34 | convolution fusion | flops 1344798720 | bytes 7995396 | tf_op jit(solution)/shard_map/dot_general | solution.py:207
  87.8 2.5 %add_convert_fusion.1 = bf16[256,2048]{1,0:T(8,128)(2,1)} fusion(bf16[256,2048]{1,0:T(8,128)(2,1)S(1)} %collective-permute-done.5, bf16[1280,6144]{1,0:T(8,128)(2,1)S(1)} %bitcast.2, bf16[1024,1280]{1,0:T(8,128)(2,1)S(1)} %copy-done, s32[]{:T(128)S(6)} %select_n.8), kind=kOutput, calls=%fused_computation.32 | convolution fusion | flops 1344798720 | bytes 7995396 | tf_op jit(solution)/shard_map/dot_general | solution.py:207
  90.3 2.5 %add_convert_fusion.2 = bf16[256,2048]{1,0:T(8,128)(2,1)} fusion(bf16[256,2048]{1,0:T(8,128)(2,1)S(1)} %collective-permute-done.4, bf16[1280,6144]{1,0:T(8,128)(2,1)S(1)} %bitcast.2, bf16[1024,1280]{1,0:T(8,128)(2,1)S(1)} %copy-done, s32[]{:T(128)S(6)} %select_n.8), kind=kOutput, calls=%fused_computation.33 | convolution fusion | flops 1344798720 | bytes 7995396 | tf_op jit(solution)/shard_map/dot_general | solution.py:207
  93.7 1.5 collective-permute-start.9
  95.8 1.5 collective-permute-start.11
  97.4 9.9 %convolution_convert_fusion = bf16[256,6144]{1,0:T(8,128)(2,1)S(1)} fusion(bf16[1280,6144]{1,0:T(8,128)(2,1)} %param.11, bf16[1024,1280]{1,0:T(8,128)(2,1)S(1)} %copy-done, s32[]{:T(128)S(6)} %select_n.21), kind=kOutput, calls=%fused_computation | convolution fusion | flops 4028104704 | bytes 19529732 | tf_op jit(solution)/shard_map/dot_general | solution.py:179
  107.3 12.6 %collective-permute-done.9 = bf16[256,2048]{1,0:T(8,128)(2,1)S(1)} collective-permute-done((bf16[256,2048]{1,0:T(8,128)(2,1)}, bf16[256,2048]{1,0:T(8,128)(2,1)S(1)}, u32[]{:S(2)}, u32[]{:S(2)}) %collective-permute-start.9) | collective-permute-done | bytes 1048608 | tf_op jit(solution)/shard_map/ppermute | solution.py:156
  119.9 22.5 %collective-permute-done.10 = bf16[256,2048]{1,0:T(8,128)(2,1)S(1)} collective-permute-done((bf16[256,2048]{1,0:T(8,128)(2,1)}, bf16[256,2048]{1,0:T(8,128)(2,1)S(1)}, u32[]{:S(2)}, u32[]{:S(2)}) %collective-permute-start.10) | collective-permute-done | bytes 1048608 | tf_op jit(solution)/shard_map/ppermute | solution.py:156
  142.4 21.7 %collective-permute-done.11 = bf16[256,2048]{1,0:T(8,128)(2,1)S(1)} collective-permute-done((bf16[256,2048]{1,0:T(8,128)(2,1)}, bf16[256,2048]{1,0:T(8,128)(2,1)S(1)}, u32[]{:S(2)}, u32[]{:S(2)}) %collective-permute-start.11) | collective-permute-done | bytes 1048608 | tf_op jit(solution)/shard_map/ppermute | solution.py:156
  164.1 3.6 %add_convert_fusion = bf16[256,6144]{1,0:T(8,128)(2,1)} fusion(bf16[256,6144]{1,0:T(8,128)(2,1)S(1)} %convolution_convert_fusion, bf16[256,2048]{1,0:T(8,128)(2,1)S(1)} %collective-permute-done.8, bf16[256,2048]{1,0:T(8,128)(2,1)S(1)} %collective-permute-done.7, bf16[256,2048]{1,0:T(8,128)(2,1)} %collective-permute-done.6, ...), kind=kLoop, calls=%fused_computation.1 | loop fusion | flops 25165824 | bytes 12582912 | tf_op jit(solution)/shard_map/convert_element_type | solution.py:220
  (32 shorter events, 7.2 us)
Async XLA Ops:
  0.0 37.8 %copy-start.1 = (f32[1280]{0:T(1024)S(1)}, f32[1280]{0:T(1024)}, u32[]{:S(2)}) copy-start(f32[1280]{0:T(1024)} %param.10) | copy-start | bytes 15364
  6.7 11.8 %collective-permute-start = (bf16[10,128,128]{2,1,0:T(8,128)(2,1)S(1)}, bf16[10,128,128]{2,1,0:T(8,128)(2,1)S(1)}, u32[]{:S(2)}, u32[]{:S(2)}) collective-permute-start(bf16[10,128,128]{2,1,0:T(8,128)(2,1)S(1)} %convert_element_type.96), channel_id=1, source_target_pairs={{0,4},{4,8},{8,12},{12,16},{16,20},{20,24},{24,28},{1,5},{5,9},{9,... | collective-permute-start | bytes 983048 | tf_op jit(solution)/shard_map/ppermute | solution.py:152
  19.7 11.5 %collective-permute-start.1 = (bf16[10,128,128]{2,1,0:T(8,128)(2,1)S(1)}, bf16[10,128,128]{2,1,0:T(8,128)(2,1)S(1)}, u32[]{:S(2)}, u32[]{:S(2)}) collective-permute-start(bf16[10,128,128]{2,1,0:T(8,128)(2,1)S(1)} %fusion.78), channel_id=1, source_target_pairs={{0,8},{4,12},{8,16},{12,20},{16,24},{20,28},{1,9},{5,13},{9,17},{1... | collective-permute-start | bytes 983048 | tf_op jit(solution)/shard_map/ppermute | solution.py:152
  32.4 20.0 %collective-permute-start.2 = (bf16[10,128,128]{2,1,0:T(8,128)(2,1)S(1)}, bf16[10,128,128]{2,1,0:T(8,128)(2,1)S(1)}, u32[]{:S(2)}, u32[]{:S(2)}) collective-permute-start(bf16[10,128,128]{2,1,0:T(8,128)(2,1)S(1)} %fusion.55), channel_id=1, source_target_pairs={{0,16},{4,20},{8,24},{12,28},{1,17},{5,21},{9,25},{13,29},{2,18},{... | collective-permute-start | bytes 983048 | tf_op jit(solution)/shard_map/ppermute | solution.py:152
  61.7 4.4 %copy-start = (bf16[1024,1280]{1,0:T(8,128)(2,1)S(1)}, bf16[1024,1280]{1,0:T(8,128)(2,1)}, u32[]{:S(2)}) copy-start(bf16[1024,1280]{1,0:T(8,128)(2,1)} %shard_map.66) | copy-start | bytes 7864324
  66.1 14.2 %slice-start = ((s8[15728640]{0:T(1024)(128)(4,1)}), s8[4194304]{0:T(1024)(128)(4,1)S(1)}, s32[]{:S(2)}) async-start(s8[15728640]{0:T(1024)(128)(4,1)} %bitcast.1), calls=%async_computation | async-start | bytes 8388608
  66.1 14.1 %slice-start.1 = ((s8[15728640]{0:T(1024)(128)(4,1)}), s8[4194304]{0:T(1024)(128)(4,1)S(1)}, s32[]{:S(2)}) async-start(s8[15728640]{0:T(1024)(128)(4,1)} %bitcast.1), calls=%async_computation.1 | async-start | bytes 8388608
  70.3 10.0 %slice-start.2 = ((s8[15728640]{0:T(1024)(128)(4,1)}), s8[4194304]{0:T(1024)(128)(4,1)S(1)}, s32[]{:S(2)}) async-start(s8[15728640]{0:T(1024)(128)(4,1)} %bitcast.1), calls=%async_computation.2 | async-start | bytes 8388608
  74.5 5.8 %slice-start.3 = ((s8[15728640]{0:T(1024)(128)(4,1)}), s8[3145728]{0:T(1024)(128)(4,1)S(1)}, s32[]{:S(2)}) async-start(s8[15728640]{0:T(1024)(128)(4,1)} %bitcast.1), calls=%async_computation.3 | async-start | bytes 6291456
  74.5 10.8 %collective-permute-start.3 = (bf16[256,2048]{1,0:T(8,128)(2,1)S(1)}, bf16[256,2048]{1,0:T(8,128)(2,1)S(1)}, u32[]{:S(2)}, u32[]{:S(2)}) collective-permute-start(bf16[256,2048]{1,0:T(8,128)(2,1)S(1)} %fusion.24), channel_id=1, source_target_pairs={{0,1},{1,0},{2,3},{3,2},{4,5},{5,4},{6,7},{7,6},{8,9},{9,8},{10,11... | collective-permute-start | bytes 3145736 | tf_op jit(solution)/shard_map/ppermute | solution.py:156
  79.8 8.1 %collective-permute-start.5 = (bf16[256,2048]{1,0:T(8,128)(2,1)S(1)}, bf16[256,2048]{1,0:T(8,128)(2,1)S(1)}, u32[]{:S(2)}, u32[]{:S(2)}) collective-permute-start(bf16[256,2048]{1,0:T(8,128)(2,1)S(1)} %fusion.48), channel_id=1, source_target_pairs={{0,1},{1,0},{2,3},{3,2},{4,5},{5,4},{6,7},{7,6},{8,9},{9,8},{10,11... | collective-permute-start | bytes 3145736 | tf_op jit(solution)/shard_map/ppermute | solution.py:156
  80.1 10.2 %collective-permute-start.4 = (bf16[256,2048]{1,0:T(8,128)(2,1)S(1)}, bf16[256,2048]{1,0:T(8,128)(2,1)S(1)}, u32[]{:S(2)}, u32[]{:S(2)}) collective-permute-start(bf16[256,2048]{1,0:T(8,128)(2,1)S(1)} %fusion.36), channel_id=1, source_target_pairs={{0,1},{1,0},{2,3},{3,2},{4,5},{5,4},{6,7},{7,6},{8,9},{9,8},{10,11... | collective-permute-start | bytes 3145736 | tf_op jit(solution)/shard_map/ppermute | solution.py:156
  92.8 3.0 %collective-permute-start.6 = (bf16[256,2048]{1,0:T(8,128)(2,1)}, bf16[256,2048]{1,0:T(8,128)(2,1)}, u32[]{:S(2)}, u32[]{:S(2)}) collective-permute-start(bf16[256,2048]{1,0:T(8,128)(2,1)} %fusion.27), channel_id=1, source_target_pairs={{0,1},{1,0},{2,3},{3,2},{4,5},{5,4},{6,7},{7,6},{8,9},{9,8},{10,11... | collective-permute-start | bytes 3145736 | tf_op jit(solution)/shard_map/ppermute | solution.py:156
  93.2 14.1 %collective-permute-start.7 = (bf16[256,2048]{1,0:T(8,128)(2,1)}, bf16[256,2048]{1,0:T(8,128)(2,1)S(1)}, u32[]{:S(2)}, u32[]{:S(2)}) collective-permute-start(bf16[256,2048]{1,0:T(8,128)(2,1)} %fusion.39), channel_id=1, source_target_pairs={{0,1},{1,0},{2,3},{3,2},{4,5},{5,4},{6,7},{7,6},{8,9},{9,8},{10,11... | collective-permute-start | bytes 3145736 | tf_op jit(solution)/shard_map/ppermute | solution.py:156
  93.3 14.0 %collective-permute-start.8 = (bf16[256,2048]{1,0:T(8,128)(2,1)}, bf16[256,2048]{1,0:T(8,128)(2,1)S(1)}, u32[]{:S(2)}, u32[]{:S(2)}) collective-permute-start(bf16[256,2048]{1,0:T(8,128)(2,1)} %fusion.51), channel_id=1, source_target_pairs={{0,1},{1,0},{2,3},{3,2},{4,5},{5,4},{6,7},{7,6},{8,9},{9,8},{10,11... | collective-permute-start | bytes 3145736 | tf_op jit(solution)/shard_map/ppermute | solution.py:156
  93.7 26.2 %collective-permute-start.9 = (bf16[256,2048]{1,0:T(8,128)(2,1)}, bf16[256,2048]{1,0:T(8,128)(2,1)S(1)}, u32[]{:S(2)}, u32[]{:S(2)}) collective-permute-start(bf16[256,2048]{1,0:T(8,128)(2,1)} %add_convert_fusion.3), channel_id=1, source_target_pairs={{0,2},{2,0},{1,3},{3,1},{4,6},{6,4},{5,7},{7,5},{8,10},{10,8},{9,1... | collective-permute-start | bytes 3145736 | tf_op jit(solution)/shard_map/ppermute | solution.py:156
  95.2 47.2 %collective-permute-start.10 = (bf16[256,2048]{1,0:T(8,128)(2,1)}, bf16[256,2048]{1,0:T(8,128)(2,1)S(1)}, u32[]{:S(2)}, u32[]{:S(2)}) collective-permute-start(bf16[256,2048]{1,0:T(8,128)(2,1)} %add_convert_fusion.2), channel_id=1, source_target_pairs={{0,2},{2,0},{1,3},{3,1},{4,6},{6,4},{5,7},{7,5},{8,10},{10,8},{9,1... | collective-permute-start | bytes 3145736 | tf_op jit(solution)/shard_map/ppermute | solution.py:156
  95.8 68.2 %collective-permute-start.11 = (bf16[256,2048]{1,0:T(8,128)(2,1)}, bf16[256,2048]{1,0:T(8,128)(2,1)S(1)}, u32[]{:S(2)}, u32[]{:S(2)}) collective-permute-start(bf16[256,2048]{1,0:T(8,128)(2,1)} %add_convert_fusion.1), channel_id=1, source_target_pairs={{0,2},{2,0},{1,3},{3,1},{4,6},{6,4},{5,7},{7,5},{8,10},{10,8},{9,1... | collective-permute-start | bytes 3145736 | tf_op jit(solution)/shard_map/ppermute | solution.py:156

commit v6 on v5

--- a/solution.py
+++ b/solution.py
@@ -190,32 +190,27 @@
 
     ty = lax.axis_index("ty")
     tc = lax.axis_index("tc")
-
-    def rows_of(owner_ty, owner_tc):
-        start = (owner_ty * tc_size + owner_tc) * block
-        return lax.dynamic_slice_in_dim(mixed_rows, start, block, axis=0)
+    pair = tc_size * block
+    far_rows = lax.dynamic_slice_in_dim(mixed_rows, (1 - ty) * pair, pair, axis=0)
+    near_rows = lax.dynamic_slice_in_dim(mixed_rows, ty * pair, pair, axis=0)
+
+    def block_of(part, owner_tc):
+        return lax.dynamic_slice_in_dim(part, owner_tc * block, block, axis=0)
 
     chunk = width // COLUMN_CHUNKS
     chip_sums = []
-    near_parts = []
     for c in range(COLUMN_CHUNKS):
-        weight = out_weight[:, c * chunk:(c + 1) * chunk]
-        partner_part = jnp.dot(
-            rows_of(1 - ty, 1 - tc), weight, preferred_element_type=jnp.float32
+        far_part = jnp.dot(
+            far_rows, out_weight[:, c * chunk:(c + 1) * chunk], preferred_element_type=jnp.float32
         ).astype(jnp.bfloat16)
-        from_partner = swap(partner_part, "tc")
-        own_part = jnp.dot(rows_of(1 - ty, tc), weight, preferred_element_type=jnp.float32)
-        chip_sum = (own_part.astype(jnp.bfloat16).astype(jnp.float32) + from_partner.astype(jnp.float32))
+        from_partner = swap(block_of(far_part, 1 - tc), "tc")
+        chip_sum = block_of(far_part, tc).astype(jnp.float32) + from_partner.astype(jnp.float32)
         chip_sums.append(chip_sum.astype(jnp.bfloat16))
-        near_parts.append(jnp.dot(
-            rows_of(ty, 1 - tc), weight, preferred_element_type=jnp.float32
-        ).astype(jnp.bfloat16))
-    chip_sums, near_parts, mixed_rows = lax.optimization_barrier((chip_sums, near_parts, mixed_rows))
+    chip_sums, near_rows = lax.optimization_barrier((chip_sums, near_rows))
     across = [swap(chip_sum, "ty") for chip_sum in chip_sums]
-    near = [swap(part, "tc") for part in near_parts]
-    mine = lax.optimization_barrier(product(rows_of(ty, tc)))
+    near = swap(product(block_of(near_rows, 1 - tc)), "tc")
+    mine = lax.optimization_barrier(product(block_of(near_rows, tc)))
     far = jnp.concatenate(across, axis=1)
-    near = jnp.concatenate(near, axis=1)
     total = mine.astype(jnp.float32) + near.astype(jnp.float32) + far.astype(jnp.float32)
     return total.astype(jnp.bfloat16)
 

time: 168 us -> 159 us (0.946)
  matrix products: 40.3 us -> 29.2 us
    dot_general x9 -> x3, matrix products: 30.4 us -> 14.9 us  [project_and_reduce(): jnp.dot(far_rows, out_weight[:, c * chunk:(c + 1) * chunk], preferred_ele...]
    dot_general x1 -> x2, matrix products: 9.92 us -> 14.4 us  [product(): jnp.dot(rows, out_weight, preferred_element_type=jnp.float32)]
    ppermute x9 -> x7, waiting for transfers between devices: 56.9 us -> 58.5 us  [swap(): return lax.ppermute(block, axis, [(0, 1), (1, 0)])]
    ppermute x9 -> x7, starting transfers between devices: 4.99 us -> 4.47 us  [swap(): return lax.ppermute(block, axis, [(0, 1), (1, 0)])]
  transfers between devices with their start and end apart: 12 -> 10, of which waited for: 6 -> 6; matrix products, arithmetic and copies ran while one was open for 15% -> 9% of each run, Pallas kernels for 8% -> 9%
where the time goes in v6:
time: 159 us; the launch traced here: 158 us
  waiting for transfers between devices  71.5 us (45%)
  matrix products  29.2 us (18%)
  Pallas kernels  27.8 us (17%)
  starting transfers between devices  20.2 us (13%)
  other arithmetic  8.51 us (5%)
    ppermute x7, waiting for transfers between devices, swap(): return lax.ppermute(block, axis, [(0, 1), (1, 0)])  58.5 us
    ppermute x3, starting transfers between devices, shift(): lax.ppermute(block, axis, [(i, i + distance) for i in range(size) if i +...  15.7 us
    dot_general x3, matrix products, project_and_reduce(): jnp.dot(far_rows, out_weight[:, c * chunk:(c + 1) * chunk], preferred_ele...  14.9 us
    dot_general x2, matrix products, product(): jnp.dot(rows, out_weight, preferred_element_type=jnp.float32)  14.4 us
    pallas_call x1, Pallas kernels, local_attention(): pl.pallas_call(local_kernel, grid=(heads,), in_specs=[head_block(tokens)]...  14 us
    ppermute x3, waiting for transfers between devices, shift(): lax.ppermute(block, axis, [(i, i + distance) for i in range(size) if i +...  13 us
    pallas_call x1, Pallas kernels, mix(): pl.pallas_call(mix_kernel, grid=(tokens // ROW_TILE,), in_specs=[row_bloc...  8.3 us
    pallas_call x1, Pallas kernels, key_value_states(): pl.pallas_call(state_kernel, grid=(tokens // ROW_TILE,), in_specs=[row_bl...  5.51 us
  transfers between devices with their start and end apart: 10, of which 6 were waited for; matrix products, arithmetic and copies ran while one was open for 9% of the time, Pallas kernels for 9%

profile of v6, /device:TPU:0, one launch (start us, length us, event | category | flops | bytes accessed | tf_op | source)
XLA Modules:
  0.0 158.5 jit_solution(9117457537354228271)
XLA Ops:
  0.0 5.5 %shard_map.65 = f32[10,128,128]{2,1,0:T(8,128)} custom-call(bf16[1024,1280]{1,0:T(8,128)(2,1)} %k_ref.3, bf16[1024,1280]{1,0:T(8,128)(2,1)} %v_ref.3), custom_call_target="tpu_custom_call" | custom-call | flops 335544320 | bytes 5898240 | tf_op jit(solution)/shard_map/pallas_call | solution.py:50
  5.5 1.1 convert_element_type.81
  6.7 4.9 %collective-permute-start = (bf16[10,128,128]{2,1,0:T(8,128)(2,1)S(1)}, bf16[10,128,128]{2,1,0:T(8,128)(2,1)S(1)}, u32[]{:S(2)}, u32[]{:S(2)}) collective-permute-start(bf16[10,128,128]{2,1,0:T(8,128)(2,1)S(1)} %convert_element_type.81), channel_id=1, source_target_pairs={{0,4},{4,8},{8,12},{12,16},{16,20},{20,24},{24,28},{1,5},{5,9},{9,... | collective-permute-start | bytes 983048 | tf_op jit(solution)/shard_map/ppermute | solution.py:152
  11.6 6.9 %collective-permute-done = bf16[10,128,128]{2,1,0:T(8,128)(2,1)S(1)} collective-permute-done((bf16[10,128,128]{2,1,0:T(8,128)(2,1)S(1)}, bf16[10,128,128]{2,1,0:T(8,128)(2,1)S(1)}, u32[]{:S(2)}, u32[]{:S(2)}) %collective-permute-start) | collective-permute-done | bytes 327712 | tf_op jit(solution)/shard_map/ppermute | solution.py:152
  18.5 1.2 fusion.22
  19.7 5.4 %collective-permute-start.1 = (bf16[10,128,128]{2,1,0:T(8,128)(2,1)S(1)}, bf16[10,128,128]{2,1,0:T(8,128)(2,1)S(1)}, u32[]{:S(2)}, u32[]{:S(2)}) collective-permute-start(bf16[10,128,128]{2,1,0:T(8,128)(2,1)S(1)} %fusion.22), channel_id=1, source_target_pairs={{0,8},{4,12},{8,16},{12,20},{16,24},{20,28},{1,9},{5,13},{9,17},{1... | collective-permute-start | bytes 983048 | tf_op jit(solution)/shard_map/ppermute | solution.py:152
  25.1 6.1 %collective-permute-done.1 = bf16[10,128,128]{2,1,0:T(8,128)(2,1)S(1)} collective-permute-done((bf16[10,128,128]{2,1,0:T(8,128)(2,1)S(1)}, bf16[10,128,128]{2,1,0:T(8,128)(2,1)S(1)}, u32[]{:S(2)}, u32[]{:S(2)}) %collective-permute-start.1) | collective-permute-done | bytes 327712 | tf_op jit(solution)/shard_map/ppermute | solution.py:152
  31.1 1.2 fusion.19
  32.3 5.4 %collective-permute-start.2 = (bf16[10,128,128]{2,1,0:T(8,128)(2,1)S(1)}, bf16[10,128,128]{2,1,0:T(8,128)(2,1)S(1)}, u32[]{:S(2)}, u32[]{:S(2)}) collective-permute-start(bf16[10,128,128]{2,1,0:T(8,128)(2,1)S(1)} %fusion.19), channel_id=1, source_target_pairs={{0,16},{4,20},{8,24},{12,28},{1,17},{5,21},{9,25},{13,29},{2,18},{... | collective-permute-start | bytes 983048 | tf_op jit(solution)/shard_map/ppermute | solution.py:152
  38.4 14.0 %shard_map.64.local_ref = f32[1024,1280]{1,0:T(8,128)} custom-call(bf16[1024,1280]{1,0:T(8,128)(2,1)} %q_ref.3, bf16[1024,1280]{1,0:T(8,128)(2,1)} %k_ref.3, bf16[1024,1280]{1,0:T(8,128)(2,1)} %v_ref.3), custom_call_target="tpu_custom_call" | custom-call | flops 3355443200 | bytes 13107200 | tf_op jit(solution)/shard_map/pallas_call | solution.py:90
  52.4 1.1 subtract_convert_fusion
  53.5 8.3 %shard_map.66 = bf16[1024,1280]{1,0:T(8,128)(2,1)} custom-call(f32[1024,1280]{1,0:T(8,128)} %shard_map.64.local_ref, bf16[1024,1280]{1,0:T(8,128)(2,1)} %q_ref.3, bf16[1024,1280]{1,0:T(8,128)(2,1)} %g_ref.1, bf16[10,128,128]{2,1,0:T(8,128)(2,1)} %get-tuple-element.14.hi_ref, bf16[10,128,128]{2,1,0:T(8,128)(2,1)} %get-tuple-element.13.lo_ref, ...), custom_call_target="tpu_custom_call" | custom-call | flops 671088640 | bytes 13107200 | tf_op jit(solution)/shard_map/pallas_call | solution.py:123
  61.8 5.9 %fusion.12 = bf16[512,2048]{1,0:T(8,128)(2,1)S(1)} fusion(bf16[1280,6144]{1,0:T(8,128)(2,1)} %param.11, bf16[1024,1280]{1,0:T(8,128)(2,1)} %shard_map.66, s32[]{:T(128)S(6)} %select_n.8), kind=kOutput, calls=%fused_computation.11 | convolution fusion | flops 2685403136 | bytes 8650756 | tf_op jit(solution)/shard_map/dot_general | solution.py:203
  67.7 5.8 %fusion.9 = bf16[512,2048]{1,0:T(8,128)(2,1)S(1)} fusion(bf16[1280,6144]{1,0:T(8,128)(2,1)} %param.11, bf16[1024,1280]{1,0:T(8,128)(2,1)S(1)} %copy-done, s32[]{:T(128)S(6)} %select_n.8), kind=kOutput, calls=%fused_computation.10 | convolution fusion | flops 2685403136 | bytes 8650756 | tf_op jit(solution)/shard_map/dot_general | solution.py:203
  74.4 3.1 %fusion.6 = bf16[512,2048]{1,0:T(8,128)(2,1)S(1)} fusion(bf16[1280,6144]{1,0:T(8,128)(2,1)S(1)} %bitcast.3, bf16[1024,1280]{1,0:T(8,128)(2,1)S(1)} %copy-done, s32[]{:T(128)S(6)} %select_n.8), kind=kOutput, calls=%fused_computation.9 | convolution fusion | flops 2685403136 | bytes 8650756 | tf_op jit(solution)/shard_map/dot_general | solution.py:203
  78.8 1.6 %collective-permute-done.3 = bf16[256,2048]{1,0:T(8,128)(2,1)S(1)} collective-permute-done((bf16[256,2048]{1,0:T(8,128)(2,1)S(1)}, bf16[256,2048]{1,0:T(8,128)(2,1)S(1)}, u32[]{:S(2)}, u32[]{:S(2)}) %collective-permute-start.3) | collective-permute-done | bytes 1048608 | tf_op jit(solution)/shard_map/ppermute | solution.py:156
  80.9 4.4 %convolution_convert_fusion = bf16[256,6144]{1,0:T(8,128)(2,1)S(1)} fusion(bf16[1280,6144]{1,0:T(8,128)(2,1)S(1)} %bitcast.3, bf16[512,1280]{1,0:T(8,128)(2,1)S(1)} %constant_dynamic-slice_fusion, s32[]{:T(128)S(6)} %select_n.20), kind=kOutput, calls=%fused_computation | convolution fusion | flops 4028104704 | bytes 19529732 | tf_op jit(solution)/shard_map/dot_general | solution.py:179
  85.5 1.5 collective-permute-start.7
  87.6 1.5 collective-permute-start.9
  89.1 9.9 %convolution_convert_fusion.1 = bf16[256,6144]{1,0:T(8,128)(2,1)S(1)} fusion(bf16[1280,6144]{1,0:T(8,128)(2,1)} %param.11, bf16[512,1280]{1,0:T(8,128)(2,1)S(1)} %constant_dynamic-slice_fusion, s32[]{:T(128)S(6)} %select_n.9), kind=kOutput, calls=%fused_computation.1 | convolution fusion | flops 4028104704 | bytes 19529732 | tf_op jit(solution)/shard_map/dot_general | solution.py:179
  99.0 12.6 %collective-permute-done.7 = bf16[256,2048]{1,0:T(8,128)(2,1)S(1)} collective-permute-done((bf16[256,2048]{1,0:T(8,128)(2,1)S(1)}, bf16[256,2048]{1,0:T(8,128)(2,1)S(1)}, u32[]{:S(2)}, u32[]{:S(2)}) %collective-permute-start.7) | collective-permute-done | bytes 1048608 | tf_op jit(solution)/shard_map/ppermute | solution.py:156
  111.6 22.5 %collective-permute-done.8 = bf16[256,2048]{1,0:T(8,128)(2,1)S(1)} collective-permute-done((bf16[256,2048]{1,0:T(8,128)(2,1)S(1)}, bf16[256,2048]{1,0:T(8,128)(2,1)S(1)}, u32[]{:S(2)}, u32[]{:S(2)}) %collective-permute-start.8) | collective-permute-done | bytes 1048608 | tf_op jit(solution)/shard_map/ppermute | solution.py:156
  134.0 21.9 %collective-permute-done.9 = bf16[256,2048]{1,0:T(8,128)(2,1)S(1)} collective-permute-done((bf16[256,2048]{1,0:T(8,128)(2,1)S(1)}, bf16[256,2048]{1,0:T(8,128)(2,1)S(1)}, u32[]{:S(2)}, u32[]{:S(2)}) %collective-permute-start.9) | collective-permute-done | bytes 1048608 | tf_op jit(solution)/shard_map/ppermute | solution.py:156
  155.9 2.6 %add_convert_fusion = bf16[256,6144]{1,0:T(8,128)(2,1)} fusion(bf16[256,6144]{1,0:T(8,128)(2,1)S(1)} %collective-permute-done.6, bf16[256,6144]{1,0:T(8,128)(2,1)S(1)} %convolution_convert_fusion.1, bf16[256,2048]{1,0:T(8,128)(2,1)S(1)} %collective-permute-done.9, bf16[256,2048]{1,0:T(8,128)(2,1)S(1)} %collective-permute-done.8, ...), kind=kLoop, calls=%fused_computation.2 | loop fusion | flops 17301504 | bytes 12582912 | tf_op jit(solution)/shard_map/convert_element_type | solution.py:215
  (30 shorter events, 3.8 us)
Async XLA Ops:
  5.5 32.3 %copy-start.1 = (f32[1280]{0:T(1024)S(1)}, f32[1280]{0:T(1024)}, u32[]{:S(2)}) copy-start(f32[1280]{0:T(1024)} %param.10) | copy-start | bytes 15364
  6.7 11.8 %collective-permute-start = (bf16[10,128,128]{2,1,0:T(8,128)(2,1)S(1)}, bf16[10,128,128]{2,1,0:T(8,128)(2,1)S(1)}, u32[]{:S(2)}, u32[]{:S(2)}) collective-permute-start(bf16[10,128,128]{2,1,0:T(8,128)(2,1)S(1)} %convert_element_type.81), channel_id=1, source_target_pairs={{0,4},{4,8},{8,12},{12,16},{16,20},{20,24},{24,28},{1,5},{5,9},{9,... | collective-permute-start | bytes 983048 | tf_op jit(solution)/shard_map/ppermute | solution.py:152
  19.7 11.5 %collective-permute-start.1 = (bf16[10,128,128]{2,1,0:T(8,128)(2,1)S(1)}, bf16[10,128,128]{2,1,0:T(8,128)(2,1)S(1)}, u32[]{:S(2)}, u32[]{:S(2)}) collective-permute-start(bf16[10,128,128]{2,1,0:T(8,128)(2,1)S(1)} %fusion.22), channel_id=1, source_target_pairs={{0,8},{4,12},{8,16},{12,20},{16,24},{20,28},{1,9},{5,13},{9,17},{1... | collective-permute-start | bytes 983048 | tf_op jit(solution)/shard_map/ppermute | solution.py:152
  32.3 20.0 %collective-permute-start.2 = (bf16[10,128,128]{2,1,0:T(8,128)(2,1)S(1)}, bf16[10,128,128]{2,1,0:T(8,128)(2,1)S(1)}, u32[]{:S(2)}, u32[]{:S(2)}) collective-permute-start(bf16[10,128,128]{2,1,0:T(8,128)(2,1)S(1)} %fusion.19), channel_id=1, source_target_pairs={{0,16},{4,20},{8,24},{12,28},{1,17},{5,21},{9,25},{13,29},{2,18},{... | collective-permute-start | bytes 983048 | tf_op jit(solution)/shard_map/ppermute | solution.py:152
  61.8 5.9 %copy-start = (bf16[1024,1280]{1,0:T(8,128)(2,1)S(1)}, bf16[1024,1280]{1,0:T(8,128)(2,1)}, u32[]{:S(2)}) copy-start(bf16[1024,1280]{1,0:T(8,128)(2,1)} %shard_map.66) | copy-start | bytes 7864324
  61.8 12.7 %slice-start = ((s8[15728640]{0:T(1024)(128)(4,1)}), s8[4194304]{0:T(1024)(128)(4,1)S(1)}, s32[]{:S(2)}) async-start(s8[15728640]{0:T(1024)(128)(4,1)} %bitcast.2), calls=%async_computation | async-start | bytes 8388608
  61.8 12.7 %slice-start.1 = ((s8[15728640]{0:T(1024)(128)(4,1)}), s8[4194304]{0:T(1024)(128)(4,1)S(1)}, s32[]{:S(2)}) async-start(s8[15728640]{0:T(1024)(128)(4,1)} %bitcast.2), calls=%async_computation.1 | async-start | bytes 8388608
  67.7 6.7 %slice-start.2 = ((s8[15728640]{0:T(1024)(128)(4,1)}), s8[4194304]{0:T(1024)(128)(4,1)S(1)}, s32[]{:S(2)}) async-start(s8[15728640]{0:T(1024)(128)(4,1)} %bitcast.2), calls=%async_computation.2 | async-start | bytes 8388608
  67.7 6.7 %slice-start.3 = ((s8[15728640]{0:T(1024)(128)(4,1)}), s8[3145728]{0:T(1024)(128)(4,1)S(1)}, s32[]{:S(2)}) async-start(s8[15728640]{0:T(1024)(128)(4,1)} %bitcast.2), calls=%async_computation.3 | async-start | bytes 6291456
  73.7 4.2 %collective-permute-start.5 = (bf16[256,2048]{1,0:T(8,128)(2,1)S(1)}, bf16[256,2048]{1,0:T(8,128)(2,1)S(1)}, u32[]{:S(2)}, u32[]{:S(2)}) collective-permute-start(bf16[256,2048]{1,0:T(8,128)(2,1)S(1)} %constant_dynamic-slice_fusion.1), channel_id=1, source_target_pairs={{0,1},{1,0},{2,3},{3,2},{4,5},{5,4},{6,7},{7,6},{8,9},{9,8},{10,11... | collective-permute-start | bytes 3145736 | tf_op jit(solution)/shard_map/ppermute | solution.py:156
  73.9 4.5 %collective-permute-start.4 = (bf16[256,2048]{1,0:T(8,128)(2,1)S(1)}, bf16[256,2048]{1,0:T(8,128)(2,1)S(1)}, u32[]{:S(2)}, u32[]{:S(2)}) collective-permute-start(bf16[256,2048]{1,0:T(8,128)(2,1)S(1)} %constant_dynamic-slice_fusion.2), channel_id=1, source_target_pairs={{0,1},{1,0},{2,3},{3,2},{4,5},{5,4},{6,7},{7,6},{8,9},{9,8},{10,11... | collective-permute-start | bytes 3145736 | tf_op jit(solution)/shard_map/ppermute | solution.py:156
  77.7 2.7 %collective-permute-start.3 = (bf16[256,2048]{1,0:T(8,128)(2,1)S(1)}, bf16[256,2048]{1,0:T(8,128)(2,1)S(1)}, u32[]{:S(2)}, u32[]{:S(2)}) collective-permute-start(bf16[256,2048]{1,0:T(8,128)(2,1)S(1)} %constant_dynamic-slice_fusion.3), channel_id=1, source_target_pairs={{0,1},{1,0},{2,3},{3,2},{4,5},{5,4},{6,7},{7,6},{8,9},{9,8},{10,11... | collective-permute-start | bytes 3145736 | tf_op jit(solution)/shard_map/ppermute | solution.py:156
  85.3 70.6 %collective-permute-start.6 = (bf16[256,6144]{1,0:T(8,128)(2,1)S(1)}, bf16[256,6144]{1,0:T(8,128)(2,1)S(1)}, u32[]{:S(2)}, u32[]{:S(2)}) collective-permute-start(bf16[256,6144]{1,0:T(8,128)(2,1)S(1)} %convolution_convert_fusion), channel_id=1, source_target_pairs={{0,1},{1,0},{2,3},{3,2},{4,5},{5,4},{6,7},{7,6},{8,9},{9,8},{10,11... | collective-permute-start | bytes 9437192 | tf_op jit(solution)/shard_map/ppermute | solution.py:156
  85.5 26.0 %collective-permute-start.7 = (bf16[256,2048]{1,0:T(8,128)(2,1)S(1)}, bf16[256,2048]{1,0:T(8,128)(2,1)S(1)}, u32[]{:S(2)}, u32[]{:S(2)}) collective-permute-start(bf16[256,2048]{1,0:T(8,128)(2,1)S(1)} %add_convert_fusion.3), channel_id=1, source_target_pairs={{0,2},{2,0},{1,3},{3,1},{4,6},{6,4},{5,7},{7,5},{8,10},{10,8},{9,1... | collective-permute-start | bytes 3145736 | tf_op jit(solution)/shard_map/ppermute | solution.py:156
  87.1 47.0 %collective-permute-start.8 = (bf16[256,2048]{1,0:T(8,128)(2,1)S(1)}, bf16[256,2048]{1,0:T(8,128)(2,1)S(1)}, u32[]{:S(2)}, u32[]{:S(2)}) collective-permute-start(bf16[256,2048]{1,0:T(8,128)(2,1)S(1)} %add_convert_fusion.2), channel_id=1, source_target_pairs={{0,2},{2,0},{1,3},{3,1},{4,6},{6,4},{5,7},{7,5},{8,10},{10,8},{9,1... | collective-permute-start | bytes 3145736 | tf_op jit(solution)/shard_map/ppermute | solution.py:156
  87.6 68.4 %collective-permute-start.9 = (bf16[256,2048]{1,0:T(8,128)(2,1)S(1)}, bf16[256,2048]{1,0:T(8,128)(2,1)S(1)}, u32[]{:S(2)}, u32[]{:S(2)}) collective-permute-start(bf16[256,2048]{1,0:T(8,128)(2,1)S(1)} %add_convert_fusion.1), channel_id=1, source_target_pairs={{0,2},{2,0},{1,3},{3,1},{4,6},{6,4},{5,7},{7,5},{8,10},{10,8},{9,1... | collective-permute-start | bytes 3145736 | tf_op jit(solution)/shard_map/ppermute | solution.py:156

commit v7 on v6

--- a/solution.py
+++ b/solution.py
@@ -101,14 +101,15 @@
     )(queries, keys, values)
 
 
-def mix_kernel(local_ref, q_ref, g_ref, hi_ref, lo_ref, gain_ref, out_ref):
+def mix_kernel(order_ref, local_ref, q_ref, g_ref, prefix_ref, gain_ref, out_ref):
     query_act = silu(q_ref[...])
     gates = g_ref[...].astype(jnp.float32)
     gate_open = 1.0 / (1.0 + jnp.exp(-gates))
-    for h in range(hi_ref.shape[0]):
+    for h in range(prefix_ref.shape[0]):
         heads = slice(h * HD, (h + 1) * HD)
-        remote = jnp.dot(query_act[:, heads], hi_ref[h], preferred_element_type=jnp.float32) + jnp.dot(
-            query_act[:, heads], lo_ref[h], preferred_element_type=jnp.float32
+        prefix_hi, prefix_lo = split_bf16(prefix_ref[h])
+        remote = jnp.dot(query_act[:, heads], prefix_hi, preferred_element_type=jnp.float32) + jnp.dot(
+            query_act[:, heads], prefix_lo, preferred_element_type=jnp.float32
         )
         attention = local_ref[:, heads] + remote
         mean_sq = jnp.mean(attention * attention, axis=-1, keepdims=True)
@@ -116,29 +117,31 @@
         out_ref[:, heads] = (normed * gate_open[:, heads]).astype(out_ref.dtype)
 
 
-def mix(local_part, queries, gates, prefix_hi, prefix_lo, gain):
+def mix(order, local_part, queries, gates, prefix, gain):
     tokens, columns = queries.shape
     heads = columns // HD
-    whole_state = pl.BlockSpec((heads, HD, HD), lambda i: (0, 0, 0))
+    picked = pl.BlockSpec((ROW_TILE, columns), lambda i, order: (order[i], 0))
     return pl.pallas_call(
         mix_kernel,
-        grid=(tokens // ROW_TILE,),
-        in_specs=[
-            row_block(columns),
-            row_block(columns),
-            row_block(columns),
-            whole_state,
-            whole_state,
-            pl.BlockSpec((1, columns), lambda i: (0, 0)),
-        ],
-        out_specs=row_block(columns),
+        grid_spec=pltpu.PrefetchScalarGridSpec(
+            num_scalar_prefetch=1,
+            grid=(tokens // ROW_TILE,),
+            in_specs=[
+                picked,
+                picked,
+                picked,
+                pl.BlockSpec((heads, HD, HD), lambda i, order: (0, 0, 0)),
+                pl.BlockSpec((1, columns), lambda i, order: (0, 0)),
+            ],
+            out_specs=pl.BlockSpec((ROW_TILE, columns), lambda i, order: (i, 0)),
+        ),
         out_shape=jax.ShapeDtypeStruct((tokens, columns), jnp.bfloat16),
         cost_estimate=pl.CostEstimate(
             flops=4 * tokens * HD * HD * heads,
             transcendentals=2 * tokens * columns,
             bytes_accessed=10 * tokens * columns,
         ),
-    )(local_part, queries, gates, prefix_hi, prefix_lo, gain.reshape(1, columns))
+    )(order, local_part, queries, gates, prefix, gain.reshape(1, columns))
 
 
 def split_bf16(x):
@@ -168,6 +171,19 @@
     return exclusive
 
 
+def reduce_order(tokens):
+    ty_size = lax.axis_size("ty")
+    tc_size = lax.axis_size("tc")
+    tiles = tokens // ROW_TILE
+    if ty_size != 2 or tc_size != 2 or tiles != 4:
+        return jnp.arange(tiles, dtype=jnp.int32)
+    ty = lax.axis_index("ty")
+    tc = lax.axis_index("tc")
+    return jnp.stack(
+        [(1 - ty) * 2 + 1 - tc, ty * 2 + 1 - tc, (1 - ty) * 2 + tc, ty * 2 + tc]
+    ).astype(jnp.int32)
+
+
 def project_and_reduce(mixed_rows, out_weight):
     tokens, columns = mixed_rows.shape
     ty_size = lax.axis_size("ty")
@@ -178,7 +194,7 @@
     def product(rows):
         return jnp.dot(rows, out_weight, preferred_element_type=jnp.float32).astype(jnp.bfloat16)
 
-    if ty_size != 2 or tc_size != 2:
+    if ty_size != 2 or tc_size != 2 or block != ROW_TILE:
         ordered = (
             mixed_rows.reshape(ty_size, tc_size, block, columns)
             .transpose(1, 0, 2, 3)
@@ -188,29 +204,24 @@
         part = lax.psum_scatter(part, "tc", scatter_dimension=0, tiled=True)
         return lax.psum_scatter(part, "ty", scatter_dimension=0, tiled=True)
 
-    ty = lax.axis_index("ty")
-    tc = lax.axis_index("tc")
-    pair = tc_size * block
-    far_rows = lax.dynamic_slice_in_dim(mixed_rows, (1 - ty) * pair, pair, axis=0)
-    near_rows = lax.dynamic_slice_in_dim(mixed_rows, ty * pair, pair, axis=0)
-
-    def block_of(part, owner_tc):
-        return lax.dynamic_slice_in_dim(part, owner_tc * block, block, axis=0)
-
+    early_rows = mixed_rows[:3 * block]
+    own_rows = mixed_rows[3 * block:]
     chunk = width // COLUMN_CHUNKS
     chip_sums = []
+    near_parts = []
     for c in range(COLUMN_CHUNKS):
-        far_part = jnp.dot(
-            far_rows, out_weight[:, c * chunk:(c + 1) * chunk], preferred_element_type=jnp.float32
+        part = jnp.dot(
+            early_rows, out_weight[:, c * chunk:(c + 1) * chunk], preferred_element_type=jnp.float32
         ).astype(jnp.bfloat16)
-        from_partner = swap(block_of(far_part, 1 - tc), "tc")
-        chip_sum = block_of(far_part, tc).astype(jnp.float32) + from_partner.astype(jnp.float32)
+        from_partner = swap(part[:2 * block], "tc")
+        chip_sum = part[2 * block:].astype(jnp.float32) + from_partner[:block].astype(jnp.float32)
         chip_sums.append(chip_sum.astype(jnp.bfloat16))
-    chip_sums, near_rows = lax.optimization_barrier((chip_sums, near_rows))
+        near_parts.append(from_partner[block:])
+    chip_sums, own_rows = lax.optimization_barrier((chip_sums, own_rows))
     across = [swap(chip_sum, "ty") for chip_sum in chip_sums]
-    near = swap(product(block_of(near_rows, 1 - tc)), "tc")
-    mine = lax.optimization_barrier(product(block_of(near_rows, tc)))
+    mine = lax.optimization_barrier(product(own_rows))
     far = jnp.concatenate(across, axis=1)
+    near = jnp.concatenate(near_parts, axis=1)
     total = mine.astype(jnp.float32) + near.astype(jnp.float32) + far.astype(jnp.float32)
     return total.astype(jnp.bfloat16)
 
@@ -219,8 +230,7 @@
     own_state = key_value_states(keys, values)
     prefix = exclusive_prefix(own_state, "ctx")
     local_part = local_attention(queries, keys, values)
-    prefix_hi, prefix_lo = split_bf16(prefix)
-    mixed_rows = mix(local_part, queries, gates, prefix_hi, prefix_lo, gain)
+    mixed_rows = mix(reduce_order(queries.shape[0]), local_part, queries, gates, prefix, gain)
     return project_and_reduce(mixed_rows, out_weight)
 
 

time: 159 us -> 165 us (1.038)
  local copies, waits for them, and re-layouts: 1.03 us -> 2.85 us
  matrix products: 29.2 us -> 31 us
    dot_general x3, matrix products: 14.9 us -> 21.1 us  [project_and_reduce(): jnp.dot(early_rows, out_weight[:, c * chunk:(c + 1) * chunk], preferred_e...]
    dot_general x2 -> x1, matrix products: 14.4 us -> 9.92 us  [product(): jnp.dot(rows, out_weight, preferred_element_type=jnp.float32)]
    ppermute x7 -> x6, waiting for transfers between devices: 58.5 us -> 59.6 us  [swap(): return lax.ppermute(block, axis, [(0, 1), (1, 0)])]
    ppermute x7 -> x6, starting transfers between devices: 4.47 us -> 4.29 us  [swap(): return lax.ppermute(block, axis, [(0, 1), (1, 0)])]
  transfers between devices with their start and end apart: 10 -> 9, of which waited for: 6 -> 6; matrix products, arithmetic and copies ran while one was open for 9% -> 16% of each run, Pallas kernels for 9% -> 9%
where the time goes in v7:
time: 165 us; the launch traced here: 164 us
  waiting for transfers between devices  72.6 us (44%)
  matrix products  31 us (19%)
  Pallas kernels  28.7 us (17%)
  starting transfers between devices  20 us (12%)
  other arithmetic  8.81 us (5%)
  local copies, waits for them, and re-layouts  2.85 us (2%)
    ppermute x6, waiting for transfers between devices, swap(): return lax.ppermute(block, axis, [(0, 1), (1, 0)])  59.6 us
    dot_general x3, matrix products, project_and_reduce(): jnp.dot(early_rows, out_weight[:, c * chunk:(c + 1) * chunk], preferred_e...  21.1 us
    ppermute x3, starting transfers between devices, shift(): lax.ppermute(block, axis, [(i, i + distance) for i in range(size) if i +...  15.7 us
    pallas_call x1, Pallas kernels, local_attention(): pl.pallas_call(local_kernel, grid=(heads,), in_specs=[head_block(tokens)]...  14 us
    ppermute x3, waiting for transfers between devices, shift(): lax.ppermute(block, axis, [(i, i + distance) for i in range(size) if i +...  13 us
    dot_general x1, matrix products, product(): jnp.dot(rows, out_weight, preferred_element_type=jnp.float32)  9.92 us
    pallas_call x1, Pallas kernels, mix(): pl.pallas_call(mix_kernel, grid_spec=pltpu.PrefetchScalarGridSpec(num_sca...  9.18 us
    pallas_call x1, Pallas kernels, key_value_states(): pl.pallas_call(state_kernel, grid=(tokens // ROW_TILE,), in_specs=[row_bl...  5.51 us
  transfers between devices with their start and end apart: 9, of which 6 were waited for; matrix products, arithmetic and copies ran while one was open for 16% of the time, Pallas kernels for 9%

profile of v7, /device:TPU:0, one launch (start us, length us, event | category | flops | bytes accessed | tf_op | source)
XLA Modules:
  0.0 164.2 jit_solution(6350079867155525175)
XLA Ops:
  0.0 5.5 %shard_map.65 = f32[10,128,128]{2,1,0:T(8,128)} custom-call(bf16[1024,1280]{1,0:T(8,128)(2,1)} %k_ref.3, bf16[1024,1280]{1,0:T(8,128)(2,1)} %v_ref.3), custom_call_target="tpu_custom_call" | custom-call | flops 335544320 | bytes 5898240 | tf_op jit(solution)/shard_map/pallas_call | solution.py:50
  5.5 1.1 convert_element_type.69
  6.7 4.9 %collective-permute-start = (bf16[10,128,128]{2,1,0:T(8,128)(2,1)S(1)}, bf16[10,128,128]{2,1,0:T(8,128)(2,1)S(1)}, u32[]{:S(2)}, u32[]{:S(2)}) collective-permute-start(bf16[10,128,128]{2,1,0:T(8,128)(2,1)S(1)} %convert_element_type.69), channel_id=1, source_target_pairs={{0,4},{4,8},{8,12},{12,16},{16,20},{20,24},{24,28},{1,5},{5,9},{9,... | collective-permute-start | bytes 983048 | tf_op jit(solution)/shard_map/ppermute | solution.py:155
  11.6 6.9 %collective-permute-done = bf16[10,128,128]{2,1,0:T(8,128)(2,1)S(1)} collective-permute-done((bf16[10,128,128]{2,1,0:T(8,128)(2,1)S(1)}, bf16[10,128,128]{2,1,0:T(8,128)(2,1)S(1)}, u32[]{:S(2)}, u32[]{:S(2)}) %collective-permute-start) | collective-permute-done | bytes 327712 | tf_op jit(solution)/shard_map/ppermute | solution.py:155
  18.5 1.2 fusion.20
  19.7 5.4 %collective-permute-start.1 = (bf16[10,128,128]{2,1,0:T(8,128)(2,1)S(1)}, bf16[10,128,128]{2,1,0:T(8,128)(2,1)S(1)}, u32[]{:S(2)}, u32[]{:S(2)}) collective-permute-start(bf16[10,128,128]{2,1,0:T(8,128)(2,1)S(1)} %fusion.20), channel_id=1, source_target_pairs={{0,8},{4,12},{8,16},{12,20},{16,24},{20,28},{1,9},{5,13},{9,17},{1... | collective-permute-start | bytes 983048 | tf_op jit(solution)/shard_map/ppermute | solution.py:155
  25.1 6.1 %collective-permute-done.1 = bf16[10,128,128]{2,1,0:T(8,128)(2,1)S(1)} collective-permute-done((bf16[10,128,128]{2,1,0:T(8,128)(2,1)S(1)}, bf16[10,128,128]{2,1,0:T(8,128)(2,1)S(1)}, u32[]{:S(2)}, u32[]{:S(2)}) %collective-permute-start.1) | collective-permute-done | bytes 327712 | tf_op jit(solution)/shard_map/ppermute | solution.py:155
  31.1 1.2 fusion.19
  32.3 5.4 %collective-permute-start.2 = (bf16[10,128,128]{2,1,0:T(8,128)(2,1)S(1)}, bf16[10,128,128]{2,1,0:T(8,128)(2,1)S(1)}, u32[]{:S(2)}, u32[]{:S(2)}) collective-permute-start(bf16[10,128,128]{2,1,0:T(8,128)(2,1)S(1)} %fusion.19), channel_id=1, source_target_pairs={{0,16},{4,20},{8,24},{12,28},{1,17},{5,21},{9,25},{13,29},{2,18},{... | collective-permute-start | bytes 983048 | tf_op jit(solution)/shard_map/ppermute | solution.py:155
  39.0 14.0 %shard_map.64.local_ref = f32[1024,1280]{1,0:T(8,128)} custom-call(bf16[1024,1280]{1,0:T(8,128)(2,1)} %q_ref.3, bf16[1024,1280]{1,0:T(8,128)(2,1)} %k_ref.3, bf16[1024,1280]{1,0:T(8,128)(2,1)} %v_ref.3), custom_call_target="tpu_custom_call" | custom-call | flops 3355443200 | bytes 13107200 | tf_op jit(solution)/shard_map/pallas_call | solution.py:90
  53.0 1.0 fusion.18.prefix_ref
  54.0 9.2 %shard_map.66 = bf16[1024,1280]{1,0:T(8,128)(2,1)} custom-call(s32[4]{0:T(128)} %pad_add_fusion.order_ref, f32[1024,1280]{1,0:T(8,128)} %shard_map.64.local_ref, bf16[1024,1280]{1,0:T(8,128)(2,1)} %q_ref.3, bf16[1024,1280]{1,0:T(8,128)(2,1)} %g_ref.1, f32[10,128,128]{2,1,0:T(8,128)} %fusion.18.prefix_ref, f32[1,1280]{1,0:T(1,128)} %reshape.3.gain_ref), custom_call_target="tpu_custom_call" | custom-call | flops 671088640 | bytes 13107200 | tf_op jit(solution)/shard_map/pallas_call | solution.py:124
  63.1 7.3 %fusion.9 = bf16[768,2048]{1,0:T(8,128)(2,1)S(1)} fusion(bf16[1280,6144]{1,0:T(8,128)(2,1)} %param.11, bf16[1024,1280]{1,0:T(8,128)(2,1)} %shard_map.66), kind=kOutput, calls=%fused_computation.9 | convolution fusion | flops 4028104704 | bytes 10354688 | tf_op jit(solution)/shard_map/dot_general | solution.py:213
  70.7 1.5 copy-done.1
  72.2 6.9 %fusion.12 = bf16[768,2048]{1,0:T(8,128)(2,1)S(1)} fusion(bf16[1280,6144]{1,0:T(8,128)(2,1)} %param.11, bf16[1024,1280]{1,0:T(8,128)(2,1)S(1)} %copy-done.1), kind=kOutput, calls=%fused_computation.10 | convolution fusion | flops 4028104704 | bytes 10354688 | tf_op jit(solution)/shard_map/dot_general | solution.py:213
  79.4 6.9 %fusion.6 = bf16[768,2048]{1,0:T(8,128)(2,1)S(1)} fusion(bf16[1280,6144]{1,0:T(8,128)(2,1)} %param.11, bf16[1024,1280]{1,0:T(8,128)(2,1)S(1)} %copy-done.1), kind=kOutput, calls=%fused_computation.8 | convolution fusion | flops 4028104704 | bytes 10354688 | tf_op jit(solution)/shard_map/dot_general | solution.py:213
  87.9 3.0 %collective-permute-done.3 = bf16[512,2048]{1,0:T(8,128)(2,1)S(1)} collective-permute-done((bf16[512,2048]{1,0:T(8,128)(2,1)S(1)}, bf16[512,2048]{1,0:T(8,128)(2,1)S(1)}, u32[]{:S(2)}, u32[]{:S(2)}) %collective-permute-start.3) | collective-permute-done | bytes 2097184 | tf_op jit(solution)/shard_map/ppermute | solution.py:159
  91.2 1.6 collective-permute-start.6
  93.3 1.5 collective-permute-start.8
  94.8 9.9 %convolution_convert_fusion = bf16[256,6144]{1,0:T(8,128)(2,1)S(1)} fusion(bf16[256,1280]{1,0:T(8,128)(2,1)S(1)} %slice-done.1, bf16[1280,6144]{1,0:T(8,128)(2,1)} %param.11), kind=kOutput, calls=%fused_computation | convolution fusion | flops 4028104704 | bytes 19529728 | tf_op jit(solution)/shard_map/dot_general | solution.py:195
  105.0 12.3 %collective-permute-done.6 = bf16[256,2048]{1,0:T(8,128)(2,1)S(1)} collective-permute-done((bf16[256,2048]{1,0:T(8,128)(2,1)S(1)}, bf16[256,2048]{1,0:T(8,128)(2,1)S(1)}, u32[]{:S(2)}, u32[]{:S(2)}) %collective-permute-start.6) | collective-permute-done | bytes 1048608 | tf_op jit(solution)/shard_map/ppermute | solution.py:159
  117.3 22.5 %collective-permute-done.7 = bf16[256,2048]{1,0:T(8,128)(2,1)S(1)} collective-permute-done((bf16[256,2048]{1,0:T(8,128)(2,1)S(1)}, bf16[256,2048]{1,0:T(8,128)(2,1)S(1)}, u32[]{:S(2)}, u32[]{:S(2)}) %collective-permute-start.7) | collective-permute-done | bytes 1048608 | tf_op jit(solution)/shard_map/ppermute | solution.py:159
  139.8 21.9 %collective-permute-done.8 = bf16[256,2048]{1,0:T(8,128)(2,1)S(1)} collective-permute-done((bf16[256,2048]{1,0:T(8,128)(2,1)S(1)}, bf16[256,2048]{1,0:T(8,128)(2,1)S(1)}, u32[]{:S(2)}, u32[]{:S(2)}) %collective-permute-start.8) | collective-permute-done | bytes 1048608 | tf_op jit(solution)/shard_map/ppermute | solution.py:159
  161.7 2.6 %add_convert_fusion = bf16[256,6144]{1,0:T(8,128)(2,1)} fusion(bf16[256,6144]{1,0:T(8,128)(2,1)S(1)} %convolution_convert_fusion, bf16[256,2048]{1,0:T(8,128)(2,1)S(1)} %slice.81, bf16[256,2048]{1,0:T(8,128)(2,1)S(1)} %slice-done, bf16[256,2048]{1,0:T(8,128)(2,1)S(1)} %slice.79, bf16[256,2048]{1,0:T(8,128)(2,1)S(1)} %collective-permute-done.8, ...), kind=kLoop, calls=%fused_computation.1 | loop fusion | flops 25165824 | bytes 12582912 | tf_op jit(solution)/shard_map/convert_element_type | solution.py:226
  (26 shorter events, 4.3 us)
Async XLA Ops:
  5.5 32.9 %copy-start.2 = (f32[1280]{0:T(1024)S(1)}, f32[1280]{0:T(1024)}, u32[]{:S(2)}) copy-start(f32[1280]{0:T(1024)} %param.10) | copy-start | bytes 15364
  6.7 11.8 %collective-permute-start = (bf16[10,128,128]{2,1,0:T(8,128)(2,1)S(1)}, bf16[10,128,128]{2,1,0:T(8,128)(2,1)S(1)}, u32[]{:S(2)}, u32[]{:S(2)}) collective-permute-start(bf16[10,128,128]{2,1,0:T(8,128)(2,1)S(1)} %convert_element_type.69), channel_id=1, source_target_pairs={{0,4},{4,8},{8,12},{12,16},{16,20},{20,24},{24,28},{1,5},{5,9},{9,... | collective-permute-start | bytes 983048 | tf_op jit(solution)/shard_map/ppermute | solution.py:155
  19.7 11.5 %collective-permute-start.1 = (bf16[10,128,128]{2,1,0:T(8,128)(2,1)S(1)}, bf16[10,128,128]{2,1,0:T(8,128)(2,1)S(1)}, u32[]{:S(2)}, u32[]{:S(2)}) collective-permute-start(bf16[10,128,128]{2,1,0:T(8,128)(2,1)S(1)} %fusion.20), channel_id=1, source_target_pairs={{0,8},{4,12},{8,16},{12,20},{16,24},{20,28},{1,9},{5,13},{9,17},{1... | collective-permute-start | bytes 983048 | tf_op jit(solution)/shard_map/ppermute | solution.py:155
  32.3 20.6 %collective-permute-start.2 = (bf16[10,128,128]{2,1,0:T(8,128)(2,1)S(1)}, bf16[10,128,128]{2,1,0:T(8,128)(2,1)S(1)}, u32[]{:S(2)}, u32[]{:S(2)}) collective-permute-start(bf16[10,128,128]{2,1,0:T(8,128)(2,1)S(1)} %fusion.19), channel_id=1, source_target_pairs={{0,16},{4,20},{8,24},{12,28},{1,17},{5,21},{9,25},{13,29},{2,18},{... | collective-permute-start | bytes 983048 | tf_op jit(solution)/shard_map/ppermute | solution.py:155
  70.5 1.7 %copy-start.1 = (bf16[1024,1280]{1,0:T(8,128)(2,1)S(1)}, bf16[1024,1280]{1,0:T(8,128)(2,1)}, u32[]{:S(2)}) copy-start(bf16[1024,1280]{1,0:T(8,128)(2,1)} %shard_map.66) | copy-start | bytes 7864324
  70.6 16.4 %collective-permute-start.4 = (bf16[512,2048]{1,0:T(8,128)(2,1)S(1)}, bf16[512,2048]{1,0:T(8,128)(2,1)S(1)}, u32[]{:S(2)}, u32[]{:S(2)}) collective-permute-start(bf16[512,2048]{1,0:T(8,128)(2,1)S(1)} %slice.73), channel_id=1, source_target_pairs={{0,1},{1,0},{2,3},{3,2},{4,5},{5,4},{6,7},{7,6},{8,9},{9,8},{10,11... | collective-permute-start | bytes 6291464 | tf_op jit(solution)/shard_map/ppermute | solution.py:159
  79.4 8.1 %collective-permute-start.5 = (bf16[512,2048]{1,0:T(8,128)(2,1)S(1)}, bf16[512,2048]{1,0:T(8,128)(2,1)S(1)}, u32[]{:S(2)}, u32[]{:S(2)}) collective-permute-start(bf16[512,2048]{1,0:T(8,128)(2,1)S(1)} %slice.76), channel_id=1, source_target_pairs={{0,1},{1,0},{2,3},{3,2},{4,5},{5,4},{6,7},{7,6},{8,9},{9,8},{10,11... | collective-permute-start | bytes 6291464 | tf_op jit(solution)/shard_map/ppermute | solution.py:159
  86.5 4.3 %collective-permute-start.3 = (bf16[512,2048]{1,0:T(8,128)(2,1)S(1)}, bf16[512,2048]{1,0:T(8,128)(2,1)S(1)}, u32[]{:S(2)}, u32[]{:S(2)}) collective-permute-start(bf16[512,2048]{1,0:T(8,128)(2,1)S(1)} %slice.70), channel_id=1, source_target_pairs={{0,1},{1,0},{2,3},{3,2},{4,5},{5,4},{6,7},{7,6},{8,9},{9,8},{10,11... | collective-permute-start | bytes 6291464 | tf_op jit(solution)/shard_map/ppermute | solution.py:159
  87.0 17.7 %copy-start = (bf16[512,2048]{1,0:T(8,128)(2,1)}, bf16[512,2048]{1,0:T(8,128)(2,1)S(1)}, u32[]{:S(2)}) copy-start(bf16[512,2048]{1,0:T(8,128)(2,1)S(1)} %collective-permute-done.4) | copy-start | bytes 6291460
  87.4 7.4 %slice-start.1 = ((bf16[1024,1280]{1,0:T(8,128)(2,1)}), bf16[256,1280]{1,0:T(8,128)(2,1)S(1)}, s32[]{:S(2)}) async-start(bf16[1024,1280]{1,0:T(8,128)(2,1)} %shard_map.66), calls=%async_computation.1 | async-start | bytes 1310720 | tf_op jit(solution)/shard_map/slice | solution.py:208
  91.2 26.1 %collective-permute-start.6 = (bf16[256,2048]{1,0:T(8,128)(2,1)S(1)}, bf16[256,2048]{1,0:T(8,128)(2,1)S(1)}, u32[]{:S(2)}, u32[]{:S(2)}) collective-permute-start(bf16[256,2048]{1,0:T(8,128)(2,1)S(1)} %add_convert_fusion.3), channel_id=1, source_target_pairs={{0,2},{2,0},{1,3},{3,1},{4,6},{6,4},{5,7},{7,5},{8,10},{10,8},{9,1... | collective-permute-start | bytes 3145736 | tf_op jit(solution)/shard_map/ppermute | solution.py:159
  92.8 47.0 %collective-permute-start.7 = (bf16[256,2048]{1,0:T(8,128)(2,1)S(1)}, bf16[256,2048]{1,0:T(8,128)(2,1)S(1)}, u32[]{:S(2)}, u32[]{:S(2)}) collective-permute-start(bf16[256,2048]{1,0:T(8,128)(2,1)S(1)} %add_convert_fusion.2), channel_id=1, source_target_pairs={{0,2},{2,0},{1,3},{3,1},{4,6},{6,4},{5,7},{7,5},{8,10},{10,8},{9,1... | collective-permute-start | bytes 3145736 | tf_op jit(solution)/shard_map/ppermute | solution.py:159
  93.3 68.4 %collective-permute-start.8 = (bf16[256,2048]{1,0:T(8,128)(2,1)S(1)}, bf16[256,2048]{1,0:T(8,128)(2,1)S(1)}, u32[]{:S(2)}, u32[]{:S(2)}) collective-permute-start(bf16[256,2048]{1,0:T(8,128)(2,1)S(1)} %add_convert_fusion.1), channel_id=1, source_target_pairs={{0,2},{2,0},{1,3},{3,1},{4,6},{6,4},{5,7},{7,5},{8,10},{10,8},{9,1... | collective-permute-start | bytes 3145736 | tf_op jit(solution)/shard_map/ppermute | solution.py:159
  104.8 56.9 %slice-start = ((bf16[512,2048]{1,0:T(8,128)(2,1)}), bf16[256,2048]{1,0:T(8,128)(2,1)S(1)}, s32[]{:S(2)}) async-start(bf16[512,2048]{1,0:T(8,128)(2,1)} %copy-done), calls=%async_computation | async-start | bytes 2097152 | tf_op jit(solution)/shard_map/slice | solution.py:219

commit v8 on v6

--- a/solution.py
+++ b/solution.py
@@ -82,41 +82,46 @@
         )
 
 
-def local_attention(queries, keys, values):
+def local_attention(queries, keys, values, first_head, heads):
     tokens, columns = queries.shape
-    heads = columns // HD
     tiles = tokens // QUERY_TILE
     pairs = QUERY_TILE * QUERY_TILE * tiles * (tiles + 1) // 2
+    picked = pl.BlockSpec((tokens, HD), lambda h: (0, h + first_head))
     return pl.pallas_call(
         local_kernel,
         grid=(heads,),
-        in_specs=[head_block(tokens)] * 3,
+        in_specs=[picked] * 3,
         out_specs=head_block(tokens),
-        out_shape=jax.ShapeDtypeStruct((tokens, columns), jnp.float32),
+        out_shape=jax.ShapeDtypeStruct((tokens, heads * HD), jnp.float32),
         cost_estimate=pl.CostEstimate(
             flops=4 * pairs * HD * heads,
-            transcendentals=2 * tokens * columns,
-            bytes_accessed=10 * tokens * columns,
+            transcendentals=2 * tokens * heads * HD,
+            bytes_accessed=10 * tokens * heads * HD,
         ),
     )(queries, keys, values)
 
 
-def mix_kernel(local_ref, q_ref, g_ref, hi_ref, lo_ref, gain_ref, out_ref):
+def mix_kernel(local_a_ref, local_b_ref, q_ref, g_ref, hi_ref, lo_ref, gain_ref, out_ref):
     query_act = silu(q_ref[...])
     gates = g_ref[...].astype(jnp.float32)
     gate_open = 1.0 / (1.0 + jnp.exp(-gates))
+    first = local_a_ref.shape[1] // HD
     for h in range(hi_ref.shape[0]):
         heads = slice(h * HD, (h + 1) * HD)
+        if h < first:
+            local = local_a_ref[:, heads]
+        else:
+            local = local_b_ref[:, (h - first) * HD:(h - first + 1) * HD]
         remote = jnp.dot(query_act[:, heads], hi_ref[h], preferred_element_type=jnp.float32) + jnp.dot(
             query_act[:, heads], lo_ref[h], preferred_element_type=jnp.float32
         )
-        attention = local_ref[:, heads] + remote
+        attention = local + remote
         mean_sq = jnp.mean(attention * attention, axis=-1, keepdims=True)
         normed = attention * lax.rsqrt(mean_sq + epsilon) * gain_ref[:, heads]
         out_ref[:, heads] = (normed * gate_open[:, heads]).astype(out_ref.dtype)
 
 
-def mix(local_part, queries, gates, prefix_hi, prefix_lo, gain):
+def mix(local_a, local_b, queries, gates, prefix_hi, prefix_lo, gain):
     tokens, columns = queries.shape
     heads = columns // HD
     whole_state = pl.BlockSpec((heads, HD, HD), lambda i: (0, 0, 0))
@@ -124,7 +129,8 @@
         mix_kernel,
         grid=(tokens // ROW_TILE,),
         in_specs=[
-            row_block(columns),
+            row_block(local_a.shape[1]),
+            row_block(local_b.shape[1]),
             row_block(columns),
             row_block(columns),
             whole_state,
@@ -138,7 +144,7 @@
             transcendentals=2 * tokens * columns,
             bytes_accessed=10 * tokens * columns,
         ),
-    )(local_part, queries, gates, prefix_hi, prefix_lo, gain.reshape(1, columns))
+    )(local_a, local_b, queries, gates, prefix_hi, prefix_lo, gain.reshape(1, columns))
 
 
 def split_bf16(x):
@@ -156,16 +162,27 @@
     return lax.ppermute(block, axis, [(0, 1), (1, 0)])
 
 
-def exclusive_prefix(state, axis):
+def exclusive_prefix(state, axis, fillers=()):
     inclusive = state
     exclusive = jnp.zeros_like(state)
     distance = 1
+    results = []
     while distance < lax.axis_size(axis):
-        arrived = shift(inclusive.astype(jnp.bfloat16), axis, distance).astype(jnp.float32)
+        sent = inclusive.astype(jnp.bfloat16)
+        arrived = shift(sent, axis, distance)
+        if len(results) < len(fillers):
+            function, operands = fillers[len(results)]
+            _, operands = lax.optimization_barrier((sent, operands))
+            result = function(*operands)
+            arrived, result = lax.optimization_barrier((arrived, result))
+            results.append(result)
+        arrived = arrived.astype(jnp.float32)
         exclusive = exclusive + arrived
         inclusive = inclusive + arrived
         distance *= 2
-    return exclusive
+    for function, operands in fillers[len(results):]:
+        results.append(function(*operands))
+    return exclusive, results
 
 
 def project_and_reduce(mixed_rows, out_weight):
@@ -217,10 +234,15 @@
 
 def on_device(queries, keys, values, gates, gain, out_weight):
     own_state = key_value_states(keys, values)
-    prefix = exclusive_prefix(own_state, "ctx")
-    local_part = local_attention(queries, keys, values)
+    head_count = queries.shape[1] // HD
+    first = (head_count + 1) // 2
+    fillers = (
+        (lambda q, k, v: local_attention(q, k, v, 0, first), (queries, keys, values)),
+        (lambda q, k, v: local_attention(q, k, v, first, head_count - first), (queries, keys, values)),
+    )
+    prefix, (local_a, local_b) = exclusive_prefix(own_state, "ctx", fillers)
     prefix_hi, prefix_lo = split_bf16(prefix)
-    mixed_rows = mix(local_part, queries, gates, prefix_hi, prefix_lo, gain)
+    mixed_rows = mix(local_a, local_b, queries, gates, prefix_hi, prefix_lo, gain)
     return project_and_reduce(mixed_rows, out_weight)
 
 

time: 159 us -> 154 us (0.969)
  the two profiles are of different devices: /device:TPU:0 before, /device:TPU:24 now
where the time goes in v8:
time: 154 us; the launch traced here: 153 us
  waiting for transfers between devices  76.4 us (50%)
  Pallas kernels  29.7 us (19%)
  matrix products  29.2 us (19%)
  starting transfers between devices  10.6 us (7%)
  other arithmetic  6.33 us (4%)
    ppermute x7, waiting for transfers between devices, swap(): return lax.ppermute(block, axis, [(0, 1), (1, 0)])  58.5 us
    ppermute x3, waiting for transfers between devices, shift(): lax.ppermute(block, axis, [(i, i + distance) for i in range(size) if i +...  17.8 us
    pallas_call x2, Pallas kernels, local_attention(): pl.pallas_call(local_kernel, grid=(heads,), in_specs=[picked] * 3, out_sp...  15.8 us
    dot_general x3, matrix products, project_and_reduce(): jnp.dot(far_rows, out_weight[:, c * chunk:(c + 1) * chunk], preferred_ele...  14.8 us
    dot_general x2, matrix products, product(): jnp.dot(rows, out_weight, preferred_element_type=jnp.float32)  14.4 us
    pallas_call x1, Pallas kernels, mix(): pl.pallas_call(mix_kernel, grid=(tokens // ROW_TILE,), in_specs=[row_bloc...  8.31 us
    ppermute x3, starting transfers between devices, shift(): lax.ppermute(block, axis, [(i, i + distance) for i in range(size) if i +...  6.12 us
    pallas_call x1, Pallas kernels, key_value_states(): pl.pallas_call(state_kernel, grid=(tokens // ROW_TILE,), in_specs=[row_bl...  5.53 us
  transfers between devices with their start and end apart: 10, of which 7 were waited for; matrix products, arithmetic and copies ran while one was open for 10% of the time, Pallas kernels for 10%

profile of v8, /device:TPU:24, one launch (start us, length us, event | category | flops | bytes accessed | tf_op | source)
XLA Modules:
  0.0 153.5 jit_solution(15648143685602725636)
XLA Ops:
  0.0 5.5 %shard_map.64 = f32[10,128,128]{2,1,0:T(8,128)} custom-call(bf16[1024,1280]{1,0:T(8,128)(2,1)} %k_ref.3, bf16[1024,1280]{1,0:T(8,128)(2,1)} %v_ref.3), custom_call_target="tpu_custom_call" | custom-call | flops 335544320 | bytes 5898240 | tf_op jit(solution)/shard_map/pallas_call | solution.py:50
  5.5 1.1 convert_element_type.81
  6.7 3.5 %collective-permute-start = (bf16[10,128,128]{2,1,0:T(8,128)(2,1)S(1)}, bf16[10,128,128]{2,1,0:T(8,128)(2,1)S(1)}, u32[]{:S(2)}, u32[]{:S(2)}) collective-permute-start(bf16[10,128,128]{2,1,0:T(8,128)(2,1)S(1)} %convert_element_type.81), channel_id=1, source_target_pairs={{0,4},{4,8},{8,12},{12,16},{16,20},{20,24},{24,28},{1,5},{5,9},{9,... | collective-permute-start | bytes 983048 | tf_op jit(solution)/shard_map/ppermute | solution.py:158
  10.2 7.9 %shard_map.65.local_a_ref = f32[1024,640]{1,0:T(8,128)} custom-call(bf16[1024,1280]{1,0:T(8,128)(2,1)} %q_ref.3, bf16[1024,1280]{1,0:T(8,128)(2,1)} %k_ref.3, bf16[1024,1280]{1,0:T(8,128)(2,1)} %v_ref.3), custom_call_target="tpu_custom_call" | custom-call | flops 1677721600 | bytes 6553600 | tf_op jit(solution)/shard_map/pallas_call | solution.py:90
  18.1 1.0 collective-permute-done
  19.2 1.3 collective-permute-start.1
  20.5 7.9 %shard_map.66.local_b_ref = f32[1024,640]{1,0:T(8,128)} custom-call(bf16[1024,1280]{1,0:T(8,128)(2,1)} %q_ref.3, bf16[1024,1280]{1,0:T(8,128)(2,1)} %k_ref.3, bf16[1024,1280]{1,0:T(8,128)(2,1)} %v_ref.3), custom_call_target="tpu_custom_call" | custom-call | flops 1677721600 | bytes 6553600 | tf_op jit(solution)/shard_map/pallas_call | solution.py:90
  28.4 1.2 collective-permute-done.1
  29.8 1.3 collective-permute-start.2
  31.7 15.6 %collective-permute-done.2 = bf16[10,128,128]{2,1,0:T(8,128)(2,1)S(1)} collective-permute-done((bf16[10,128,128]{2,1,0:T(8,128)(2,1)S(1)}, bf16[10,128,128]{2,1,0:T(8,128)(2,1)S(1)}, u32[]{:S(2)}, u32[]{:S(2)}) %collective-permute-start.2) | collective-permute-done | bytes 327712 | tf_op jit(solution)/shard_map/ppermute | solution.py:158
  47.4 1.1 subtract_convert_fusion
  48.4 8.3 %shard_map.67 = bf16[1024,1280]{1,0:T(8,128)(2,1)} custom-call(f32[1024,640]{1,0:T(8,128)} %shard_map.65.local_a_ref, f32[1024,640]{1,0:T(8,128)} %shard_map.66.local_b_ref, bf16[1024,1280]{1,0:T(8,128)(2,1)} %q_ref.3, bf16[1024,1280]{1,0:T(8,128)(2,1)} %g_ref.1, bf16[10,128,128]{2,1,0:T(8,128)(2,1)} %get-tuple-element.34.hi_ref, ...), custom_call_target="tpu_custom_call" | custom-call | flops 671088640 | bytes 13107200 | tf_op jit(solution)/shard_map/pallas_call | solution.py:128
  56.7 5.9 %fusion.12 = bf16[512,2048]{1,0:T(8,128)(2,1)S(1)} fusion(bf16[1280,6144]{1,0:T(8,128)(2,1)} %param.11, bf16[1024,1280]{1,0:T(8,128)(2,1)} %shard_map.67, s32[]{:T(128)S(6)} %select_n.8), kind=kOutput, calls=%fused_computation.11 | convolution fusion | flops 2685403136 | bytes 8650756 | tf_op jit(solution)/shard_map/dot_general | solution.py:220
  62.7 5.8 %fusion.9 = bf16[512,2048]{1,0:T(8,128)(2,1)S(1)} fusion(bf16[1280,6144]{1,0:T(8,128)(2,1)} %param.11, bf16[1024,1280]{1,0:T(8,128)(2,1)S(1)} %copy-done.1, s32[]{:T(128)S(6)} %select_n.8), kind=kOutput, calls=%fused_computation.10 | convolution fusion | flops 2685403136 | bytes 8650756 | tf_op jit(solution)/shard_map/dot_general | solution.py:220
  69.4 3.1 %fusion.6 = bf16[512,2048]{1,0:T(8,128)(2,1)S(1)} fusion(bf16[1280,6144]{1,0:T(8,128)(2,1)S(1)} %bitcast.3, bf16[1024,1280]{1,0:T(8,128)(2,1)S(1)} %copy-done.1, s32[]{:T(128)S(6)} %select_n.8), kind=kOutput, calls=%fused_computation.9 | convolution fusion | flops 2685403136 | bytes 8650756 | tf_op jit(solution)/shard_map/dot_general | solution.py:220
  73.8 1.6 %collective-permute-done.3 = bf16[256,2048]{1,0:T(8,128)(2,1)S(1)} collective-permute-done((bf16[256,2048]{1,0:T(8,128)(2,1)S(1)}, bf16[256,2048]{1,0:T(8,128)(2,1)S(1)}, u32[]{:S(2)}, u32[]{:S(2)}) %collective-permute-start.3) | collective-permute-done | bytes 1048608 | tf_op jit(solution)/shard_map/ppermute | solution.py:162
  75.8 4.4 %convolution_convert_fusion = bf16[256,6144]{1,0:T(8,128)(2,1)S(1)} fusion(bf16[1280,6144]{1,0:T(8,128)(2,1)S(1)} %bitcast.3, bf16[512,1280]{1,0:T(8,128)(2,1)S(1)} %constant_dynamic-slice_fusion, s32[]{:T(128)S(6)} %select_n.20), kind=kOutput, calls=%fused_computation | convolution fusion | flops 4028104704 | bytes 19529732 | tf_op jit(solution)/shard_map/dot_general | solution.py:196
  80.5 1.5 collective-permute-start.7
  82.5 1.5 collective-permute-start.9
  84.0 9.9 %convolution_convert_fusion.1 = bf16[256,6144]{1,0:T(8,128)(2,1)S(1)} fusion(bf16[1280,6144]{1,0:T(8,128)(2,1)} %param.11, bf16[512,1280]{1,0:T(8,128)(2,1)S(1)} %constant_dynamic-slice_fusion, s32[]{:T(128)S(6)} %select_n.9), kind=kOutput, calls=%fused_computation.1 | convolution fusion | flops 4028104704 | bytes 19529732 | tf_op jit(solution)/shard_map/dot_general | solution.py:196
  94.0 12.6 %collective-permute-done.7 = bf16[256,2048]{1,0:T(8,128)(2,1)S(1)} collective-permute-done((bf16[256,2048]{1,0:T(8,128)(2,1)S(1)}, bf16[256,2048]{1,0:T(8,128)(2,1)S(1)}, u32[]{:S(2)}, u32[]{:S(2)}) %collective-permute-start.7) | collective-permute-done | bytes 1048608 | tf_op jit(solution)/shard_map/ppermute | solution.py:162
  106.5 22.5 %collective-permute-done.8 = bf16[256,2048]{1,0:T(8,128)(2,1)S(1)} collective-permute-done((bf16[256,2048]{1,0:T(8,128)(2,1)S(1)}, bf16[256,2048]{1,0:T(8,128)(2,1)S(1)}, u32[]{:S(2)}, u32[]{:S(2)}) %collective-permute-start.8) | collective-permute-done | bytes 1048608 | tf_op jit(solution)/shard_map/ppermute | solution.py:162
  129.0 21.9 %collective-permute-done.9 = bf16[256,2048]{1,0:T(8,128)(2,1)S(1)} collective-permute-done((bf16[256,2048]{1,0:T(8,128)(2,1)S(1)}, bf16[256,2048]{1,0:T(8,128)(2,1)S(1)}, u32[]{:S(2)}, u32[]{:S(2)}) %collective-permute-start.9) | collective-permute-done | bytes 1048608 | tf_op jit(solution)/shard_map/ppermute | solution.py:162
  150.9 2.6 %add_convert_fusion = bf16[256,6144]{1,0:T(8,128)(2,1)} fusion(bf16[256,6144]{1,0:T(8,128)(2,1)S(1)} %collective-permute-done.6, bf16[256,6144]{1,0:T(8,128)(2,1)S(1)} %convolution_convert_fusion.1, bf16[256,2048]{1,0:T(8,128)(2,1)S(1)} %collective-permute-done.9, bf16[256,2048]{1,0:T(8,128)(2,1)S(1)} %collective-permute-done.8, ...), kind=kLoop, calls=%fused_computation.2 | loop fusion | flops 17301504 | bytes 12582912 | tf_op jit(solution)/shard_map/convert_element_type | solution.py:232
  (33 shorter events, 4.1 us)
Async XLA Ops:
  6.7 12.4 %copy-start = (f32[10,128,128]{2,1,0:T(8,128)S(1)}, f32[10,128,128]{2,1,0:T(8,128)}, u32[]{:S(2)}) copy-start(f32[10,128,128]{2,1,0:T(8,128)} %shard_map.64) | copy-start | bytes 1966084
  6.7 12.4 %collective-permute-start = (bf16[10,128,128]{2,1,0:T(8,128)(2,1)S(1)}, bf16[10,128,128]{2,1,0:T(8,128)(2,1)S(1)}, u32[]{:S(2)}, u32[]{:S(2)}) collective-permute-start(bf16[10,128,128]{2,1,0:T(8,128)(2,1)S(1)} %convert_element_type.81), channel_id=1, source_target_pairs={{0,4},{4,8},{8,12},{12,16},{16,20},{20,24},{24,28},{1,5},{5,9},{9,... | collective-permute-start | bytes 983048 | tf_op jit(solution)/shard_map/ppermute | solution.py:158
  19.2 12.0 %copy-start.2 = (f32[1280]{0:T(1024)S(1)}, f32[1280]{0:T(1024)}, u32[]{:S(2)}) copy-start(f32[1280]{0:T(1024)} %param.10) | copy-start | bytes 15364
  19.2 10.5 %collective-permute-start.1 = (bf16[10,128,128]{2,1,0:T(8,128)(2,1)S(1)}, bf16[10,128,128]{2,1,0:T(8,128)(2,1)S(1)}, u32[]{:S(2)}, u32[]{:S(2)}) collective-permute-start(bf16[10,128,128]{2,1,0:T(8,128)(2,1)S(1)} %fusion.22), channel_id=1, source_target_pairs={{0,8},{4,12},{8,16},{12,20},{16,24},{20,28},{1,9},{5,13},{9,17},{1... | collective-permute-start | bytes 983048 | tf_op jit(solution)/shard_map/ppermute | solution.py:158
  29.8 17.6 %collective-permute-start.2 = (bf16[10,128,128]{2,1,0:T(8,128)(2,1)S(1)}, bf16[10,128,128]{2,1,0:T(8,128)(2,1)S(1)}, u32[]{:S(2)}, u32[]{:S(2)}) collective-permute-start(bf16[10,128,128]{2,1,0:T(8,128)(2,1)S(1)} %fusion.19), channel_id=1, source_target_pairs={{0,16},{4,20},{8,24},{12,28},{1,17},{5,21},{9,25},{13,29},{2,18},{... | collective-permute-start | bytes 983048 | tf_op jit(solution)/shard_map/ppermute | solution.py:158
  56.7 5.9 %copy-start.1 = (bf16[1024,1280]{1,0:T(8,128)(2,1)S(1)}, bf16[1024,1280]{1,0:T(8,128)(2,1)}, u32[]{:S(2)}) copy-start(bf16[1024,1280]{1,0:T(8,128)(2,1)} %shard_map.67) | copy-start | bytes 7864324
  56.7 12.7 %slice-start = ((s8[15728640]{0:T(1024)(128)(4,1)}), s8[4194304]{0:T(1024)(128)(4,1)S(1)}, s32[]{:S(2)}) async-start(s8[15728640]{0:T(1024)(128)(4,1)} %bitcast.2), calls=%async_computation | async-start | bytes 8388608
  56.7 12.7 %slice-start.1 = ((s8[15728640]{0:T(1024)(128)(4,1)}), s8[4194304]{0:T(1024)(128)(4,1)S(1)}, s32[]{:S(2)}) async-start(s8[15728640]{0:T(1024)(128)(4,1)} %bitcast.2), calls=%async_computation.1 | async-start | bytes 8388608
  62.7 6.7 %slice-start.2 = ((s8[15728640]{0:T(1024)(128)(4,1)}), s8[4194304]{0:T(1024)(128)(4,1)S(1)}, s32[]{:S(2)}) async-start(s8[15728640]{0:T(1024)(128)(4,1)} %bitcast.2), calls=%async_computation.2 | async-start | bytes 8388608
  62.7 6.7 %slice-start.3 = ((s8[15728640]{0:T(1024)(128)(4,1)}), s8[3145728]{0:T(1024)(128)(4,1)S(1)}, s32[]{:S(2)}) async-start(s8[15728640]{0:T(1024)(128)(4,1)} %bitcast.2), calls=%async_computation.3 | async-start | bytes 6291456
  68.6 4.2 %collective-permute-start.5 = (bf16[256,2048]{1,0:T(8,128)(2,1)S(1)}, bf16[256,2048]{1,0:T(8,128)(2,1)S(1)}, u32[]{:S(2)}, u32[]{:S(2)}) collective-permute-start(bf16[256,2048]{1,0:T(8,128)(2,1)S(1)} %constant_dynamic-slice_fusion.1), channel_id=1, source_target_pairs={{0,1},{1,0},{2,3},{3,2},{4,5},{5,4},{6,7},{7,6},{8,9},{9,8},{10,11... | collective-permute-start | bytes 3145736 | tf_op jit(solution)/shard_map/ppermute | solution.py:162
  68.8 4.5 %collective-permute-start.4 = (bf16[256,2048]{1,0:T(8,128)(2,1)S(1)}, bf16[256,2048]{1,0:T(8,128)(2,1)S(1)}, u32[]{:S(2)}, u32[]{:S(2)}) collective-permute-start(bf16[256,2048]{1,0:T(8,128)(2,1)S(1)} %constant_dynamic-slice_fusion.2), channel_id=1, source_target_pairs={{0,1},{1,0},{2,3},{3,2},{4,5},{5,4},{6,7},{7,6},{8,9},{9,8},{10,11... | collective-permute-start | bytes 3145736 | tf_op jit(solution)/shard_map/ppermute | solution.py:162
  72.6 2.7 %collective-permute-start.3 = (bf16[256,2048]{1,0:T(8,128)(2,1)S(1)}, bf16[256,2048]{1,0:T(8,128)(2,1)S(1)}, u32[]{:S(2)}, u32[]{:S(2)}) collective-permute-start(bf16[256,2048]{1,0:T(8,128)(2,1)S(1)} %constant_dynamic-slice_fusion.3), channel_id=1, source_target_pairs={{0,1},{1,0},{2,3},{3,2},{4,5},{5,4},{6,7},{7,6},{8,9},{9,8},{10,11... | collective-permute-start | bytes 3145736 | tf_op jit(solution)/shard_map/ppermute | solution.py:162
  80.3 70.6 %collective-permute-start.6 = (bf16[256,6144]{1,0:T(8,128)(2,1)S(1)}, bf16[256,6144]{1,0:T(8,128)(2,1)S(1)}, u32[]{:S(2)}, u32[]{:S(2)}) collective-permute-start(bf16[256,6144]{1,0:T(8,128)(2,1)S(1)} %convolution_convert_fusion), channel_id=1, source_target_pairs={{0,1},{1,0},{2,3},{3,2},{4,5},{5,4},{6,7},{7,6},{8,9},{9,8},{10,11... | collective-permute-start | bytes 9437192 | tf_op jit(solution)/shard_map/ppermute | solution.py:162
  80.5 26.0 %collective-permute-start.7 = (bf16[256,2048]{1,0:T(8,128)(2,1)S(1)}, bf16[256,2048]{1,0:T(8,128)(2,1)S(1)}, u32[]{:S(2)}, u32[]{:S(2)}) collective-permute-start(bf16[256,2048]{1,0:T(8,128)(2,1)S(1)} %add_convert_fusion.3), channel_id=1, source_target_pairs={{0,2},{2,0},{1,3},{3,1},{4,6},{6,4},{5,7},{7,5},{8,10},{10,8},{9,1... | collective-permute-start | bytes 3145736 | tf_op jit(solution)/shard_map/ppermute | solution.py:162
  82.0 47.0 %collective-permute-start.8 = (bf16[256,2048]{1,0:T(8,128)(2,1)S(1)}, bf16[256,2048]{1,0:T(8,128)(2,1)S(1)}, u32[]{:S(2)}, u32[]{:S(2)}) collective-permute-start(bf16[256,2048]{1,0:T(8,128)(2,1)S(1)} %add_convert_fusion.2), channel_id=1, source_target_pairs={{0,2},{2,0},{1,3},{3,1},{4,6},{6,4},{5,7},{7,5},{8,10},{10,8},{9,1... | collective-permute-start | bytes 3145736 | tf_op jit(solution)/shard_map/ppermute | solution.py:162
  82.5 68.4 %collective-permute-start.9 = (bf16[256,2048]{1,0:T(8,128)(2,1)S(1)}, bf16[256,2048]{1,0:T(8,128)(2,1)S(1)}, u32[]{:S(2)}, u32[]{:S(2)}) collective-permute-start(bf16[256,2048]{1,0:T(8,128)(2,1)S(1)} %add_convert_fusion.1), channel_id=1, source_target_pairs={{0,2},{2,0},{1,3},{3,1},{4,6},{6,4},{5,7},{7,5},{8,10},{10,8},{9,1... | collective-permute-start | bytes 3145736 | tf_op jit(solution)/shard_map/ppermute | solution.py:162

commit v9 on v8

--- a/solution.py
+++ b/solution.py
@@ -101,19 +101,20 @@
     )(queries, keys, values)
 
 
-def mix_kernel(local_a_ref, local_b_ref, q_ref, g_ref, hi_ref, lo_ref, gain_ref, out_ref):
+def mix_kernel(order_ref, local_a_ref, local_b_ref, q_ref, g_ref, prefix_ref, gain_ref, out_ref):
     query_act = silu(q_ref[...])
     gates = g_ref[...].astype(jnp.float32)
     gate_open = 1.0 / (1.0 + jnp.exp(-gates))
     first = local_a_ref.shape[1] // HD
-    for h in range(hi_ref.shape[0]):
+    for h in range(prefix_ref.shape[0]):
         heads = slice(h * HD, (h + 1) * HD)
         if h < first:
             local = local_a_ref[:, heads]
         else:
             local = local_b_ref[:, (h - first) * HD:(h - first + 1) * HD]
-        remote = jnp.dot(query_act[:, heads], hi_ref[h], preferred_element_type=jnp.float32) + jnp.dot(
-            query_act[:, heads], lo_ref[h], preferred_element_type=jnp.float32
+        prefix_hi, prefix_lo = split_bf16(prefix_ref[h])
+        remote = jnp.dot(query_act[:, heads], prefix_hi, preferred_element_type=jnp.float32) + jnp.dot(
+            query_act[:, heads], prefix_lo, preferred_element_type=jnp.float32
         )
         attention = local + remote
         mean_sq = jnp.mean(attention * attention, axis=-1, keepdims=True)
@@ -121,30 +122,35 @@
         out_ref[:, heads] = (normed * gate_open[:, heads]).astype(out_ref.dtype)
 
 
-def mix(local_a, local_b, queries, gates, prefix_hi, prefix_lo, gain):
+def mix(order, local_a, local_b, queries, gates, prefix, gain):
     tokens, columns = queries.shape
     heads = columns // HD
-    whole_state = pl.BlockSpec((heads, HD, HD), lambda i: (0, 0, 0))
+
+    def picked(width):
+        return pl.BlockSpec((ROW_TILE, width), lambda i, order: (order[i], 0))
+
     return pl.pallas_call(
         mix_kernel,
-        grid=(tokens // ROW_TILE,),
-        in_specs=[
-            row_block(local_a.shape[1]),
-            row_block(local_b.shape[1]),
-            row_block(columns),
-            row_block(columns),
-            whole_state,
-            whole_state,
-            pl.BlockSpec((1, columns), lambda i: (0, 0)),
-        ],
-        out_specs=row_block(columns),
+        grid_spec=pltpu.PrefetchScalarGridSpec(
+            num_scalar_prefetch=1,
+            grid=(tokens // ROW_TILE,),
+            in_specs=[
+                picked(local_a.shape[1]),
+                picked(local_b.shape[1]),
+                picked(columns),
+                picked(columns),
+                pl.BlockSpec((heads, HD, HD), lambda i, order: (0, 0, 0)),
+                pl.BlockSpec((1, columns), lambda i, order: (0, 0)),
+            ],
+            out_specs=pl.BlockSpec((ROW_TILE, columns), lambda i, order: (i, 0)),
+        ),
         out_shape=jax.ShapeDtypeStruct((tokens, columns), jnp.bfloat16),
         cost_estimate=pl.CostEstimate(
             flops=4 * tokens * HD * HD * heads,
             transcendentals=2 * tokens * columns,
             bytes_accessed=10 * tokens * columns,
         ),
-    )(local_a, local_b, queries, gates, prefix_hi, prefix_lo, gain.reshape(1, columns))
+    )(order, local_a, local_b, queries, gates, prefix, gain.reshape(1, columns))
 
 
 def split_bf16(x):
@@ -185,6 +191,19 @@
     return exclusive, results
 
 
+def reduce_order(tokens):
+    ty_size = lax.axis_size("ty")
+    tc_size = lax.axis_size("tc")
+    tiles = tokens // ROW_TILE
+    if ty_size != 2 or tc_size != 2 or tiles != 4:
+        return jnp.arange(tiles, dtype=jnp.int32)
+    ty = lax.axis_index("ty")
+    tc = lax.axis_index("tc")
+    return jnp.stack(
+        [(1 - ty) * 2 + 1 - tc, (1 - ty) * 2 + tc, ty * 2 + 1 - tc, ty * 2 + tc]
+    ).astype(jnp.int32)
+
+
 def project_and_reduce(mixed_rows, out_weight):
     tokens, columns = mixed_rows.shape
     ty_size = lax.axis_size("ty")
@@ -195,7 +214,7 @@
     def product(rows):
         return jnp.dot(rows, out_weight, preferred_element_type=jnp.float32).astype(jnp.bfloat16)
 
-    if ty_size != 2 or tc_size != 2:
+    if ty_size != 2 or tc_size != 2 or block != ROW_TILE:
         ordered = (
             mixed_rows.reshape(ty_size, tc_size, block, columns)
             .transpose(1, 0, 2, 3)
@@ -205,28 +224,22 @@
         part = lax.psum_scatter(part, "tc", scatter_dimension=0, tiled=True)
         return lax.psum_scatter(part, "ty", scatter_dimension=0, tiled=True)
 
-    ty = lax.axis_index("ty")
-    tc = lax.axis_index("tc")
-    pair = tc_size * block
-    far_rows = lax.dynamic_slice_in_dim(mixed_rows, (1 - ty) * pair, pair, axis=0)
-    near_rows = lax.dynamic_slice_in_dim(mixed_rows, ty * pair, pair, axis=0)
-
-    def block_of(part, owner_tc):
-        return lax.dynamic_slice_in_dim(part, owner_tc * block, block, axis=0)
-
+    far_rows = mixed_rows[:2 * block]
+    partner_rows = mixed_rows[2 * block:3 * block]
+    own_rows = mixed_rows[3 * block:]
     chunk = width // COLUMN_CHUNKS
     chip_sums = []
     for c in range(COLUMN_CHUNKS):
         far_part = jnp.dot(
             far_rows, out_weight[:, c * chunk:(c + 1) * chunk], preferred_element_type=jnp.float32
         ).astype(jnp.bfloat16)
-        from_partner = swap(block_of(far_part, 1 - tc), "tc")
-        chip_sum = block_of(far_part, tc).astype(jnp.float32) + from_partner.astype(jnp.float32)
+        from_partner = swap(far_part[:block], "tc")
+        chip_sum = far_part[block:].astype(jnp.float32) + from_partner.astype(jnp.float32)
         chip_sums.append(chip_sum.astype(jnp.bfloat16))
-    chip_sums, near_rows = lax.optimization_barrier((chip_sums, near_rows))
+    chip_sums, partner_rows, own_rows = lax.optimization_barrier((chip_sums, partner_rows, own_rows))
     across = [swap(chip_sum, "ty") for chip_sum in chip_sums]
-    near = swap(product(block_of(near_rows, 1 - tc)), "tc")
-    mine = lax.optimization_barrier(product(block_of(near_rows, tc)))
+    near = swap(product(partner_rows), "tc")
+    mine = lax.optimization_barrier(product(own_rows))
     far = jnp.concatenate(across, axis=1)
     total = mine.astype(jnp.float32) + near.astype(jnp.float32) + far.astype(jnp.float32)
     return total.astype(jnp.bfloat16)
@@ -241,8 +254,7 @@
         (lambda q, k, v: local_attention(q, k, v, first, head_count - first), (queries, keys, values)),
     )
     prefix, (local_a, local_b) = exclusive_prefix(own_state, "ctx", fillers)
-    prefix_hi, prefix_lo = split_bf16(prefix)
-    mixed_rows = mix(local_a, local_b, queries, gates, prefix_hi, prefix_lo, gain)
+    mixed_rows = mix(reduce_order(queries.shape[0]), local_a, local_b, queries, gates, prefix, gain)
     return project_and_reduce(mixed_rows, out_weight)
 
 

time: 154 us -> 155 us (level)
  no operation moved by 1% of the time
where the time goes in v9:
time: 155 us; the launch traced here: 154 us
  waiting for transfers between devices  75.8 us (49%)
  Pallas kernels  30.7 us (20%)
  matrix products  29.2 us (19%)
  starting transfers between devices  10.6 us (7%)
  other arithmetic  6.7 us (4%)
    ppermute x7, waiting for transfers between devices, swap(): return lax.ppermute(block, axis, [(0, 1), (1, 0)])  58.6 us
    ppermute x3, waiting for transfers between devices, shift(): lax.ppermute(block, axis, [(i, i + distance) for i in range(size) if i +...  17.2 us
    pallas_call x2, Pallas kernels, local_attention(): pl.pallas_call(local_kernel, grid=(heads,), in_specs=[picked] * 3, out_sp...  15.8 us
    dot_general x3, matrix products, project_and_reduce(): jnp.dot(far_rows, out_weight[:, c * chunk:(c + 1) * chunk], preferred_ele...  14.8 us
    dot_general x2, matrix products, product(): jnp.dot(rows, out_weight, preferred_element_type=jnp.float32)  14.4 us
    pallas_call x1, Pallas kernels, mix(): pl.pallas_call(mix_kernel, grid_spec=pltpu.PrefetchScalarGridSpec(num_sca...  9.39 us
    ppermute x3, starting transfers between devices, shift(): lax.ppermute(block, axis, [(i, i + distance) for i in range(size) if i +...  6.12 us
    pallas_call x1, Pallas kernels, key_value_states(): pl.pallas_call(state_kernel, grid=(tokens // ROW_TILE,), in_specs=[row_bl...  5.53 us
  transfers between devices with their start and end apart: 10, of which 7 were waited for; matrix products, arithmetic and copies ran while one was open for 10% of the time, Pallas kernels for 10%

profile of v9, /device:TPU:24, one launch (start us, length us, event | category | flops | bytes accessed | tf_op | source)
XLA Modules:
  0.0 154.3 jit_solution(4614466284790190271)
XLA Ops:
  0.0 5.5 %shard_map.64 = f32[10,128,128]{2,1,0:T(8,128)} custom-call(bf16[1024,1280]{1,0:T(8,128)(2,1)} %k_ref.3, bf16[1024,1280]{1,0:T(8,128)(2,1)} %v_ref.3), custom_call_target="tpu_custom_call" | custom-call | flops 335544320 | bytes 5898240 | tf_op jit(solution)/shard_map/pallas_call | solution.py:50
  5.5 1.1 convert_element_type.72
  6.7 3.5 %collective-permute-start = (bf16[10,128,128]{2,1,0:T(8,128)(2,1)S(1)}, bf16[10,128,128]{2,1,0:T(8,128)(2,1)S(1)}, u32[]{:S(2)}, u32[]{:S(2)}) collective-permute-start(bf16[10,128,128]{2,1,0:T(8,128)(2,1)S(1)} %convert_element_type.72), channel_id=1, source_target_pairs={{0,4},{4,8},{8,12},{12,16},{16,20},{20,24},{24,28},{1,5},{5,9},{9,... | collective-permute-start | bytes 983048 | tf_op jit(solution)/shard_map/ppermute | solution.py:164
  10.2 7.9 %shard_map.65.local_a_ref = f32[1024,640]{1,0:T(8,128)} custom-call(bf16[1024,1280]{1,0:T(8,128)(2,1)} %q_ref.3, bf16[1024,1280]{1,0:T(8,128)(2,1)} %k_ref.3, bf16[1024,1280]{1,0:T(8,128)(2,1)} %v_ref.3), custom_call_target="tpu_custom_call" | custom-call | flops 1677721600 | bytes 6553600 | tf_op jit(solution)/shard_map/pallas_call | solution.py:90
  18.1 1.0 collective-permute-done
  19.2 1.3 collective-permute-start.1
  20.5 7.9 %shard_map.66.local_b_ref = f32[1024,640]{1,0:T(8,128)} custom-call(bf16[1024,1280]{1,0:T(8,128)(2,1)} %q_ref.3, bf16[1024,1280]{1,0:T(8,128)(2,1)} %k_ref.3, bf16[1024,1280]{1,0:T(8,128)(2,1)} %v_ref.3), custom_call_target="tpu_custom_call" | custom-call | flops 1677721600 | bytes 6553600 | tf_op jit(solution)/shard_map/pallas_call | solution.py:90
  28.4 1.2 collective-permute-done.1
  29.8 1.3 collective-permute-start.2
  32.4 15.0 %collective-permute-done.2 = bf16[10,128,128]{2,1,0:T(8,128)(2,1)S(1)} collective-permute-done((bf16[10,128,128]{2,1,0:T(8,128)(2,1)S(1)}, bf16[10,128,128]{2,1,0:T(8,128)(2,1)S(1)}, u32[]{:S(2)}, u32[]{:S(2)}) %collective-permute-start.2) | collective-permute-done | bytes 327712 | tf_op jit(solution)/shard_map/ppermute | solution.py:164
  47.4 1.0 fusion.18.prefix_ref
  48.3 9.4 %shard_map.67 = bf16[1024,1280]{1,0:T(8,128)(2,1)} custom-call(s32[4]{0:T(128)} %pad_add_fusion.order_ref, f32[1024,640]{1,0:T(8,128)} %shard_map.65.local_a_ref, f32[1024,640]{1,0:T(8,128)} %shard_map.66.local_b_ref, bf16[1024,1280]{1,0:T(8,128)(2,1)} %q_ref.3, bf16[1024,1280]{1,0:T(8,128)(2,1)} %g_ref.1, f32[10,128,128]{2,1,0:T(8,128)} %fusion.18.prefix_ref, ...), custom_call_target="tpu_custom_call" | custom-call | flops 671088640 | bytes 13107200 | tf_op jit(solution)/shard_map/pallas_call | solution.py:132
  57.7 5.9 %fusion.12 = bf16[512,2048]{1,0:T(8,128)(2,1)S(1)} fusion(bf16[1280,6144]{1,0:T(8,128)(2,1)} %param.11, bf16[1024,1280]{1,0:T(8,128)(2,1)} %shard_map.67), kind=kOutput, calls=%fused_computation.11 | convolution fusion | flops 2685403136 | bytes 8650752 | tf_op jit(solution)/shard_map/dot_general | solution.py:233
  63.7 5.8 %fusion.9 = bf16[512,2048]{1,0:T(8,128)(2,1)S(1)} fusion(bf16[1280,6144]{1,0:T(8,128)(2,1)} %param.11, bf16[1024,1280]{1,0:T(8,128)(2,1)S(1)} %copy-done.1), kind=kOutput, calls=%fused_computation.10 | convolution fusion | flops 2685403136 | bytes 8650752 | tf_op jit(solution)/shard_map/dot_general | solution.py:233
  70.3 3.1 %fusion.6 = bf16[512,2048]{1,0:T(8,128)(2,1)S(1)} fusion(bf16[1280,6144]{1,0:T(8,128)(2,1)S(1)} %bitcast.9, bf16[1024,1280]{1,0:T(8,128)(2,1)S(1)} %copy-done.1), kind=kOutput, calls=%fused_computation.9 | convolution fusion | flops 2685403136 | bytes 8650752 | tf_op jit(solution)/shard_map/dot_general | solution.py:233
  74.6 1.7 %collective-permute-done.3 = bf16[256,2048]{1,0:T(8,128)(2,1)S(1)} collective-permute-done((bf16[256,2048]{1,0:T(8,128)(2,1)S(1)}, bf16[256,2048]{1,0:T(8,128)(2,1)S(1)}, u32[]{:S(2)}, u32[]{:S(2)}) %collective-permute-start.3) | collective-permute-done | bytes 1048608 | tf_op jit(solution)/shard_map/ppermute | solution.py:168
  76.7 4.4 %convolution_convert_fusion = bf16[256,6144]{1,0:T(8,128)(2,1)S(1)} fusion(bf16[256,1280]{1,0:T(8,128)(2,1)S(1)} %get-tuple-element.31, bf16[1280,6144]{1,0:T(8,128)(2,1)S(1)} %bitcast.9), kind=kOutput, calls=%fused_computation | convolution fusion | flops 4028104704 | bytes 19529728 | tf_op jit(solution)/shard_map/dot_general | solution.py:215
  81.4 1.5 collective-permute-start.7
  83.4 1.5 collective-permute-start.9
  84.9 9.9 %convolution_convert_fusion.1 = bf16[256,6144]{1,0:T(8,128)(2,1)S(1)} fusion(bf16[256,1280]{1,0:T(8,128)(2,1)S(1)} %get-tuple-element.30, bf16[1280,6144]{1,0:T(8,128)(2,1)} %param.11), kind=kOutput, calls=%fused_computation.1 | convolution fusion | flops 4028104704 | bytes 19529728 | tf_op jit(solution)/shard_map/dot_general | solution.py:215
  94.8 12.6 %collective-permute-done.7 = bf16[256,2048]{1,0:T(8,128)(2,1)S(1)} collective-permute-done((bf16[256,2048]{1,0:T(8,128)(2,1)S(1)}, bf16[256,2048]{1,0:T(8,128)(2,1)S(1)}, u32[]{:S(2)}, u32[]{:S(2)}) %collective-permute-start.7) | collective-permute-done | bytes 1048608 | tf_op jit(solution)/shard_map/ppermute | solution.py:168
  107.4 22.5 %collective-permute-done.8 = bf16[256,2048]{1,0:T(8,128)(2,1)S(1)} collective-permute-done((bf16[256,2048]{1,0:T(8,128)(2,1)S(1)}, bf16[256,2048]{1,0:T(8,128)(2,1)S(1)}, u32[]{:S(2)}, u32[]{:S(2)}) %collective-permute-start.8) | collective-permute-done | bytes 1048608 | tf_op jit(solution)/shard_map/ppermute | solution.py:168
  129.9 21.9 %collective-permute-done.9 = bf16[256,2048]{1,0:T(8,128)(2,1)S(1)} collective-permute-done((bf16[256,2048]{1,0:T(8,128)(2,1)S(1)}, bf16[256,2048]{1,0:T(8,128)(2,1)S(1)}, u32[]{:S(2)}, u32[]{:S(2)}) %collective-permute-start.9) | collective-permute-done | bytes 1048608 | tf_op jit(solution)/shard_map/ppermute | solution.py:168
  151.7 2.6 %add_convert_fusion = bf16[256,6144]{1,0:T(8,128)(2,1)} fusion(bf16[256,6144]{1,0:T(8,128)(2,1)S(1)} %collective-permute-done.6, bf16[256,6144]{1,0:T(8,128)(2,1)S(1)} %convolution_convert_fusion.1, bf16[256,2048]{1,0:T(8,128)(2,1)S(1)} %collective-permute-done.9, bf16[256,2048]{1,0:T(8,128)(2,1)S(1)} %collective-permute-done.8, ...), kind=kLoop, calls=%fused_computation.2 | loop fusion | flops 17301504 | bytes 12582912 | tf_op jit(solution)/shard_map/convert_element_type | solution.py:245
  (34 shorter events, 4.5 us)
Async XLA Ops:
  6.7 12.4 %copy-start = (f32[10,128,128]{2,1,0:T(8,128)S(1)}, f32[10,128,128]{2,1,0:T(8,128)}, u32[]{:S(2)}) copy-start(f32[10,128,128]{2,1,0:T(8,128)} %shard_map.64) | copy-start | bytes 1966084
  6.7 12.4 %collective-permute-start = (bf16[10,128,128]{2,1,0:T(8,128)(2,1)S(1)}, bf16[10,128,128]{2,1,0:T(8,128)(2,1)S(1)}, u32[]{:S(2)}, u32[]{:S(2)}) collective-permute-start(bf16[10,128,128]{2,1,0:T(8,128)(2,1)S(1)} %convert_element_type.72), channel_id=1, source_target_pairs={{0,4},{4,8},{8,12},{12,16},{16,20},{20,24},{24,28},{1,5},{5,9},{9,... | collective-permute-start | bytes 983048 | tf_op jit(solution)/shard_map/ppermute | solution.py:164
  19.2 12.0 %copy-start.2 = (f32[1280]{0:T(1024)S(1)}, f32[1280]{0:T(1024)}, u32[]{:S(2)}) copy-start(f32[1280]{0:T(1024)} %param.10) | copy-start | bytes 15364
  19.2 10.5 %collective-permute-start.1 = (bf16[10,128,128]{2,1,0:T(8,128)(2,1)S(1)}, bf16[10,128,128]{2,1,0:T(8,128)(2,1)S(1)}, u32[]{:S(2)}, u32[]{:S(2)}) collective-permute-start(bf16[10,128,128]{2,1,0:T(8,128)(2,1)S(1)} %fusion.20), channel_id=1, source_target_pairs={{0,8},{4,12},{8,16},{12,20},{16,24},{20,28},{1,9},{5,13},{9,17},{1... | collective-permute-start | bytes 983048 | tf_op jit(solution)/shard_map/ppermute | solution.py:164
  29.8 17.6 %collective-permute-start.2 = (bf16[10,128,128]{2,1,0:T(8,128)(2,1)S(1)}, bf16[10,128,128]{2,1,0:T(8,128)(2,1)S(1)}, u32[]{:S(2)}, u32[]{:S(2)}) collective-permute-start(bf16[10,128,128]{2,1,0:T(8,128)(2,1)S(1)} %fusion.19), channel_id=1, source_target_pairs={{0,16},{4,20},{8,24},{12,28},{1,17},{5,21},{9,25},{13,29},{2,18},{... | collective-permute-start | bytes 983048 | tf_op jit(solution)/shard_map/ppermute | solution.py:164
  57.7 5.9 %copy-start.1 = (bf16[1024,1280]{1,0:T(8,128)(2,1)S(1)}, bf16[1024,1280]{1,0:T(8,128)(2,1)}, u32[]{:S(2)}) copy-start(bf16[1024,1280]{1,0:T(8,128)(2,1)} %shard_map.67) | copy-start | bytes 7864324
  57.7 12.6 %slice-start = ((s8[15728640]{0:T(1024)(128)(4,1)}), s8[4194304]{0:T(1024)(128)(4,1)S(1)}, s32[]{:S(2)}) async-start(s8[15728640]{0:T(1024)(128)(4,1)} %bitcast.8), calls=%async_computation | async-start | bytes 8388608
  57.7 12.6 %slice-start.1 = ((s8[15728640]{0:T(1024)(128)(4,1)}), s8[4194304]{0:T(1024)(128)(4,1)S(1)}, s32[]{:S(2)}) async-start(s8[15728640]{0:T(1024)(128)(4,1)} %bitcast.8), calls=%async_computation.1 | async-start | bytes 8388608
  63.7 6.7 %slice-start.2 = ((s8[15728640]{0:T(1024)(128)(4,1)}), s8[4194304]{0:T(1024)(128)(4,1)S(1)}, s32[]{:S(2)}) async-start(s8[15728640]{0:T(1024)(128)(4,1)} %bitcast.8), calls=%async_computation.2 | async-start | bytes 8388608
  63.7 6.7 %slice-start.3 = ((s8[15728640]{0:T(1024)(128)(4,1)}), s8[3145728]{0:T(1024)(128)(4,1)S(1)}, s32[]{:S(2)}) async-start(s8[15728640]{0:T(1024)(128)(4,1)} %bitcast.8), calls=%async_computation.3 | async-start | bytes 6291456
  69.6 4.2 %collective-permute-start.5 = (bf16[256,2048]{1,0:T(8,128)(2,1)S(1)}, bf16[256,2048]{1,0:T(8,128)(2,1)S(1)}, u32[]{:S(2)}, u32[]{:S(2)}) collective-permute-start(bf16[256,2048]{1,0:T(8,128)(2,1)S(1)} %slice.54), channel_id=1, source_target_pairs={{0,1},{1,0},{2,3},{3,2},{4,5},{5,4},{6,7},{7,6},{8,9},{9,8},{10,11... | collective-permute-start | bytes 3145736 | tf_op jit(solution)/shard_map/ppermute | solution.py:168
  69.8 4.4 %collective-permute-start.4 = (bf16[256,2048]{1,0:T(8,128)(2,1)S(1)}, bf16[256,2048]{1,0:T(8,128)(2,1)S(1)}, u32[]{:S(2)}, u32[]{:S(2)}) collective-permute-start(bf16[256,2048]{1,0:T(8,128)(2,1)S(1)} %slice.52), channel_id=1, source_target_pairs={{0,1},{1,0},{2,3},{3,2},{4,5},{5,4},{6,7},{7,6},{8,9},{9,8},{10,11... | collective-permute-start | bytes 3145736 | tf_op jit(solution)/shard_map/ppermute | solution.py:168
  73.6 2.7 %collective-permute-start.3 = (bf16[256,2048]{1,0:T(8,128)(2,1)S(1)}, bf16[256,2048]{1,0:T(8,128)(2,1)S(1)}, u32[]{:S(2)}, u32[]{:S(2)}) collective-permute-start(bf16[256,2048]{1,0:T(8,128)(2,1)S(1)} %slice.50), channel_id=1, source_target_pairs={{0,1},{1,0},{2,3},{3,2},{4,5},{5,4},{6,7},{7,6},{8,9},{9,8},{10,11... | collective-permute-start | bytes 3145736 | tf_op jit(solution)/shard_map/ppermute | solution.py:168
  81.2 70.6 %collective-permute-start.6 = (bf16[256,6144]{1,0:T(8,128)(2,1)S(1)}, bf16[256,6144]{1,0:T(8,128)(2,1)S(1)}, u32[]{:S(2)}, u32[]{:S(2)}) collective-permute-start(bf16[256,6144]{1,0:T(8,128)(2,1)S(1)} %convolution_convert_fusion), channel_id=1, source_target_pairs={{0,1},{1,0},{2,3},{3,2},{4,5},{5,4},{6,7},{7,6},{8,9},{9,8},{10,11... | collective-permute-start | bytes 9437192 | tf_op jit(solution)/shard_map/ppermute | solution.py:168
  81.4 26.0 %collective-permute-start.7 = (bf16[256,2048]{1,0:T(8,128)(2,1)S(1)}, bf16[256,2048]{1,0:T(8,128)(2,1)S(1)}, u32[]{:S(2)}, u32[]{:S(2)}) collective-permute-start(bf16[256,2048]{1,0:T(8,128)(2,1)S(1)} %add_convert_fusion.3), channel_id=1, source_target_pairs={{0,2},{2,0},{1,3},{3,1},{4,6},{6,4},{5,7},{7,5},{8,10},{10,8},{9,1... | collective-permute-start | bytes 3145736 | tf_op jit(solution)/shard_map/ppermute | solution.py:168
  82.9 47.0 %collective-permute-start.8 = (bf16[256,2048]{1,0:T(8,128)(2,1)S(1)}, bf16[256,2048]{1,0:T(8,128)(2,1)S(1)}, u32[]{:S(2)}, u32[]{:S(2)}) collective-permute-start(bf16[256,2048]{1,0:T(8,128)(2,1)S(1)} %add_convert_fusion.2), channel_id=1, source_target_pairs={{0,2},{2,0},{1,3},{3,1},{4,6},{6,4},{5,7},{7,5},{8,10},{10,8},{9,1... | collective-permute-start | bytes 3145736 | tf_op jit(solution)/shard_map/ppermute | solution.py:168
  83.4 68.4 %collective-permute-start.9 = (bf16[256,2048]{1,0:T(8,128)(2,1)S(1)}, bf16[256,2048]{1,0:T(8,128)(2,1)S(1)}, u32[]{:S(2)}, u32[]{:S(2)}) collective-permute-start(bf16[256,2048]{1,0:T(8,128)(2,1)S(1)} %add_convert_fusion.1), channel_id=1, source_target_pairs={{0,2},{2,0},{1,3},{3,1},{4,6},{6,4},{5,7},{7,5},{8,10},{10,8},{9,1... | collective-permute-start | bytes 3145736 | tf_op jit(solution)/shard_map/ppermute | solution.py:168

commit v10 on v9

--- a/solution.py
+++ b/solution.py
@@ -204,6 +204,47 @@
     ).astype(jnp.int32)
 
 
+PRODUCT_TILE = 512
+
+
+def early_product_kernel(far_ref, near_ref, w_ref, far_out_ref, near_out_ref):
+    weight = w_ref[...]
+    far_out_ref[...] = jnp.dot(far_ref[...], weight, preferred_element_type=jnp.float32).astype(
+        far_out_ref.dtype
+    )
+    near_out_ref[...] = jnp.dot(near_ref[...], weight, preferred_element_type=jnp.float32).astype(
+        near_out_ref.dtype
+    )
+
+
+def early_products(mixed_rows, out_weight, block, first_column, width):
+    columns = mixed_rows.shape[1]
+    tiles = width // PRODUCT_TILE
+    offset = first_column // PRODUCT_TILE
+    return pl.pallas_call(
+        early_product_kernel,
+        grid=(tiles,),
+        in_specs=[
+            pl.BlockSpec((2 * block, columns), lambda j: (0, 0)),
+            pl.BlockSpec((block, columns), lambda j: (2, 0)),
+            pl.BlockSpec((columns, PRODUCT_TILE), lambda j: (0, j + offset)),
+        ],
+        out_specs=[
+            pl.BlockSpec((2 * block, PRODUCT_TILE), lambda j: (0, j)),
+            pl.BlockSpec((block, PRODUCT_TILE), lambda j: (0, j)),
+        ],
+        out_shape=[
+            jax.ShapeDtypeStruct((2 * block, width), jnp.bfloat16),
+            jax.ShapeDtypeStruct((block, width), jnp.bfloat16),
+        ],
+        cost_estimate=pl.CostEstimate(
+            flops=2 * 3 * block * columns * width,
+            transcendentals=0,
+            bytes_accessed=2 * (3 * block * columns + columns * width + 3 * block * width),
+        ),
+    )(mixed_rows, mixed_rows, out_weight)
+
+
 def project_and_reduce(mixed_rows, out_weight):
     tokens, columns = mixed_rows.shape
     ty_size = lax.axis_size("ty")
@@ -224,21 +265,19 @@
         part = lax.psum_scatter(part, "tc", scatter_dimension=0, tiled=True)
         return lax.psum_scatter(part, "ty", scatter_dimension=0, tiled=True)
 
-    far_rows = mixed_rows[:2 * block]
-    partner_rows = mixed_rows[2 * block:3 * block]
     own_rows = mixed_rows[3 * block:]
     chunk = width // COLUMN_CHUNKS
     chip_sums = []
+    near_parts = []
     for c in range(COLUMN_CHUNKS):
-        far_part = jnp.dot(
-            far_rows, out_weight[:, c * chunk:(c + 1) * chunk], preferred_element_type=jnp.float32
-        ).astype(jnp.bfloat16)
+        far_part, near_part = early_products(mixed_rows, out_weight, block, c * chunk, chunk)
         from_partner = swap(far_part[:block], "tc")
         chip_sum = far_part[block:].astype(jnp.float32) + from_partner.astype(jnp.float32)
         chip_sums.append(chip_sum.astype(jnp.bfloat16))
-    chip_sums, partner_rows, own_rows = lax.optimization_barrier((chip_sums, partner_rows, own_rows))
+        near_parts.append(near_part)
+    chip_sums, near_parts, own_rows = lax.optimization_barrier((chip_sums, near_parts, own_rows))
     across = [swap(chip_sum, "ty") for chip_sum in chip_sums]
-    near = swap(product(partner_rows), "tc")
+    near = swap(jnp.concatenate(near_parts, axis=1), "tc")
     mine = lax.optimization_barrier(product(own_rows))
     far = jnp.concatenate(across, axis=1)
     total = mine.astype(jnp.float32) + near.astype(jnp.float32) + far.astype(jnp.float32)

time: 155 us -> 165 us (1.065)
  Pallas kernels: 30.7 us -> 53.8 us
  matrix products: 29.2 us -> 9.92 us
  local copies, waits for them, and re-layouts: 0.99 us -> 6.79 us
    pallas_call x0 -> x3, Pallas kernels: none -> 23.2 us  [early_products(): pl.pallas_call(early_product_kernel, grid=(tiles,), in_specs=[pl.BlockSpe...]
    dot_general x3 -> x0, matrix products: 14.8 us -> none  [project_and_reduce(): jnp.dot(far_rows, out_weight[:, c * chunk:(c + 1) * chunk], preferred_ele...]
    slice x3, local copies, waits for them, and re-layouts: 0.27 us -> 6.16 us  [project_and_reduce(): from_partner = swap(far_part[:block], 'tc')]
    dot_general x2 -> x1, matrix products: 14.4 us -> 9.92 us  [product(): jnp.dot(rows, out_weight, preferred_element_type=jnp.float32)]
  transfers between devices with their start and end apart: 10 -> 10, of which waited for: 7 -> 7; matrix products, arithmetic and copies ran while one was open for 10% -> 10% of each run, Pallas kernels for 10% -> 19%
where the time goes in v10:
time: 165 us; the launch traced here: 164 us
  waiting for transfers between devices  74.5 us (45%)
  Pallas kernels  53.8 us (33%)
  starting transfers between devices  10.5 us (6%)
  matrix products  9.92 us (6%)
  other arithmetic  8.35 us (5%)
  local copies, waits for them, and re-layouts  6.79 us (4%)
    ppermute x7, waiting for transfers between devices, swap(): return lax.ppermute(block, axis, [(0, 1), (1, 0)])  57.3 us
    pallas_call x3, Pallas kernels, early_products(): pl.pallas_call(early_product_kernel, grid=(tiles,), in_specs=[pl.BlockSpe...  23.2 us
    ppermute x3, waiting for transfers between devices, shift(): lax.ppermute(block, axis, [(i, i + distance) for i in range(size) if i +...  17.2 us
    pallas_call x2, Pallas kernels, local_attention(): pl.pallas_call(local_kernel, grid=(heads,), in_specs=[picked] * 3, out_sp...  15.8 us
    dot_general x1, matrix products, product(): jnp.dot(rows, out_weight, preferred_element_type=jnp.float32)  9.92 us
    pallas_call x1, Pallas kernels, mix(): pl.pallas_call(mix_kernel, grid_spec=pltpu.PrefetchScalarGridSpec(num_sca...  9.21 us
    slice x3, local copies, waits for them, and re-layouts, project_and_reduce(): from_partner = swap(far_part[:block], 'tc')  6.16 us
    ppermute x3, starting transfers between devices, shift(): lax.ppermute(block, axis, [(i, i + distance) for i in range(size) if i +...  6.11 us
  transfers between devices with their start and end apart: 10, of which 7 were waited for; matrix products, arithmetic and copies ran while one was open for 10% of the time, Pallas kernels for 19%

profile of v10, /device:TPU:24, one launch (start us, length us, event | category | flops | bytes accessed | tf_op | source)
XLA Modules:
  0.0 164.1 jit_solution(4670006314242646474)
XLA Ops:
  0.0 5.5 %shard_map.64 = f32[10,128,128]{2,1,0:T(8,128)} custom-call(bf16[1024,1280]{1,0:T(8,128)(2,1)} %k_ref.3, bf16[1024,1280]{1,0:T(8,128)(2,1)} %v_ref.3), custom_call_target="tpu_custom_call" | custom-call | flops 335544320 | bytes 5898240 | tf_op jit(solution)/shard_map/pallas_call | solution.py:50
  5.6 1.1 convert_element_type.60
  6.7 3.5 %collective-permute-start = (bf16[10,128,128]{2,1,0:T(8,128)(2,1)S(1)}, bf16[10,128,128]{2,1,0:T(8,128)(2,1)S(1)}, u32[]{:S(2)}, u32[]{:S(2)}) collective-permute-start(bf16[10,128,128]{2,1,0:T(8,128)(2,1)S(1)} %convert_element_type.60), channel_id=1, source_target_pairs={{0,4},{4,8},{8,12},{12,16},{16,20},{20,24},{24,28},{1,5},{5,9},{9,... | collective-permute-start | bytes 983048 | tf_op jit(solution)/shard_map/ppermute | solution.py:164
  10.2 7.9 %shard_map.65.local_a_ref = f32[1024,640]{1,0:T(8,128)} custom-call(bf16[1024,1280]{1,0:T(8,128)(2,1)} %q_ref.3, bf16[1024,1280]{1,0:T(8,128)(2,1)} %k_ref.3, bf16[1024,1280]{1,0:T(8,128)(2,1)} %v_ref.3), custom_call_target="tpu_custom_call" | custom-call | flops 1677721600 | bytes 6553600 | tf_op jit(solution)/shard_map/pallas_call | solution.py:90
  19.2 1.3 collective-permute-start.1
  20.5 7.9 %shard_map.66.local_b_ref = f32[1024,640]{1,0:T(8,128)} custom-call(bf16[1024,1280]{1,0:T(8,128)(2,1)} %q_ref.3, bf16[1024,1280]{1,0:T(8,128)(2,1)} %k_ref.3, bf16[1024,1280]{1,0:T(8,128)(2,1)} %v_ref.3), custom_call_target="tpu_custom_call" | custom-call | flops 1677721600 | bytes 6553600 | tf_op jit(solution)/shard_map/pallas_call | solution.py:90
  28.4 1.2 collective-permute-done.1
  29.8 1.3 collective-permute-start.2
  32.3 15.0 %collective-permute-done.2 = bf16[10,128,128]{2,1,0:T(8,128)(2,1)S(1)} collective-permute-done((bf16[10,128,128]{2,1,0:T(8,128)(2,1)S(1)}, bf16[10,128,128]{2,1,0:T(8,128)(2,1)S(1)}, u32[]{:S(2)}, u32[]{:S(2)}) %collective-permute-start.2) | collective-permute-done | bytes 327712 | tf_op jit(solution)/shard_map/ppermute | solution.py:164
  48.3 9.2 %shard_map.67.far_ref.near_ref = bf16[1024,1280]{1,0:T(8,128)(2,1)} custom-call(s32[4]{0:T(128)} %pad_add_fusion.order_ref, f32[1024,640]{1,0:T(8,128)} %shard_map.65.local_a_ref, f32[1024,640]{1,0:T(8,128)} %shard_map.66.local_b_ref, bf16[1024,1280]{1,0:T(8,128)(2,1)} %q_ref.3, bf16[1024,1280]{1,0:T(8,128)(2,1)} %g_ref.1, f32[10,128,128]{2,1,0:T(8,128)} %fusion.prefix_ref, ...), custom_call_target="tpu_custom_call" | custom-call | flops 671088640 | bytes 13107200 | tf_op jit(solution)/shard_map/pallas_call | solution.py:132
  57.5 7.7 %shard_map.70 = (bf16[512,2048]{1,0:T(8,128)(2,1)}, bf16[256,2048]{1,0:T(8,128)(2,1)}) custom-call(bf16[1024,1280]{1,0:T(8,128)(2,1)} %shard_map.67.far_ref.near_ref, bf16[1024,1280]{1,0:T(8,128)(2,1)} %shard_map.67.far_ref.near_ref, bf16[1280,6144]{1,0:T(8,128)(2,1)} %w_ref.5), custom_call_target="tpu_custom_call" | custom-call | flops 4026531840 | bytes 10354688 | tf_op jit(solution)/shard_map/pallas_call | solution.py:224
  65.2 2.3 %slice.26 = bf16[256,2048]{1,0:T(8,128)(2,1)} slice(bf16[512,2048]{1,0:T(8,128)(2,1)} %get-tuple-element.40), slice={[0:256], [0:2048]} | slice | bytes 2097152 | tf_op jit(solution)/shard_map/slice | solution.py:274
  67.5 7.7 %shard_map.69 = (bf16[512,2048]{1,0:T(8,128)(2,1)}, bf16[256,2048]{1,0:T(8,128)(2,1)}) custom-call(bf16[1024,1280]{1,0:T(8,128)(2,1)} %shard_map.67.far_ref.near_ref, bf16[1024,1280]{1,0:T(8,128)(2,1)} %shard_map.67.far_ref.near_ref, bf16[1280,6144]{1,0:T(8,128)(2,1)} %w_ref.5), custom_call_target="tpu_custom_call" | custom-call | flops 4026531840 | bytes 10354688 | tf_op jit(solution)/shard_map/pallas_call | solution.py:224
  75.2 2.4 %slice.24 = bf16[256,2048]{1,0:T(8,128)(2,1)} slice(bf16[512,2048]{1,0:T(8,128)(2,1)} %get-tuple-element.39), slice={[0:256], [0:2048]} | slice | bytes 2097152 | tf_op jit(solution)/shard_map/slice | solution.py:274
  78.1 7.8 %shard_map.68 = (bf16[512,2048]{1,0:T(8,128)(2,1)}, bf16[256,2048]{1,0:T(8,128)(2,1)}) custom-call(bf16[1024,1280]{1,0:T(8,128)(2,1)} %shard_map.67.far_ref.near_ref, bf16[1024,1280]{1,0:T(8,128)(2,1)} %shard_map.67.far_ref.near_ref, bf16[1280,6144]{1,0:T(8,128)(2,1)} %w_ref.5), custom_call_target="tpu_custom_call" | custom-call | flops 4026531840 | bytes 10354688 | tf_op jit(solution)/shard_map/pallas_call | solution.py:224
  85.9 1.5 slice.22
  88.0 1.8 %add_convert_fusion.2 = bf16[256,2048]{1,0:T(8,128)(2,1)S(1)} fusion(bf16[256,2048]{1,0:T(8,128)(2,1)} %collective-permute-done.4, bf16[512,2048]{1,0:T(8,128)(2,1)S(1)} %copy-done.2), kind=kLoop, calls=%fused_computation.4 | loop fusion | flops 2097152 | bytes 3145728 | tf_op jit(solution)/shard_map/convert_element_type | solution.py:276
  91.2 1.5 collective-permute-start.7
  93.2 1.5 collective-permute-start.9
  94.7 9.9 %convolution_convert_fusion = bf16[256,6144]{1,0:T(8,128)(2,1)S(1)} fusion(bf16[256,1280]{1,0:T(8,128)(2,1)S(1)} %slice-done, bf16[1280,6144]{1,0:T(8,128)(2,1)} %w_ref.5), kind=kOutput, calls=%fused_computation | convolution fusion | flops 4028104704 | bytes 19529728 | tf_op jit(solution)/shard_map/dot_general | solution.py:256
  104.6 12.5 %collective-permute-done.7 = bf16[256,2048]{1,0:T(8,128)(2,1)S(1)} collective-permute-done((bf16[256,2048]{1,0:T(8,128)(2,1)S(1)}, bf16[256,2048]{1,0:T(8,128)(2,1)S(1)}, u32[]{:S(2)}, u32[]{:S(2)}) %collective-permute-start.7) | collective-permute-done | bytes 1048608 | tf_op jit(solution)/shard_map/ppermute | solution.py:168
  117.2 22.5 %collective-permute-done.8 = bf16[256,2048]{1,0:T(8,128)(2,1)S(1)} collective-permute-done((bf16[256,2048]{1,0:T(8,128)(2,1)S(1)}, bf16[256,2048]{1,0:T(8,128)(2,1)S(1)}, u32[]{:S(2)}, u32[]{:S(2)}) %collective-permute-start.8) | collective-permute-done | bytes 1048608 | tf_op jit(solution)/shard_map/ppermute | solution.py:168
  139.7 21.9 %collective-permute-done.9 = bf16[256,2048]{1,0:T(8,128)(2,1)S(1)} collective-permute-done((bf16[256,2048]{1,0:T(8,128)(2,1)S(1)}, bf16[256,2048]{1,0:T(8,128)(2,1)S(1)}, u32[]{:S(2)}, u32[]{:S(2)}) %collective-permute-start.9) | collective-permute-done | bytes 1048608 | tf_op jit(solution)/shard_map/ppermute | solution.py:168
  161.5 2.6 %add_convert_fusion = bf16[256,6144]{1,0:T(8,128)(2,1)} fusion(bf16[256,6144]{1,0:T(8,128)(2,1)S(1)} %collective-permute-done.6, bf16[256,6144]{1,0:T(8,128)(2,1)S(1)} %convolution_convert_fusion, bf16[256,2048]{1,0:T(8,128)(2,1)S(1)} %collective-permute-done.9, bf16[256,2048]{1,0:T(8,128)(2,1)S(1)} %collective-permute-done.8, ...), kind=kLoop, calls=%fused_computation.1 | loop fusion | flops 17301504 | bytes 12582912 | tf_op jit(solution)/shard_map/convert_element_type | solution.py:284
  (36 shorter events, 6.2 us)
Async XLA Ops:
  6.7 12.4 %copy-start = (f32[10,128,128]{2,1,0:T(8,128)S(1)}, f32[10,128,128]{2,1,0:T(8,128)}, u32[]{:S(2)}) copy-start(f32[10,128,128]{2,1,0:T(8,128)} %shard_map.64) | copy-start | bytes 1966084
  6.7 12.4 %collective-permute-start = (bf16[10,128,128]{2,1,0:T(8,128)(2,1)S(1)}, bf16[10,128,128]{2,1,0:T(8,128)(2,1)S(1)}, u32[]{:S(2)}, u32[]{:S(2)}) collective-permute-start(bf16[10,128,128]{2,1,0:T(8,128)(2,1)S(1)} %convert_element_type.60), channel_id=1, source_target_pairs={{0,4},{4,8},{8,12},{12,16},{16,20},{20,24},{24,28},{1,5},{5,9},{9,... | collective-permute-start | bytes 983048 | tf_op jit(solution)/shard_map/ppermute | solution.py:164
  19.2 11.9 %copy-start.7 = (f32[1280]{0:T(1024)S(1)}, f32[1280]{0:T(1024)}, u32[]{:S(2)}) copy-start(f32[1280]{0:T(1024)} %param.10) | copy-start | bytes 15364
  19.2 10.5 %collective-permute-start.1 = (bf16[10,128,128]{2,1,0:T(8,128)(2,1)S(1)}, bf16[10,128,128]{2,1,0:T(8,128)(2,1)S(1)}, u32[]{:S(2)}, u32[]{:S(2)}) collective-permute-start(bf16[10,128,128]{2,1,0:T(8,128)(2,1)S(1)} %fusion.2), channel_id=1, source_target_pairs={{0,8},{4,12},{8,16},{12,20},{16,24},{20,28},{1,9},{5,13},{9,17},{1... | collective-permute-start | bytes 983048 | tf_op jit(solution)/shard_map/ppermute | solution.py:164
  29.8 17.5 %collective-permute-start.2 = (bf16[10,128,128]{2,1,0:T(8,128)(2,1)S(1)}, bf16[10,128,128]{2,1,0:T(8,128)(2,1)S(1)}, u32[]{:S(2)}, u32[]{:S(2)}) collective-permute-start(bf16[10,128,128]{2,1,0:T(8,128)(2,1)S(1)} %fusion.1), channel_id=1, source_target_pairs={{0,16},{4,20},{8,24},{12,28},{1,17},{5,21},{9,25},{13,29},{2,18},{... | collective-permute-start | bytes 983048 | tf_op jit(solution)/shard_map/ppermute | solution.py:164
  67.5 20.0 %collective-permute-start.5 = (bf16[256,2048]{1,0:T(8,128)(2,1)}, bf16[256,2048]{1,0:T(8,128)(2,1)S(1)}, u32[]{:S(2)}, u32[]{:S(2)}) collective-permute-start(bf16[256,2048]{1,0:T(8,128)(2,1)} %slice.26), channel_id=1, source_target_pairs={{0,1},{1,0},{2,3},{3,2},{4,5},{5,4},{6,7},{7,6},{8,9},{9,8},{10,11... | collective-permute-start | bytes 3145736 | tf_op jit(solution)/shard_map/ppermute | solution.py:168
  77.6 10.4 %collective-permute-start.4 = (bf16[256,2048]{1,0:T(8,128)(2,1)}, bf16[256,2048]{1,0:T(8,128)(2,1)}, u32[]{:S(2)}, u32[]{:S(2)}) collective-permute-start(bf16[256,2048]{1,0:T(8,128)(2,1)} %slice.24), channel_id=1, source_target_pairs={{0,1},{1,0},{2,3},{3,2},{4,5},{5,4},{6,7},{7,6},{8,9},{9,8},{10,11... | collective-permute-start | bytes 3145736 | tf_op jit(solution)/shard_map/ppermute | solution.py:168
  78.1 9.4 %copy-start.1 = (bf16[512,2048]{1,0:T(8,128)(2,1)S(1)}, bf16[512,2048]{1,0:T(8,128)(2,1)}, u32[]{:S(2)}) copy-start(bf16[512,2048]{1,0:T(8,128)(2,1)} %get-tuple-element.40) | copy-start | bytes 6291460
  85.9 2.0 %copy-start.2 = (bf16[512,2048]{1,0:T(8,128)(2,1)S(1)}, bf16[512,2048]{1,0:T(8,128)(2,1)}, u32[]{:S(2)}) copy-start(bf16[512,2048]{1,0:T(8,128)(2,1)} %get-tuple-element.39) | copy-start | bytes 6291460
  87.4 2.7 %copy-start.3 = (bf16[512,2048]{1,0:T(8,128)(2,1)S(1)}, bf16[512,2048]{1,0:T(8,128)(2,1)}, u32[]{:S(2)}) copy-start(bf16[512,2048]{1,0:T(8,128)(2,1)} %get-tuple-element.38) | copy-start | bytes 6291460
  87.4 2.7 %collective-permute-start.3 = (bf16[256,2048]{1,0:T(8,128)(2,1)S(1)}, bf16[256,2048]{1,0:T(8,128)(2,1)S(1)}, u32[]{:S(2)}, u32[]{:S(2)}) collective-permute-start(bf16[256,2048]{1,0:T(8,128)(2,1)S(1)} %slice.22), channel_id=1, source_target_pairs={{0,1},{1,0},{2,3},{3,2},{4,5},{5,4},{6,7},{7,6},{8,9},{9,8},{10,11... | collective-permute-start | bytes 3145736 | tf_op jit(solution)/shard_map/ppermute | solution.py:168
  87.9 2.6 %copy-start.4 = (bf16[256,2048]{1,0:T(8,128)(2,1)S(1)}, bf16[256,2048]{1,0:T(8,128)(2,1)}, u32[]{:S(2)}) copy-start(bf16[256,2048]{1,0:T(8,128)(2,1)} %get-tuple-element.47) | copy-start | bytes 3145732
  87.9 2.6 %copy-start.5 = (bf16[256,2048]{1,0:T(8,128)(2,1)S(1)}, bf16[256,2048]{1,0:T(8,128)(2,1)}, u32[]{:S(2)}) copy-start(bf16[256,2048]{1,0:T(8,128)(2,1)} %get-tuple-element.46) | copy-start | bytes 3145732
  87.9 2.6 %copy-start.6 = (bf16[256,2048]{1,0:T(8,128)(2,1)S(1)}, bf16[256,2048]{1,0:T(8,128)(2,1)}, u32[]{:S(2)}) copy-start(bf16[256,2048]{1,0:T(8,128)(2,1)} %get-tuple-element.45) | copy-start | bytes 3145732
  90.6 4.2 %slice-start = ((bf16[1024,1280]{1,0:T(8,128)(2,1)}), bf16[256,1280]{1,0:T(8,128)(2,1)S(1)}, s32[]{:S(2)}) async-start(bf16[1024,1280]{1,0:T(8,128)(2,1)} %shard_map.67.far_ref.near_ref), calls=%async_computation | async-start | bytes 1310720 | tf_op jit(solution)/shard_map/slice | solution.py:268
  90.9 70.6 %collective-permute-start.6 = (bf16[256,6144]{1,0:T(8,128)(2,1)S(1)}, bf16[256,6144]{1,0:T(8,128)(2,1)S(1)}, u32[]{:S(2)}, u32[]{:S(2)}) collective-permute-start(bf16[256,6144]{1,0:T(8,128)(2,1)S(1)} %pad_maximum_fusion), channel_id=1, source_target_pairs={{0,1},{1,0},{2,3},{3,2},{4,5},{5,4},{6,7},{7,6},{8,9},{9,8},{10,11... | collective-permute-start | bytes 9437192 | tf_op jit(solution)/shard_map/ppermute | solution.py:168
  91.2 26.0 %collective-permute-start.7 = (bf16[256,2048]{1,0:T(8,128)(2,1)S(1)}, bf16[256,2048]{1,0:T(8,128)(2,1)S(1)}, u32[]{:S(2)}, u32[]{:S(2)}) collective-permute-start(bf16[256,2048]{1,0:T(8,128)(2,1)S(1)} %add_convert_fusion.3), channel_id=1, source_target_pairs={{0,2},{2,0},{1,3},{3,1},{4,6},{6,4},{5,7},{7,5},{8,10},{10,8},{9,1... | collective-permute-start | bytes 3145736 | tf_op jit(solution)/shard_map/ppermute | solution.py:168
  92.7 47.0 %collective-permute-start.8 = (bf16[256,2048]{1,0:T(8,128)(2,1)S(1)}, bf16[256,2048]{1,0:T(8,128)(2,1)S(1)}, u32[]{:S(2)}, u32[]{:S(2)}) collective-permute-start(bf16[256,2048]{1,0:T(8,128)(2,1)S(1)} %add_convert_fusion.2), channel_id=1, source_target_pairs={{0,2},{2,0},{1,3},{3,1},{4,6},{6,4},{5,7},{7,5},{8,10},{10,8},{9,1... | collective-permute-start | bytes 3145736 | tf_op jit(solution)/shard_map/ppermute | solution.py:168
  93.2 68.4 %collective-permute-start.9 = (bf16[256,2048]{1,0:T(8,128)(2,1)S(1)}, bf16[256,2048]{1,0:T(8,128)(2,1)S(1)}, u32[]{:S(2)}, u32[]{:S(2)}) collective-permute-start(bf16[256,2048]{1,0:T(8,128)(2,1)S(1)} %add_convert_fusion.1), channel_id=1, source_target_pairs={{0,2},{2,0},{1,3},{3,1},{4,6},{6,4},{5,7},{7,5},{8,10},{10,8},{9,1... | collective-permute-start | bytes 3145736 | tf_op jit(solution)/shard_map/ppermute | solution.py:168

commit v11 on v8

--- a/solution.py
+++ b/solution.py
@@ -101,10 +101,33 @@
     )(queries, keys, values)
 
 
-def mix_kernel(local_a_ref, local_b_ref, q_ref, g_ref, hi_ref, lo_ref, gain_ref, out_ref):
-    query_act = silu(q_ref[...])
+def gate_kernel(q_ref, g_ref, gain_ref, query_act_ref, scale_ref):
+    query_act_ref[...] = silu(q_ref[...])
     gates = g_ref[...].astype(jnp.float32)
-    gate_open = 1.0 / (1.0 + jnp.exp(-gates))
+    scale_ref[...] = gain_ref[...] * (1.0 / (1.0 + jnp.exp(-gates)))
+
+
+def query_and_gate(queries, gates, gain):
+    tokens, columns = queries.shape
+    return pl.pallas_call(
+        gate_kernel,
+        grid=(tokens // ROW_TILE,),
+        in_specs=[row_block(columns), row_block(columns), pl.BlockSpec((1, columns), lambda i: (0, 0))],
+        out_specs=[row_block(columns), row_block(columns)],
+        out_shape=[
+            jax.ShapeDtypeStruct((tokens, columns), jnp.bfloat16),
+            jax.ShapeDtypeStruct((tokens, columns), jnp.float32),
+        ],
+        cost_estimate=pl.CostEstimate(
+            flops=8 * tokens * columns,
+            transcendentals=2 * tokens * columns,
+            bytes_accessed=10 * tokens * columns,
+        ),
+    )(queries, gates, gain.reshape(1, columns))
+
+
+def mix_kernel(local_a_ref, local_b_ref, q_ref, scale_ref, hi_ref, lo_ref, out_ref):
+    query_act = q_ref[...]
     first = local_a_ref.shape[1] // HD
     for h in range(hi_ref.shape[0]):
         heads = slice(h * HD, (h + 1) * HD)
@@ -117,12 +140,13 @@
         )
         attention = local + remote
         mean_sq = jnp.mean(attention * attention, axis=-1, keepdims=True)
-        normed = attention * lax.rsqrt(mean_sq + epsilon) * gain_ref[:, heads]
-        out_ref[:, heads] = (normed * gate_open[:, heads]).astype(out_ref.dtype)
-
-
-def mix(local_a, local_b, queries, gates, prefix_hi, prefix_lo, gain):
-    tokens, columns = queries.shape
+        out_ref[:, heads] = (attention * lax.rsqrt(mean_sq + epsilon) * scale_ref[:, heads]).astype(
+            out_ref.dtype
+        )
+
+
+def mix(local_a, local_b, query_act, scale, prefix_hi, prefix_lo):
+    tokens, columns = query_act.shape
     heads = columns // HD
     whole_state = pl.BlockSpec((heads, HD, HD), lambda i: (0, 0, 0))
     return pl.pallas_call(
@@ -135,16 +159,15 @@
             row_block(columns),
             whole_state,
             whole_state,
-            pl.BlockSpec((1, columns), lambda i: (0, 0)),
         ],
         out_specs=row_block(columns),
         out_shape=jax.ShapeDtypeStruct((tokens, columns), jnp.bfloat16),
         cost_estimate=pl.CostEstimate(
             flops=4 * tokens * HD * HD * heads,
-            transcendentals=2 * tokens * columns,
-            bytes_accessed=10 * tokens * columns,
-        ),
-    )(local_a, local_b, queries, gates, prefix_hi, prefix_lo, gain.reshape(1, columns))
+            transcendentals=tokens * heads,
+            bytes_accessed=12 * tokens * columns,
+        ),
+    )(local_a, local_b, query_act, scale, prefix_hi, prefix_lo)
 
 
 def split_bf16(x):
@@ -239,10 +262,11 @@
     fillers = (
         (lambda q, k, v: local_attention(q, k, v, 0, first), (queries, keys, values)),
         (lambda q, k, v: local_attention(q, k, v, first, head_count - first), (queries, keys, values)),
+        (query_and_gate, (queries, gates, gain)),
     )
-    prefix, (local_a, local_b) = exclusive_prefix(own_state, "ctx", fillers)
+    prefix, (local_a, local_b, (query_act, scale)) = exclusive_prefix(own_state, "ctx", fillers)
     prefix_hi, prefix_lo = split_bf16(prefix)
-    mixed_rows = mix(local_a, local_b, queries, gates, prefix_hi, prefix_lo, gain)
+    mixed_rows = mix(local_a, local_b, query_act, scale, prefix_hi, prefix_lo)
     return project_and_reduce(mixed_rows, out_weight)
 
 

time: 154 us -> 154 us (level)
  waiting for transfers between devices: 76.4 us -> 69.4 us
  Pallas kernels: 29.7 us -> 36 us
    ppermute x3, waiting for transfers between devices: 17.8 us -> 10.9 us  [shift(): lax.ppermute(block, axis, [(i, i + distance) for i in range(size) if i +...]
    pallas_call x0 -> x1, Pallas kernels: none -> 6.72 us  [query_and_gate(): pl.pallas_call(gate_kernel, grid=(tokens // ROW_TILE,), in_specs=[row_blo...]
  transfers between devices with their start and end apart: 10 -> 10, of which waited for: 7 -> 7; matrix products, arithmetic and copies ran while one was open for 10% -> 10% of each run, Pallas kernels for 10% -> 15%
where the time goes in v11:
time: 154 us; the launch traced here: 153 us
  waiting for transfers between devices  69.4 us (45%)
  Pallas kernels  36 us (23%)
  matrix products  29.2 us (19%)
  starting transfers between devices  10.8 us (7%)
  other arithmetic  6.32 us (4%)
    ppermute x7, waiting for transfers between devices, swap(): return lax.ppermute(block, axis, [(0, 1), (1, 0)])  58.5 us
    pallas_call x2, Pallas kernels, local_attention(): pl.pallas_call(local_kernel, grid=(heads,), in_specs=[picked] * 3, out_sp...  15.8 us
    dot_general x3, matrix products, project_and_reduce(): jnp.dot(far_rows, out_weight[:, c * chunk:(c + 1) * chunk], preferred_ele...  14.8 us
    dot_general x2, matrix products, product(): jnp.dot(rows, out_weight, preferred_element_type=jnp.float32)  14.4 us
    ppermute x3, waiting for transfers between devices, shift(): lax.ppermute(block, axis, [(i, i + distance) for i in range(size) if i +...  10.9 us
    pallas_call x1, Pallas kernels, mix(): pl.pallas_call(mix_kernel, grid=(tokens // ROW_TILE,), in_specs=[row_bloc...  7.94 us
    pallas_call x1, Pallas kernels, query_and_gate(): pl.pallas_call(gate_kernel, grid=(tokens // ROW_TILE,), in_specs=[row_blo...  6.72 us
    ppermute x3, starting transfers between devices, shift(): lax.ppermute(block, axis, [(i, i + distance) for i in range(size) if i +...  6.3 us
  transfers between devices with their start and end apart: 10, of which 7 were waited for; matrix products, arithmetic and copies ran while one was open for 10% of the time, Pallas kernels for 15%

profile of v11, /device:TPU:24, one launch (start us, length us, event | category | flops | bytes accessed | tf_op | source)
XLA Modules:
  0.0 153.1 jit_solution(6769321724355751441)
XLA Ops:
  0.0 5.5 %shard_map.64 = f32[10,128,128]{2,1,0:T(8,128)} custom-call(bf16[1024,1280]{1,0:T(8,128)(2,1)} %k_ref.3, bf16[1024,1280]{1,0:T(8,128)(2,1)} %v_ref.3), custom_call_target="tpu_custom_call" | custom-call | flops 335544320 | bytes 5898240 | tf_op jit(solution)/shard_map/pallas_call | solution.py:50
  5.5 1.1 convert_element_type.81
  6.7 3.5 %collective-permute-start = (bf16[10,128,128]{2,1,0:T(8,128)(2,1)S(1)}, bf16[10,128,128]{2,1,0:T(8,128)(2,1)S(1)}, u32[]{:S(2)}, u32[]{:S(2)}) collective-permute-start(bf16[10,128,128]{2,1,0:T(8,128)(2,1)S(1)} %convert_element_type.81), channel_id=1, source_target_pairs={{0,4},{4,8},{8,12},{12,16},{16,20},{20,24},{24,28},{1,5},{5,9},{9,... | collective-permute-start | bytes 983048 | tf_op jit(solution)/shard_map/ppermute | solution.py:181
  10.2 7.9 %shard_map.65.local_a_ref = f32[1024,640]{1,0:T(8,128)} custom-call(bf16[1024,1280]{1,0:T(8,128)(2,1)} %q_ref.2, bf16[1024,1280]{1,0:T(8,128)(2,1)} %k_ref.3, bf16[1024,1280]{1,0:T(8,128)(2,1)} %v_ref.3), custom_call_target="tpu_custom_call" | custom-call | flops 1677721600 | bytes 6553600 | tf_op jit(solution)/shard_map/pallas_call | solution.py:90
  19.2 1.3 collective-permute-start.1
  20.5 8.0 %shard_map.66.local_b_ref = f32[1024,640]{1,0:T(8,128)} custom-call(bf16[1024,1280]{1,0:T(8,128)(2,1)} %q_ref.2, bf16[1024,1280]{1,0:T(8,128)(2,1)} %k_ref.3, bf16[1024,1280]{1,0:T(8,128)(2,1)} %v_ref.3), custom_call_target="tpu_custom_call" | custom-call | flops 1677721600 | bytes 6553600 | tf_op jit(solution)/shard_map/pallas_call | solution.py:90
  28.4 1.2 collective-permute-done.1
  29.8 1.5 collective-permute-start.2
  31.9 6.7 %shard_map.67 = (bf16[1024,1280]{1,0:T(8,128)(2,1)}, f32[1024,1280]{1,0:T(8,128)}) custom-call(bf16[1024,1280]{1,0:T(8,128)(2,1)} %q_ref.2, bf16[1024,1280]{1,0:T(8,128)(2,1)} %g_ref, f32[1,1280]{1,0:T(1,128)} %reshape.3.gain_ref), custom_call_target="tpu_custom_call" | custom-call | flops 10485760 | bytes 13107200 | tf_op jit(solution)/shard_map/pallas_call | solution.py:112
  38.6 8.7 %collective-permute-done.2 = bf16[10,128,128]{2,1,0:T(8,128)(2,1)S(1)} collective-permute-done((bf16[10,128,128]{2,1,0:T(8,128)(2,1)S(1)}, bf16[10,128,128]{2,1,0:T(8,128)(2,1)S(1)}, u32[]{:S(2)}, u32[]{:S(2)}) %collective-permute-start.2) | collective-permute-done | bytes 327712 | tf_op jit(solution)/shard_map/ppermute | solution.py:181
  47.4 1.0 subtract_convert_fusion
  48.4 7.9 %shard_map.68 = bf16[1024,1280]{1,0:T(8,128)(2,1)} custom-call(f32[1024,640]{1,0:T(8,128)} %shard_map.65.local_a_ref, f32[1024,640]{1,0:T(8,128)} %shard_map.66.local_b_ref, bf16[1024,1280]{1,0:T(8,128)(2,1)} %get-tuple-element.42.q_ref, f32[1024,1280]{1,0:T(8,128)} %get-tuple-element.43.scale_ref, bf16[10,128,128]{2,1,0:T(8,128)(2,1)} %get-tuple-element.50.hi_ref, ...), custom_call_target="tpu_custom_call" | custom-call | flops 671088640 | bytes 15728640 | tf_op jit(solution)/shard_map/pallas_call | solution.py:152
  56.4 5.9 %fusion.12 = bf16[512,2048]{1,0:T(8,128)(2,1)S(1)} fusion(bf16[1280,6144]{1,0:T(8,128)(2,1)} %param.11, bf16[1024,1280]{1,0:T(8,128)(2,1)} %shard_map.68, s32[]{:T(128)S(6)} %select_n.8), kind=kOutput, calls=%fused_computation.11 | convolution fusion | flops 2685403136 | bytes 8650756 | tf_op jit(solution)/shard_map/dot_general | solution.py:243
  62.3 5.8 %fusion.9 = bf16[512,2048]{1,0:T(8,128)(2,1)S(1)} fusion(bf16[1280,6144]{1,0:T(8,128)(2,1)} %param.11, bf16[1024,1280]{1,0:T(8,128)(2,1)S(1)} %copy-done.1, s32[]{:T(128)S(6)} %select_n.8), kind=kOutput, calls=%fused_computation.10 | convolution fusion | flops 2685403136 | bytes 8650756 | tf_op jit(solution)/shard_map/dot_general | solution.py:243
  69.0 3.1 %fusion.6 = bf16[512,2048]{1,0:T(8,128)(2,1)S(1)} fusion(bf16[1280,6144]{1,0:T(8,128)(2,1)S(1)} %bitcast.3, bf16[1024,1280]{1,0:T(8,128)(2,1)S(1)} %copy-done.1, s32[]{:T(128)S(6)} %select_n.8), kind=kOutput, calls=%fused_computation.9 | convolution fusion | flops 2685403136 | bytes 8650756 | tf_op jit(solution)/shard_map/dot_general | solution.py:243
  73.4 1.6 %collective-permute-done.3 = bf16[256,2048]{1,0:T(8,128)(2,1)S(1)} collective-permute-done((bf16[256,2048]{1,0:T(8,128)(2,1)S(1)}, bf16[256,2048]{1,0:T(8,128)(2,1)S(1)}, u32[]{:S(2)}, u32[]{:S(2)}) %collective-permute-start.3) | collective-permute-done | bytes 1048608 | tf_op jit(solution)/shard_map/ppermute | solution.py:185
  75.5 4.4 %convolution_convert_fusion = bf16[256,6144]{1,0:T(8,128)(2,1)S(1)} fusion(bf16[1280,6144]{1,0:T(8,128)(2,1)S(1)} %bitcast.3, bf16[512,1280]{1,0:T(8,128)(2,1)S(1)} %constant_dynamic-slice_fusion, s32[]{:T(128)S(6)} %select_n.20), kind=kOutput, calls=%fused_computation | convolution fusion | flops 4028104704 | bytes 19529732 | tf_op jit(solution)/shard_map/dot_general | solution.py:219
  80.1 1.5 collective-permute-start.7
  82.2 1.5 collective-permute-start.9
  83.7 9.9 %convolution_convert_fusion.1 = bf16[256,6144]{1,0:T(8,128)(2,1)S(1)} fusion(bf16[1280,6144]{1,0:T(8,128)(2,1)} %param.11, bf16[512,1280]{1,0:T(8,128)(2,1)S(1)} %constant_dynamic-slice_fusion, s32[]{:T(128)S(6)} %select_n.9), kind=kOutput, calls=%fused_computation.1 | convolution fusion | flops 4028104704 | bytes 19529732 | tf_op jit(solution)/shard_map/dot_general | solution.py:219
  93.6 12.6 %collective-permute-done.7 = bf16[256,2048]{1,0:T(8,128)(2,1)S(1)} collective-permute-done((bf16[256,2048]{1,0:T(8,128)(2,1)S(1)}, bf16[256,2048]{1,0:T(8,128)(2,1)S(1)}, u32[]{:S(2)}, u32[]{:S(2)}) %collective-permute-start.7) | collective-permute-done | bytes 1048608 | tf_op jit(solution)/shard_map/ppermute | solution.py:185
  106.2 22.5 %collective-permute-done.8 = bf16[256,2048]{1,0:T(8,128)(2,1)S(1)} collective-permute-done((bf16[256,2048]{1,0:T(8,128)(2,1)S(1)}, bf16[256,2048]{1,0:T(8,128)(2,1)S(1)}, u32[]{:S(2)}, u32[]{:S(2)}) %collective-permute-start.8) | collective-permute-done | bytes 1048608 | tf_op jit(solution)/shard_map/ppermute | solution.py:185
  128.6 21.9 %collective-permute-done.9 = bf16[256,2048]{1,0:T(8,128)(2,1)S(1)} collective-permute-done((bf16[256,2048]{1,0:T(8,128)(2,1)S(1)}, bf16[256,2048]{1,0:T(8,128)(2,1)S(1)}, u32[]{:S(2)}, u32[]{:S(2)}) %collective-permute-start.9) | collective-permute-done | bytes 1048608 | tf_op jit(solution)/shard_map/ppermute | solution.py:185
  150.5 2.6 %add_convert_fusion = bf16[256,6144]{1,0:T(8,128)(2,1)} fusion(bf16[256,6144]{1,0:T(8,128)(2,1)S(1)} %collective-permute-done.6, bf16[256,6144]{1,0:T(8,128)(2,1)S(1)} %convolution_convert_fusion.1, bf16[256,2048]{1,0:T(8,128)(2,1)S(1)} %collective-permute-done.9, bf16[256,2048]{1,0:T(8,128)(2,1)S(1)} %collective-permute-done.8, ...), kind=kLoop, calls=%fused_computation.2 | loop fusion | flops 17301504 | bytes 12582912 | tf_op jit(solution)/shard_map/convert_element_type | solution.py:255
  (34 shorter events, 5.0 us)
Async XLA Ops:
  6.7 12.4 %copy-start = (f32[10,128,128]{2,1,0:T(8,128)S(1)}, f32[10,128,128]{2,1,0:T(8,128)}, u32[]{:S(2)}) copy-start(f32[10,128,128]{2,1,0:T(8,128)} %shard_map.64) | copy-start | bytes 1966084
  6.7 12.4 %collective-permute-start = (bf16[10,128,128]{2,1,0:T(8,128)(2,1)S(1)}, bf16[10,128,128]{2,1,0:T(8,128)(2,1)S(1)}, u32[]{:S(2)}, u32[]{:S(2)}) collective-permute-start(bf16[10,128,128]{2,1,0:T(8,128)(2,1)S(1)} %convert_element_type.81), channel_id=1, source_target_pairs={{0,4},{4,8},{8,12},{12,16},{16,20},{20,24},{24,28},{1,5},{5,9},{9,... | collective-permute-start | bytes 983048 | tf_op jit(solution)/shard_map/ppermute | solution.py:181
  19.2 12.1 %copy-start.2 = (f32[1280]{0:T(1024)S(1)}, f32[1280]{0:T(1024)}, u32[]{:S(2)}) copy-start(f32[1280]{0:T(1024)} %param.10) | copy-start | bytes 15364
  19.2 10.5 %collective-permute-start.1 = (bf16[10,128,128]{2,1,0:T(8,128)(2,1)S(1)}, bf16[10,128,128]{2,1,0:T(8,128)(2,1)S(1)}, u32[]{:S(2)}, u32[]{:S(2)}) collective-permute-start(bf16[10,128,128]{2,1,0:T(8,128)(2,1)S(1)} %fusion.22), channel_id=1, source_target_pairs={{0,8},{4,12},{8,16},{12,20},{16,24},{20,28},{1,9},{5,13},{9,17},{1... | collective-permute-start | bytes 983048 | tf_op jit(solution)/shard_map/ppermute | solution.py:181
  29.8 17.6 %collective-permute-start.2 = (bf16[10,128,128]{2,1,0:T(8,128)(2,1)S(1)}, bf16[10,128,128]{2,1,0:T(8,128)(2,1)S(1)}, u32[]{:S(2)}, u32[]{:S(2)}) collective-permute-start(bf16[10,128,128]{2,1,0:T(8,128)(2,1)S(1)} %fusion.18), channel_id=1, source_target_pairs={{0,16},{4,20},{8,24},{12,28},{1,17},{5,21},{9,25},{13,29},{2,18},{... | collective-permute-start | bytes 983048 | tf_op jit(solution)/shard_map/ppermute | solution.py:181
  56.3 5.9 %copy-start.1 = (bf16[1024,1280]{1,0:T(8,128)(2,1)S(1)}, bf16[1024,1280]{1,0:T(8,128)(2,1)}, u32[]{:S(2)}) copy-start(bf16[1024,1280]{1,0:T(8,128)(2,1)} %shard_map.68) | copy-start | bytes 7864324
  56.3 12.7 %slice-start = ((s8[15728640]{0:T(1024)(128)(4,1)}), s8[4194304]{0:T(1024)(128)(4,1)S(1)}, s32[]{:S(2)}) async-start(s8[15728640]{0:T(1024)(128)(4,1)} %bitcast.2), calls=%async_computation | async-start | bytes 8388608
  56.4 12.7 %slice-start.1 = ((s8[15728640]{0:T(1024)(128)(4,1)}), s8[4194304]{0:T(1024)(128)(4,1)S(1)}, s32[]{:S(2)}) async-start(s8[15728640]{0:T(1024)(128)(4,1)} %bitcast.2), calls=%async_computation.1 | async-start | bytes 8388608
  62.3 6.7 %slice-start.2 = ((s8[15728640]{0:T(1024)(128)(4,1)}), s8[4194304]{0:T(1024)(128)(4,1)S(1)}, s32[]{:S(2)}) async-start(s8[15728640]{0:T(1024)(128)(4,1)} %bitcast.2), calls=%async_computation.2 | async-start | bytes 8388608
  62.3 6.7 %slice-start.3 = ((s8[15728640]{0:T(1024)(128)(4,1)}), s8[3145728]{0:T(1024)(128)(4,1)S(1)}, s32[]{:S(2)}) async-start(s8[15728640]{0:T(1024)(128)(4,1)} %bitcast.2), calls=%async_computation.3 | async-start | bytes 6291456
  68.3 4.2 %collective-permute-start.5 = (bf16[256,2048]{1,0:T(8,128)(2,1)S(1)}, bf16[256,2048]{1,0:T(8,128)(2,1)S(1)}, u32[]{:S(2)}, u32[]{:S(2)}) collective-permute-start(bf16[256,2048]{1,0:T(8,128)(2,1)S(1)} %constant_dynamic-slice_fusion.1), channel_id=1, source_target_pairs={{0,1},{1,0},{2,3},{3,2},{4,5},{5,4},{6,7},{7,6},{8,9},{9,8},{10,11... | collective-permute-start | bytes 3145736 | tf_op jit(solution)/shard_map/ppermute | solution.py:185
  68.5 4.5 %collective-permute-start.4 = (bf16[256,2048]{1,0:T(8,128)(2,1)S(1)}, bf16[256,2048]{1,0:T(8,128)(2,1)S(1)}, u32[]{:S(2)}, u32[]{:S(2)}) collective-permute-start(bf16[256,2048]{1,0:T(8,128)(2,1)S(1)} %constant_dynamic-slice_fusion.2), channel_id=1, source_target_pairs={{0,1},{1,0},{2,3},{3,2},{4,5},{5,4},{6,7},{7,6},{8,9},{9,8},{10,11... | collective-permute-start | bytes 3145736 | tf_op jit(solution)/shard_map/ppermute | solution.py:185
  72.3 2.7 %collective-permute-start.3 = (bf16[256,2048]{1,0:T(8,128)(2,1)S(1)}, bf16[256,2048]{1,0:T(8,128)(2,1)S(1)}, u32[]{:S(2)}, u32[]{:S(2)}) collective-permute-start(bf16[256,2048]{1,0:T(8,128)(2,1)S(1)} %constant_dynamic-slice_fusion.3), channel_id=1, source_target_pairs={{0,1},{1,0},{2,3},{3,2},{4,5},{5,4},{6,7},{7,6},{8,9},{9,8},{10,11... | collective-permute-start | bytes 3145736 | tf_op jit(solution)/shard_map/ppermute | solution.py:185
  79.9 70.6 %collective-permute-start.6 = (bf16[256,6144]{1,0:T(8,128)(2,1)S(1)}, bf16[256,6144]{1,0:T(8,128)(2,1)S(1)}, u32[]{:S(2)}, u32[]{:S(2)}) collective-permute-start(bf16[256,6144]{1,0:T(8,128)(2,1)S(1)} %convolution_convert_fusion), channel_id=1, source_target_pairs={{0,1},{1,0},{2,3},{3,2},{4,5},{5,4},{6,7},{7,6},{8,9},{9,8},{10,11... | collective-permute-start | bytes 9437192 | tf_op jit(solution)/shard_map/ppermute | solution.py:185
  80.1 26.0 %collective-permute-start.7 = (bf16[256,2048]{1,0:T(8,128)(2,1)S(1)}, bf16[256,2048]{1,0:T(8,128)(2,1)S(1)}, u32[]{:S(2)}, u32[]{:S(2)}) collective-permute-start(bf16[256,2048]{1,0:T(8,128)(2,1)S(1)} %add_convert_fusion.3), channel_id=1, source_target_pairs={{0,2},{2,0},{1,3},{3,1},{4,6},{6,4},{5,7},{7,5},{8,10},{10,8},{9,1... | collective-permute-start | bytes 3145736 | tf_op jit(solution)/shard_map/ppermute | solution.py:185
  81.6 47.0 %collective-permute-start.8 = (bf16[256,2048]{1,0:T(8,128)(2,1)S(1)}, bf16[256,2048]{1,0:T(8,128)(2,1)S(1)}, u32[]{:S(2)}, u32[]{:S(2)}) collective-permute-start(bf16[256,2048]{1,0:T(8,128)(2,1)S(1)} %add_convert_fusion.2), channel_id=1, source_target_pairs={{0,2},{2,0},{1,3},{3,1},{4,6},{6,4},{5,7},{7,5},{8,10},{10,8},{9,1... | collective-permute-start | bytes 3145736 | tf_op jit(solution)/shard_map/ppermute | solution.py:185
  82.2 68.4 %collective-permute-start.9 = (bf16[256,2048]{1,0:T(8,128)(2,1)S(1)}, bf16[256,2048]{1,0:T(8,128)(2,1)S(1)}, u32[]{:S(2)}, u32[]{:S(2)}) collective-permute-start(bf16[256,2048]{1,0:T(8,128)(2,1)S(1)} %add_convert_fusion.1), channel_id=1, source_target_pairs={{0,2},{2,0},{1,3},{3,1},{4,6},{6,4},{5,7},{7,5},{8,10},{10,8},{9,1... | collective-permute-start | bytes 3145736 | tf_op jit(solution)/shard_map/ppermute | solution.py:185

commit v12 on v11

--- a/solution.py
+++ b/solution.py
@@ -79,7 +79,7 @@
         scores = jnp.where(row >= col, scores, 0.0).astype(jnp.bfloat16)
         out_ref[tile * QUERY_TILE:seen, :] = jnp.dot(
             scores, value_rows[:seen], preferred_element_type=jnp.float32
-        )
+        ).astype(out_ref.dtype)
 
 
 def local_attention(queries, keys, values, first_head, heads):
@@ -92,7 +92,7 @@
         grid=(heads,),
         in_specs=[picked] * 3,
         out_specs=head_block(tokens),
-        out_shape=jax.ShapeDtypeStruct((tokens, heads * HD), jnp.float32),
+        out_shape=jax.ShapeDtypeStruct((tokens, heads * HD), jnp.bfloat16),
         cost_estimate=pl.CostEstimate(
             flops=4 * pairs * HD * heads,
             transcendentals=2 * tokens * heads * HD,
@@ -104,7 +104,7 @@
 def gate_kernel(q_ref, g_ref, gain_ref, query_act_ref, scale_ref):
     query_act_ref[...] = silu(q_ref[...])
     gates = g_ref[...].astype(jnp.float32)
-    scale_ref[...] = gain_ref[...] * (1.0 / (1.0 + jnp.exp(-gates)))
+    scale_ref[...] = (gain_ref[...] * (1.0 / (1.0 + jnp.exp(-gates)))).astype(scale_ref.dtype)
 
 
 def query_and_gate(queries, gates, gain):
@@ -116,7 +116,7 @@
         out_specs=[row_block(columns), row_block(columns)],
         out_shape=[
             jax.ShapeDtypeStruct((tokens, columns), jnp.bfloat16),
-            jax.ShapeDtypeStruct((tokens, columns), jnp.float32),
+            jax.ShapeDtypeStruct((tokens, columns), jnp.bfloat16),
         ],
         cost_estimate=pl.CostEstimate(
             flops=8 * tokens * columns,
@@ -135,12 +135,14 @@
             local = local_a_ref[:, heads]
         else:
             local = local_b_ref[:, (h - first) * HD:(h - first + 1) * HD]
+        local = local.astype(jnp.float32)
         remote = jnp.dot(query_act[:, heads], hi_ref[h], preferred_element_type=jnp.float32) + jnp.dot(
             query_act[:, heads], lo_ref[h], preferred_element_type=jnp.float32
         )
         attention = local + remote
         mean_sq = jnp.mean(attention * attention, axis=-1, keepdims=True)
-        out_ref[:, heads] = (attention * lax.rsqrt(mean_sq + epsilon) * scale_ref[:, heads]).astype(
+        scale = scale_ref[:, heads].astype(jnp.float32)
+        out_ref[:, heads] = (attention * lax.rsqrt(mean_sq + epsilon) * scale).astype(
             out_ref.dtype
         )
 

time: 154 us -> 153 us (level)
  Pallas kernels: 36 us -> 33.7 us
  transfers between devices with their start and end apart: 10 -> 10, of which waited for: 7 -> 7; matrix products, arithmetic and copies ran while one was open for 10% -> 10% of each run, Pallas kernels for 15% -> 14%
where the time goes in v12:
time: 153 us; the launch traced here: 152 us
  waiting for transfers between devices  70.5 us (46%)
  Pallas kernels  33.7 us (22%)
  matrix products  29.2 us (19%)
  starting transfers between devices  10.8 us (7%)
  other arithmetic  6.38 us (4%)
    ppermute x7, waiting for transfers between devices, swap(): return lax.ppermute(block, axis, [(0, 1), (1, 0)])  58.5 us
    pallas_call x2, Pallas kernels, local_attention(): pl.pallas_call(local_kernel, grid=(heads,), in_specs=[picked] * 3, out_sp...  15.2 us
    dot_general x3, matrix products, project_and_reduce(): jnp.dot(far_rows, out_weight[:, c * chunk:(c + 1) * chunk], preferred_ele...  14.8 us
    dot_general x2, matrix products, product(): jnp.dot(rows, out_weight, preferred_element_type=jnp.float32)  14.4 us
    ppermute x3, waiting for transfers between devices, shift(): lax.ppermute(block, axis, [(i, i + distance) for i in range(size) if i +...  12 us
    pallas_call x1, Pallas kernels, mix(): pl.pallas_call(mix_kernel, grid=(tokens // ROW_TILE,), in_specs=[row_bloc...  6.73 us
    ppermute x3, starting transfers between devices, shift(): lax.ppermute(block, axis, [(i, i + distance) for i in range(size) if i +...  6.3 us
    pallas_call x1, Pallas kernels, query_and_gate(): pl.pallas_call(gate_kernel, grid=(tokens // ROW_TILE,), in_specs=[row_blo...  6.22 us
  transfers between devices with their start and end apart: 10, of which 7 were waited for; matrix products, arithmetic and copies ran while one was open for 10% of the time, Pallas kernels for 14%

profile of v12, /device:TPU:24, one launch (start us, length us, event | category | flops | bytes accessed | tf_op | source)
XLA Modules:
  0.0 151.9 jit_solution(17328669993034847581)
XLA Ops:
  0.0 5.5 %shard_map.64 = f32[10,128,128]{2,1,0:T(8,128)} custom-call(bf16[1024,1280]{1,0:T(8,128)(2,1)} %k_ref.3, bf16[1024,1280]{1,0:T(8,128)(2,1)} %v_ref.3), custom_call_target="tpu_custom_call" | custom-call | flops 335544320 | bytes 5898240 | tf_op jit(solution)/shard_map/pallas_call | solution.py:50
  5.5 1.1 convert_element_type.81
  6.7 3.5 %collective-permute-start = (bf16[10,128,128]{2,1,0:T(8,128)(2,1)S(1)}, bf16[10,128,128]{2,1,0:T(8,128)(2,1)S(1)}, u32[]{:S(2)}, u32[]{:S(2)}) collective-permute-start(bf16[10,128,128]{2,1,0:T(8,128)(2,1)S(1)} %convert_element_type.81), channel_id=1, source_target_pairs={{0,4},{4,8},{8,12},{12,16},{16,20},{20,24},{24,28},{1,5},{5,9},{9,... | collective-permute-start | bytes 983048 | tf_op jit(solution)/shard_map/ppermute | solution.py:183
  10.2 7.6 %shard_map.65.local_a_ref = bf16[1024,640]{1,0:T(8,128)(2,1)} custom-call(bf16[1024,1280]{1,0:T(8,128)(2,1)} %q_ref.2, bf16[1024,1280]{1,0:T(8,128)(2,1)} %k_ref.3, bf16[1024,1280]{1,0:T(8,128)(2,1)} %v_ref.3), custom_call_target="tpu_custom_call" | custom-call | flops 1677721600 | bytes 6553600 | tf_op jit(solution)/shard_map/pallas_call | solution.py:90
  17.8 1.2 collective-permute-done
  19.2 1.3 collective-permute-start.1
  20.5 7.6 %shard_map.66.local_b_ref = bf16[1024,640]{1,0:T(8,128)(2,1)} custom-call(bf16[1024,1280]{1,0:T(8,128)(2,1)} %q_ref.2, bf16[1024,1280]{1,0:T(8,128)(2,1)} %k_ref.3, bf16[1024,1280]{1,0:T(8,128)(2,1)} %v_ref.3), custom_call_target="tpu_custom_call" | custom-call | flops 1677721600 | bytes 6553600 | tf_op jit(solution)/shard_map/pallas_call | solution.py:90
  28.1 1.6 %collective-permute-done.1 = bf16[10,128,128]{2,1,0:T(8,128)(2,1)S(1)} collective-permute-done((bf16[10,128,128]{2,1,0:T(8,128)(2,1)S(1)}, bf16[10,128,128]{2,1,0:T(8,128)(2,1)S(1)}, u32[]{:S(2)}, u32[]{:S(2)}) %collective-permute-start.1) | collective-permute-done | bytes 327712 | tf_op jit(solution)/shard_map/ppermute | solution.py:183
  29.8 1.5 collective-permute-start.2
  31.9 6.2 %shard_map.67 = (bf16[1024,1280]{1,0:T(8,128)(2,1)}, bf16[1024,1280]{1,0:T(8,128)(2,1)}) custom-call(bf16[1024,1280]{1,0:T(8,128)(2,1)} %q_ref.2, bf16[1024,1280]{1,0:T(8,128)(2,1)} %g_ref, f32[1,1280]{1,0:T(1,128)} %reshape.3.gain_ref), custom_call_target="tpu_custom_call" | custom-call | flops 10485760 | bytes 13107200 | tf_op jit(solution)/shard_map/pallas_call | solution.py:112
  38.1 9.2 %collective-permute-done.2 = bf16[10,128,128]{2,1,0:T(8,128)(2,1)S(1)} collective-permute-done((bf16[10,128,128]{2,1,0:T(8,128)(2,1)S(1)}, bf16[10,128,128]{2,1,0:T(8,128)(2,1)S(1)}, u32[]{:S(2)}, u32[]{:S(2)}) %collective-permute-start.2) | collective-permute-done | bytes 327712 | tf_op jit(solution)/shard_map/ppermute | solution.py:183
  48.4 6.7 %shard_map.68 = bf16[1024,1280]{1,0:T(8,128)(2,1)} custom-call(bf16[1024,640]{1,0:T(8,128)(2,1)} %shard_map.65.local_a_ref, bf16[1024,640]{1,0:T(8,128)(2,1)} %shard_map.66.local_b_ref, bf16[1024,1280]{1,0:T(8,128)(2,1)} %get-tuple-element.42.q_ref, bf16[1024,1280]{1,0:T(8,128)(2,1)} %get-tuple-element.43.scale_ref, ...), custom_call_target="tpu_custom_call" | custom-call | flops 671088640 | bytes 15728640 | tf_op jit(solution)/shard_map/pallas_call | solution.py:154
  55.2 5.9 %fusion.12 = bf16[512,2048]{1,0:T(8,128)(2,1)S(1)} fusion(bf16[1280,6144]{1,0:T(8,128)(2,1)} %param.11, bf16[1024,1280]{1,0:T(8,128)(2,1)} %shard_map.68, s32[]{:T(128)S(6)} %select_n.8), kind=kOutput, calls=%fused_computation.11 | convolution fusion | flops 2685403136 | bytes 8650756 | tf_op jit(solution)/shard_map/dot_general | solution.py:245
  61.1 5.8 %fusion.9 = bf16[512,2048]{1,0:T(8,128)(2,1)S(1)} fusion(bf16[1280,6144]{1,0:T(8,128)(2,1)} %param.11, bf16[1024,1280]{1,0:T(8,128)(2,1)S(1)} %copy-done.1, s32[]{:T(128)S(6)} %select_n.8), kind=kOutput, calls=%fused_computation.10 | convolution fusion | flops 2685403136 | bytes 8650756 | tf_op jit(solution)/shard_map/dot_general | solution.py:245
  67.8 3.1 %fusion.6 = bf16[512,2048]{1,0:T(8,128)(2,1)S(1)} fusion(bf16[1280,6144]{1,0:T(8,128)(2,1)S(1)} %bitcast.3, bf16[1024,1280]{1,0:T(8,128)(2,1)S(1)} %copy-done.1, s32[]{:T(128)S(6)} %select_n.8), kind=kOutput, calls=%fused_computation.9 | convolution fusion | flops 2685403136 | bytes 8650756 | tf_op jit(solution)/shard_map/dot_general | solution.py:245
  72.2 1.6 %collective-permute-done.3 = bf16[256,2048]{1,0:T(8,128)(2,1)S(1)} collective-permute-done((bf16[256,2048]{1,0:T(8,128)(2,1)S(1)}, bf16[256,2048]{1,0:T(8,128)(2,1)S(1)}, u32[]{:S(2)}, u32[]{:S(2)}) %collective-permute-start.3) | collective-permute-done | bytes 1048608 | tf_op jit(solution)/shard_map/ppermute | solution.py:187
  74.3 4.4 %convolution_convert_fusion = bf16[256,6144]{1,0:T(8,128)(2,1)S(1)} fusion(bf16[1280,6144]{1,0:T(8,128)(2,1)S(1)} %bitcast.3, bf16[512,1280]{1,0:T(8,128)(2,1)S(1)} %constant_dynamic-slice_fusion, s32[]{:T(128)S(6)} %select_n.20), kind=kOutput, calls=%fused_computation | convolution fusion | flops 4028104704 | bytes 19529732 | tf_op jit(solution)/shard_map/dot_general | solution.py:221
  78.9 1.5 collective-permute-start.7
  81.0 1.5 collective-permute-start.9
  82.5 9.9 %convolution_convert_fusion.1 = bf16[256,6144]{1,0:T(8,128)(2,1)S(1)} fusion(bf16[1280,6144]{1,0:T(8,128)(2,1)} %param.11, bf16[512,1280]{1,0:T(8,128)(2,1)S(1)} %constant_dynamic-slice_fusion, s32[]{:T(128)S(6)} %select_n.9), kind=kOutput, calls=%fused_computation.1 | convolution fusion | flops 4028104704 | bytes 19529732 | tf_op jit(solution)/shard_map/dot_general | solution.py:221
  92.4 12.6 %collective-permute-done.7 = bf16[256,2048]{1,0:T(8,128)(2,1)S(1)} collective-permute-done((bf16[256,2048]{1,0:T(8,128)(2,1)S(1)}, bf16[256,2048]{1,0:T(8,128)(2,1)S(1)}, u32[]{:S(2)}, u32[]{:S(2)}) %collective-permute-start.7) | collective-permute-done | bytes 1048608 | tf_op jit(solution)/shard_map/ppermute | solution.py:187
  105.0 22.5 %collective-permute-done.8 = bf16[256,2048]{1,0:T(8,128)(2,1)S(1)} collective-permute-done((bf16[256,2048]{1,0:T(8,128)(2,1)S(1)}, bf16[256,2048]{1,0:T(8,128)(2,1)S(1)}, u32[]{:S(2)}, u32[]{:S(2)}) %collective-permute-start.8) | collective-permute-done | bytes 1048608 | tf_op jit(solution)/shard_map/ppermute | solution.py:187
  127.4 21.9 %collective-permute-done.9 = bf16[256,2048]{1,0:T(8,128)(2,1)S(1)} collective-permute-done((bf16[256,2048]{1,0:T(8,128)(2,1)S(1)}, bf16[256,2048]{1,0:T(8,128)(2,1)S(1)}, u32[]{:S(2)}, u32[]{:S(2)}) %collective-permute-start.9) | collective-permute-done | bytes 1048608 | tf_op jit(solution)/shard_map/ppermute | solution.py:187
  149.3 2.6 %add_convert_fusion = bf16[256,6144]{1,0:T(8,128)(2,1)} fusion(bf16[256,6144]{1,0:T(8,128)(2,1)S(1)} %collective-permute-done.6, bf16[256,6144]{1,0:T(8,128)(2,1)S(1)} %convolution_convert_fusion.1, bf16[256,2048]{1,0:T(8,128)(2,1)S(1)} %collective-permute-done.9, bf16[256,2048]{1,0:T(8,128)(2,1)S(1)} %collective-permute-done.8, ...), kind=kLoop, calls=%fused_computation.2 | loop fusion | flops 17301504 | bytes 12582912 | tf_op jit(solution)/shard_map/convert_element_type | solution.py:257
  (34 shorter events, 5.2 us)
Async XLA Ops:
  6.7 12.4 %copy-start = (f32[10,128,128]{2,1,0:T(8,128)S(1)}, f32[10,128,128]{2,1,0:T(8,128)}, u32[]{:S(2)}) copy-start(f32[10,128,128]{2,1,0:T(8,128)} %shard_map.64) | copy-start | bytes 1966084
  6.7 12.4 %collective-permute-start = (bf16[10,128,128]{2,1,0:T(8,128)(2,1)S(1)}, bf16[10,128,128]{2,1,0:T(8,128)(2,1)S(1)}, u32[]{:S(2)}, u32[]{:S(2)}) collective-permute-start(bf16[10,128,128]{2,1,0:T(8,128)(2,1)S(1)} %convert_element_type.81), channel_id=1, source_target_pairs={{0,4},{4,8},{8,12},{12,16},{16,20},{20,24},{24,28},{1,5},{5,9},{9,... | collective-permute-start | bytes 983048 | tf_op jit(solution)/shard_map/ppermute | solution.py:183
  19.1 12.1 %copy-start.2 = (f32[1280]{0:T(1024)S(1)}, f32[1280]{0:T(1024)}, u32[]{:S(2)}) copy-start(f32[1280]{0:T(1024)} %param.10) | copy-start | bytes 15364
  19.2 10.5 %collective-permute-start.1 = (bf16[10,128,128]{2,1,0:T(8,128)(2,1)S(1)}, bf16[10,128,128]{2,1,0:T(8,128)(2,1)S(1)}, u32[]{:S(2)}, u32[]{:S(2)}) collective-permute-start(bf16[10,128,128]{2,1,0:T(8,128)(2,1)S(1)} %fusion.22), channel_id=1, source_target_pairs={{0,8},{4,12},{8,16},{12,20},{16,24},{20,28},{1,9},{5,13},{9,17},{1... | collective-permute-start | bytes 983048 | tf_op jit(solution)/shard_map/ppermute | solution.py:183
  29.8 17.6 %collective-permute-start.2 = (bf16[10,128,128]{2,1,0:T(8,128)(2,1)S(1)}, bf16[10,128,128]{2,1,0:T(8,128)(2,1)S(1)}, u32[]{:S(2)}, u32[]{:S(2)}) collective-permute-start(bf16[10,128,128]{2,1,0:T(8,128)(2,1)S(1)} %fusion.18), channel_id=1, source_target_pairs={{0,16},{4,20},{8,24},{12,28},{1,17},{5,21},{9,25},{13,29},{2,18},{... | collective-permute-start | bytes 983048 | tf_op jit(solution)/shard_map/ppermute | solution.py:183
  55.2 5.9 %copy-start.1 = (bf16[1024,1280]{1,0:T(8,128)(2,1)S(1)}, bf16[1024,1280]{1,0:T(8,128)(2,1)}, u32[]{:S(2)}) copy-start(bf16[1024,1280]{1,0:T(8,128)(2,1)} %shard_map.68) | copy-start | bytes 7864324
  55.2 12.7 %slice-start = ((s8[15728640]{0:T(1024)(128)(4,1)}), s8[4194304]{0:T(1024)(128)(4,1)S(1)}, s32[]{:S(2)}) async-start(s8[15728640]{0:T(1024)(128)(4,1)} %bitcast.2), calls=%async_computation | async-start | bytes 8388608
  55.2 12.7 %slice-start.1 = ((s8[15728640]{0:T(1024)(128)(4,1)}), s8[4194304]{0:T(1024)(128)(4,1)S(1)}, s32[]{:S(2)}) async-start(s8[15728640]{0:T(1024)(128)(4,1)} %bitcast.2), calls=%async_computation.1 | async-start | bytes 8388608
  61.1 6.7 %slice-start.2 = ((s8[15728640]{0:T(1024)(128)(4,1)}), s8[4194304]{0:T(1024)(128)(4,1)S(1)}, s32[]{:S(2)}) async-start(s8[15728640]{0:T(1024)(128)(4,1)} %bitcast.2), calls=%async_computation.2 | async-start | bytes 8388608
  61.1 6.7 %slice-start.3 = ((s8[15728640]{0:T(1024)(128)(4,1)}), s8[3145728]{0:T(1024)(128)(4,1)S(1)}, s32[]{:S(2)}) async-start(s8[15728640]{0:T(1024)(128)(4,1)} %bitcast.2), calls=%async_computation.3 | async-start | bytes 6291456
  67.1 4.2 %collective-permute-start.5 = (bf16[256,2048]{1,0:T(8,128)(2,1)S(1)}, bf16[256,2048]{1,0:T(8,128)(2,1)S(1)}, u32[]{:S(2)}, u32[]{:S(2)}) collective-permute-start(bf16[256,2048]{1,0:T(8,128)(2,1)S(1)} %constant_dynamic-slice_fusion.1), channel_id=1, source_target_pairs={{0,1},{1,0},{2,3},{3,2},{4,5},{5,4},{6,7},{7,6},{8,9},{9,8},{10,11... | collective-permute-start | bytes 3145736 | tf_op jit(solution)/shard_map/ppermute | solution.py:187
  67.3 4.5 %collective-permute-start.4 = (bf16[256,2048]{1,0:T(8,128)(2,1)S(1)}, bf16[256,2048]{1,0:T(8,128)(2,1)S(1)}, u32[]{:S(2)}, u32[]{:S(2)}) collective-permute-start(bf16[256,2048]{1,0:T(8,128)(2,1)S(1)} %constant_dynamic-slice_fusion.2), channel_id=1, source_target_pairs={{0,1},{1,0},{2,3},{3,2},{4,5},{5,4},{6,7},{7,6},{8,9},{9,8},{10,11... | collective-permute-start | bytes 3145736 | tf_op jit(solution)/shard_map/ppermute | solution.py:187
  71.1 2.7 %collective-permute-start.3 = (bf16[256,2048]{1,0:T(8,128)(2,1)S(1)}, bf16[256,2048]{1,0:T(8,128)(2,1)S(1)}, u32[]{:S(2)}, u32[]{:S(2)}) collective-permute-start(bf16[256,2048]{1,0:T(8,128)(2,1)S(1)} %constant_dynamic-slice_fusion.3), channel_id=1, source_target_pairs={{0,1},{1,0},{2,3},{3,2},{4,5},{5,4},{6,7},{7,6},{8,9},{9,8},{10,11... | collective-permute-start | bytes 3145736 | tf_op jit(solution)/shard_map/ppermute | solution.py:187
  78.7 70.6 %collective-permute-start.6 = (bf16[256,6144]{1,0:T(8,128)(2,1)S(1)}, bf16[256,6144]{1,0:T(8,128)(2,1)S(1)}, u32[]{:S(2)}, u32[]{:S(2)}) collective-permute-start(bf16[256,6144]{1,0:T(8,128)(2,1)S(1)} %convolution_convert_fusion), channel_id=1, source_target_pairs={{0,1},{1,0},{2,3},{3,2},{4,5},{5,4},{6,7},{7,6},{8,9},{9,8},{10,11... | collective-permute-start | bytes 9437192 | tf_op jit(solution)/shard_map/ppermute | solution.py:187
  78.9 26.0 %collective-permute-start.7 = (bf16[256,2048]{1,0:T(8,128)(2,1)S(1)}, bf16[256,2048]{1,0:T(8,128)(2,1)S(1)}, u32[]{:S(2)}, u32[]{:S(2)}) collective-permute-start(bf16[256,2048]{1,0:T(8,128)(2,1)S(1)} %add_convert_fusion.3), channel_id=1, source_target_pairs={{0,2},{2,0},{1,3},{3,1},{4,6},{6,4},{5,7},{7,5},{8,10},{10,8},{9,1... | collective-permute-start | bytes 3145736 | tf_op jit(solution)/shard_map/ppermute | solution.py:187
  80.5 47.0 %collective-permute-start.8 = (bf16[256,2048]{1,0:T(8,128)(2,1)S(1)}, bf16[256,2048]{1,0:T(8,128)(2,1)S(1)}, u32[]{:S(2)}, u32[]{:S(2)}) collective-permute-start(bf16[256,2048]{1,0:T(8,128)(2,1)S(1)} %add_convert_fusion.2), channel_id=1, source_target_pairs={{0,2},{2,0},{1,3},{3,1},{4,6},{6,4},{5,7},{7,5},{8,10},{10,8},{9,1... | collective-permute-start | bytes 3145736 | tf_op jit(solution)/shard_map/ppermute | solution.py:187
  81.0 68.4 %collective-permute-start.9 = (bf16[256,2048]{1,0:T(8,128)(2,1)S(1)}, bf16[256,2048]{1,0:T(8,128)(2,1)S(1)}, u32[]{:S(2)}, u32[]{:S(2)}) collective-permute-start(bf16[256,2048]{1,0:T(8,128)(2,1)S(1)} %add_convert_fusion.1), channel_id=1, source_target_pairs={{0,2},{2,0},{1,3},{3,1},{4,6},{6,4},{5,7},{7,5},{8,10},{10,8},{9,1... | collective-permute-start | bytes 3145736 | tf_op jit(solution)/shard_map/ppermute | solution.py:187

commit v13 on v12

--- a/solution.py
+++ b/solution.py
@@ -25,7 +25,7 @@
     return pl.BlockSpec((tokens, HD), lambda h: (0, h))
 
 
-def state_kernel(k_ref, v_ref, state_ref):
+def state_kernel(k_ref, v_ref, state_ref, sent_ref):
     @pl.when(pl.program_id(0) == 0)
     def _():
         state_ref[...] = jnp.zeros_like(state_ref)
@@ -39,6 +39,10 @@
             preferred_element_type=jnp.float32,
         )
 
+    @pl.when(pl.program_id(0) == pl.num_programs(0) - 1)
+    def _():
+        sent_ref[...] = state_ref[...].astype(sent_ref.dtype)
+
 
 def row_block(columns):
     return pl.BlockSpec((ROW_TILE, columns), lambda i: (i, 0))
@@ -51,8 +55,11 @@
         state_kernel,
         grid=(tokens // ROW_TILE,),
         in_specs=[row_block(columns), row_block(columns)],
-        out_specs=pl.BlockSpec((heads, HD, HD), lambda i: (0, 0, 0)),
-        out_shape=jax.ShapeDtypeStruct((heads, HD, HD), jnp.float32),
+        out_specs=[pl.BlockSpec((heads, HD, HD), lambda i: (0, 0, 0))] * 2,
+        out_shape=[
+            jax.ShapeDtypeStruct((heads, HD, HD), jnp.float32),
+            jax.ShapeDtypeStruct((heads, HD, HD), jnp.bfloat16),
+        ],
         cost_estimate=pl.CostEstimate(
             flops=2 * tokens * HD * HD * heads,
             transcendentals=tokens * columns,
@@ -126,18 +133,19 @@
     )(queries, gates, gain.reshape(1, columns))
 
 
-def mix_kernel(local_a_ref, local_b_ref, q_ref, scale_ref, hi_ref, lo_ref, out_ref):
+def mix_kernel(local_a_ref, local_b_ref, q_ref, scale_ref, prefix_ref, out_ref):
     query_act = q_ref[...]
     first = local_a_ref.shape[1] // HD
-    for h in range(hi_ref.shape[0]):
+    for h in range(prefix_ref.shape[0]):
         heads = slice(h * HD, (h + 1) * HD)
+        prefix_hi, prefix_lo = split_bf16(prefix_ref[h])
         if h < first:
             local = local_a_ref[:, heads]
         else:
             local = local_b_ref[:, (h - first) * HD:(h - first + 1) * HD]
         local = local.astype(jnp.float32)
-        remote = jnp.dot(query_act[:, heads], hi_ref[h], preferred_element_type=jnp.float32) + jnp.dot(
-            query_act[:, heads], lo_ref[h], preferred_element_type=jnp.float32
+        remote = jnp.dot(query_act[:, heads], prefix_hi, preferred_element_type=jnp.float32) + jnp.dot(
+            query_act[:, heads], prefix_lo, preferred_element_type=jnp.float32
         )
         attention = local + remote
         mean_sq = jnp.mean(attention * attention, axis=-1, keepdims=True)
@@ -147,7 +155,7 @@
         )
 
 
-def mix(local_a, local_b, query_act, scale, prefix_hi, prefix_lo):
+def mix(local_a, local_b, query_act, scale, prefix):
     tokens, columns = query_act.shape
     heads = columns // HD
     whole_state = pl.BlockSpec((heads, HD, HD), lambda i: (0, 0, 0))
@@ -160,7 +168,6 @@
             row_block(columns),
             row_block(columns),
             whole_state,
-            whole_state,
         ],
         out_specs=row_block(columns),
         out_shape=jax.ShapeDtypeStruct((tokens, columns), jnp.bfloat16),
@@ -169,7 +176,7 @@
             transcendentals=tokens * heads,
             bytes_accessed=12 * tokens * columns,
         ),
-    )(local_a, local_b, query_act, scale, prefix_hi, prefix_lo)
+    )(local_a, local_b, query_act, scale, prefix)
 
 
 def split_bf16(x):
@@ -187,13 +194,13 @@
     return lax.ppermute(block, axis, [(0, 1), (1, 0)])
 
 
-def exclusive_prefix(state, axis, fillers=()):
+def exclusive_prefix(state, axis, fillers=(), sent_first=None):
     inclusive = state
     exclusive = jnp.zeros_like(state)
     distance = 1
     results = []
     while distance < lax.axis_size(axis):
-        sent = inclusive.astype(jnp.bfloat16)
+        sent = inclusive.astype(jnp.bfloat16) if distance > 1 or sent_first is None else sent_first
         arrived = shift(sent, axis, distance)
         if len(results) < len(fillers):
             function, operands = fillers[len(results)]
@@ -258,7 +265,7 @@
 
 
 def on_device(queries, keys, values, gates, gain, out_weight):
-    own_state = key_value_states(keys, values)
+    own_state, own_sent = key_value_states(keys, values)
     head_count = queries.shape[1] // HD
     first = (head_count + 1) // 2
     fillers = (
@@ -266,9 +273,8 @@
         (lambda q, k, v: local_attention(q, k, v, first, head_count - first), (queries, keys, values)),
         (query_and_gate, (queries, gates, gain)),
     )
-    prefix, (local_a, local_b, (query_act, scale)) = exclusive_prefix(own_state, "ctx", fillers)
-    prefix_hi, prefix_lo = split_bf16(prefix)
-    mixed_rows = mix(local_a, local_b, query_act, scale, prefix_hi, prefix_lo)
+    prefix, (local_a, local_b, (query_act, scale)) = exclusive_prefix(own_state, "ctx", fillers, own_sent)
+    mixed_rows = mix(local_a, local_b, query_act, scale, prefix)
     return project_and_reduce(mixed_rows, out_weight)
 
 

time: 153 us -> 152 us (level)
    convert_element_type x4 -> x2, other arithmetic: 2.45 us -> 0.22 us  [exclusive_prefix(): inclusive.astype(jnp.bfloat16)]
where the time goes in v13:
time: 152 us; the launch traced here: 151 us
  waiting for transfers between devices  70.8 us (47%)
  Pallas kernels  33.9 us (22%)
  matrix products  29.2 us (19%)
  starting transfers between devices  10.8 us (7%)
  other arithmetic  5.17 us (3%)
    ppermute x7, waiting for transfers between devices, swap(): return lax.ppermute(block, axis, [(0, 1), (1, 0)])  58.5 us
    pallas_call x2, Pallas kernels, local_attention(): pl.pallas_call(local_kernel, grid=(heads,), in_specs=[picked] * 3, out_sp...  15.2 us
    dot_general x3, matrix products, project_and_reduce(): jnp.dot(far_rows, out_weight[:, c * chunk:(c + 1) * chunk], preferred_ele...  14.9 us
    dot_general x2, matrix products, product(): jnp.dot(rows, out_weight, preferred_element_type=jnp.float32)  14.4 us
    ppermute x3, waiting for transfers between devices, shift(): lax.ppermute(block, axis, [(i, i + distance) for i in range(size) if i +...  12.2 us
    pallas_call x1, Pallas kernels, mix(): pl.pallas_call(mix_kernel, grid=(tokens // ROW_TILE,), in_specs=[row_bloc...  6.76 us
    ppermute x3, starting transfers between devices, shift(): lax.ppermute(block, axis, [(i, i + distance) for i in range(size) if i +...  6.28 us
    pallas_call x1, Pallas kernels, query_and_gate(): pl.pallas_call(gate_kernel, grid=(tokens // ROW_TILE,), in_specs=[row_blo...  6.22 us
  transfers between devices with their start and end apart: 10, of which 7 were waited for; matrix products, arithmetic and copies ran while one was open for 10% of the time, Pallas kernels for 14%

profile of v13, /device:TPU:24, one launch (start us, length us, event | category | flops | bytes accessed | tf_op | source)
XLA Modules:
  0.0 151.0 jit_solution(9454900468737195445)
XLA Ops:
  0.0 5.6 %shard_map.64 = (f32[10,128,128]{2,1,0:T(8,128)}, bf16[10,128,128]{2,1,0:T(8,128)(2,1)}) custom-call(bf16[1024,1280]{1,0:T(8,128)(2,1)} %k_ref.3, bf16[1024,1280]{1,0:T(8,128)(2,1)} %v_ref.3), custom_call_target="tpu_custom_call" | custom-call | flops 335544320 | bytes 5898240 | tf_op jit(solution)/shard_map/pallas_call | solution.py:54
  5.6 3.5 %collective-permute-start = (bf16[10,128,128]{2,1,0:T(8,128)(2,1)}, bf16[10,128,128]{2,1,0:T(8,128)(2,1)S(1)}, u32[]{:S(2)}, u32[]{:S(2)}) collective-permute-start(bf16[10,128,128]{2,1,0:T(8,128)(2,1)} %get-tuple-element.29), channel_id=1, source_target_pairs={{0,4},{4,8},{8,12},{12,16},{16,20},{20,24},{24,28},{1,5},{5,9},{9,... | collective-permute-start | bytes 983048 | tf_op jit(solution)/shard_map/ppermute | solution.py:190
  9.2 7.6 %shard_map.65.local_a_ref = bf16[1024,640]{1,0:T(8,128)(2,1)} custom-call(bf16[1024,1280]{1,0:T(8,128)(2,1)} %q_ref.2, bf16[1024,1280]{1,0:T(8,128)(2,1)} %k_ref.3, bf16[1024,1280]{1,0:T(8,128)(2,1)} %v_ref.3), custom_call_target="tpu_custom_call" | custom-call | flops 1677721600 | bytes 6553600 | tf_op jit(solution)/shard_map/pallas_call | solution.py:97
  16.8 1.4 collective-permute-done
  18.3 1.3 collective-permute-start.1
  19.6 7.6 %shard_map.66.local_b_ref = bf16[1024,640]{1,0:T(8,128)(2,1)} custom-call(bf16[1024,1280]{1,0:T(8,128)(2,1)} %q_ref.2, bf16[1024,1280]{1,0:T(8,128)(2,1)} %k_ref.3, bf16[1024,1280]{1,0:T(8,128)(2,1)} %v_ref.3), custom_call_target="tpu_custom_call" | custom-call | flops 1677721600 | bytes 6553600 | tf_op jit(solution)/shard_map/pallas_call | solution.py:97
  27.3 1.6 %collective-permute-done.1 = bf16[10,128,128]{2,1,0:T(8,128)(2,1)S(1)} collective-permute-done((bf16[10,128,128]{2,1,0:T(8,128)(2,1)S(1)}, bf16[10,128,128]{2,1,0:T(8,128)(2,1)S(1)}, u32[]{:S(2)}, u32[]{:S(2)}) %collective-permute-start.1) | collective-permute-done | bytes 327712 | tf_op jit(solution)/shard_map/ppermute | solution.py:190
  29.0 1.5 collective-permute-start.2
  31.1 6.2 %shard_map.67 = (bf16[1024,1280]{1,0:T(8,128)(2,1)}, bf16[1024,1280]{1,0:T(8,128)(2,1)}) custom-call(bf16[1024,1280]{1,0:T(8,128)(2,1)} %q_ref.2, bf16[1024,1280]{1,0:T(8,128)(2,1)} %g_ref, f32[1,1280]{1,0:T(1,128)} %reshape.3.gain_ref), custom_call_target="tpu_custom_call" | custom-call | flops 10485760 | bytes 13107200 | tf_op jit(solution)/shard_map/pallas_call | solution.py:119
  37.3 9.2 %collective-permute-done.2 = bf16[10,128,128]{2,1,0:T(8,128)(2,1)S(1)} collective-permute-done((bf16[10,128,128]{2,1,0:T(8,128)(2,1)S(1)}, bf16[10,128,128]{2,1,0:T(8,128)(2,1)S(1)}, u32[]{:S(2)}, u32[]{:S(2)}) %collective-permute-start.2) | collective-permute-done | bytes 327712 | tf_op jit(solution)/shard_map/ppermute | solution.py:190
  46.5 1.0 fusion.19.prefix_ref
  47.5 6.8 %shard_map.68 = bf16[1024,1280]{1,0:T(8,128)(2,1)} custom-call(bf16[1024,640]{1,0:T(8,128)(2,1)} %shard_map.65.local_a_ref, bf16[1024,640]{1,0:T(8,128)(2,1)} %shard_map.66.local_b_ref, bf16[1024,1280]{1,0:T(8,128)(2,1)} %get-tuple-element.46.q_ref, bf16[1024,1280]{1,0:T(8,128)(2,1)} %get-tuple-element.47.scale_ref, f32[10,128,128]{2,1,0:T(8,128)} %fusion.19.prefix_ref), custom_call_target="tpu_custom_call" | custom-call | flops 671088640 | bytes 15728640 | tf_op jit(solution)/shard_map/pallas_call | solution.py:162
  54.3 5.9 %fusion.12 = bf16[512,2048]{1,0:T(8,128)(2,1)S(1)} fusion(bf16[1280,6144]{1,0:T(8,128)(2,1)} %param.11, bf16[1024,1280]{1,0:T(8,128)(2,1)} %shard_map.68, s32[]{:T(128)S(6)} %select_n.8), kind=kOutput, calls=%fused_computation.11 | convolution fusion | flops 2685403136 | bytes 8650756 | tf_op jit(solution)/shard_map/dot_general | solution.py:252
  60.3 5.8 %fusion.9 = bf16[512,2048]{1,0:T(8,128)(2,1)S(1)} fusion(bf16[1280,6144]{1,0:T(8,128)(2,1)} %param.11, bf16[1024,1280]{1,0:T(8,128)(2,1)S(1)} %copy-done, s32[]{:T(128)S(6)} %select_n.8), kind=kOutput, calls=%fused_computation.10 | convolution fusion | flops 2685403136 | bytes 8650756 | tf_op jit(solution)/shard_map/dot_general | solution.py:252
  67.0 3.1 %fusion.6 = bf16[512,2048]{1,0:T(8,128)(2,1)S(1)} fusion(bf16[1280,6144]{1,0:T(8,128)(2,1)S(1)} %bitcast.3, bf16[1024,1280]{1,0:T(8,128)(2,1)S(1)} %copy-done, s32[]{:T(128)S(6)} %select_n.8), kind=kOutput, calls=%fused_computation.9 | convolution fusion | flops 2685403136 | bytes 8650756 | tf_op jit(solution)/shard_map/dot_general | solution.py:252
  71.4 1.6 %collective-permute-done.3 = bf16[256,2048]{1,0:T(8,128)(2,1)S(1)} collective-permute-done((bf16[256,2048]{1,0:T(8,128)(2,1)S(1)}, bf16[256,2048]{1,0:T(8,128)(2,1)S(1)}, u32[]{:S(2)}, u32[]{:S(2)}) %collective-permute-start.3) | collective-permute-done | bytes 1048608 | tf_op jit(solution)/shard_map/ppermute | solution.py:194
  73.4 4.4 %convolution_convert_fusion = bf16[256,6144]{1,0:T(8,128)(2,1)S(1)} fusion(bf16[1280,6144]{1,0:T(8,128)(2,1)S(1)} %bitcast.3, bf16[512,1280]{1,0:T(8,128)(2,1)S(1)} %constant_dynamic-slice_fusion, s32[]{:T(128)S(6)} %select_n.20), kind=kOutput, calls=%fused_computation | convolution fusion | flops 4028104704 | bytes 19529732 | tf_op jit(solution)/shard_map/dot_general | solution.py:228
  78.1 1.5 %collective-permute-start.7 = (bf16[256,2048]{1,0:T(8,128)(2,1)S(1)}, bf16[256,2048]{1,0:T(8,128)(2,1)S(1)}, u32[]{:S(2)}, u32[]{:S(2)}) collective-permute-start(bf16[256,2048]{1,0:T(8,128)(2,1)S(1)} %add_convert_fusion.3), channel_id=1, source_target_pairs={{0,2},{2,0},{1,3},{3,1},{4,6},{6,4},{5,7},{7,5},{8,10},{10,8},{9,1... | collective-permute-start | bytes 3145736 | tf_op jit(solution)/shard_map/ppermute | solution.py:194
  80.1 1.5 %collective-permute-start.9 = (bf16[256,2048]{1,0:T(8,128)(2,1)S(1)}, bf16[256,2048]{1,0:T(8,128)(2,1)S(1)}, u32[]{:S(2)}, u32[]{:S(2)}) collective-permute-start(bf16[256,2048]{1,0:T(8,128)(2,1)S(1)} %add_convert_fusion.1), channel_id=1, source_target_pairs={{0,2},{2,0},{1,3},{3,1},{4,6},{6,4},{5,7},{7,5},{8,10},{10,8},{9,1... | collective-permute-start | bytes 3145736 | tf_op jit(solution)/shard_map/ppermute | solution.py:194
  81.6 9.9 %convolution_convert_fusion.1 = bf16[256,6144]{1,0:T(8,128)(2,1)S(1)} fusion(bf16[1280,6144]{1,0:T(8,128)(2,1)} %param.11, bf16[512,1280]{1,0:T(8,128)(2,1)S(1)} %constant_dynamic-slice_fusion, s32[]{:T(128)S(6)} %select_n.9), kind=kOutput, calls=%fused_computation.1 | convolution fusion | flops 4028104704 | bytes 19529732 | tf_op jit(solution)/shard_map/dot_general | solution.py:228
  91.6 12.6 %collective-permute-done.7 = bf16[256,2048]{1,0:T(8,128)(2,1)S(1)} collective-permute-done((bf16[256,2048]{1,0:T(8,128)(2,1)S(1)}, bf16[256,2048]{1,0:T(8,128)(2,1)S(1)}, u32[]{:S(2)}, u32[]{:S(2)}) %collective-permute-start.7) | collective-permute-done | bytes 1048608 | tf_op jit(solution)/shard_map/ppermute | solution.py:194
  104.1 22.5 %collective-permute-done.8 = bf16[256,2048]{1,0:T(8,128)(2,1)S(1)} collective-permute-done((bf16[256,2048]{1,0:T(8,128)(2,1)S(1)}, bf16[256,2048]{1,0:T(8,128)(2,1)S(1)}, u32[]{:S(2)}, u32[]{:S(2)}) %collective-permute-start.8) | collective-permute-done | bytes 1048608 | tf_op jit(solution)/shard_map/ppermute | solution.py:194
  126.6 21.9 %collective-permute-done.9 = bf16[256,2048]{1,0:T(8,128)(2,1)S(1)} collective-permute-done((bf16[256,2048]{1,0:T(8,128)(2,1)S(1)}, bf16[256,2048]{1,0:T(8,128)(2,1)S(1)}, u32[]{:S(2)}, u32[]{:S(2)}) %collective-permute-start.9) | collective-permute-done | bytes 1048608 | tf_op jit(solution)/shard_map/ppermute | solution.py:194
  148.5 2.6 %add_convert_fusion = bf16[256,6144]{1,0:T(8,128)(2,1)} fusion(bf16[256,6144]{1,0:T(8,128)(2,1)S(1)} %collective-permute-done.6, bf16[256,6144]{1,0:T(8,128)(2,1)S(1)} %convolution_convert_fusion.1, bf16[256,2048]{1,0:T(8,128)(2,1)S(1)} %collective-permute-done.9, bf16[256,2048]{1,0:T(8,128)(2,1)S(1)} %collective-permute-done.8, ...), kind=kLoop, calls=%fused_computation.2 | loop fusion | flops 17301504 | bytes 12582912 | tf_op jit(solution)/shard_map/convert_element_type | solution.py:264
  (33 shorter events, 4.1 us)
Async XLA Ops:
  5.6 12.6 %copy-start.1 = (f32[10,128,128]{2,1,0:T(8,128)S(1)}, f32[10,128,128]{2,1,0:T(8,128)}, u32[]{:S(2)}) copy-start(f32[10,128,128]{2,1,0:T(8,128)} %get-tuple-element.34) | copy-start | bytes 1966084
  5.6 12.6 %collective-permute-start = (bf16[10,128,128]{2,1,0:T(8,128)(2,1)}, bf16[10,128,128]{2,1,0:T(8,128)(2,1)S(1)}, u32[]{:S(2)}, u32[]{:S(2)}) collective-permute-start(bf16[10,128,128]{2,1,0:T(8,128)(2,1)} %get-tuple-element.29), channel_id=1, source_target_pairs={{0,4},{4,8},{8,12},{12,16},{16,20},{20,24},{24,28},{1,5},{5,9},{9,... | collective-permute-start | bytes 983048 | tf_op jit(solution)/shard_map/ppermute | solution.py:190
  18.3 12.1 %copy-start.2 = (f32[1280]{0:T(1024)S(1)}, f32[1280]{0:T(1024)}, u32[]{:S(2)}) copy-start(f32[1280]{0:T(1024)} %param.10) | copy-start | bytes 15364
  18.3 10.5 %collective-permute-start.1 = (bf16[10,128,128]{2,1,0:T(8,128)(2,1)S(1)}, bf16[10,128,128]{2,1,0:T(8,128)(2,1)S(1)}, u32[]{:S(2)}, u32[]{:S(2)}) collective-permute-start(bf16[10,128,128]{2,1,0:T(8,128)(2,1)S(1)} %fusion.22), channel_id=1, source_target_pairs={{0,8},{4,12},{8,16},{12,20},{16,24},{20,28},{1,9},{5,13},{9,17},{1... | collective-permute-start | bytes 983048 | tf_op jit(solution)/shard_map/ppermute | solution.py:190
  29.0 17.6 %collective-permute-start.2 = (bf16[10,128,128]{2,1,0:T(8,128)(2,1)S(1)}, bf16[10,128,128]{2,1,0:T(8,128)(2,1)S(1)}, u32[]{:S(2)}, u32[]{:S(2)}) collective-permute-start(bf16[10,128,128]{2,1,0:T(8,128)(2,1)S(1)} %fusion.18), channel_id=1, source_target_pairs={{0,16},{4,20},{8,24},{12,28},{1,17},{5,21},{9,25},{13,29},{2,18},{... | collective-permute-start | bytes 983048 | tf_op jit(solution)/shard_map/ppermute | solution.py:190
  54.3 5.9 %copy-start = (bf16[1024,1280]{1,0:T(8,128)(2,1)S(1)}, bf16[1024,1280]{1,0:T(8,128)(2,1)}, u32[]{:S(2)}) copy-start(bf16[1024,1280]{1,0:T(8,128)(2,1)} %shard_map.68) | copy-start | bytes 7864324
  54.3 12.7 %slice-start = ((s8[15728640]{0:T(1024)(128)(4,1)}), s8[4194304]{0:T(1024)(128)(4,1)S(1)}, s32[]{:S(2)}) async-start(s8[15728640]{0:T(1024)(128)(4,1)} %bitcast.2), calls=%async_computation | async-start | bytes 8388608
  54.3 12.7 %slice-start.1 = ((s8[15728640]{0:T(1024)(128)(4,1)}), s8[4194304]{0:T(1024)(128)(4,1)S(1)}, s32[]{:S(2)}) async-start(s8[15728640]{0:T(1024)(128)(4,1)} %bitcast.2), calls=%async_computation.1 | async-start | bytes 8388608
  60.2 6.7 %slice-start.2 = ((s8[15728640]{0:T(1024)(128)(4,1)}), s8[4194304]{0:T(1024)(128)(4,1)S(1)}, s32[]{:S(2)}) async-start(s8[15728640]{0:T(1024)(128)(4,1)} %bitcast.2), calls=%async_computation.2 | async-start | bytes 8388608
  60.3 6.7 %slice-start.3 = ((s8[15728640]{0:T(1024)(128)(4,1)}), s8[3145728]{0:T(1024)(128)(4,1)S(1)}, s32[]{:S(2)}) async-start(s8[15728640]{0:T(1024)(128)(4,1)} %bitcast.2), calls=%async_computation.3 | async-start | bytes 6291456
  66.2 4.2 %collective-permute-start.5 = (bf16[256,2048]{1,0:T(8,128)(2,1)S(1)}, bf16[256,2048]{1,0:T(8,128)(2,1)S(1)}, u32[]{:S(2)}, u32[]{:S(2)}) collective-permute-start(bf16[256,2048]{1,0:T(8,128)(2,1)S(1)} %constant_dynamic-slice_fusion.1), channel_id=1, source_target_pairs={{0,1},{1,0},{2,3},{3,2},{4,5},{5,4},{6,7},{7,6},{8,9},{9,8},{10,11... | collective-permute-start | bytes 3145736 | tf_op jit(solution)/shard_map/ppermute | solution.py:194
  66.4 4.5 %collective-permute-start.4 = (bf16[256,2048]{1,0:T(8,128)(2,1)S(1)}, bf16[256,2048]{1,0:T(8,128)(2,1)S(1)}, u32[]{:S(2)}, u32[]{:S(2)}) collective-permute-start(bf16[256,2048]{1,0:T(8,128)(2,1)S(1)} %constant_dynamic-slice_fusion.2), channel_id=1, source_target_pairs={{0,1},{1,0},{2,3},{3,2},{4,5},{5,4},{6,7},{7,6},{8,9},{9,8},{10,11... | collective-permute-start | bytes 3145736 | tf_op jit(solution)/shard_map/ppermute | solution.py:194
  70.2 2.7 %collective-permute-start.3 = (bf16[256,2048]{1,0:T(8,128)(2,1)S(1)}, bf16[256,2048]{1,0:T(8,128)(2,1)S(1)}, u32[]{:S(2)}, u32[]{:S(2)}) collective-permute-start(bf16[256,2048]{1,0:T(8,128)(2,1)S(1)} %constant_dynamic-slice_fusion.3), channel_id=1, source_target_pairs={{0,1},{1,0},{2,3},{3,2},{4,5},{5,4},{6,7},{7,6},{8,9},{9,8},{10,11... | collective-permute-start | bytes 3145736 | tf_op jit(solution)/shard_map/ppermute | solution.py:194
  77.9 70.6 %collective-permute-start.6 = (bf16[256,6144]{1,0:T(8,128)(2,1)S(1)}, bf16[256,6144]{1,0:T(8,128)(2,1)S(1)}, u32[]{:S(2)}, u32[]{:S(2)}) collective-permute-start(bf16[256,6144]{1,0:T(8,128)(2,1)S(1)} %convolution_convert_fusion), channel_id=1, source_target_pairs={{0,1},{1,0},{2,3},{3,2},{4,5},{5,4},{6,7},{7,6},{8,9},{9,8},{10,11... | collective-permute-start | bytes 9437192 | tf_op jit(solution)/shard_map/ppermute | solution.py:194
  78.1 26.0 %collective-permute-start.7 = (bf16[256,2048]{1,0:T(8,128)(2,1)S(1)}, bf16[256,2048]{1,0:T(8,128)(2,1)S(1)}, u32[]{:S(2)}, u32[]{:S(2)}) collective-permute-start(bf16[256,2048]{1,0:T(8,128)(2,1)S(1)} %add_convert_fusion.3), channel_id=1, source_target_pairs={{0,2},{2,0},{1,3},{3,1},{4,6},{6,4},{5,7},{7,5},{8,10},{10,8},{9,1... | collective-permute-start | bytes 3145736 | tf_op jit(solution)/shard_map/ppermute | solution.py:194
  79.6 47.0 %collective-permute-start.8 = (bf16[256,2048]{1,0:T(8,128)(2,1)S(1)}, bf16[256,2048]{1,0:T(8,128)(2,1)S(1)}, u32[]{:S(2)}, u32[]{:S(2)}) collective-permute-start(bf16[256,2048]{1,0:T(8,128)(2,1)S(1)} %add_convert_fusion.2), channel_id=1, source_target_pairs={{0,2},{2,0},{1,3},{3,1},{4,6},{6,4},{5,7},{7,5},{8,10},{10,8},{9,1... | collective-permute-start | bytes 3145736 | tf_op jit(solution)/shard_map/ppermute | solution.py:194
  80.1 68.4 %collective-permute-start.9 = (bf16[256,2048]{1,0:T(8,128)(2,1)S(1)}, bf16[256,2048]{1,0:T(8,128)(2,1)S(1)}, u32[]{:S(2)}, u32[]{:S(2)}) collective-permute-start(bf16[256,2048]{1,0:T(8,128)(2,1)S(1)} %add_convert_fusion.1), channel_id=1, source_target_pairs={{0,2},{2,0},{1,3},{3,1},{4,6},{6,4},{5,7},{7,5},{8,10},{10,8},{9,1... | collective-permute-start | bytes 3145736 | tf_op jit(solution)/shard_map/ppermute | solution.py:194

commit v14 on v13

--- a/solution.py
+++ b/solution.py
@@ -8,7 +8,7 @@
 from jax.sharding import PartitionSpec as P
 
 HD = 128
-COLUMN_CHUNKS = 3
+COLUMN_CHUNKS = 2
 QUERY_TILE = 256
 ROW_TILE = 256
 

time: 152 us -> 166 us (1.092)
  matrix products: 29.2 us -> 35.4 us
  local copies, waits for them, and re-layouts: 1.04 us -> 7.11 us
  other arithmetic: 5.17 us -> 8.4 us
  starting transfers between devices: 10.8 us -> 8.51 us
    dot_general x2, matrix products: 14.4 us -> 19.9 us  [product(): jnp.dot(rows, out_weight, preferred_element_type=jnp.float32)]
    unnamed x14 -> x12, local copies, waits for them, and re-layouts: 0.03 us -> 3.83 us
    convert_element_type x3 -> x2, other arithmetic: 1.35 us -> 4.6 us  [project_and_reduce(): chip_sums.append(chip_sum.astype(jnp.bfloat16))]
    dynamic_slice x3 -> x2, local copies, waits for them, and re-layouts: 0.32 us -> 2.6 us  [block_of(): return lax.dynamic_slice_in_dim(part, owner_tc * block, block, axis=0)]
    ppermute x7 -> x5, starting transfers between devices: 4.47 us -> 2.23 us  [swap(): return lax.ppermute(block, axis, [(0, 1), (1, 0)])]
    ppermute x7 -> x5, waiting for transfers between devices: 58.5 us -> 59.5 us  [swap(): return lax.ppermute(block, axis, [(0, 1), (1, 0)])]
    dot_general x3 -> x2, matrix products: 14.9 us -> 15.5 us  [project_and_reduce(): jnp.dot(far_rows, out_weight[:, c * chunk:(c + 1) * chunk], preferred_ele...]
  transfers between devices with their start and end apart: 10 -> 8, of which waited for: 7 -> 6; matrix products, arithmetic and copies ran while one was open for 10% -> 13% of each run, Pallas kernels for 14% -> 13%
where the time goes in v14:
time: 166 us; the launch traced here: 165 us
  waiting for transfers between devices  71.7 us (43%)
  matrix products  35.4 us (21%)
  Pallas kernels  33.9 us (20%)
  starting transfers between devices  8.51 us (5%)
  other arithmetic  8.4 us (5%)
  local copies, waits for them, and re-layouts  7.11 us (4%)
    ppermute x5, waiting for transfers between devices, swap(): return lax.ppermute(block, axis, [(0, 1), (1, 0)])  59.5 us
    dot_general x2, matrix products, product(): jnp.dot(rows, out_weight, preferred_element_type=jnp.float32)  19.9 us
    dot_general x2, matrix products, project_and_reduce(): jnp.dot(far_rows, out_weight[:, c * chunk:(c + 1) * chunk], preferred_ele...  15.5 us
    pallas_call x2, Pallas kernels, local_attention(): pl.pallas_call(local_kernel, grid=(heads,), in_specs=[picked] * 3, out_sp...  15.2 us
    ppermute x3, waiting for transfers between devices, shift(): lax.ppermute(block, axis, [(i, i + distance) for i in range(size) if i +...  12.2 us
    pallas_call x1, Pallas kernels, mix(): pl.pallas_call(mix_kernel, grid=(tokens // ROW_TILE,), in_specs=[row_bloc...  6.76 us
    ppermute x3, starting transfers between devices, shift(): lax.ppermute(block, axis, [(i, i + distance) for i in range(size) if i +...  6.28 us
    pallas_call x1, Pallas kernels, query_and_gate(): pl.pallas_call(gate_kernel, grid=(tokens // ROW_TILE,), in_specs=[row_blo...  6.24 us
  transfers between devices with their start and end apart: 8, of which 6 were waited for; matrix products, arithmetic and copies ran while one was open for 13% of the time, Pallas kernels for 13%

profile of v14, /device:TPU:24, one launch (start us, length us, event | category | flops | bytes accessed | tf_op | source)
XLA Modules:
  0.0 165.1 jit_solution(14850258833476937050)
XLA Ops:
  0.0 5.6 %shard_map.64 = (f32[10,128,128]{2,1,0:T(8,128)}, bf16[10,128,128]{2,1,0:T(8,128)(2,1)}) custom-call(bf16[1024,1280]{1,0:T(8,128)(2,1)} %k_ref.3, bf16[1024,1280]{1,0:T(8,128)(2,1)} %v_ref.3), custom_call_target="tpu_custom_call" | custom-call | flops 335544320 | bytes 5898240 | tf_op jit(solution)/shard_map/pallas_call | solution.py:54
  5.6 3.5 %collective-permute-start = (bf16[10,128,128]{2,1,0:T(8,128)(2,1)}, bf16[10,128,128]{2,1,0:T(8,128)(2,1)S(1)}, u32[]{:S(2)}, u32[]{:S(2)}) collective-permute-start(bf16[10,128,128]{2,1,0:T(8,128)(2,1)} %get-tuple-element.28), channel_id=1, source_target_pairs={{0,4},{4,8},{8,12},{12,16},{16,20},{20,24},{24,28},{1,5},{5,9},{9,... | collective-permute-start | bytes 983048 | tf_op jit(solution)/shard_map/ppermute | solution.py:190
  9.2 7.6 %shard_map.65.local_a_ref = bf16[1024,640]{1,0:T(8,128)(2,1)} custom-call(bf16[1024,1280]{1,0:T(8,128)(2,1)} %q_ref.2, bf16[1024,1280]{1,0:T(8,128)(2,1)} %k_ref.3, bf16[1024,1280]{1,0:T(8,128)(2,1)} %v_ref.3), custom_call_target="tpu_custom_call" | custom-call | flops 1677721600 | bytes 6553600 | tf_op jit(solution)/shard_map/pallas_call | solution.py:97
  16.8 1.4 collective-permute-done
  18.3 1.3 collective-permute-start.1
  19.6 7.6 %shard_map.66.local_b_ref = bf16[1024,640]{1,0:T(8,128)(2,1)} custom-call(bf16[1024,1280]{1,0:T(8,128)(2,1)} %q_ref.2, bf16[1024,1280]{1,0:T(8,128)(2,1)} %k_ref.3, bf16[1024,1280]{1,0:T(8,128)(2,1)} %v_ref.3), custom_call_target="tpu_custom_call" | custom-call | flops 1677721600 | bytes 6553600 | tf_op jit(solution)/shard_map/pallas_call | solution.py:97
  27.2 1.6 collective-permute-done.1
  29.0 1.5 collective-permute-start.2
  31.1 6.2 %shard_map.67 = (bf16[1024,1280]{1,0:T(8,128)(2,1)}, bf16[1024,1280]{1,0:T(8,128)(2,1)}) custom-call(bf16[1024,1280]{1,0:T(8,128)(2,1)} %q_ref.2, bf16[1024,1280]{1,0:T(8,128)(2,1)} %g_ref, f32[1,1280]{1,0:T(1,128)} %reshape.3.gain_ref), custom_call_target="tpu_custom_call" | custom-call | flops 10485760 | bytes 13107200 | tf_op jit(solution)/shard_map/pallas_call | solution.py:119
  37.3 9.2 %collective-permute-done.2 = bf16[10,128,128]{2,1,0:T(8,128)(2,1)S(1)} collective-permute-done((bf16[10,128,128]{2,1,0:T(8,128)(2,1)S(1)}, bf16[10,128,128]{2,1,0:T(8,128)(2,1)S(1)}, u32[]{:S(2)}, u32[]{:S(2)}) %collective-permute-start.2) | collective-permute-done | bytes 327712 | tf_op jit(solution)/shard_map/ppermute | solution.py:190
  47.5 6.8 %shard_map.68 = bf16[1024,1280]{1,0:T(8,128)(2,1)} custom-call(bf16[1024,640]{1,0:T(8,128)(2,1)} %shard_map.65.local_a_ref, bf16[1024,640]{1,0:T(8,128)(2,1)} %shard_map.66.local_b_ref, bf16[1024,1280]{1,0:T(8,128)(2,1)} %get-tuple-element.45.q_ref, bf16[1024,1280]{1,0:T(8,128)(2,1)} %get-tuple-element.46.scale_ref, f32[10,128,128]{2,1,0:T(8,128)} %fusion.13.prefix_ref), custom_call_target="tpu_custom_call" | custom-call | flops 671088640 | bytes 15728640 | tf_op jit(solution)/shard_map/pallas_call | solution.py:162
  54.3 7.9 %fusion.7 = bf16[512,3072]{1,0:T(8,128)(2,1)S(1)} fusion(bf16[1280,6144]{1,0:T(8,128)(2,1)} %param.11, bf16[1024,1280]{1,0:T(8,128)(2,1)} %shard_map.68, s32[]{:T(128)S(6)} %select_n.16), kind=kOutput, calls=%fused_computation.8 | convolution fusion | flops 4028104704 | bytes 12320772 | tf_op jit(solution)/shard_map/dot_general | solution.py:252
  62.2 1.3 constant_dynamic-slice_fusion.1
  65.6 7.7 %fusion.4 = bf16[512,3072]{1,0:T(8,128)(2,1)S(1)} fusion(bf16[1280,6144]{1,0:T(8,128)(2,1)} %param.11, bf16[1024,1280]{1,0:T(8,128)(2,1)S(1)} %copy-done, s32[]{:T(128)S(6)} %select_n.16), kind=kOutput, calls=%fused_computation.7 | convolution fusion | flops 4028104704 | bytes 12320772 | tf_op jit(solution)/shard_map/dot_general | solution.py:252
  73.3 1.6 copy-done.1
  74.9 1.3 constant_dynamic-slice_fusion.2
  76.4 2.6 %add_convert_fusion.1 = bf16[256,3072]{1,0:T(8,128)(2,1)S(1)} fusion(bf16[256,3072]{1,0:T(8,128)(2,1)} %collective-permute-done.4, bf16[512,3072]{1,0:T(8,128)(2,1)} %copy-done.3, s32[]{:T(128)S(6)} %select_n.17), kind=kLoop, calls=%fused_computation.9 | loop fusion | flops 3145728 | bytes 4718596 | tf_op jit(solution)/shard_map/convert_element_type | solution.py:257
  80.0 2.0 %add_convert_fusion.2 = bf16[256,3072]{1,0:T(8,128)(2,1)S(1)} fusion(bf16[256,3072]{1,0:T(8,128)(2,1)} %collective-permute-done.3, bf16[512,3072]{1,0:T(8,128)(2,1)S(1)} %copy-done.2, s32[]{:T(128)S(6)} %select_n.17), kind=kLoop, calls=%fused_computation.10 | loop fusion | flops 3145728 | bytes 4718596 | tf_op jit(solution)/shard_map/convert_element_type | solution.py:257
  82.0 9.9 %convolution_convert_fusion = bf16[256,6144]{1,0:T(8,128)(2,1)S(1)} fusion(bf16[1280,6144]{1,0:T(8,128)(2,1)} %param.11, bf16[512,1280]{1,0:T(8,128)(2,1)S(1)} %constant_dynamic-slice_fusion, s32[]{:T(128)S(6)} %select_n.18), kind=kOutput, calls=%fused_computation.4 | convolution fusion | flops 4028104704 | bytes 19529732 | tf_op jit(solution)/shard_map/dot_general | solution.py:228
  92.2 1.5 collective-permute-start.6
  94.2 9.9 %convolution_convert_fusion.1 = bf16[256,6144]{1,0:T(8,128)(2,1)S(1)} fusion(bf16[1280,6144]{1,0:T(8,128)(2,1)} %param.11, bf16[512,1280]{1,0:T(8,128)(2,1)S(1)} %constant_dynamic-slice_fusion, s32[]{:T(128)S(6)} %select_n.17), kind=kOutput, calls=%fused_computation.5 | convolution fusion | flops 4028104704 | bytes 19529732 | tf_op jit(solution)/shard_map/dot_general | solution.py:228
  104.1 25.3 %collective-permute-done.6 = bf16[256,3072]{1,0:T(8,128)(2,1)S(1)} collective-permute-done((bf16[256,3072]{1,0:T(8,128)(2,1)S(1)}, bf16[256,3072]{1,0:T(8,128)(2,1)S(1)}, u32[]{:S(2)}, u32[]{:S(2)}) %collective-permute-start.6) | collective-permute-done | bytes 1572896 | tf_op jit(solution)/shard_map/ppermute | solution.py:194
  129.4 33.1 %collective-permute-done.7 = bf16[256,3072]{1,0:T(8,128)(2,1)S(1)} collective-permute-done((bf16[256,3072]{1,0:T(8,128)(2,1)S(1)}, bf16[256,3072]{1,0:T(8,128)(2,1)S(1)}, u32[]{:S(2)}, u32[]{:S(2)}) %collective-permute-start.7) | collective-permute-done | bytes 1572896 | tf_op jit(solution)/shard_map/ppermute | solution.py:194
  162.6 2.6 %add_convert_fusion = bf16[256,6144]{1,0:T(8,128)(2,1)} fusion(bf16[256,6144]{1,0:T(8,128)(2,1)S(1)} %collective-permute-done.5, bf16[256,6144]{1,0:T(8,128)(2,1)S(1)} %convolution_convert_fusion.1, bf16[256,3072]{1,0:T(8,128)(2,1)S(1)} %collective-permute-done.7, bf16[256,3072]{1,0:T(8,128)(2,1)S(1)} %collective-permute-done.6), kind=kLoop, calls=%fused_computation.6 | loop fusion | flops 14155776 | bytes 12582912 | tf_op jit(solution)/shard_map/convert_element_type | solution.py:264
  (23 shorter events, 5.8 us)
Async XLA Ops:
  5.6 12.6 %copy-start.4 = (f32[10,128,128]{2,1,0:T(8,128)S(1)}, f32[10,128,128]{2,1,0:T(8,128)}, u32[]{:S(2)}) copy-start(f32[10,128,128]{2,1,0:T(8,128)} %get-tuple-element.33) | copy-start | bytes 1966084
  5.6 12.6 %collective-permute-start = (bf16[10,128,128]{2,1,0:T(8,128)(2,1)}, bf16[10,128,128]{2,1,0:T(8,128)(2,1)S(1)}, u32[]{:S(2)}, u32[]{:S(2)}) collective-permute-start(bf16[10,128,128]{2,1,0:T(8,128)(2,1)} %get-tuple-element.28), channel_id=1, source_target_pairs={{0,4},{4,8},{8,12},{12,16},{16,20},{20,24},{24,28},{1,5},{5,9},{9,... | collective-permute-start | bytes 983048 | tf_op jit(solution)/shard_map/ppermute | solution.py:190
  18.3 12.1 %copy-start.5 = (f32[1280]{0:T(1024)S(1)}, f32[1280]{0:T(1024)}, u32[]{:S(2)}) copy-start(f32[1280]{0:T(1024)} %param.10) | copy-start | bytes 15364
  18.3 10.5 %collective-permute-start.1 = (bf16[10,128,128]{2,1,0:T(8,128)(2,1)S(1)}, bf16[10,128,128]{2,1,0:T(8,128)(2,1)S(1)}, u32[]{:S(2)}, u32[]{:S(2)}) collective-permute-start(bf16[10,128,128]{2,1,0:T(8,128)(2,1)S(1)} %fusion.16), channel_id=1, source_target_pairs={{0,8},{4,12},{8,16},{12,20},{16,24},{20,28},{1,9},{5,13},{9,17},{1... | collective-permute-start | bytes 983048 | tf_op jit(solution)/shard_map/ppermute | solution.py:190
  29.0 17.6 %collective-permute-start.2 = (bf16[10,128,128]{2,1,0:T(8,128)(2,1)S(1)}, bf16[10,128,128]{2,1,0:T(8,128)(2,1)S(1)}, u32[]{:S(2)}, u32[]{:S(2)}) collective-permute-start(bf16[10,128,128]{2,1,0:T(8,128)(2,1)S(1)} %fusion.12), channel_id=1, source_target_pairs={{0,16},{4,20},{8,24},{12,28},{1,17},{5,21},{9,25},{13,29},{2,18},{... | collective-permute-start | bytes 983048 | tf_op jit(solution)/shard_map/ppermute | solution.py:190
  62.2 2.4 %copy-start.3 = (bf16[512,3072]{1,0:T(8,128)(2,1)}, bf16[512,3072]{1,0:T(8,128)(2,1)S(1)}, u32[]{:S(2)}) copy-start(bf16[512,3072]{1,0:T(8,128)(2,1)S(1)} %fusion.7) | copy-start | bytes 9437188
  62.2 3.4 %copy-start = (bf16[1024,1280]{1,0:T(8,128)(2,1)S(1)}, bf16[1024,1280]{1,0:T(8,128)(2,1)}, u32[]{:S(2)}) copy-start(bf16[1024,1280]{1,0:T(8,128)(2,1)} %shard_map.68) | copy-start | bytes 7864324
  64.6 11.8 %collective-permute-start.4 = (bf16[256,3072]{1,0:T(8,128)(2,1)}, bf16[256,3072]{1,0:T(8,128)(2,1)}, u32[]{:S(2)}, u32[]{:S(2)}) collective-permute-start(bf16[256,3072]{1,0:T(8,128)(2,1)} %constant_dynamic-slice_fusion.1), channel_id=1, source_target_pairs={{0,1},{1,0},{2,3},{3,2},{4,5},{5,4},{6,7},{7,6},{8,9},{9,8},{10,11... | collective-permute-start | bytes 4718600 | tf_op jit(solution)/shard_map/ppermute | solution.py:194
  73.3 1.6 copy-start.1
  76.3 3.8 %collective-permute-start.3 = (bf16[256,3072]{1,0:T(8,128)(2,1)}, bf16[256,3072]{1,0:T(8,128)(2,1)}, u32[]{:S(2)}, u32[]{:S(2)}) collective-permute-start(bf16[256,3072]{1,0:T(8,128)(2,1)} %constant_dynamic-slice_fusion.2), channel_id=1, source_target_pairs={{0,1},{1,0},{2,3},{3,2},{4,5},{5,4},{6,7},{7,6},{8,9},{9,8},{10,11... | collective-permute-start | bytes 4718600 | tf_op jit(solution)/shard_map/ppermute | solution.py:194
  76.3 3.8 %copy-start.2 = (bf16[512,3072]{1,0:T(8,128)(2,1)S(1)}, bf16[512,3072]{1,0:T(8,128)(2,1)}, u32[]{:S(2)}) copy-start(bf16[512,3072]{1,0:T(8,128)(2,1)} %copy-done.1) | copy-start | bytes 9437188
  92.0 70.6 %collective-permute-start.5 = (bf16[256,6144]{1,0:T(8,128)(2,1)S(1)}, bf16[256,6144]{1,0:T(8,128)(2,1)S(1)}, u32[]{:S(2)}, u32[]{:S(2)}) collective-permute-start(bf16[256,6144]{1,0:T(8,128)(2,1)S(1)} %convolution_convert_fusion), channel_id=1, source_target_pairs={{0,1},{1,0},{2,3},{3,2},{4,5},{5,4},{6,7},{7,6},{8,9},{9,8},{10,11... | collective-permute-start | bytes 9437192 | tf_op jit(solution)/shard_map/ppermute | solution.py:194
  92.2 37.3 %collective-permute-start.6 = (bf16[256,3072]{1,0:T(8,128)(2,1)S(1)}, bf16[256,3072]{1,0:T(8,128)(2,1)S(1)}, u32[]{:S(2)}, u32[]{:S(2)}) collective-permute-start(bf16[256,3072]{1,0:T(8,128)(2,1)S(1)} %add_convert_fusion.2), channel_id=1, source_target_pairs={{0,2},{2,0},{1,3},{3,1},{4,6},{6,4},{5,7},{7,5},{8,10},{10,8},{9,1... | collective-permute-start | bytes 4718600 | tf_op jit(solution)/shard_map/ppermute | solution.py:194
  93.7 68.9 %collective-permute-start.7 = (bf16[256,3072]{1,0:T(8,128)(2,1)S(1)}, bf16[256,3072]{1,0:T(8,128)(2,1)S(1)}, u32[]{:S(2)}, u32[]{:S(2)}) collective-permute-start(bf16[256,3072]{1,0:T(8,128)(2,1)S(1)} %add_convert_fusion.1), channel_id=1, source_target_pairs={{0,2},{2,0},{1,3},{3,1},{4,6},{6,4},{5,7},{7,5},{8,10},{10,8},{9,1... | collective-permute-start | bytes 4718600 | tf_op jit(solution)/shard_map/ppermute | solution.py:194

commit v15 on v14

--- a/solution.py
+++ b/solution.py
@@ -8,7 +8,7 @@
 from jax.sharding import PartitionSpec as P
 
 HD = 128
-COLUMN_CHUNKS = 2
+COLUMN_CHUNKS = 4
 QUERY_TILE = 256
 ROW_TILE = 256
 

time: 166 us -> 155 us (0.934)
  local copies, waits for them, and re-layouts: 7.11 us -> 0.95 us
  matrix products: 35.4 us -> 30.4 us
  other arithmetic: 8.4 us -> 4.52 us
  starting transfers between devices: 8.51 us -> 11.8 us
    dot_general x2, matrix products: 19.9 us -> 14.4 us  [product(): jnp.dot(rows, out_weight, preferred_element_type=jnp.float32)]
    convert_element_type x2 -> x4, other arithmetic: 4.6 us -> 0.81 us  [project_and_reduce(): chip_sums.append(chip_sum.astype(jnp.bfloat16))]
    unnamed x12 -> x14, local copies, waits for them, and re-layouts: 3.83 us -> 0.04 us
    ppermute x5 -> x9, starting transfers between devices: 2.23 us -> 5.51 us  [swap(): return lax.ppermute(block, axis, [(0, 1), (1, 0)])]
    dynamic_slice x2 -> x4, local copies, waits for them, and re-layouts: 2.6 us -> 0.23 us  [block_of(): return lax.dynamic_slice_in_dim(part, owner_tc * block, block, axis=0)]
    ppermute x5 -> x9, waiting for transfers between devices: 59.5 us -> 60 us  [swap(): return lax.ppermute(block, axis, [(0, 1), (1, 0)])]
    dot_general x2 -> x4, matrix products: 15.5 us -> 16 us  [project_and_reduce(): jnp.dot(far_rows, out_weight[:, c * chunk:(c + 1) * chunk], preferred_ele...]
  transfers between devices with their start and end apart: 8 -> 12, of which waited for: 6 -> 11; matrix products, arithmetic and copies ran while one was open for 13% -> 7% of each run, Pallas kernels for 13% -> 14%
where the time goes in v15:
time: 155 us; the launch traced here: 154 us
  waiting for transfers between devices  72.2 us (47%)
  Pallas kernels  33.9 us (22%)
  matrix products  30.4 us (20%)
  starting transfers between devices  11.8 us (8%)
  other arithmetic  4.52 us (3%)
    ppermute x9, waiting for transfers between devices, swap(): return lax.ppermute(block, axis, [(0, 1), (1, 0)])  60 us
    dot_general x4, matrix products, project_and_reduce(): jnp.dot(far_rows, out_weight[:, c * chunk:(c + 1) * chunk], preferred_ele...  16 us
    pallas_call x2, Pallas kernels, local_attention(): pl.pallas_call(local_kernel, grid=(heads,), in_specs=[picked] * 3, out_sp...  15.2 us
    dot_general x2, matrix products, product(): jnp.dot(rows, out_weight, preferred_element_type=jnp.float32)  14.4 us
    ppermute x3, waiting for transfers between devices, shift(): lax.ppermute(block, axis, [(i, i + distance) for i in range(size) if i +...  12.2 us
    pallas_call x1, Pallas kernels, mix(): pl.pallas_call(mix_kernel, grid=(tokens // ROW_TILE,), in_specs=[row_bloc...  6.78 us
    ppermute x3, starting transfers between devices, shift(): lax.ppermute(block, axis, [(i, i + distance) for i in range(size) if i +...  6.28 us
    pallas_call x1, Pallas kernels, query_and_gate(): pl.pallas_call(gate_kernel, grid=(tokens // ROW_TILE,), in_specs=[row_blo...  6.22 us
  transfers between devices with their start and end apart: 12, of which 11 were waited for; matrix products, arithmetic and copies ran while one was open for 7% of the time, Pallas kernels for 14%

profile of v15, /device:TPU:24, one launch (start us, length us, event | category | flops | bytes accessed | tf_op | source)
XLA Modules:
  0.0 154.0 jit_solution(72787400015809485)
XLA Ops:
  0.0 5.7 %shard_map.64 = (f32[10,128,128]{2,1,0:T(8,128)}, bf16[10,128,128]{2,1,0:T(8,128)(2,1)}) custom-call(bf16[1024,1280]{1,0:T(8,128)(2,1)} %k_ref.3, bf16[1024,1280]{1,0:T(8,128)(2,1)} %v_ref.3), custom_call_target="tpu_custom_call" | custom-call | flops 335544320 | bytes 5898240 | tf_op jit(solution)/shard_map/pallas_call | solution.py:54
  5.7 3.5 %collective-permute-start = (bf16[10,128,128]{2,1,0:T(8,128)(2,1)}, bf16[10,128,128]{2,1,0:T(8,128)(2,1)S(1)}, u32[]{:S(2)}, u32[]{:S(2)}) collective-permute-start(bf16[10,128,128]{2,1,0:T(8,128)(2,1)} %get-tuple-element.30), channel_id=1, source_target_pairs={{0,4},{4,8},{8,12},{12,16},{16,20},{20,24},{24,28},{1,5},{5,9},{9,... | collective-permute-start | bytes 983048 | tf_op jit(solution)/shard_map/ppermute | solution.py:190
  9.2 7.6 %shard_map.65.local_a_ref = bf16[1024,640]{1,0:T(8,128)(2,1)} custom-call(bf16[1024,1280]{1,0:T(8,128)(2,1)} %q_ref.2, bf16[1024,1280]{1,0:T(8,128)(2,1)} %k_ref.3, bf16[1024,1280]{1,0:T(8,128)(2,1)} %v_ref.3), custom_call_target="tpu_custom_call" | custom-call | flops 1677721600 | bytes 6553600 | tf_op jit(solution)/shard_map/pallas_call | solution.py:97
  16.8 1.4 collective-permute-done
  18.3 1.3 collective-permute-start.1
  19.6 7.6 %shard_map.66.local_b_ref = bf16[1024,640]{1,0:T(8,128)(2,1)} custom-call(bf16[1024,1280]{1,0:T(8,128)(2,1)} %q_ref.2, bf16[1024,1280]{1,0:T(8,128)(2,1)} %k_ref.3, bf16[1024,1280]{1,0:T(8,128)(2,1)} %v_ref.3), custom_call_target="tpu_custom_call" | custom-call | flops 1677721600 | bytes 6553600 | tf_op jit(solution)/shard_map/pallas_call | solution.py:97
  27.2 1.6 %collective-permute-done.1 = bf16[10,128,128]{2,1,0:T(8,128)(2,1)S(1)} collective-permute-done((bf16[10,128,128]{2,1,0:T(8,128)(2,1)S(1)}, bf16[10,128,128]{2,1,0:T(8,128)(2,1)S(1)}, u32[]{:S(2)}, u32[]{:S(2)}) %collective-permute-start.1) | collective-permute-done | bytes 327712 | tf_op jit(solution)/shard_map/ppermute | solution.py:190
  29.0 1.5 collective-permute-start.2
  31.1 6.2 %shard_map.67 = (bf16[1024,1280]{1,0:T(8,128)(2,1)}, bf16[1024,1280]{1,0:T(8,128)(2,1)}) custom-call(bf16[1024,1280]{1,0:T(8,128)(2,1)} %q_ref.2, bf16[1024,1280]{1,0:T(8,128)(2,1)} %g_ref, f32[1,1280]{1,0:T(1,128)} %reshape.3.gain_ref), custom_call_target="tpu_custom_call" | custom-call | flops 10485760 | bytes 13107200 | tf_op jit(solution)/shard_map/pallas_call | solution.py:119
  37.3 9.2 %collective-permute-done.2 = bf16[10,128,128]{2,1,0:T(8,128)(2,1)S(1)} collective-permute-done((bf16[10,128,128]{2,1,0:T(8,128)(2,1)S(1)}, bf16[10,128,128]{2,1,0:T(8,128)(2,1)S(1)}, u32[]{:S(2)}, u32[]{:S(2)}) %collective-permute-start.2) | collective-permute-done | bytes 327712 | tf_op jit(solution)/shard_map/ppermute | solution.py:190
  47.5 6.8 %shard_map.68 = bf16[1024,1280]{1,0:T(8,128)(2,1)} custom-call(bf16[1024,640]{1,0:T(8,128)(2,1)} %shard_map.65.local_a_ref, bf16[1024,640]{1,0:T(8,128)(2,1)} %shard_map.66.local_b_ref, bf16[1024,1280]{1,0:T(8,128)(2,1)} %get-tuple-element.47.q_ref, bf16[1024,1280]{1,0:T(8,128)(2,1)} %get-tuple-element.48.scale_ref, f32[10,128,128]{2,1,0:T(8,128)} %fusion.25.prefix_ref), custom_call_target="tpu_custom_call" | custom-call | flops 671088640 | bytes 15728640 | tf_op jit(solution)/shard_map/pallas_call | solution.py:162
  54.3 4.9 %fusion.17 = bf16[512,1536]{1,0:T(8,128)(2,1)S(1)} fusion(bf16[1280,6144]{1,0:T(8,128)(2,1)} %param.11, bf16[1024,1280]{1,0:T(8,128)(2,1)} %shard_map.68, s32[]{:T(128)S(6)} %select_n.8), kind=kOutput, calls=%fused_computation.14 | convolution fusion | flops 2014052352 | bytes 6815748 | tf_op jit(solution)/shard_map/dot_general | solution.py:252
  59.2 4.5 %fusion.14 = bf16[512,1536]{1,0:T(8,128)(2,1)S(1)} fusion(bf16[1280,6144]{1,0:T(8,128)(2,1)} %param.11, bf16[1024,1280]{1,0:T(8,128)(2,1)S(1)} %copy-done, s32[]{:T(128)S(6)} %select_n.8), kind=kOutput, calls=%fused_computation.13 | convolution fusion | flops 2014052352 | bytes 6815748 | tf_op jit(solution)/shard_map/dot_general | solution.py:252
  63.7 4.5 %fusion.11 = bf16[512,1536]{1,0:T(8,128)(2,1)S(1)} fusion(bf16[1280,6144]{1,0:T(8,128)(2,1)} %param.11, bf16[1024,1280]{1,0:T(8,128)(2,1)S(1)} %copy-done, s32[]{:T(128)S(6)} %select_n.8), kind=kOutput, calls=%fused_computation.12 | convolution fusion | flops 2014052352 | bytes 6815748 | tf_op jit(solution)/shard_map/dot_general | solution.py:252
  68.2 2.2 %fusion.8 = bf16[512,1536]{1,0:T(8,128)(2,1)S(1)} fusion(bf16[1280,6144]{1,0:T(8,128)(2,1)S(1)} %bitcast.3, bf16[1024,1280]{1,0:T(8,128)(2,1)S(1)} %copy-done, s32[]{:T(128)S(6)} %select_n.8), kind=kOutput, calls=%fused_computation.11 | convolution fusion | flops 2014052352 | bytes 6815748 | tf_op jit(solution)/shard_map/dot_general | solution.py:252
  76.5 4.4 %convolution_convert_fusion = bf16[256,6144]{1,0:T(8,128)(2,1)S(1)} fusion(bf16[1280,6144]{1,0:T(8,128)(2,1)S(1)} %bitcast.3, bf16[512,1280]{1,0:T(8,128)(2,1)S(1)} %constant_dynamic-slice_fusion, s32[]{:T(128)S(6)} %select_n.10), kind=kOutput, calls=%fused_computation | convolution fusion | flops 4028104704 | bytes 19529732 | tf_op jit(solution)/shard_map/dot_general | solution.py:228
  81.1 1.5 collective-permute-start.10
  83.2 1.5 collective-permute-start.8
  85.2 9.9 %convolution_convert_fusion.1 = bf16[256,6144]{1,0:T(8,128)(2,1)S(1)} fusion(bf16[1280,6144]{1,0:T(8,128)(2,1)} %param.11, bf16[512,1280]{1,0:T(8,128)(2,1)S(1)} %constant_dynamic-slice_fusion, s32[]{:T(128)S(6)} %select_n.9), kind=kOutput, calls=%fused_computation.1 | convolution fusion | flops 4028104704 | bytes 19529732 | tf_op jit(solution)/shard_map/dot_general | solution.py:228
  95.1 6.4 %collective-permute-done.10 = bf16[256,1536]{1,0:T(8,128)(2,1)S(1)} collective-permute-done((bf16[256,1536]{1,0:T(8,128)(2,1)S(1)}, bf16[256,1536]{1,0:T(8,128)(2,1)S(1)}, u32[]{:S(2)}, u32[]{:S(2)}) %collective-permute-start.10) | collective-permute-done | bytes 786464 | tf_op jit(solution)/shard_map/ppermute | solution.py:194
  101.5 16.9 %collective-permute-done.11 = bf16[256,1536]{1,0:T(8,128)(2,1)S(1)} collective-permute-done((bf16[256,1536]{1,0:T(8,128)(2,1)S(1)}, bf16[256,1536]{1,0:T(8,128)(2,1)S(1)}, u32[]{:S(2)}, u32[]{:S(2)}) %collective-permute-start.11) | collective-permute-done | bytes 786464 | tf_op jit(solution)/shard_map/ppermute | solution.py:194
  118.4 16.9 %collective-permute-done.8 = bf16[256,1536]{1,0:T(8,128)(2,1)S(1)} collective-permute-done((bf16[256,1536]{1,0:T(8,128)(2,1)S(1)}, bf16[256,1536]{1,0:T(8,128)(2,1)S(1)}, u32[]{:S(2)}, u32[]{:S(2)}) %collective-permute-start.8) | collective-permute-done | bytes 786464 | tf_op jit(solution)/shard_map/ppermute | solution.py:194
  135.2 16.3 %collective-permute-done.9 = bf16[256,1536]{1,0:T(8,128)(2,1)S(1)} collective-permute-done((bf16[256,1536]{1,0:T(8,128)(2,1)S(1)}, bf16[256,1536]{1,0:T(8,128)(2,1)S(1)}, u32[]{:S(2)}, u32[]{:S(2)}) %collective-permute-start.9) | collective-permute-done | bytes 786464 | tf_op jit(solution)/shard_map/ppermute | solution.py:194
  151.5 2.5 %add_convert_fusion = bf16[256,6144]{1,0:T(8,128)(2,1)} fusion(bf16[256,6144]{1,0:T(8,128)(2,1)S(1)} %collective-permute-done.7, bf16[256,6144]{1,0:T(8,128)(2,1)S(1)} %convolution_convert_fusion.1, bf16[256,1536]{1,0:T(8,128)(2,1)S(1)} %collective-permute-done.11, bf16[256,1536]{1,0:T(8,128)(2,1)S(1)} %collective-permute-done.10, ...), kind=kLoop, calls=%fused_computation.2 | loop fusion | flops 20447232 | bytes 12582912 | tf_op jit(solution)/shard_map/convert_element_type | solution.py:264
  (40 shorter events, 9.0 us)
Async XLA Ops:
  5.7 12.6 %copy-start.1 = (f32[10,128,128]{2,1,0:T(8,128)S(1)}, f32[10,128,128]{2,1,0:T(8,128)}, u32[]{:S(2)}) copy-start(f32[10,128,128]{2,1,0:T(8,128)} %get-tuple-element.35) | copy-start | bytes 1966084
  5.7 12.6 %collective-permute-start = (bf16[10,128,128]{2,1,0:T(8,128)(2,1)}, bf16[10,128,128]{2,1,0:T(8,128)(2,1)S(1)}, u32[]{:S(2)}, u32[]{:S(2)}) collective-permute-start(bf16[10,128,128]{2,1,0:T(8,128)(2,1)} %get-tuple-element.30), channel_id=1, source_target_pairs={{0,4},{4,8},{8,12},{12,16},{16,20},{20,24},{24,28},{1,5},{5,9},{9,... | collective-permute-start | bytes 983048 | tf_op jit(solution)/shard_map/ppermute | solution.py:190
  18.3 12.1 %copy-start.2 = (f32[1280]{0:T(1024)S(1)}, f32[1280]{0:T(1024)}, u32[]{:S(2)}) copy-start(f32[1280]{0:T(1024)} %param.10) | copy-start | bytes 15364
  18.3 10.5 %collective-permute-start.1 = (bf16[10,128,128]{2,1,0:T(8,128)(2,1)S(1)}, bf16[10,128,128]{2,1,0:T(8,128)(2,1)S(1)}, u32[]{:S(2)}, u32[]{:S(2)}) collective-permute-start(bf16[10,128,128]{2,1,0:T(8,128)(2,1)S(1)} %fusion.28), channel_id=1, source_target_pairs={{0,8},{4,12},{8,16},{12,20},{16,24},{20,28},{1,9},{5,13},{9,17},{1... | collective-permute-start | bytes 983048 | tf_op jit(solution)/shard_map/ppermute | solution.py:190
  29.0 17.6 %collective-permute-start.2 = (bf16[10,128,128]{2,1,0:T(8,128)(2,1)S(1)}, bf16[10,128,128]{2,1,0:T(8,128)(2,1)S(1)}, u32[]{:S(2)}, u32[]{:S(2)}) collective-permute-start(bf16[10,128,128]{2,1,0:T(8,128)(2,1)S(1)} %fusion.24), channel_id=1, source_target_pairs={{0,16},{4,20},{8,24},{12,28},{1,17},{5,21},{9,25},{13,29},{2,18},{... | collective-permute-start | bytes 983048 | tf_op jit(solution)/shard_map/ppermute | solution.py:190
  54.3 4.9 %copy-start = (bf16[1024,1280]{1,0:T(8,128)(2,1)S(1)}, bf16[1024,1280]{1,0:T(8,128)(2,1)}, u32[]{:S(2)}) copy-start(bf16[1024,1280]{1,0:T(8,128)(2,1)} %shard_map.68) | copy-start | bytes 7864324
  54.3 13.9 %slice-start = ((s8[15728640]{0:T(1024)(128)(4,1)}), s8[4194304]{0:T(1024)(128)(4,1)S(1)}, s32[]{:S(2)}) async-start(s8[15728640]{0:T(1024)(128)(4,1)} %bitcast.2), calls=%async_computation | async-start | bytes 8388608
  54.3 13.9 %slice-start.1 = ((s8[15728640]{0:T(1024)(128)(4,1)}), s8[4194304]{0:T(1024)(128)(4,1)S(1)}, s32[]{:S(2)}) async-start(s8[15728640]{0:T(1024)(128)(4,1)} %bitcast.2), calls=%async_computation.1 | async-start | bytes 8388608
  59.2 9.0 %slice-start.2 = ((s8[15728640]{0:T(1024)(128)(4,1)}), s8[4194304]{0:T(1024)(128)(4,1)S(1)}, s32[]{:S(2)}) async-start(s8[15728640]{0:T(1024)(128)(4,1)} %bitcast.2), calls=%async_computation.2 | async-start | bytes 8388608
  63.7 4.5 %slice-start.3 = ((s8[15728640]{0:T(1024)(128)(4,1)}), s8[3145728]{0:T(1024)(128)(4,1)S(1)}, s32[]{:S(2)}) async-start(s8[15728640]{0:T(1024)(128)(4,1)} %bitcast.2), calls=%async_computation.3 | async-start | bytes 6291456
  70.5 2.4 %collective-permute-start.6 = (bf16[256,1536]{1,0:T(8,128)(2,1)S(1)}, bf16[256,1536]{1,0:T(8,128)(2,1)S(1)}, u32[]{:S(2)}, u32[]{:S(2)}) collective-permute-start(bf16[256,1536]{1,0:T(8,128)(2,1)S(1)} %constant_dynamic-slice_fusion.1), channel_id=1, source_target_pairs={{0,1},{1,0},{2,3},{3,2},{4,5},{5,4},{6,7},{7,6},{8,9},{9,8},{10,11... | collective-permute-start | bytes 2359304 | tf_op jit(solution)/shard_map/ppermute | solution.py:194
  70.7 3.3 %collective-permute-start.5 = (bf16[256,1536]{1,0:T(8,128)(2,1)S(1)}, bf16[256,1536]{1,0:T(8,128)(2,1)S(1)}, u32[]{:S(2)}, u32[]{:S(2)}) collective-permute-start(bf16[256,1536]{1,0:T(8,128)(2,1)S(1)} %constant_dynamic-slice_fusion.2), channel_id=1, source_target_pairs={{0,1},{1,0},{2,3},{3,2},{4,5},{5,4},{6,7},{7,6},{8,9},{9,8},{10,11... | collective-permute-start | bytes 2359304 | tf_op jit(solution)/shard_map/ppermute | solution.py:194
  71.3 3.8 %collective-permute-start.4 = (bf16[256,1536]{1,0:T(8,128)(2,1)S(1)}, bf16[256,1536]{1,0:T(8,128)(2,1)S(1)}, u32[]{:S(2)}, u32[]{:S(2)}) collective-permute-start(bf16[256,1536]{1,0:T(8,128)(2,1)S(1)} %constant_dynamic-slice_fusion.3), channel_id=1, source_target_pairs={{0,1},{1,0},{2,3},{3,2},{4,5},{5,4},{6,7},{7,6},{8,9},{9,8},{10,11... | collective-permute-start | bytes 2359304 | tf_op jit(solution)/shard_map/ppermute | solution.py:194
  71.4 4.8 %collective-permute-start.3 = (bf16[256,1536]{1,0:T(8,128)(2,1)S(1)}, bf16[256,1536]{1,0:T(8,128)(2,1)S(1)}, u32[]{:S(2)}, u32[]{:S(2)}) collective-permute-start(bf16[256,1536]{1,0:T(8,128)(2,1)S(1)} %constant_dynamic-slice_fusion.4), channel_id=1, source_target_pairs={{0,1},{1,0},{2,3},{3,2},{4,5},{5,4},{6,7},{7,6},{8,9},{9,8},{10,11... | collective-permute-start | bytes 2359304 | tf_op jit(solution)/shard_map/ppermute | solution.py:194
  80.9 70.6 %collective-permute-start.7 = (bf16[256,6144]{1,0:T(8,128)(2,1)S(1)}, bf16[256,6144]{1,0:T(8,128)(2,1)S(1)}, u32[]{:S(2)}, u32[]{:S(2)}) collective-permute-start(bf16[256,6144]{1,0:T(8,128)(2,1)S(1)} %convolution_convert_fusion), channel_id=1, source_target_pairs={{0,1},{1,0},{2,3},{3,2},{4,5},{5,4},{6,7},{7,6},{8,9},{9,8},{10,11... | collective-permute-start | bytes 9437192 | tf_op jit(solution)/shard_map/ppermute | solution.py:194
  81.1 20.4 %collective-permute-start.10 = (bf16[256,1536]{1,0:T(8,128)(2,1)S(1)}, bf16[256,1536]{1,0:T(8,128)(2,1)S(1)}, u32[]{:S(2)}, u32[]{:S(2)}) collective-permute-start(bf16[256,1536]{1,0:T(8,128)(2,1)S(1)} %add_convert_fusion.2), channel_id=1, source_target_pairs={{0,2},{2,0},{1,3},{3,1},{4,6},{6,4},{5,7},{7,5},{8,10},{10,8},{9,1... | collective-permute-start | bytes 2359304 | tf_op jit(solution)/shard_map/ppermute | solution.py:194
  82.6 35.7 %collective-permute-start.11 = (bf16[256,1536]{1,0:T(8,128)(2,1)S(1)}, bf16[256,1536]{1,0:T(8,128)(2,1)S(1)}, u32[]{:S(2)}, u32[]{:S(2)}) collective-permute-start(bf16[256,1536]{1,0:T(8,128)(2,1)S(1)} %add_convert_fusion.1), channel_id=1, source_target_pairs={{0,2},{2,0},{1,3},{3,1},{4,6},{6,4},{5,7},{7,5},{8,10},{10,8},{9,1... | collective-permute-start | bytes 2359304 | tf_op jit(solution)/shard_map/ppermute | solution.py:194
  83.2 52.1 %collective-permute-start.8 = (bf16[256,1536]{1,0:T(8,128)(2,1)S(1)}, bf16[256,1536]{1,0:T(8,128)(2,1)S(1)}, u32[]{:S(2)}, u32[]{:S(2)}) collective-permute-start(bf16[256,1536]{1,0:T(8,128)(2,1)S(1)} %add_convert_fusion.4), channel_id=1, source_target_pairs={{0,2},{2,0},{1,3},{3,1},{4,6},{6,4},{5,7},{7,5},{8,10},{10,8},{9,1... | collective-permute-start | bytes 2359304 | tf_op jit(solution)/shard_map/ppermute | solution.py:194
  84.7 66.8 %collective-permute-start.9 = (bf16[256,1536]{1,0:T(8,128)(2,1)S(1)}, bf16[256,1536]{1,0:T(8,128)(2,1)S(1)}, u32[]{:S(2)}, u32[]{:S(2)}) collective-permute-start(bf16[256,1536]{1,0:T(8,128)(2,1)S(1)} %add_convert_fusion.3), channel_id=1, source_target_pairs={{0,2},{2,0},{1,3},{3,1},{4,6},{6,4},{5,7},{7,5},{8,10},{10,8},{9,1... | collective-permute-start | bytes 2359304 | tf_op jit(solution)/shard_map/ppermute | solution.py:194

commit v16 on v13

--- a/solution.py
+++ b/solution.py
@@ -9,7 +9,7 @@
 
 HD = 128
 COLUMN_CHUNKS = 3
-QUERY_TILE = 256
+QUERY_TILE = 128
 ROW_TILE = 256
 
 

time: 152 us -> 154 us (1.013)
  Pallas kernels: 33.9 us -> 37.6 us
  waiting for transfers between devices: 70.8 us -> 69.2 us
    pallas_call x2, Pallas kernels: 15.2 us -> 18.9 us  [local_attention(): pl.pallas_call(local_kernel, grid=(heads,), in_specs=[picked] * 3, out_sp...]
    ppermute x3, waiting for transfers between devices: 12.2 us -> 10.7 us  [shift(): lax.ppermute(block, axis, [(i, i + distance) for i in range(size) if i +...]
  transfers between devices with their start and end apart: 10 -> 10, of which waited for: 7 -> 6; matrix products, arithmetic and copies ran while one was open for 10% -> 10% of each run, Pallas kernels for 14% -> 16%
where the time goes in v16:
time: 154 us; the launch traced here: 153 us
  waiting for transfers between devices  69.2 us (45%)
  Pallas kernels  37.6 us (24%)
  matrix products  29.2 us (19%)
  starting transfers between devices  10.8 us (7%)
  other arithmetic  5.17 us (3%)
    ppermute x7, waiting for transfers between devices, swap(): return lax.ppermute(block, axis, [(0, 1), (1, 0)])  58.5 us
    pallas_call x2, Pallas kernels, local_attention(): pl.pallas_call(local_kernel, grid=(heads,), in_specs=[picked] * 3, out_sp...  18.9 us
    dot_general x3, matrix products, project_and_reduce(): jnp.dot(far_rows, out_weight[:, c * chunk:(c + 1) * chunk], preferred_ele...  14.8 us
    dot_general x2, matrix products, product(): jnp.dot(rows, out_weight, preferred_element_type=jnp.float32)  14.4 us
    ppermute x3, waiting for transfers between devices, shift(): lax.ppermute(block, axis, [(i, i + distance) for i in range(size) if i +...  10.7 us
    pallas_call x1, Pallas kernels, mix(): pl.pallas_call(mix_kernel, grid=(tokens // ROW_TILE,), in_specs=[row_bloc...  6.76 us
    ppermute x3, starting transfers between devices, shift(): lax.ppermute(block, axis, [(i, i + distance) for i in range(size) if i +...  6.28 us
    pallas_call x1, Pallas kernels, query_and_gate(): pl.pallas_call(gate_kernel, grid=(tokens // ROW_TILE,), in_specs=[row_blo...  6.22 us
  transfers between devices with their start and end apart: 10, of which 6 were waited for; matrix products, arithmetic and copies ran while one was open for 10% of the time, Pallas kernels for 16%

profile of v16, /device:TPU:24, one launch (start us, length us, event | category | flops | bytes accessed | tf_op | source)
XLA Modules:
  0.0 153.2 jit_solution(3943866324887678336)
XLA Ops:
  0.0 5.6 %shard_map.64 = (f32[10,128,128]{2,1,0:T(8,128)}, bf16[10,128,128]{2,1,0:T(8,128)(2,1)}) custom-call(bf16[1024,1280]{1,0:T(8,128)(2,1)} %k_ref.3, bf16[1024,1280]{1,0:T(8,128)(2,1)} %v_ref.3), custom_call_target="tpu_custom_call" | custom-call | flops 335544320 | bytes 5898240 | tf_op jit(solution)/shard_map/pallas_call | solution.py:54
  5.6 3.5 %collective-permute-start = (bf16[10,128,128]{2,1,0:T(8,128)(2,1)}, bf16[10,128,128]{2,1,0:T(8,128)(2,1)S(1)}, u32[]{:S(2)}, u32[]{:S(2)}) collective-permute-start(bf16[10,128,128]{2,1,0:T(8,128)(2,1)} %get-tuple-element.29), channel_id=1, source_target_pairs={{0,4},{4,8},{8,12},{12,16},{16,20},{20,24},{24,28},{1,5},{5,9},{9,... | collective-permute-start | bytes 983048 | tf_op jit(solution)/shard_map/ppermute | solution.py:190
  9.2 9.5 %shard_map.65.local_a_ref = bf16[1024,640]{1,0:T(8,128)(2,1)} custom-call(bf16[1024,1280]{1,0:T(8,128)(2,1)} %q_ref.2, bf16[1024,1280]{1,0:T(8,128)(2,1)} %k_ref.3, bf16[1024,1280]{1,0:T(8,128)(2,1)} %v_ref.3), custom_call_target="tpu_custom_call" | custom-call | flops 1509949440 | bytes 6553600 | tf_op jit(solution)/shard_map/pallas_call | solution.py:97
  18.8 1.3 collective-permute-start.1
  20.1 9.5 %shard_map.66.local_b_ref = bf16[1024,640]{1,0:T(8,128)(2,1)} custom-call(bf16[1024,1280]{1,0:T(8,128)(2,1)} %q_ref.2, bf16[1024,1280]{1,0:T(8,128)(2,1)} %k_ref.3, bf16[1024,1280]{1,0:T(8,128)(2,1)} %v_ref.3), custom_call_target="tpu_custom_call" | custom-call | flops 1509949440 | bytes 6553600 | tf_op jit(solution)/shard_map/pallas_call | solution.py:97
  30.0 1.5 collective-permute-start.2
  31.5 0.6 reshape.3.gain_ref
  32.0 6.2 %shard_map.67 = (bf16[1024,1280]{1,0:T(8,128)(2,1)}, bf16[1024,1280]{1,0:T(8,128)(2,1)}) custom-call(bf16[1024,1280]{1,0:T(8,128)(2,1)} %q_ref.2, bf16[1024,1280]{1,0:T(8,128)(2,1)} %g_ref, f32[1,1280]{1,0:T(1,128)} %reshape.3.gain_ref), custom_call_target="tpu_custom_call" | custom-call | flops 10485760 | bytes 13107200 | tf_op jit(solution)/shard_map/pallas_call | solution.py:119
  38.3 10.4 %collective-permute-done.2 = bf16[10,128,128]{2,1,0:T(8,128)(2,1)S(1)} collective-permute-done((bf16[10,128,128]{2,1,0:T(8,128)(2,1)S(1)}, bf16[10,128,128]{2,1,0:T(8,128)(2,1)S(1)}, u32[]{:S(2)}, u32[]{:S(2)}) %collective-permute-start.2) | collective-permute-done | bytes 327712 | tf_op jit(solution)/shard_map/ppermute | solution.py:190
  48.7 1.0 fusion.19.prefix_ref
  49.7 6.8 %shard_map.68 = bf16[1024,1280]{1,0:T(8,128)(2,1)} custom-call(bf16[1024,640]{1,0:T(8,128)(2,1)} %shard_map.65.local_a_ref, bf16[1024,640]{1,0:T(8,128)(2,1)} %shard_map.66.local_b_ref, bf16[1024,1280]{1,0:T(8,128)(2,1)} %get-tuple-element.46.q_ref, bf16[1024,1280]{1,0:T(8,128)(2,1)} %get-tuple-element.47.scale_ref, f32[10,128,128]{2,1,0:T(8,128)} %fusion.19.prefix_ref), custom_call_target="tpu_custom_call" | custom-call | flops 671088640 | bytes 15728640 | tf_op jit(solution)/shard_map/pallas_call | solution.py:162
  56.5 5.9 %fusion.12 = bf16[512,2048]{1,0:T(8,128)(2,1)S(1)} fusion(bf16[1280,6144]{1,0:T(8,128)(2,1)} %param.11, bf16[1024,1280]{1,0:T(8,128)(2,1)} %shard_map.68, s32[]{:T(128)S(6)} %select_n.8), kind=kOutput, calls=%fused_computation.11 | convolution fusion | flops 2685403136 | bytes 8650756 | tf_op jit(solution)/shard_map/dot_general | solution.py:252
  62.4 5.8 %fusion.9 = bf16[512,2048]{1,0:T(8,128)(2,1)S(1)} fusion(bf16[1280,6144]{1,0:T(8,128)(2,1)} %param.11, bf16[1024,1280]{1,0:T(8,128)(2,1)S(1)} %copy-done, s32[]{:T(128)S(6)} %select_n.8), kind=kOutput, calls=%fused_computation.10 | convolution fusion | flops 2685403136 | bytes 8650756 | tf_op jit(solution)/shard_map/dot_general | solution.py:252
  68.5 0.6 collective-permute-start.4
  69.1 3.1 %fusion.6 = bf16[512,2048]{1,0:T(8,128)(2,1)S(1)} fusion(bf16[1280,6144]{1,0:T(8,128)(2,1)S(1)} %bitcast.3, bf16[1024,1280]{1,0:T(8,128)(2,1)S(1)} %copy-done, s32[]{:T(128)S(6)} %select_n.8), kind=kOutput, calls=%fused_computation.9 | convolution fusion | flops 2685403136 | bytes 8650756 | tf_op jit(solution)/shard_map/dot_general | solution.py:252
  73.5 1.6 %collective-permute-done.3 = bf16[256,2048]{1,0:T(8,128)(2,1)S(1)} collective-permute-done((bf16[256,2048]{1,0:T(8,128)(2,1)S(1)}, bf16[256,2048]{1,0:T(8,128)(2,1)S(1)}, u32[]{:S(2)}, u32[]{:S(2)}) %collective-permute-start.3) | collective-permute-done | bytes 1048608 | tf_op jit(solution)/shard_map/ppermute | solution.py:194
  75.6 4.4 %convolution_convert_fusion = bf16[256,6144]{1,0:T(8,128)(2,1)S(1)} fusion(bf16[1280,6144]{1,0:T(8,128)(2,1)S(1)} %bitcast.3, bf16[512,1280]{1,0:T(8,128)(2,1)S(1)} %constant_dynamic-slice_fusion, s32[]{:T(128)S(6)} %select_n.20), kind=kOutput, calls=%fused_computation | convolution fusion | flops 4028104704 | bytes 19529732 | tf_op jit(solution)/shard_map/dot_general | solution.py:228
  80.2 1.5 collective-permute-start.7
  82.2 1.5 collective-permute-start.9
  83.8 9.9 %convolution_convert_fusion.1 = bf16[256,6144]{1,0:T(8,128)(2,1)S(1)} fusion(bf16[1280,6144]{1,0:T(8,128)(2,1)} %param.11, bf16[512,1280]{1,0:T(8,128)(2,1)S(1)} %constant_dynamic-slice_fusion, s32[]{:T(128)S(6)} %select_n.9), kind=kOutput, calls=%fused_computation.1 | convolution fusion | flops 4028104704 | bytes 19529732 | tf_op jit(solution)/shard_map/dot_general | solution.py:228
  93.7 12.6 %collective-permute-done.7 = bf16[256,2048]{1,0:T(8,128)(2,1)S(1)} collective-permute-done((bf16[256,2048]{1,0:T(8,128)(2,1)S(1)}, bf16[256,2048]{1,0:T(8,128)(2,1)S(1)}, u32[]{:S(2)}, u32[]{:S(2)}) %collective-permute-start.7) | collective-permute-done | bytes 1048608 | tf_op jit(solution)/shard_map/ppermute | solution.py:194
  106.3 22.5 %collective-permute-done.8 = bf16[256,2048]{1,0:T(8,128)(2,1)S(1)} collective-permute-done((bf16[256,2048]{1,0:T(8,128)(2,1)S(1)}, bf16[256,2048]{1,0:T(8,128)(2,1)S(1)}, u32[]{:S(2)}, u32[]{:S(2)}) %collective-permute-start.8) | collective-permute-done | bytes 1048608 | tf_op jit(solution)/shard_map/ppermute | solution.py:194
  128.7 21.9 %collective-permute-done.9 = bf16[256,2048]{1,0:T(8,128)(2,1)S(1)} collective-permute-done((bf16[256,2048]{1,0:T(8,128)(2,1)S(1)}, bf16[256,2048]{1,0:T(8,128)(2,1)S(1)}, u32[]{:S(2)}, u32[]{:S(2)}) %collective-permute-start.9) | collective-permute-done | bytes 1048608 | tf_op jit(solution)/shard_map/ppermute | solution.py:194
  150.6 2.6 %add_convert_fusion = bf16[256,6144]{1,0:T(8,128)(2,1)} fusion(bf16[256,6144]{1,0:T(8,128)(2,1)S(1)} %collective-permute-done.6, bf16[256,6144]{1,0:T(8,128)(2,1)S(1)} %convolution_convert_fusion.1, bf16[256,2048]{1,0:T(8,128)(2,1)S(1)} %collective-permute-done.9, bf16[256,2048]{1,0:T(8,128)(2,1)S(1)} %collective-permute-done.8, ...), kind=kLoop, calls=%fused_computation.2 | loop fusion | flops 17301504 | bytes 12582912 | tf_op jit(solution)/shard_map/convert_element_type | solution.py:264
  (33 shorter events, 3.2 us)
Async XLA Ops:
  5.6 13.0 %copy-start.1 = (f32[10,128,128]{2,1,0:T(8,128)S(1)}, f32[10,128,128]{2,1,0:T(8,128)}, u32[]{:S(2)}) copy-start(f32[10,128,128]{2,1,0:T(8,128)} %get-tuple-element.34) | copy-start | bytes 1966084
  5.6 13.0 %collective-permute-start = (bf16[10,128,128]{2,1,0:T(8,128)(2,1)}, bf16[10,128,128]{2,1,0:T(8,128)(2,1)S(1)}, u32[]{:S(2)}, u32[]{:S(2)}) collective-permute-start(bf16[10,128,128]{2,1,0:T(8,128)(2,1)} %get-tuple-element.29), channel_id=1, source_target_pairs={{0,4},{4,8},{8,12},{12,16},{16,20},{20,24},{24,28},{1,5},{5,9},{9,... | collective-permute-start | bytes 983048 | tf_op jit(solution)/shard_map/ppermute | solution.py:190
  18.7 12.7 %copy-start.2 = (f32[1280]{0:T(1024)S(1)}, f32[1280]{0:T(1024)}, u32[]{:S(2)}) copy-start(f32[1280]{0:T(1024)} %param.10) | copy-start | bytes 15364
  18.8 11.1 %collective-permute-start.1 = (bf16[10,128,128]{2,1,0:T(8,128)(2,1)S(1)}, bf16[10,128,128]{2,1,0:T(8,128)(2,1)S(1)}, u32[]{:S(2)}, u32[]{:S(2)}) collective-permute-start(bf16[10,128,128]{2,1,0:T(8,128)(2,1)S(1)} %fusion.22), channel_id=1, source_target_pairs={{0,8},{4,12},{8,16},{12,20},{16,24},{20,28},{1,9},{5,13},{9,17},{1... | collective-permute-start | bytes 983048 | tf_op jit(solution)/shard_map/ppermute | solution.py:190
  30.0 18.7 %collective-permute-start.2 = (bf16[10,128,128]{2,1,0:T(8,128)(2,1)S(1)}, bf16[10,128,128]{2,1,0:T(8,128)(2,1)S(1)}, u32[]{:S(2)}, u32[]{:S(2)}) collective-permute-start(bf16[10,128,128]{2,1,0:T(8,128)(2,1)S(1)} %fusion.18), channel_id=1, source_target_pairs={{0,16},{4,20},{8,24},{12,28},{1,17},{5,21},{9,25},{13,29},{2,18},{... | collective-permute-start | bytes 983048 | tf_op jit(solution)/shard_map/ppermute | solution.py:190
  56.4 5.9 %copy-start = (bf16[1024,1280]{1,0:T(8,128)(2,1)S(1)}, bf16[1024,1280]{1,0:T(8,128)(2,1)}, u32[]{:S(2)}) copy-start(bf16[1024,1280]{1,0:T(8,128)(2,1)} %shard_map.68) | copy-start | bytes 7864324
  56.4 12.7 %slice-start = ((s8[15728640]{0:T(1024)(128)(4,1)}), s8[4194304]{0:T(1024)(128)(4,1)S(1)}, s32[]{:S(2)}) async-start(s8[15728640]{0:T(1024)(128)(4,1)} %bitcast.2), calls=%async_computation | async-start | bytes 8388608
  56.5 12.7 %slice-start.1 = ((s8[15728640]{0:T(1024)(128)(4,1)}), s8[4194304]{0:T(1024)(128)(4,1)S(1)}, s32[]{:S(2)}) async-start(s8[15728640]{0:T(1024)(128)(4,1)} %bitcast.2), calls=%async_computation.1 | async-start | bytes 8388608
  62.4 6.7 %slice-start.2 = ((s8[15728640]{0:T(1024)(128)(4,1)}), s8[4194304]{0:T(1024)(128)(4,1)S(1)}, s32[]{:S(2)}) async-start(s8[15728640]{0:T(1024)(128)(4,1)} %bitcast.2), calls=%async_computation.2 | async-start | bytes 8388608
  62.4 6.7 %slice-start.3 = ((s8[15728640]{0:T(1024)(128)(4,1)}), s8[3145728]{0:T(1024)(128)(4,1)S(1)}, s32[]{:S(2)}) async-start(s8[15728640]{0:T(1024)(128)(4,1)} %bitcast.2), calls=%async_computation.3 | async-start | bytes 6291456
  68.4 4.2 %collective-permute-start.5 = (bf16[256,2048]{1,0:T(8,128)(2,1)S(1)}, bf16[256,2048]{1,0:T(8,128)(2,1)S(1)}, u32[]{:S(2)}, u32[]{:S(2)}) collective-permute-start(bf16[256,2048]{1,0:T(8,128)(2,1)S(1)} %constant_dynamic-slice_fusion.1), channel_id=1, source_target_pairs={{0,1},{1,0},{2,3},{3,2},{4,5},{5,4},{6,7},{7,6},{8,9},{9,8},{10,11... | collective-permute-start | bytes 3145736 | tf_op jit(solution)/shard_map/ppermute | solution.py:194
  68.5 4.5 %collective-permute-start.4 = (bf16[256,2048]{1,0:T(8,128)(2,1)S(1)}, bf16[256,2048]{1,0:T(8,128)(2,1)S(1)}, u32[]{:S(2)}, u32[]{:S(2)}) collective-permute-start(bf16[256,2048]{1,0:T(8,128)(2,1)S(1)} %constant_dynamic-slice_fusion.2), channel_id=1, source_target_pairs={{0,1},{1,0},{2,3},{3,2},{4,5},{5,4},{6,7},{7,6},{8,9},{9,8},{10,11... | collective-permute-start | bytes 3145736 | tf_op jit(solution)/shard_map/ppermute | solution.py:194
  72.4 2.7 %collective-permute-start.3 = (bf16[256,2048]{1,0:T(8,128)(2,1)S(1)}, bf16[256,2048]{1,0:T(8,128)(2,1)S(1)}, u32[]{:S(2)}, u32[]{:S(2)}) collective-permute-start(bf16[256,2048]{1,0:T(8,128)(2,1)S(1)} %constant_dynamic-slice_fusion.3), channel_id=1, source_target_pairs={{0,1},{1,0},{2,3},{3,2},{4,5},{5,4},{6,7},{7,6},{8,9},{9,8},{10,11... | collective-permute-start | bytes 3145736 | tf_op jit(solution)/shard_map/ppermute | solution.py:194
  80.0 70.6 %collective-permute-start.6 = (bf16[256,6144]{1,0:T(8,128)(2,1)S(1)}, bf16[256,6144]{1,0:T(8,128)(2,1)S(1)}, u32[]{:S(2)}, u32[]{:S(2)}) collective-permute-start(bf16[256,6144]{1,0:T(8,128)(2,1)S(1)} %convolution_convert_fusion), channel_id=1, source_target_pairs={{0,1},{1,0},{2,3},{3,2},{4,5},{5,4},{6,7},{7,6},{8,9},{9,8},{10,11... | collective-permute-start | bytes 9437192 | tf_op jit(solution)/shard_map/ppermute | solution.py:194
  80.2 26.0 %collective-permute-start.7 = (bf16[256,2048]{1,0:T(8,128)(2,1)S(1)}, bf16[256,2048]{1,0:T(8,128)(2,1)S(1)}, u32[]{:S(2)}, u32[]{:S(2)}) collective-permute-start(bf16[256,2048]{1,0:T(8,128)(2,1)S(1)} %add_convert_fusion.3), channel_id=1, source_target_pairs={{0,2},{2,0},{1,3},{3,1},{4,6},{6,4},{5,7},{7,5},{8,10},{10,8},{9,1... | collective-permute-start | bytes 3145736 | tf_op jit(solution)/shard_map/ppermute | solution.py:194
  81.7 47.0 %collective-permute-start.8 = (bf16[256,2048]{1,0:T(8,128)(2,1)S(1)}, bf16[256,2048]{1,0:T(8,128)(2,1)S(1)}, u32[]{:S(2)}, u32[]{:S(2)}) collective-permute-start(bf16[256,2048]{1,0:T(8,128)(2,1)S(1)} %add_convert_fusion.2), channel_id=1, source_target_pairs={{0,2},{2,0},{1,3},{3,1},{4,6},{6,4},{5,7},{7,5},{8,10},{10,8},{9,1... | collective-permute-start | bytes 3145736 | tf_op jit(solution)/shard_map/ppermute | solution.py:194
  82.2 68.4 %collective-permute-start.9 = (bf16[256,2048]{1,0:T(8,128)(2,1)S(1)}, bf16[256,2048]{1,0:T(8,128)(2,1)S(1)}, u32[]{:S(2)}, u32[]{:S(2)}) collective-permute-start(bf16[256,2048]{1,0:T(8,128)(2,1)S(1)} %add_convert_fusion.1), channel_id=1, source_target_pairs={{0,2},{2,0},{1,3},{3,1},{4,6},{6,4},{5,7},{7,5},{8,10},{10,8},{9,1... | collective-permute-start | bytes 3145736 | tf_op jit(solution)/shard_map/ppermute | solution.py:194

commit v17 on v13

--- a/solution.py
+++ b/solution.py
@@ -246,6 +246,9 @@
     def block_of(part, owner_tc):
         return lax.dynamic_slice_in_dim(part, owner_tc * block, block, axis=0)
 
+    partner_part = product(block_of(near_rows, 1 - tc))
+    partner_part, far_rows = lax.optimization_barrier((partner_part, far_rows))
+    near = swap(partner_part, "tc")
     chunk = width // COLUMN_CHUNKS
     chip_sums = []
     for c in range(COLUMN_CHUNKS):
@@ -257,7 +260,6 @@
         chip_sums.append(chip_sum.astype(jnp.bfloat16))
     chip_sums, near_rows = lax.optimization_barrier((chip_sums, near_rows))
     across = [swap(chip_sum, "ty") for chip_sum in chip_sums]
-    near = swap(product(block_of(near_rows, 1 - tc)), "tc")
     mine = lax.optimization_barrier(product(block_of(near_rows, tc)))
     far = jnp.concatenate(across, axis=1)
     total = mine.astype(jnp.float32) + near.astype(jnp.float32) + far.astype(jnp.float32)

time: 152 us -> 163 us (1.072)
  local copies, waits for them, and re-layouts: 1.04 us -> 7.94 us
  other arithmetic: 5.17 us -> 9.19 us
  waiting for transfers between devices: 70.8 us -> 69 us
  matrix products: 29.2 us -> 30.9 us
    dot_general x2, matrix products: 14.4 us -> 21.6 us  [product(): jnp.dot(rows, out_weight, preferred_element_type=jnp.float32)]
    dot_general x3, matrix products: 14.9 us -> 9.25 us  [project_and_reduce(): jnp.dot(far_rows, out_weight[:, c * chunk:(c + 1) * chunk], preferred_ele...]
    convert_element_type x3, other arithmetic: 1.35 us -> 5.38 us  [project_and_reduce(): chip_sums.append(chip_sum.astype(jnp.bfloat16))]
    dynamic_slice x3, local copies, waits for them, and re-layouts: 0.32 us -> 3.65 us  [block_of(): return lax.dynamic_slice_in_dim(part, owner_tc * block, block, axis=0)]
    dynamic_slice x1, local copies, waits for them, and re-layouts: 0.09 us -> 3.1 us  [project_and_reduce(): near_rows = lax.dynamic_slice_in_dim(mixed_rows, ty * pair, pair, axis=0)]
    ppermute x7, waiting for transfers between devices: 58.5 us -> 56.8 us  [swap(): return lax.ppermute(block, axis, [(0, 1), (1, 0)])]
  transfers between devices with their start and end apart: 10 -> 10, of which waited for: 7 -> 6; matrix products, arithmetic and copies ran while one was open for 10% -> 14% of each run, Pallas kernels for 14% -> 13%
where the time goes in v17:
time: 163 us; the launch traced here: 162 us
  waiting for transfers between devices  69 us (42%)
  Pallas kernels  33.9 us (21%)
  matrix products  30.9 us (19%)
  starting transfers between devices  10.7 us (7%)
  other arithmetic  9.19 us (6%)
  local copies, waits for them, and re-layouts  7.94 us (5%)
    ppermute x7, waiting for transfers between devices, swap(): return lax.ppermute(block, axis, [(0, 1), (1, 0)])  56.8 us
    dot_general x2, matrix products, product(): jnp.dot(rows, out_weight, preferred_element_type=jnp.float32)  21.6 us
    pallas_call x2, Pallas kernels, local_attention(): pl.pallas_call(local_kernel, grid=(heads,), in_specs=[picked] * 3, out_sp...  15.2 us
    ppermute x3, waiting for transfers between devices, shift(): lax.ppermute(block, axis, [(i, i + distance) for i in range(size) if i +...  12.2 us
    dot_general x3, matrix products, project_and_reduce(): jnp.dot(far_rows, out_weight[:, c * chunk:(c + 1) * chunk], preferred_ele...  9.25 us
    pallas_call x1, Pallas kernels, mix(): pl.pallas_call(mix_kernel, grid=(tokens // ROW_TILE,), in_specs=[row_bloc...  6.76 us
    ppermute x3, starting transfers between devices, shift(): lax.ppermute(block, axis, [(i, i + distance) for i in range(size) if i +...  6.28 us
    pallas_call x1, Pallas kernels, query_and_gate(): pl.pallas_call(gate_kernel, grid=(tokens // ROW_TILE,), in_specs=[row_blo...  6.24 us
  transfers between devices with their start and end apart: 10, of which 6 were waited for; matrix products, arithmetic and copies ran while one was open for 14% of the time, Pallas kernels for 13%

profile of v17, /device:TPU:24, one launch (start us, length us, event | category | flops | bytes accessed | tf_op | source)
XLA Modules:
  0.0 161.9 jit_solution(10634338221725297852)
XLA Ops:
  0.0 5.7 %shard_map.64 = (f32[10,128,128]{2,1,0:T(8,128)}, bf16[10,128,128]{2,1,0:T(8,128)(2,1)}) custom-call(bf16[1024,1280]{1,0:T(8,128)(2,1)} %k_ref.3, bf16[1024,1280]{1,0:T(8,128)(2,1)} %v_ref.3), custom_call_target="tpu_custom_call" | custom-call | flops 335544320 | bytes 5898240 | tf_op jit(solution)/shard_map/pallas_call | solution.py:54
  5.7 3.5 %collective-permute-start = (bf16[10,128,128]{2,1,0:T(8,128)(2,1)}, bf16[10,128,128]{2,1,0:T(8,128)(2,1)S(1)}, u32[]{:S(2)}, u32[]{:S(2)}) collective-permute-start(bf16[10,128,128]{2,1,0:T(8,128)(2,1)} %get-tuple-element.31), channel_id=1, source_target_pairs={{0,4},{4,8},{8,12},{12,16},{16,20},{20,24},{24,28},{1,5},{5,9},{9,... | collective-permute-start | bytes 983048 | tf_op jit(solution)/shard_map/ppermute | solution.py:190
  9.2 7.6 %shard_map.65.local_a_ref = bf16[1024,640]{1,0:T(8,128)(2,1)} custom-call(bf16[1024,1280]{1,0:T(8,128)(2,1)} %q_ref.2, bf16[1024,1280]{1,0:T(8,128)(2,1)} %k_ref.3, bf16[1024,1280]{1,0:T(8,128)(2,1)} %v_ref.3), custom_call_target="tpu_custom_call" | custom-call | flops 1677721600 | bytes 6553600 | tf_op jit(solution)/shard_map/pallas_call | solution.py:97
  19.6 7.6 %shard_map.66.local_b_ref = bf16[1024,640]{1,0:T(8,128)(2,1)} custom-call(bf16[1024,1280]{1,0:T(8,128)(2,1)} %q_ref.2, bf16[1024,1280]{1,0:T(8,128)(2,1)} %k_ref.3, bf16[1024,1280]{1,0:T(8,128)(2,1)} %v_ref.3), custom_call_target="tpu_custom_call" | custom-call | flops 1677721600 | bytes 6553600 | tf_op jit(solution)/shard_map/pallas_call | solution.py:97
  27.3 1.6 collective-permute-done.1
  29.0 1.5 collective-permute-start.2
  31.1 6.2 %shard_map.67 = (bf16[1024,1280]{1,0:T(8,128)(2,1)}, bf16[1024,1280]{1,0:T(8,128)(2,1)}) custom-call(bf16[1024,1280]{1,0:T(8,128)(2,1)} %q_ref.2, bf16[1024,1280]{1,0:T(8,128)(2,1)} %g_ref, f32[1,1280]{1,0:T(1,128)} %reshape.3.gain_ref), custom_call_target="tpu_custom_call" | custom-call | flops 10485760 | bytes 13107200 | tf_op jit(solution)/shard_map/pallas_call | solution.py:119
  37.3 9.2 %collective-permute-done.2 = bf16[10,128,128]{2,1,0:T(8,128)(2,1)S(1)} collective-permute-done((bf16[10,128,128]{2,1,0:T(8,128)(2,1)S(1)}, bf16[10,128,128]{2,1,0:T(8,128)(2,1)S(1)}, u32[]{:S(2)}, u32[]{:S(2)}) %collective-permute-start.2) | collective-permute-done | bytes 327712 | tf_op jit(solution)/shard_map/ppermute | solution.py:190
  47.5 6.8 %shard_map.68 = bf16[1024,1280]{1,0:T(8,128)(2,1)} custom-call(bf16[1024,640]{1,0:T(8,128)(2,1)} %shard_map.65.local_a_ref, bf16[1024,640]{1,0:T(8,128)(2,1)} %shard_map.66.local_b_ref, bf16[1024,1280]{1,0:T(8,128)(2,1)} %get-tuple-element.48.q_ref, bf16[1024,1280]{1,0:T(8,128)(2,1)} %get-tuple-element.49.scale_ref, f32[10,128,128]{2,1,0:T(8,128)} %fusion.16.prefix_ref), custom_call_target="tpu_custom_call" | custom-call | flops 671088640 | bytes 15728640 | tf_op jit(solution)/shard_map/pallas_call | solution.py:162
  54.3 3.1 %constant_dynamic-slice_fusion = (bf16[512,1280]{1,0:T(8,128)(2,1)}, bf16[512,1280]{1,0:T(8,128)(2,1)S(1)}) fusion(bf16[1024,1280]{1,0:T(8,128)(2,1)} %shard_map.68, s32[]{:T(128)S(6)} %select_n.24, s32[]{:T(128)S(6)} %select_n.26), kind=kLoop, calls=%fused_computation.24 | loop fusion | bytes 5242888 | tf_op jit(solution)/shard_map/dynamic_slice | solution.py:244
  57.4 11.7 %convolution_convert_fusion.1 = bf16[256,6144]{1,0:T(8,128)(2,1)} fusion(bf16[1280,6144]{1,0:T(8,128)(2,1)} %param.11, bf16[1024,1280]{1,0:T(8,128)(2,1)} %shard_map.68, s32[]{:T(128)S(6)} %dynamic_slice.33), kind=kOutput, calls=%fused_computation.1 | convolution fusion | flops 4028104704 | bytes 19529732 | tf_op jit(solution)/shard_map/dot_general | solution.py:228
  69.2 3.1 %fusion.6 = bf16[512,2048]{1,0:T(8,128)(2,1)S(1)} fusion(bf16[512,1280]{1,0:T(8,128)(2,1)S(1)} %get-tuple-element.51, bf16[1280,6144]{1,0:T(8,128)(2,1)S(1)} %bitcast.6), kind=kOutput, calls=%fused_computation.9 | convolution fusion | flops 2685403136 | bytes 8650752 | tf_op jit(solution)/shard_map/dot_general | solution.py:255
  72.3 3.1 %fusion.9 = bf16[512,2048]{1,0:T(8,128)(2,1)S(1)} fusion(bf16[512,1280]{1,0:T(8,128)(2,1)S(1)} %get-tuple-element.51, bf16[1280,6144]{1,0:T(8,128)(2,1)S(1)} %bitcast.6), kind=kOutput, calls=%fused_computation.10 | convolution fusion | flops 2685403136 | bytes 8650752 | tf_op jit(solution)/shard_map/dot_general | solution.py:255
  78.4 3.1 %fusion.12 = bf16[512,2048]{1,0:T(8,128)(2,1)S(1)} fusion(bf16[512,1280]{1,0:T(8,128)(2,1)S(1)} %get-tuple-element.51, bf16[1280,6144]{1,0:T(8,128)(2,1)S(1)} %bitcast.6), kind=kOutput, calls=%fused_computation.11 | convolution fusion | flops 2685403136 | bytes 8650752 | tf_op jit(solution)/shard_map/dot_general | solution.py:255
  83.4 2.1 %add_convert_fusion.3 = bf16[256,2048]{1,0:T(8,128)(2,1)S(1)} fusion(bf16[256,2048]{1,0:T(8,128)(2,1)} %collective-permute-done.3, bf16[512,2048]{1,0:T(8,128)(2,1)} %copy-done.3, s32[]{:T(128)S(6)} %select_n.27), kind=kLoop, calls=%fused_computation.14 | loop fusion | flops 2097152 | bytes 3145732 | tf_op jit(solution)/shard_map/convert_element_type | solution.py:260
  85.6 1.7 %add_convert_fusion.2 = bf16[256,2048]{1,0:T(8,128)(2,1)S(1)} fusion(bf16[256,2048]{1,0:T(8,128)(2,1)} %collective-permute-done.4, bf16[512,2048]{1,0:T(8,128)(2,1)S(1)} %copy-done.2, s32[]{:T(128)S(6)} %select_n.27), kind=kLoop, calls=%fused_computation.13 | loop fusion | flops 2097152 | bytes 3145732 | tf_op jit(solution)/shard_map/convert_element_type | solution.py:260
  87.4 1.6 add_convert_fusion.1
  89.0 1.6 collective-permute-start.9
  91.1 1.5 collective-permute-start.7
  92.6 9.9 %convolution_convert_fusion = bf16[256,6144]{1,0:T(8,128)(2,1)S(1)} fusion(bf16[1280,6144]{1,0:T(8,128)(2,1)} %param.11, bf16[512,1280]{1,0:T(8,128)(2,1)S(1)} %copy-done.6, s32[]{:T(128)S(6)} %select_n.27), kind=kOutput, calls=%fused_computation | convolution fusion | flops 4028104704 | bytes 19529732 | tf_op jit(solution)/shard_map/dot_general | solution.py:228
  102.5 12.6 %collective-permute-done.9 = bf16[256,2048]{1,0:T(8,128)(2,1)S(1)} collective-permute-done((bf16[256,2048]{1,0:T(8,128)(2,1)S(1)}, bf16[256,2048]{1,0:T(8,128)(2,1)S(1)}, u32[]{:S(2)}, u32[]{:S(2)}) %collective-permute-start.9) | collective-permute-done | bytes 1048608 | tf_op jit(solution)/shard_map/ppermute | solution.py:194
  115.1 22.5 %collective-permute-done.8 = bf16[256,2048]{1,0:T(8,128)(2,1)S(1)} collective-permute-done((bf16[256,2048]{1,0:T(8,128)(2,1)S(1)}, bf16[256,2048]{1,0:T(8,128)(2,1)S(1)}, u32[]{:S(2)}, u32[]{:S(2)}) %collective-permute-start.8) | collective-permute-done | bytes 1048608 | tf_op jit(solution)/shard_map/ppermute | solution.py:194
  137.5 21.8 %collective-permute-done.7 = bf16[256,2048]{1,0:T(8,128)(2,1)S(1)} collective-permute-done((bf16[256,2048]{1,0:T(8,128)(2,1)S(1)}, bf16[256,2048]{1,0:T(8,128)(2,1)S(1)}, u32[]{:S(2)}, u32[]{:S(2)}) %collective-permute-start.7) | collective-permute-done | bytes 1048608 | tf_op jit(solution)/shard_map/ppermute | solution.py:194
  159.3 2.6 %add_convert_fusion = bf16[256,6144]{1,0:T(8,128)(2,1)} fusion(bf16[256,6144]{1,0:T(8,128)(2,1)S(1)} %collective-permute-done.6, bf16[256,6144]{1,0:T(8,128)(2,1)S(1)} %convolution_convert_fusion, bf16[256,2048]{1,0:T(8,128)(2,1)S(1)} %collective-permute-done.9, bf16[256,2048]{1,0:T(8,128)(2,1)S(1)} %collective-permute-done.8, ...), kind=kLoop, calls=%fused_computation.2 | loop fusion | flops 17301504 | bytes 12582912 | tf_op jit(solution)/shard_map/convert_element_type | solution.py:266
  (43 shorter events, 10.2 us)
Async XLA Ops:
  5.7 12.6 %copy-start = (f32[10,128,128]{2,1,0:T(8,128)S(1)}, f32[10,128,128]{2,1,0:T(8,128)}, u32[]{:S(2)}) copy-start(f32[10,128,128]{2,1,0:T(8,128)} %get-tuple-element.36) | copy-start | bytes 1966084
  5.7 12.6 %collective-permute-start = (bf16[10,128,128]{2,1,0:T(8,128)(2,1)}, bf16[10,128,128]{2,1,0:T(8,128)(2,1)S(1)}, u32[]{:S(2)}, u32[]{:S(2)}) collective-permute-start(bf16[10,128,128]{2,1,0:T(8,128)(2,1)} %get-tuple-element.31), channel_id=1, source_target_pairs={{0,4},{4,8},{8,12},{12,16},{16,20},{20,24},{24,28},{1,5},{5,9},{9,... | collective-permute-start | bytes 983048 | tf_op jit(solution)/shard_map/ppermute | solution.py:190
  18.3 12.1 %copy-start.7 = (f32[1280]{0:T(1024)S(1)}, f32[1280]{0:T(1024)}, u32[]{:S(2)}) copy-start(f32[1280]{0:T(1024)} %param.10) | copy-start | bytes 15364
  18.3 10.5 %collective-permute-start.1 = (bf16[10,128,128]{2,1,0:T(8,128)(2,1)S(1)}, bf16[10,128,128]{2,1,0:T(8,128)(2,1)S(1)}, u32[]{:S(2)}, u32[]{:S(2)}) collective-permute-start(bf16[10,128,128]{2,1,0:T(8,128)(2,1)S(1)} %fusion.19), channel_id=1, source_target_pairs={{0,8},{4,12},{8,16},{12,20},{16,24},{20,28},{1,9},{5,13},{9,17},{1... | collective-permute-start | bytes 983048 | tf_op jit(solution)/shard_map/ppermute | solution.py:190
  29.0 17.6 %collective-permute-start.2 = (bf16[10,128,128]{2,1,0:T(8,128)(2,1)S(1)}, bf16[10,128,128]{2,1,0:T(8,128)(2,1)S(1)}, u32[]{:S(2)}, u32[]{:S(2)}) collective-permute-start(bf16[10,128,128]{2,1,0:T(8,128)(2,1)S(1)} %fusion.15), channel_id=1, source_target_pairs={{0,16},{4,20},{8,24},{12,28},{1,17},{5,21},{9,25},{13,29},{2,18},{... | collective-permute-start | bytes 983048 | tf_op jit(solution)/shard_map/ppermute | solution.py:190
  54.3 14.8 %slice-start = ((s8[15728640]{0:T(1024)(128)(4,1)}), s8[4194304]{0:T(1024)(128)(4,1)S(1)}, s32[]{:S(2)}) async-start(s8[15728640]{0:T(1024)(128)(4,1)} %bitcast.5), calls=%async_computation | async-start | bytes 8388608
  57.4 11.7 %slice-start.1 = ((s8[15728640]{0:T(1024)(128)(4,1)}), s8[4194304]{0:T(1024)(128)(4,1)S(1)}, s32[]{:S(2)}) async-start(s8[15728640]{0:T(1024)(128)(4,1)} %bitcast.5), calls=%async_computation.1 | async-start | bytes 8388608
  57.4 11.7 %slice-start.2 = ((s8[15728640]{0:T(1024)(128)(4,1)}), s8[4194304]{0:T(1024)(128)(4,1)S(1)}, s32[]{:S(2)}) async-start(s8[15728640]{0:T(1024)(128)(4,1)} %bitcast.5), calls=%async_computation.2 | async-start | bytes 8388608
  57.4 11.7 %slice-start.3 = ((s8[15728640]{0:T(1024)(128)(4,1)}), s8[3145728]{0:T(1024)(128)(4,1)S(1)}, s32[]{:S(2)}) async-start(s8[15728640]{0:T(1024)(128)(4,1)} %bitcast.5), calls=%async_computation.3 | async-start | bytes 6291456
  72.3 3.2 %copy-start.3 = (bf16[512,2048]{1,0:T(8,128)(2,1)}, bf16[512,2048]{1,0:T(8,128)(2,1)S(1)}, u32[]{:S(2)}) copy-start(bf16[512,2048]{1,0:T(8,128)(2,1)S(1)} %fusion.6) | copy-start | bytes 6291460
  75.4 6.1 %copy-start.1 = (bf16[512,2048]{1,0:T(8,128)(2,1)}, bf16[512,2048]{1,0:T(8,128)(2,1)S(1)}, u32[]{:S(2)}) copy-start(bf16[512,2048]{1,0:T(8,128)(2,1)S(1)} %fusion.9) | copy-start | bytes 6291460
  75.4 83.9 %collective-permute-start.6 = (bf16[256,6144]{1,0:T(8,128)(2,1)}, bf16[256,6144]{1,0:T(8,128)(2,1)S(1)}, u32[]{:S(2)}, u32[]{:S(2)}) collective-permute-start(bf16[256,6144]{1,0:T(8,128)(2,1)} %convolution_convert_fusion.1), channel_id=1, source_target_pairs={{0,1},{1,0},{2,3},{3,2},{4,5},{5,4},{6,7},{7,6},{8,9},{9,8},{10,11... | collective-permute-start | bytes 9437192 | tf_op jit(solution)/shard_map/ppermute | solution.py:194
  76.8 6.7 %collective-permute-start.3 = (bf16[256,2048]{1,0:T(8,128)(2,1)}, bf16[256,2048]{1,0:T(8,128)(2,1)}, u32[]{:S(2)}, u32[]{:S(2)}) collective-permute-start(bf16[256,2048]{1,0:T(8,128)(2,1)} %constant_dynamic-slice_fusion.3), channel_id=1, source_target_pairs={{0,1},{1,0},{2,3},{3,2},{4,5},{5,4},{6,7},{7,6},{8,9},{9,8},{10,11... | collective-permute-start | bytes 3145736 | tf_op jit(solution)/shard_map/ppermute | solution.py:194
  78.1 7.4 %collective-permute-start.4 = (bf16[256,2048]{1,0:T(8,128)(2,1)}, bf16[256,2048]{1,0:T(8,128)(2,1)}, u32[]{:S(2)}, u32[]{:S(2)}) collective-permute-start(bf16[256,2048]{1,0:T(8,128)(2,1)} %constant_dynamic-slice_fusion.2), channel_id=1, source_target_pairs={{0,1},{1,0},{2,3},{3,2},{4,5},{5,4},{6,7},{7,6},{8,9},{9,8},{10,11... | collective-permute-start | bytes 3145736 | tf_op jit(solution)/shard_map/ppermute | solution.py:194
  81.5 1.7 %copy-start.4 = (bf16[512,2048]{1,0:T(8,128)(2,1)}, bf16[512,2048]{1,0:T(8,128)(2,1)S(1)}, u32[]{:S(2)}) copy-start(bf16[512,2048]{1,0:T(8,128)(2,1)S(1)} %fusion.12) | copy-start | bytes 6291460
  83.2 4.2 %collective-permute-start.5 = (bf16[256,2048]{1,0:T(8,128)(2,1)}, bf16[256,2048]{1,0:T(8,128)(2,1)}, u32[]{:S(2)}, u32[]{:S(2)}) collective-permute-start(bf16[256,2048]{1,0:T(8,128)(2,1)} %constant_dynamic-slice_fusion.1), channel_id=1, source_target_pairs={{0,1},{1,0},{2,3},{3,2},{4,5},{5,4},{6,7},{7,6},{8,9},{9,8},{10,11... | collective-permute-start | bytes 3145736 | tf_op jit(solution)/shard_map/ppermute | solution.py:194
  83.4 2.2 %copy-start.2 = (bf16[512,2048]{1,0:T(8,128)(2,1)S(1)}, bf16[512,2048]{1,0:T(8,128)(2,1)}, u32[]{:S(2)}) copy-start(bf16[512,2048]{1,0:T(8,128)(2,1)} %copy-done.1) | copy-start | bytes 6291460
  83.4 3.9 %copy-start.5 = (bf16[512,2048]{1,0:T(8,128)(2,1)S(1)}, bf16[512,2048]{1,0:T(8,128)(2,1)}, u32[]{:S(2)}) copy-start(bf16[512,2048]{1,0:T(8,128)(2,1)} %copy-done.4) | copy-start | bytes 6291460
  85.5 7.1 %copy-start.6 = (bf16[512,1280]{1,0:T(8,128)(2,1)S(1)}, bf16[512,1280]{1,0:T(8,128)(2,1)}, u32[]{:S(2)}) copy-start(bf16[512,1280]{1,0:T(8,128)(2,1)} %get-tuple-element.52) | copy-start | bytes 3932164
  89.0 26.1 %collective-permute-start.9 = (bf16[256,2048]{1,0:T(8,128)(2,1)S(1)}, bf16[256,2048]{1,0:T(8,128)(2,1)S(1)}, u32[]{:S(2)}, u32[]{:S(2)}) collective-permute-start(bf16[256,2048]{1,0:T(8,128)(2,1)S(1)} %add_convert_fusion.1), channel_id=1, source_target_pairs={{0,2},{2,0},{1,3},{3,1},{4,6},{6,4},{5,7},{7,5},{8,10},{10,8},{9,1... | collective-permute-start | bytes 3145736 | tf_op jit(solution)/shard_map/ppermute | solution.py:194
  90.6 47.0 %collective-permute-start.8 = (bf16[256,2048]{1,0:T(8,128)(2,1)S(1)}, bf16[256,2048]{1,0:T(8,128)(2,1)S(1)}, u32[]{:S(2)}, u32[]{:S(2)}) collective-permute-start(bf16[256,2048]{1,0:T(8,128)(2,1)S(1)} %add_convert_fusion.2), channel_id=1, source_target_pairs={{0,2},{2,0},{1,3},{3,1},{4,6},{6,4},{5,7},{7,5},{8,10},{10,8},{9,1... | collective-permute-start | bytes 3145736 | tf_op jit(solution)/shard_map/ppermute | solution.py:194
  91.1 68.2 %collective-permute-start.7 = (bf16[256,2048]{1,0:T(8,128)(2,1)S(1)}, bf16[256,2048]{1,0:T(8,128)(2,1)S(1)}, u32[]{:S(2)}, u32[]{:S(2)}) collective-permute-start(bf16[256,2048]{1,0:T(8,128)(2,1)S(1)} %add_convert_fusion.3), channel_id=1, source_target_pairs={{0,2},{2,0},{1,3},{3,1},{4,6},{6,4},{5,7},{7,5},{8,10},{10,8},{9,1... | collective-permute-start | bytes 3145736 | tf_op jit(solution)/shard_map/ppermute | solution.py:194

commit v18 on v13

--- a/solution.py
+++ b/solution.py
@@ -201,7 +201,9 @@
     results = []
     while distance < lax.axis_size(axis):
         sent = inclusive.astype(jnp.bfloat16) if distance > 1 or sent_first is None else sent_first
-        arrived = shift(sent, axis, distance)
+        size = lax.axis_size(axis)
+        arrived = lax.ppermute(sent, axis, [(i, (i + distance) % size) for i in range(size)])
+        arrived = jnp.where(lax.axis_index(axis) >= distance, arrived, jnp.zeros_like(arrived))
         if len(results) < len(fillers):
             function, operands = fillers[len(results)]
             _, operands = lax.optimization_barrier((sent, operands))

time: 152 us -> 150 us (0.987)
  the two profiles are of different devices: /device:TPU:24 before, /device:TPU:0 now
where the time goes in v18:
time: 150 us
  waiting for transfers between devices  72.8 us (49%)
  Pallas kernels  33.9 us (23%)
  matrix products  29.2 us (19%)
  starting transfers between devices  7.39 us (5%)
  other arithmetic  5.25 us (4%)
    ppermute x7, waiting for transfers between devices, swap(): return lax.ppermute(block, axis, [(0, 1), (1, 0)])  58.7 us
    pallas_call x2, Pallas kernels, local_attention(): pl.pallas_call(local_kernel, grid=(heads,), in_specs=[picked] * 3, out_sp...  15.3 us
    dot_general x3, matrix products, project_and_reduce(): jnp.dot(far_rows, out_weight[:, c * chunk:(c + 1) * chunk], preferred_ele...  14.8 us
    dot_general x2, matrix products, product(): jnp.dot(rows, out_weight, preferred_element_type=jnp.float32)  14.4 us
    ppermute x3, waiting for transfers between devices, exclusive_prefix(): lax.ppermute(sent, axis, [(i, (i + distance) % size) for i in range(size)])  14.1 us
    pallas_call x1, Pallas kernels, mix(): pl.pallas_call(mix_kernel, grid=(tokens // ROW_TILE,), in_specs=[row_bloc...  6.76 us
    pallas_call x1, Pallas kernels, query_and_gate(): pl.pallas_call(gate_kernel, grid=(tokens // ROW_TILE,), in_specs=[row_blo...  6.22 us
    pallas_call x1, Pallas kernels, key_value_states(): pl.pallas_call(state_kernel, grid=(tokens // ROW_TILE,), in_specs=[row_bl...  5.64 us
  transfers between devices with their start and end apart: 10, of which 7 were waited for; matrix products, arithmetic and copies ran while one was open for 10% of the time, Pallas kernels for 14%

profile of v18, /device:TPU:0, one launch (start us, length us, event | category | flops | bytes accessed | tf_op | source)
XLA Modules:
  0.0 149.9 jit_solution(2954006993694611856)
XLA Ops:
  0.0 5.6 %shard_map.64 = (f32[10,128,128]{2,1,0:T(8,128)}, bf16[10,128,128]{2,1,0:T(8,128)(2,1)}) custom-call(bf16[1024,1280]{1,0:T(8,128)(2,1)} %k_ref.3, bf16[1024,1280]{1,0:T(8,128)(2,1)} %v_ref.3), custom_call_target="tpu_custom_call" | custom-call | flops 335544320 | bytes 5898240 | tf_op jit(solution)/shard_map/pallas_call | solution.py:54
  5.6 3.0 %collective-permute-start = (bf16[10,128,128]{2,1,0:T(8,128)(2,1)}, bf16[10,128,128]{2,1,0:T(8,128)(2,1)S(1)}, u32[]{:S(2)}, u32[]{:S(2)}) collective-permute-start(bf16[10,128,128]{2,1,0:T(8,128)(2,1)} %get-tuple-element.29), channel_id=1, source_target_pairs={{0,4},{4,8},{8,12},{12,16},{16,20},{20,24},{24,28},{28,0},{1,5},{5... | collective-permute-start | bytes 983048 | tf_op jit(solution)/shard_map/ppermute | solution.py:205
  8.6 7.7 %shard_map.65.local_a_ref = bf16[1024,640]{1,0:T(8,128)(2,1)} custom-call(bf16[1024,1280]{1,0:T(8,128)(2,1)} %q_ref.2, bf16[1024,1280]{1,0:T(8,128)(2,1)} %k_ref.3, bf16[1024,1280]{1,0:T(8,128)(2,1)} %v_ref.3), custom_call_target="tpu_custom_call" | custom-call | flops 1677721600 | bytes 6553600 | tf_op jit(solution)/shard_map/pallas_call | solution.py:97
  16.3 3.3 %collective-permute-done = bf16[10,128,128]{2,1,0:T(8,128)(2,1)S(1)} collective-permute-done((bf16[10,128,128]{2,1,0:T(8,128)(2,1)}, bf16[10,128,128]{2,1,0:T(8,128)(2,1)S(1)}, u32[]{:S(2)}, u32[]{:S(2)}) %collective-permute-start) | collective-permute-done | bytes 327712 | tf_op jit(solution)/shard_map/ppermute | solution.py:205
  19.8 7.6 %shard_map.66.local_b_ref = bf16[1024,640]{1,0:T(8,128)(2,1)} custom-call(bf16[1024,1280]{1,0:T(8,128)(2,1)} %q_ref.2, bf16[1024,1280]{1,0:T(8,128)(2,1)} %k_ref.3, bf16[1024,1280]{1,0:T(8,128)(2,1)} %v_ref.3), custom_call_target="tpu_custom_call" | custom-call | flops 1677721600 | bytes 6553600 | tf_op jit(solution)/shard_map/pallas_call | solution.py:97
  27.4 3.0 %collective-permute-done.1 = bf16[10,128,128]{2,1,0:T(8,128)(2,1)S(1)} collective-permute-done((bf16[10,128,128]{2,1,0:T(8,128)(2,1)S(1)}, bf16[10,128,128]{2,1,0:T(8,128)(2,1)S(1)}, u32[]{:S(2)}, u32[]{:S(2)}) %collective-permute-start.1) | collective-permute-done | bytes 327712 | tf_op jit(solution)/shard_map/ppermute | solution.py:205
  30.7 0.6 reshape.3.gain_ref
  31.3 6.2 %shard_map.67 = (bf16[1024,1280]{1,0:T(8,128)(2,1)}, bf16[1024,1280]{1,0:T(8,128)(2,1)}) custom-call(bf16[1024,1280]{1,0:T(8,128)(2,1)} %q_ref.2, bf16[1024,1280]{1,0:T(8,128)(2,1)} %g_ref, f32[1,1280]{1,0:T(1,128)} %reshape.3.gain_ref), custom_call_target="tpu_custom_call" | custom-call | flops 10485760 | bytes 13107200 | tf_op jit(solution)/shard_map/pallas_call | solution.py:119
  37.5 7.8 %collective-permute-done.2 = bf16[10,128,128]{2,1,0:T(8,128)(2,1)S(1)} collective-permute-done((bf16[10,128,128]{2,1,0:T(8,128)(2,1)S(1)}, bf16[10,128,128]{2,1,0:T(8,128)(2,1)S(1)}, u32[]{:S(2)}, u32[]{:S(2)}) %collective-permute-start.2) | collective-permute-done | bytes 327712 | tf_op jit(solution)/shard_map/ppermute | solution.py:205
  45.3 1.0 fusion.19.prefix_ref
  46.4 6.8 %shard_map.68 = bf16[1024,1280]{1,0:T(8,128)(2,1)} custom-call(bf16[1024,640]{1,0:T(8,128)(2,1)} %shard_map.65.local_a_ref, bf16[1024,640]{1,0:T(8,128)(2,1)} %shard_map.66.local_b_ref, bf16[1024,1280]{1,0:T(8,128)(2,1)} %get-tuple-element.46.q_ref, bf16[1024,1280]{1,0:T(8,128)(2,1)} %get-tuple-element.47.scale_ref, f32[10,128,128]{2,1,0:T(8,128)} %fusion.19.prefix_ref), custom_call_target="tpu_custom_call" | custom-call | flops 671088640 | bytes 15728640 | tf_op jit(solution)/shard_map/pallas_call | solution.py:162
  53.2 5.9 %fusion.12 = bf16[512,2048]{1,0:T(8,128)(2,1)S(1)} fusion(bf16[1280,6144]{1,0:T(8,128)(2,1)} %param.11, bf16[1024,1280]{1,0:T(8,128)(2,1)} %shard_map.68, s32[]{:T(128)S(6)} %select_n.44), kind=kOutput, calls=%fused_computation.11 | convolution fusion | flops 2685403136 | bytes 8650756 | tf_op jit(solution)/shard_map/dot_general | solution.py:254
  59.1 5.8 %fusion.9 = bf16[512,2048]{1,0:T(8,128)(2,1)S(1)} fusion(bf16[1280,6144]{1,0:T(8,128)(2,1)} %param.11, bf16[1024,1280]{1,0:T(8,128)(2,1)S(1)} %copy-done, s32[]{:T(128)S(6)} %select_n.44), kind=kOutput, calls=%fused_computation.10 | convolution fusion | flops 2685403136 | bytes 8650756 | tf_op jit(solution)/shard_map/dot_general | solution.py:254
  65.8 3.1 %fusion.6 = bf16[512,2048]{1,0:T(8,128)(2,1)S(1)} fusion(bf16[1280,6144]{1,0:T(8,128)(2,1)S(1)} %bitcast.3, bf16[1024,1280]{1,0:T(8,128)(2,1)S(1)} %copy-done, s32[]{:T(128)S(6)} %select_n.44), kind=kOutput, calls=%fused_computation.9 | convolution fusion | flops 2685403136 | bytes 8650756 | tf_op jit(solution)/shard_map/dot_general | solution.py:254
  70.2 1.6 %collective-permute-done.3 = bf16[256,2048]{1,0:T(8,128)(2,1)S(1)} collective-permute-done((bf16[256,2048]{1,0:T(8,128)(2,1)S(1)}, bf16[256,2048]{1,0:T(8,128)(2,1)S(1)}, u32[]{:S(2)}, u32[]{:S(2)}) %collective-permute-start.3) | collective-permute-done | bytes 1048608 | tf_op jit(solution)/shard_map/ppermute | solution.py:194
  72.3 4.4 %convolution_convert_fusion = bf16[256,6144]{1,0:T(8,128)(2,1)S(1)} fusion(bf16[1280,6144]{1,0:T(8,128)(2,1)S(1)} %bitcast.3, bf16[512,1280]{1,0:T(8,128)(2,1)S(1)} %constant_dynamic-slice_fusion, s32[]{:T(128)S(6)} %select_n.46), kind=kOutput, calls=%fused_computation | convolution fusion | flops 4028104704 | bytes 19529732 | tf_op jit(solution)/shard_map/dot_general | solution.py:230
  76.9 1.3 collective-permute-start.7
  78.2 0.7 collective-permute-start.8
  78.9 1.3 collective-permute-start.9
  80.3 9.9 %convolution_convert_fusion.1 = bf16[256,6144]{1,0:T(8,128)(2,1)S(1)} fusion(bf16[1280,6144]{1,0:T(8,128)(2,1)} %param.11, bf16[512,1280]{1,0:T(8,128)(2,1)S(1)} %constant_dynamic-slice_fusion, s32[]{:T(128)S(6)} %select_n.45), kind=kOutput, calls=%fused_computation.1 | convolution fusion | flops 4028104704 | bytes 19529732 | tf_op jit(solution)/shard_map/dot_general | solution.py:230
  90.2 12.7 %collective-permute-done.7 = bf16[256,2048]{1,0:T(8,128)(2,1)S(1)} collective-permute-done((bf16[256,2048]{1,0:T(8,128)(2,1)S(1)}, bf16[256,2048]{1,0:T(8,128)(2,1)S(1)}, u32[]{:S(2)}, u32[]{:S(2)}) %collective-permute-start.7) | collective-permute-done | bytes 1048608 | tf_op jit(solution)/shard_map/ppermute | solution.py:194
  102.9 22.5 %collective-permute-done.8 = bf16[256,2048]{1,0:T(8,128)(2,1)S(1)} collective-permute-done((bf16[256,2048]{1,0:T(8,128)(2,1)S(1)}, bf16[256,2048]{1,0:T(8,128)(2,1)S(1)}, u32[]{:S(2)}, u32[]{:S(2)}) %collective-permute-start.8) | collective-permute-done | bytes 1048608 | tf_op jit(solution)/shard_map/ppermute | solution.py:194
  125.4 21.9 %collective-permute-done.9 = bf16[256,2048]{1,0:T(8,128)(2,1)S(1)} collective-permute-done((bf16[256,2048]{1,0:T(8,128)(2,1)S(1)}, bf16[256,2048]{1,0:T(8,128)(2,1)S(1)}, u32[]{:S(2)}, u32[]{:S(2)}) %collective-permute-start.9) | collective-permute-done | bytes 1048608 | tf_op jit(solution)/shard_map/ppermute | solution.py:194
  147.3 2.6 %add_convert_fusion = bf16[256,6144]{1,0:T(8,128)(2,1)} fusion(bf16[256,6144]{1,0:T(8,128)(2,1)S(1)} %collective-permute-done.6, bf16[256,6144]{1,0:T(8,128)(2,1)S(1)} %convolution_convert_fusion.1, bf16[256,2048]{1,0:T(8,128)(2,1)S(1)} %collective-permute-done.9, bf16[256,2048]{1,0:T(8,128)(2,1)S(1)} %collective-permute-done.8, ...), kind=kLoop, calls=%fused_computation.2 | loop fusion | flops 17301504 | bytes 12582912 | tf_op jit(solution)/shard_map/convert_element_type | solution.py:266
  (36 shorter events, 3.2 us)
Async XLA Ops:
  5.6 13.9 %collective-permute-start = (bf16[10,128,128]{2,1,0:T(8,128)(2,1)}, bf16[10,128,128]{2,1,0:T(8,128)(2,1)S(1)}, u32[]{:S(2)}, u32[]{:S(2)}) collective-permute-start(bf16[10,128,128]{2,1,0:T(8,128)(2,1)} %get-tuple-element.29), channel_id=1, source_target_pairs={{0,4},{4,8},{8,12},{12,16},{16,20},{20,24},{24,28},{28,0},{1,5},{5... | collective-permute-start | bytes 983048 | tf_op jit(solution)/shard_map/ppermute | solution.py:205
  8.6 11.0 %copy-start.1 = (f32[10,128,128]{2,1,0:T(8,128)S(1)}, f32[10,128,128]{2,1,0:T(8,128)}, u32[]{:S(2)}) copy-start(f32[10,128,128]{2,1,0:T(8,128)} %get-tuple-element.34) | copy-start | bytes 1966084
  19.7 10.7 %collective-permute-start.1 = (bf16[10,128,128]{2,1,0:T(8,128)(2,1)S(1)}, bf16[10,128,128]{2,1,0:T(8,128)(2,1)S(1)}, u32[]{:S(2)}, u32[]{:S(2)}) collective-permute-start(bf16[10,128,128]{2,1,0:T(8,128)(2,1)S(1)} %fusion.22), channel_id=1, source_target_pairs={{0,8},{4,12},{8,16},{12,20},{16,24},{20,28},{24,0},{28,4},{1,9},{5... | collective-permute-start | bytes 983048 | tf_op jit(solution)/shard_map/ppermute | solution.py:205
  19.8 10.9 %copy-start.2 = (f32[1280]{0:T(1024)S(1)}, f32[1280]{0:T(1024)}, u32[]{:S(2)}) copy-start(f32[1280]{0:T(1024)} %param.10) | copy-start | bytes 15364
  30.6 14.7 %collective-permute-start.2 = (bf16[10,128,128]{2,1,0:T(8,128)(2,1)S(1)}, bf16[10,128,128]{2,1,0:T(8,128)(2,1)S(1)}, u32[]{:S(2)}, u32[]{:S(2)}) collective-permute-start(bf16[10,128,128]{2,1,0:T(8,128)(2,1)S(1)} %fusion.18), channel_id=1, source_target_pairs={{0,16},{4,20},{8,24},{12,28},{16,0},{20,4},{24,8},{28,12},{1,17},{... | collective-permute-start | bytes 983048 | tf_op jit(solution)/shard_map/ppermute | solution.py:205
  53.1 5.9 %copy-start = (bf16[1024,1280]{1,0:T(8,128)(2,1)S(1)}, bf16[1024,1280]{1,0:T(8,128)(2,1)}, u32[]{:S(2)}) copy-start(bf16[1024,1280]{1,0:T(8,128)(2,1)} %shard_map.68) | copy-start | bytes 7864324
  53.1 12.7 %slice-start = ((s8[15728640]{0:T(1024)(128)(4,1)}), s8[4194304]{0:T(1024)(128)(4,1)S(1)}, s32[]{:S(2)}) async-start(s8[15728640]{0:T(1024)(128)(4,1)} %bitcast.2), calls=%async_computation | async-start | bytes 8388608
  53.1 12.7 %slice-start.1 = ((s8[15728640]{0:T(1024)(128)(4,1)}), s8[4194304]{0:T(1024)(128)(4,1)S(1)}, s32[]{:S(2)}) async-start(s8[15728640]{0:T(1024)(128)(4,1)} %bitcast.2), calls=%async_computation.1 | async-start | bytes 8388608
  59.1 6.7 %slice-start.2 = ((s8[15728640]{0:T(1024)(128)(4,1)}), s8[4194304]{0:T(1024)(128)(4,1)S(1)}, s32[]{:S(2)}) async-start(s8[15728640]{0:T(1024)(128)(4,1)} %bitcast.2), calls=%async_computation.2 | async-start | bytes 8388608
  59.1 6.7 %slice-start.3 = ((s8[15728640]{0:T(1024)(128)(4,1)}), s8[3145728]{0:T(1024)(128)(4,1)S(1)}, s32[]{:S(2)}) async-start(s8[15728640]{0:T(1024)(128)(4,1)} %bitcast.2), calls=%async_computation.3 | async-start | bytes 6291456
  65.0 4.2 %collective-permute-start.5 = (bf16[256,2048]{1,0:T(8,128)(2,1)S(1)}, bf16[256,2048]{1,0:T(8,128)(2,1)S(1)}, u32[]{:S(2)}, u32[]{:S(2)}) collective-permute-start(bf16[256,2048]{1,0:T(8,128)(2,1)S(1)} %constant_dynamic-slice_fusion.1), channel_id=1, source_target_pairs={{0,1},{1,0},{2,3},{3,2},{4,5},{5,4},{6,7},{7,6},{8,9},{9,8},{10,11... | collective-permute-start | bytes 3145736 | tf_op jit(solution)/shard_map/ppermute | solution.py:194
  65.2 4.5 %collective-permute-start.4 = (bf16[256,2048]{1,0:T(8,128)(2,1)S(1)}, bf16[256,2048]{1,0:T(8,128)(2,1)S(1)}, u32[]{:S(2)}, u32[]{:S(2)}) collective-permute-start(bf16[256,2048]{1,0:T(8,128)(2,1)S(1)} %constant_dynamic-slice_fusion.2), channel_id=1, source_target_pairs={{0,1},{1,0},{2,3},{3,2},{4,5},{5,4},{6,7},{7,6},{8,9},{9,8},{10,11... | collective-permute-start | bytes 3145736 | tf_op jit(solution)/shard_map/ppermute | solution.py:194
  69.1 2.7 %collective-permute-start.3 = (bf16[256,2048]{1,0:T(8,128)(2,1)S(1)}, bf16[256,2048]{1,0:T(8,128)(2,1)S(1)}, u32[]{:S(2)}, u32[]{:S(2)}) collective-permute-start(bf16[256,2048]{1,0:T(8,128)(2,1)S(1)} %constant_dynamic-slice_fusion.3), channel_id=1, source_target_pairs={{0,1},{1,0},{2,3},{3,2},{4,5},{5,4},{6,7},{7,6},{8,9},{9,8},{10,11... | collective-permute-start | bytes 3145736 | tf_op jit(solution)/shard_map/ppermute | solution.py:194
  76.7 70.6 %collective-permute-start.6 = (bf16[256,6144]{1,0:T(8,128)(2,1)S(1)}, bf16[256,6144]{1,0:T(8,128)(2,1)S(1)}, u32[]{:S(2)}, u32[]{:S(2)}) collective-permute-start(bf16[256,6144]{1,0:T(8,128)(2,1)S(1)} %convolution_convert_fusion), channel_id=1, source_target_pairs={{0,1},{1,0},{2,3},{3,2},{4,5},{5,4},{6,7},{7,6},{8,9},{9,8},{10,11... | collective-permute-start | bytes 9437192 | tf_op jit(solution)/shard_map/ppermute | solution.py:194
  76.9 26.0 %collective-permute-start.7 = (bf16[256,2048]{1,0:T(8,128)(2,1)S(1)}, bf16[256,2048]{1,0:T(8,128)(2,1)S(1)}, u32[]{:S(2)}, u32[]{:S(2)}) collective-permute-start(bf16[256,2048]{1,0:T(8,128)(2,1)S(1)} %add_convert_fusion.3), channel_id=1, source_target_pairs={{0,2},{2,0},{1,3},{3,1},{4,6},{6,4},{5,7},{7,5},{8,10},{10,8},{9,1... | collective-permute-start | bytes 3145736 | tf_op jit(solution)/shard_map/ppermute | solution.py:194
  78.2 47.2 %collective-permute-start.8 = (bf16[256,2048]{1,0:T(8,128)(2,1)S(1)}, bf16[256,2048]{1,0:T(8,128)(2,1)S(1)}, u32[]{:S(2)}, u32[]{:S(2)}) collective-permute-start(bf16[256,2048]{1,0:T(8,128)(2,1)S(1)} %add_convert_fusion.2), channel_id=1, source_target_pairs={{0,2},{2,0},{1,3},{3,1},{4,6},{6,4},{5,7},{7,5},{8,10},{10,8},{9,1... | collective-permute-start | bytes 3145736 | tf_op jit(solution)/shard_map/ppermute | solution.py:194
  78.9 68.4 %collective-permute-start.9 = (bf16[256,2048]{1,0:T(8,128)(2,1)S(1)}, bf16[256,2048]{1,0:T(8,128)(2,1)S(1)}, u32[]{:S(2)}, u32[]{:S(2)}) collective-permute-start(bf16[256,2048]{1,0:T(8,128)(2,1)S(1)} %add_convert_fusion.1), channel_id=1, source_target_pairs={{0,2},{2,0},{1,3},{3,1},{4,6},{6,4},{5,7},{7,5},{8,10},{10,8},{9,1... | collective-permute-start | bytes 3145736 | tf_op jit(solution)/shard_map/ppermute | solution.py:194

commit v19 on v18

--- a/solution.py
+++ b/solution.py
@@ -68,9 +68,10 @@
     )(keys, values)
 
 
-def local_kernel(q_ref, k_ref, v_ref, out_ref):
+def local_kernel(q_ref, k_ref, v_ref, out_ref, query_act_ref):
     tokens = q_ref.shape[0]
     query_act = silu(q_ref[...])
+    query_act_ref[...] = query_act
     key_act = silu(k_ref[...])
     value_rows = v_ref[...]
     for tile in range(tokens // QUERY_TILE):
@@ -98,8 +99,8 @@
         local_kernel,
         grid=(heads,),
         in_specs=[picked] * 3,
-        out_specs=head_block(tokens),
-        out_shape=jax.ShapeDtypeStruct((tokens, heads * HD), jnp.bfloat16),
+        out_specs=[head_block(tokens), head_block(tokens)],
+        out_shape=[jax.ShapeDtypeStruct((tokens, heads * HD), jnp.bfloat16)] * 2,
         cost_estimate=pl.CostEstimate(
             flops=4 * pairs * HD * heads,
             transcendentals=2 * tokens * heads * HD,
@@ -108,44 +109,41 @@
     )(queries, keys, values)
 
 
-def gate_kernel(q_ref, g_ref, gain_ref, query_act_ref, scale_ref):
-    query_act_ref[...] = silu(q_ref[...])
+def gate_kernel(g_ref, gain_ref, scale_ref):
     gates = g_ref[...].astype(jnp.float32)
     scale_ref[...] = (gain_ref[...] * (1.0 / (1.0 + jnp.exp(-gates)))).astype(scale_ref.dtype)
 
 
-def query_and_gate(queries, gates, gain):
-    tokens, columns = queries.shape
+def gate_scale(gates, gain):
+    tokens, columns = gates.shape
     return pl.pallas_call(
         gate_kernel,
         grid=(tokens // ROW_TILE,),
-        in_specs=[row_block(columns), row_block(columns), pl.BlockSpec((1, columns), lambda i: (0, 0))],
-        out_specs=[row_block(columns), row_block(columns)],
-        out_shape=[
-            jax.ShapeDtypeStruct((tokens, columns), jnp.bfloat16),
-            jax.ShapeDtypeStruct((tokens, columns), jnp.bfloat16),
-        ],
+        in_specs=[row_block(columns), pl.BlockSpec((1, columns), lambda i: (0, 0))],
+        out_specs=row_block(columns),
+        out_shape=jax.ShapeDtypeStruct((tokens, columns), jnp.bfloat16),
         cost_estimate=pl.CostEstimate(
-            flops=8 * tokens * columns,
-            transcendentals=2 * tokens * columns,
-            bytes_accessed=10 * tokens * columns,
-        ),
-    )(queries, gates, gain.reshape(1, columns))
-
-
-def mix_kernel(local_a_ref, local_b_ref, q_ref, scale_ref, prefix_ref, out_ref):
-    query_act = q_ref[...]
+            flops=4 * tokens * columns,
+            transcendentals=tokens * columns,
+            bytes_accessed=4 * tokens * columns,
+        ),
+    )(gates, gain.reshape(1, columns))
+
+
+def mix_kernel(local_a_ref, local_b_ref, qa_a_ref, qa_b_ref, scale_ref, prefix_ref, out_ref):
     first = local_a_ref.shape[1] // HD
     for h in range(prefix_ref.shape[0]):
         heads = slice(h * HD, (h + 1) * HD)
         prefix_hi, prefix_lo = split_bf16(prefix_ref[h])
         if h < first:
             local = local_a_ref[:, heads]
+            query_act = qa_a_ref[:, heads]
         else:
             local = local_b_ref[:, (h - first) * HD:(h - first + 1) * HD]
+            query_act = qa_b_ref[:, (h - first) * HD:(h - first + 1) * HD]
         local = local.astype(jnp.float32)
-        remote = jnp.dot(query_act[:, heads], prefix_hi, preferred_element_type=jnp.float32) + jnp.dot(
-            query_act[:, heads], prefix_lo, preferred_element_type=jnp.float32
+        remote = jnp.dot(query_act, prefix_hi, preferred_element_type=jnp.float32) + jnp.dot(
+            query_act, prefix_lo, preferred_element_type=jnp.float32
         )
         attention = local + remote
         mean_sq = jnp.mean(attention * attention, axis=-1, keepdims=True)
@@ -155,8 +153,8 @@
         )
 
 
-def mix(local_a, local_b, query_act, scale, prefix):
-    tokens, columns = query_act.shape
+def mix(local_a, local_b, qa_a, qa_b, scale, prefix):
+    tokens, columns = scale.shape
     heads = columns // HD
     whole_state = pl.BlockSpec((heads, HD, HD), lambda i: (0, 0, 0))
     return pl.pallas_call(
@@ -165,7 +163,8 @@
         in_specs=[
             row_block(local_a.shape[1]),
             row_block(local_b.shape[1]),
-            row_block(columns),
+            row_block(qa_a.shape[1]),
+            row_block(qa_b.shape[1]),
             row_block(columns),
             whole_state,
         ],
@@ -176,7 +175,7 @@
             transcendentals=tokens * heads,
             bytes_accessed=12 * tokens * columns,
         ),
-    )(local_a, local_b, query_act, scale, prefix)
+    )(local_a, local_b, qa_a, qa_b, scale, prefix)
 
 
 def split_bf16(x):
@@ -273,10 +272,10 @@
     fillers = (
         (lambda q, k, v: local_attention(q, k, v, 0, first), (queries, keys, values)),
         (lambda q, k, v: local_attention(q, k, v, first, head_count - first), (queries, keys, values)),
-        (query_and_gate, (queries, gates, gain)),
+        (gate_scale, (gates, gain)),
     )
-    prefix, (local_a, local_b, (query_act, scale)) = exclusive_prefix(own_state, "ctx", fillers, own_sent)
-    mixed_rows = mix(local_a, local_b, query_act, scale, prefix)
+    prefix, ((local_a, qa_a), (local_b, qa_b), scale) = exclusive_prefix(own_state, "ctx", fillers, own_sent)
+    mixed_rows = mix(local_a, local_b, qa_a, qa_b, scale, prefix)
     return project_and_reduce(mixed_rows, out_weight)
 
 

time: 150 us -> 150 us (level)
  waiting for transfers between devices: 72.8 us -> 74.4 us
  Pallas kernels: 33.9 us -> 32.3 us
    pallas_call x1, Pallas kernels: 6.22 us -> 4.6 us  [gate_scale(): pl.pallas_call(gate_kernel, grid=(tokens // ROW_TILE,), in_specs=[row_blo...]
    ppermute x3, waiting for transfers between devices: 14.1 us -> 15.7 us  [exclusive_prefix(): lax.ppermute(sent, axis, [(i, (i + distance) % size) for i in range(size)])]
  transfers between devices with their start and end apart: 10 -> 10, of which waited for: 7 -> 7; matrix products, arithmetic and copies ran while one was open for 10% -> 10% of each run, Pallas kernels for 14% -> 13%
where the time goes in v19:
time: 150 us
  waiting for transfers between devices  74.4 us (50%)
  Pallas kernels  32.3 us (22%)
  matrix products  29.2 us (19%)
  starting transfers between devices  7.38 us (5%)
  other arithmetic  5.24 us (3%)
    ppermute x7, waiting for transfers between devices, swap(): return lax.ppermute(block, axis, [(0, 1), (1, 0)])  58.7 us
    ppermute x3, waiting for transfers between devices, exclusive_prefix(): lax.ppermute(sent, axis, [(i, (i + distance) % size) for i in range(size)])  15.7 us
    pallas_call x2, Pallas kernels, local_attention(): pl.pallas_call(local_kernel, grid=(heads,), in_specs=[picked] * 3, out_sp...  15.3 us
    dot_general x3, matrix products, project_and_reduce(): jnp.dot(far_rows, out_weight[:, c * chunk:(c + 1) * chunk], preferred_ele...  14.9 us
    dot_general x2, matrix products, product(): jnp.dot(rows, out_weight, preferred_element_type=jnp.float32)  14.4 us
    pallas_call x1, Pallas kernels, mix(): pl.pallas_call(mix_kernel, grid=(tokens // ROW_TILE,), in_specs=[row_bloc...  6.74 us
    pallas_call x1, Pallas kernels, key_value_states(): pl.pallas_call(state_kernel, grid=(tokens // ROW_TILE,), in_specs=[row_bl...  5.64 us
    pallas_call x1, Pallas kernels, gate_scale(): pl.pallas_call(gate_kernel, grid=(tokens // ROW_TILE,), in_specs=[row_blo...  4.6 us
  transfers between devices with their start and end apart: 10, of which 7 were waited for; matrix products, arithmetic and copies ran while one was open for 10% of the time, Pallas kernels for 13%

profile of v19, /device:TPU:0, one launch (start us, length us, event | category | flops | bytes accessed | tf_op | source)
XLA Modules:
  0.0 149.8 jit_solution(16555140713430903307)
XLA Ops:
  0.0 5.6 %shard_map.64 = (f32[10,128,128]{2,1,0:T(8,128)}, bf16[10,128,128]{2,1,0:T(8,128)(2,1)}) custom-call(bf16[1024,1280]{1,0:T(8,128)(2,1)} %k_ref.3, bf16[1024,1280]{1,0:T(8,128)(2,1)} %v_ref.3), custom_call_target="tpu_custom_call" | custom-call | flops 335544320 | bytes 5898240 | tf_op jit(solution)/shard_map/pallas_call | solution.py:54
  5.6 3.0 %collective-permute-start = (bf16[10,128,128]{2,1,0:T(8,128)(2,1)}, bf16[10,128,128]{2,1,0:T(8,128)(2,1)S(1)}, u32[]{:S(2)}, u32[]{:S(2)}) collective-permute-start(bf16[10,128,128]{2,1,0:T(8,128)(2,1)} %get-tuple-element.31), channel_id=1, source_target_pairs={{0,4},{4,8},{8,12},{12,16},{16,20},{20,24},{24,28},{28,0},{1,5},{5... | collective-permute-start | bytes 983048 | tf_op jit(solution)/shard_map/ppermute | solution.py:204
  8.6 7.7 %shard_map.65 = (bf16[1024,640]{1,0:T(8,128)(2,1)}, bf16[1024,640]{1,0:T(8,128)(2,1)}) custom-call(bf16[1024,1280]{1,0:T(8,128)(2,1)} %q_ref.1, bf16[1024,1280]{1,0:T(8,128)(2,1)} %k_ref.3, bf16[1024,1280]{1,0:T(8,128)(2,1)} %v_ref.3), custom_call_target="tpu_custom_call" | custom-call | flops 1677721600 | bytes 6553600 | tf_op jit(solution)/shard_map/pallas_call | solution.py:98
  16.3 3.3 %collective-permute-done = bf16[10,128,128]{2,1,0:T(8,128)(2,1)S(1)} collective-permute-done((bf16[10,128,128]{2,1,0:T(8,128)(2,1)}, bf16[10,128,128]{2,1,0:T(8,128)(2,1)S(1)}, u32[]{:S(2)}, u32[]{:S(2)}) %collective-permute-start) | collective-permute-done | bytes 327712 | tf_op jit(solution)/shard_map/ppermute | solution.py:204
  19.8 7.6 %shard_map.66 = (bf16[1024,640]{1,0:T(8,128)(2,1)}, bf16[1024,640]{1,0:T(8,128)(2,1)}) custom-call(bf16[1024,1280]{1,0:T(8,128)(2,1)} %q_ref.1, bf16[1024,1280]{1,0:T(8,128)(2,1)} %k_ref.3, bf16[1024,1280]{1,0:T(8,128)(2,1)} %v_ref.3), custom_call_target="tpu_custom_call" | custom-call | flops 1677721600 | bytes 6553600 | tf_op jit(solution)/shard_map/pallas_call | solution.py:98
  27.4 3.0 %collective-permute-done.1 = bf16[10,128,128]{2,1,0:T(8,128)(2,1)S(1)} collective-permute-done((bf16[10,128,128]{2,1,0:T(8,128)(2,1)S(1)}, bf16[10,128,128]{2,1,0:T(8,128)(2,1)S(1)}, u32[]{:S(2)}, u32[]{:S(2)}) %collective-permute-start.1) | collective-permute-done | bytes 327712 | tf_op jit(solution)/shard_map/ppermute | solution.py:204
  30.7 0.6 reshape.3.gain_ref
  31.3 4.6 %shard_map.67.scale_ref = bf16[1024,1280]{1,0:T(8,128)(2,1)} custom-call(bf16[1024,1280]{1,0:T(8,128)(2,1)} %g_ref, f32[1,1280]{1,0:T(1,128)} %reshape.3.gain_ref), custom_call_target="tpu_custom_call" | custom-call | flops 5242880 | bytes 5242880 | tf_op jit(solution)/shard_map/pallas_call | solution.py:119
  35.9 9.4 %collective-permute-done.2 = bf16[10,128,128]{2,1,0:T(8,128)(2,1)S(1)} collective-permute-done((bf16[10,128,128]{2,1,0:T(8,128)(2,1)S(1)}, bf16[10,128,128]{2,1,0:T(8,128)(2,1)S(1)}, u32[]{:S(2)}, u32[]{:S(2)}) %collective-permute-start.2) | collective-permute-done | bytes 327712 | tf_op jit(solution)/shard_map/ppermute | solution.py:204
  45.3 1.0 fusion.19.prefix_ref
  46.4 6.7 %shard_map.68 = bf16[1024,1280]{1,0:T(8,128)(2,1)} custom-call(bf16[1024,640]{1,0:T(8,128)(2,1)} %get-tuple-element.37.local_a_ref, bf16[1024,640]{1,0:T(8,128)(2,1)} %get-tuple-element.45.local_b_ref, bf16[1024,640]{1,0:T(8,128)(2,1)} %get-tuple-element.46.qa_a_ref, bf16[1024,640]{1,0:T(8,128)(2,1)} %get-tuple-element.47.qa_b_ref, ...), custom_call_target="tpu_custom_call" | custom-call | flops 671088640 | bytes 15728640 | tf_op jit(solution)/shard_map/pallas_call | solution.py:160
  53.1 5.9 %fusion.12 = bf16[512,2048]{1,0:T(8,128)(2,1)S(1)} fusion(bf16[1280,6144]{1,0:T(8,128)(2,1)} %param.11, bf16[1024,1280]{1,0:T(8,128)(2,1)} %shard_map.68, s32[]{:T(128)S(6)} %select_n.44), kind=kOutput, calls=%fused_computation.11 | convolution fusion | flops 2685403136 | bytes 8650756 | tf_op jit(solution)/shard_map/dot_general | solution.py:253
  59.1 5.8 %fusion.9 = bf16[512,2048]{1,0:T(8,128)(2,1)S(1)} fusion(bf16[1280,6144]{1,0:T(8,128)(2,1)} %param.11, bf16[1024,1280]{1,0:T(8,128)(2,1)S(1)} %copy-done, s32[]{:T(128)S(6)} %select_n.44), kind=kOutput, calls=%fused_computation.10 | convolution fusion | flops 2685403136 | bytes 8650756 | tf_op jit(solution)/shard_map/dot_general | solution.py:253
  65.8 3.1 %fusion.6 = bf16[512,2048]{1,0:T(8,128)(2,1)S(1)} fusion(bf16[1280,6144]{1,0:T(8,128)(2,1)S(1)} %bitcast.3, bf16[1024,1280]{1,0:T(8,128)(2,1)S(1)} %copy-done, s32[]{:T(128)S(6)} %select_n.44), kind=kOutput, calls=%fused_computation.9 | convolution fusion | flops 2685403136 | bytes 8650756 | tf_op jit(solution)/shard_map/dot_general | solution.py:253
  70.1 1.6 %collective-permute-done.3 = bf16[256,2048]{1,0:T(8,128)(2,1)S(1)} collective-permute-done((bf16[256,2048]{1,0:T(8,128)(2,1)S(1)}, bf16[256,2048]{1,0:T(8,128)(2,1)S(1)}, u32[]{:S(2)}, u32[]{:S(2)}) %collective-permute-start.3) | collective-permute-done | bytes 1048608 | tf_op jit(solution)/shard_map/ppermute | solution.py:193
  72.2 4.4 %convolution_convert_fusion = bf16[256,6144]{1,0:T(8,128)(2,1)S(1)} fusion(bf16[1280,6144]{1,0:T(8,128)(2,1)S(1)} %bitcast.3, bf16[512,1280]{1,0:T(8,128)(2,1)S(1)} %constant_dynamic-slice_fusion, s32[]{:T(128)S(6)} %select_n.46), kind=kOutput, calls=%fused_computation | convolution fusion | flops 4028104704 | bytes 19529732 | tf_op jit(solution)/shard_map/dot_general | solution.py:229
  76.9 1.3 collective-permute-start.7
  78.2 0.7 collective-permute-start.8
  78.9 1.3 collective-permute-start.9
  80.2 9.9 %convolution_convert_fusion.1 = bf16[256,6144]{1,0:T(8,128)(2,1)S(1)} fusion(bf16[1280,6144]{1,0:T(8,128)(2,1)} %param.11, bf16[512,1280]{1,0:T(8,128)(2,1)S(1)} %constant_dynamic-slice_fusion, s32[]{:T(128)S(6)} %select_n.45), kind=kOutput, calls=%fused_computation.1 | convolution fusion | flops 4028104704 | bytes 19529732 | tf_op jit(solution)/shard_map/dot_general | solution.py:229
  90.1 12.8 %collective-permute-done.7 = bf16[256,2048]{1,0:T(8,128)(2,1)S(1)} collective-permute-done((bf16[256,2048]{1,0:T(8,128)(2,1)S(1)}, bf16[256,2048]{1,0:T(8,128)(2,1)S(1)}, u32[]{:S(2)}, u32[]{:S(2)}) %collective-permute-start.7) | collective-permute-done | bytes 1048608 | tf_op jit(solution)/shard_map/ppermute | solution.py:193
  102.9 22.5 %collective-permute-done.8 = bf16[256,2048]{1,0:T(8,128)(2,1)S(1)} collective-permute-done((bf16[256,2048]{1,0:T(8,128)(2,1)S(1)}, bf16[256,2048]{1,0:T(8,128)(2,1)S(1)}, u32[]{:S(2)}, u32[]{:S(2)}) %collective-permute-start.8) | collective-permute-done | bytes 1048608 | tf_op jit(solution)/shard_map/ppermute | solution.py:193
  125.4 21.9 %collective-permute-done.9 = bf16[256,2048]{1,0:T(8,128)(2,1)S(1)} collective-permute-done((bf16[256,2048]{1,0:T(8,128)(2,1)S(1)}, bf16[256,2048]{1,0:T(8,128)(2,1)S(1)}, u32[]{:S(2)}, u32[]{:S(2)}) %collective-permute-start.9) | collective-permute-done | bytes 1048608 | tf_op jit(solution)/shard_map/ppermute | solution.py:193
  147.3 2.6 %add_convert_fusion = bf16[256,6144]{1,0:T(8,128)(2,1)} fusion(bf16[256,6144]{1,0:T(8,128)(2,1)S(1)} %collective-permute-done.6, bf16[256,6144]{1,0:T(8,128)(2,1)S(1)} %convolution_convert_fusion.1, bf16[256,2048]{1,0:T(8,128)(2,1)S(1)} %collective-permute-done.9, bf16[256,2048]{1,0:T(8,128)(2,1)S(1)} %collective-permute-done.8, ...), kind=kLoop, calls=%fused_computation.2 | loop fusion | flops 17301504 | bytes 12582912 | tf_op jit(solution)/shard_map/convert_element_type | solution.py:265
  (36 shorter events, 3.2 us)
Async XLA Ops:
  5.6 13.9 %collective-permute-start = (bf16[10,128,128]{2,1,0:T(8,128)(2,1)}, bf16[10,128,128]{2,1,0:T(8,128)(2,1)S(1)}, u32[]{:S(2)}, u32[]{:S(2)}) collective-permute-start(bf16[10,128,128]{2,1,0:T(8,128)(2,1)} %get-tuple-element.31), channel_id=1, source_target_pairs={{0,4},{4,8},{8,12},{12,16},{16,20},{20,24},{24,28},{28,0},{1,5},{5... | collective-permute-start | bytes 983048 | tf_op jit(solution)/shard_map/ppermute | solution.py:204
  8.6 11.0 %copy-start.1 = (f32[10,128,128]{2,1,0:T(8,128)S(1)}, f32[10,128,128]{2,1,0:T(8,128)}, u32[]{:S(2)}) copy-start(f32[10,128,128]{2,1,0:T(8,128)} %get-tuple-element.38) | copy-start | bytes 1966084
  19.7 10.7 %collective-permute-start.1 = (bf16[10,128,128]{2,1,0:T(8,128)(2,1)S(1)}, bf16[10,128,128]{2,1,0:T(8,128)(2,1)S(1)}, u32[]{:S(2)}, u32[]{:S(2)}) collective-permute-start(bf16[10,128,128]{2,1,0:T(8,128)(2,1)S(1)} %fusion.22), channel_id=1, source_target_pairs={{0,8},{4,12},{8,16},{12,20},{16,24},{20,28},{24,0},{28,4},{1,9},{5... | collective-permute-start | bytes 983048 | tf_op jit(solution)/shard_map/ppermute | solution.py:204
  19.8 10.9 %copy-start.2 = (f32[1280]{0:T(1024)S(1)}, f32[1280]{0:T(1024)}, u32[]{:S(2)}) copy-start(f32[1280]{0:T(1024)} %param.10) | copy-start | bytes 15364
  30.6 14.7 %collective-permute-start.2 = (bf16[10,128,128]{2,1,0:T(8,128)(2,1)S(1)}, bf16[10,128,128]{2,1,0:T(8,128)(2,1)S(1)}, u32[]{:S(2)}, u32[]{:S(2)}) collective-permute-start(bf16[10,128,128]{2,1,0:T(8,128)(2,1)S(1)} %fusion.18), channel_id=1, source_target_pairs={{0,16},{4,20},{8,24},{12,28},{16,0},{20,4},{24,8},{28,12},{1,17},{... | collective-permute-start | bytes 983048 | tf_op jit(solution)/shard_map/ppermute | solution.py:204
  53.1 5.9 %copy-start = (bf16[1024,1280]{1,0:T(8,128)(2,1)S(1)}, bf16[1024,1280]{1,0:T(8,128)(2,1)}, u32[]{:S(2)}) copy-start(bf16[1024,1280]{1,0:T(8,128)(2,1)} %shard_map.68) | copy-start | bytes 7864324
  53.1 12.7 %slice-start = ((s8[15728640]{0:T(1024)(128)(4,1)}), s8[4194304]{0:T(1024)(128)(4,1)S(1)}, s32[]{:S(2)}) async-start(s8[15728640]{0:T(1024)(128)(4,1)} %bitcast.2), calls=%async_computation | async-start | bytes 8388608
  53.1 12.7 %slice-start.1 = ((s8[15728640]{0:T(1024)(128)(4,1)}), s8[4194304]{0:T(1024)(128)(4,1)S(1)}, s32[]{:S(2)}) async-start(s8[15728640]{0:T(1024)(128)(4,1)} %bitcast.2), calls=%async_computation.1 | async-start | bytes 8388608
  59.0 6.7 %slice-start.2 = ((s8[15728640]{0:T(1024)(128)(4,1)}), s8[4194304]{0:T(1024)(128)(4,1)S(1)}, s32[]{:S(2)}) async-start(s8[15728640]{0:T(1024)(128)(4,1)} %bitcast.2), calls=%async_computation.2 | async-start | bytes 8388608
  59.0 6.7 %slice-start.3 = ((s8[15728640]{0:T(1024)(128)(4,1)}), s8[3145728]{0:T(1024)(128)(4,1)S(1)}, s32[]{:S(2)}) async-start(s8[15728640]{0:T(1024)(128)(4,1)} %bitcast.2), calls=%async_computation.3 | async-start | bytes 6291456
  65.0 4.2 %collective-permute-start.5 = (bf16[256,2048]{1,0:T(8,128)(2,1)S(1)}, bf16[256,2048]{1,0:T(8,128)(2,1)S(1)}, u32[]{:S(2)}, u32[]{:S(2)}) collective-permute-start(bf16[256,2048]{1,0:T(8,128)(2,1)S(1)} %constant_dynamic-slice_fusion.1), channel_id=1, source_target_pairs={{0,1},{1,0},{2,3},{3,2},{4,5},{5,4},{6,7},{7,6},{8,9},{9,8},{10,11... | collective-permute-start | bytes 3145736 | tf_op jit(solution)/shard_map/ppermute | solution.py:193
  65.2 4.5 %collective-permute-start.4 = (bf16[256,2048]{1,0:T(8,128)(2,1)S(1)}, bf16[256,2048]{1,0:T(8,128)(2,1)S(1)}, u32[]{:S(2)}, u32[]{:S(2)}) collective-permute-start(bf16[256,2048]{1,0:T(8,128)(2,1)S(1)} %constant_dynamic-slice_fusion.2), channel_id=1, source_target_pairs={{0,1},{1,0},{2,3},{3,2},{4,5},{5,4},{6,7},{7,6},{8,9},{9,8},{10,11... | collective-permute-start | bytes 3145736 | tf_op jit(solution)/shard_map/ppermute | solution.py:193
  69.0 2.7 %collective-permute-start.3 = (bf16[256,2048]{1,0:T(8,128)(2,1)S(1)}, bf16[256,2048]{1,0:T(8,128)(2,1)S(1)}, u32[]{:S(2)}, u32[]{:S(2)}) collective-permute-start(bf16[256,2048]{1,0:T(8,128)(2,1)S(1)} %constant_dynamic-slice_fusion.3), channel_id=1, source_target_pairs={{0,1},{1,0},{2,3},{3,2},{4,5},{5,4},{6,7},{7,6},{8,9},{9,8},{10,11... | collective-permute-start | bytes 3145736 | tf_op jit(solution)/shard_map/ppermute | solution.py:193
  76.7 70.6 %collective-permute-start.6 = (bf16[256,6144]{1,0:T(8,128)(2,1)S(1)}, bf16[256,6144]{1,0:T(8,128)(2,1)S(1)}, u32[]{:S(2)}, u32[]{:S(2)}) collective-permute-start(bf16[256,6144]{1,0:T(8,128)(2,1)S(1)} %convolution_convert_fusion), channel_id=1, source_target_pairs={{0,1},{1,0},{2,3},{3,2},{4,5},{5,4},{6,7},{7,6},{8,9},{9,8},{10,11... | collective-permute-start | bytes 9437192 | tf_op jit(solution)/shard_map/ppermute | solution.py:193
  76.9 26.0 %collective-permute-start.7 = (bf16[256,2048]{1,0:T(8,128)(2,1)S(1)}, bf16[256,2048]{1,0:T(8,128)(2,1)S(1)}, u32[]{:S(2)}, u32[]{:S(2)}) collective-permute-start(bf16[256,2048]{1,0:T(8,128)(2,1)S(1)} %add_convert_fusion.3), channel_id=1, source_target_pairs={{0,2},{2,0},{1,3},{3,1},{4,6},{6,4},{5,7},{7,5},{8,10},{10,8},{9,1... | collective-permute-start | bytes 3145736 | tf_op jit(solution)/shard_map/ppermute | solution.py:193
  78.2 47.2 %collective-permute-start.8 = (bf16[256,2048]{1,0:T(8,128)(2,1)S(1)}, bf16[256,2048]{1,0:T(8,128)(2,1)S(1)}, u32[]{:S(2)}, u32[]{:S(2)}) collective-permute-start(bf16[256,2048]{1,0:T(8,128)(2,1)S(1)} %add_convert_fusion.2), channel_id=1, source_target_pairs={{0,2},{2,0},{1,3},{3,1},{4,6},{6,4},{5,7},{7,5},{8,10},{10,8},{9,1... | collective-permute-start | bytes 3145736 | tf_op jit(solution)/shard_map/ppermute | solution.py:193
  78.9 68.4 %collective-permute-start.9 = (bf16[256,2048]{1,0:T(8,128)(2,1)S(1)}, bf16[256,2048]{1,0:T(8,128)(2,1)S(1)}, u32[]{:S(2)}, u32[]{:S(2)}) collective-permute-start(bf16[256,2048]{1,0:T(8,128)(2,1)S(1)} %add_convert_fusion.1), channel_id=1, source_target_pairs={{0,2},{2,0},{1,3},{3,1},{4,6},{6,4},{5,7},{7,5},{8,10},{10,8},{9,1... | collective-permute-start | bytes 3145736 | tf_op jit(solution)/shard_map/ppermute | solution.py:193

commit v20 on v19

--- a/solution.py
+++ b/solution.py
@@ -10,7 +10,7 @@
 HD = 128
 COLUMN_CHUNKS = 3
 QUERY_TILE = 256
-ROW_TILE = 256
+ROW_TILE = 512
 
 
 epsilon = 1e-05

time: 150 us -> 150 us (level)
  Pallas kernels: 32.3 us -> 30.6 us
where the time goes in v20:
time: 150 us; the launch traced here: 149 us
  waiting for transfers between devices  75.2 us (50%)
  Pallas kernels  30.6 us (20%)
  matrix products  29.2 us (19%)
  starting transfers between devices  7.57 us (5%)
  other arithmetic  5.24 us (3%)
    ppermute x7, waiting for transfers between devices, swap(): return lax.ppermute(block, axis, [(0, 1), (1, 0)])  58.7 us
    ppermute x3, waiting for transfers between devices, exclusive_prefix(): lax.ppermute(sent, axis, [(i, (i + distance) % size) for i in range(size)])  16.5 us
    pallas_call x2, Pallas kernels, local_attention(): pl.pallas_call(local_kernel, grid=(heads,), in_specs=[picked] * 3, out_sp...  15.3 us
    dot_general x3, matrix products, project_and_reduce(): jnp.dot(far_rows, out_weight[:, c * chunk:(c + 1) * chunk], preferred_ele...  14.8 us
    dot_general x2, matrix products, product(): jnp.dot(rows, out_weight, preferred_element_type=jnp.float32)  14.4 us
    pallas_call x1, Pallas kernels, mix(): pl.pallas_call(mix_kernel, grid=(tokens // ROW_TILE,), in_specs=[row_bloc...  6.41 us
    pallas_call x1, Pallas kernels, key_value_states(): pl.pallas_call(state_kernel, grid=(tokens // ROW_TILE,), in_specs=[row_bl...  5.11 us
    ppermute x7, starting transfers between devices, swap(): return lax.ppermute(block, axis, [(0, 1), (1, 0)])  4.28 us
  transfers between devices with their start and end apart: 10, of which 7 were waited for; matrix products, arithmetic and copies ran while one was open for 10% of the time, Pallas kernels for 13%

profile of v20, /device:TPU:0, one launch (start us, length us, event | category | flops | bytes accessed | tf_op | source)
XLA Modules:
  0.0 149.2 jit_solution(14772054217011578469)
XLA Ops:
  0.0 5.1 %shard_map.64 = (f32[10,128,128]{2,1,0:T(8,128)}, bf16[10,128,128]{2,1,0:T(8,128)(2,1)}) custom-call(bf16[1024,1280]{1,0:T(8,128)(2,1)} %k_ref.3, bf16[1024,1280]{1,0:T(8,128)(2,1)} %v_ref.3), custom_call_target="tpu_custom_call" | custom-call | flops 335544320 | bytes 5898240 | tf_op jit(solution)/shard_map/pallas_call | solution.py:54
  5.1 3.0 %collective-permute-start = (bf16[10,128,128]{2,1,0:T(8,128)(2,1)}, bf16[10,128,128]{2,1,0:T(8,128)(2,1)S(1)}, u32[]{:S(2)}, u32[]{:S(2)}) collective-permute-start(bf16[10,128,128]{2,1,0:T(8,128)(2,1)} %get-tuple-element.31), channel_id=1, source_target_pairs={{0,4},{4,8},{8,12},{12,16},{16,20},{20,24},{24,28},{28,0},{1,5},{5... | collective-permute-start | bytes 983048 | tf_op jit(solution)/shard_map/ppermute | solution.py:204
  8.1 7.7 %shard_map.65 = (bf16[1024,640]{1,0:T(8,128)(2,1)}, bf16[1024,640]{1,0:T(8,128)(2,1)}) custom-call(bf16[1024,1280]{1,0:T(8,128)(2,1)} %q_ref.1, bf16[1024,1280]{1,0:T(8,128)(2,1)} %k_ref.3, bf16[1024,1280]{1,0:T(8,128)(2,1)} %v_ref.3), custom_call_target="tpu_custom_call" | custom-call | flops 1677721600 | bytes 6553600 | tf_op jit(solution)/shard_map/pallas_call | solution.py:98
  15.8 3.2 %collective-permute-done = bf16[10,128,128]{2,1,0:T(8,128)(2,1)S(1)} collective-permute-done((bf16[10,128,128]{2,1,0:T(8,128)(2,1)}, bf16[10,128,128]{2,1,0:T(8,128)(2,1)S(1)}, u32[]{:S(2)}, u32[]{:S(2)}) %collective-permute-start) | collective-permute-done | bytes 327712 | tf_op jit(solution)/shard_map/ppermute | solution.py:204
  19.4 7.6 %shard_map.66 = (bf16[1024,640]{1,0:T(8,128)(2,1)}, bf16[1024,640]{1,0:T(8,128)(2,1)}) custom-call(bf16[1024,1280]{1,0:T(8,128)(2,1)} %q_ref.1, bf16[1024,1280]{1,0:T(8,128)(2,1)} %k_ref.3, bf16[1024,1280]{1,0:T(8,128)(2,1)} %v_ref.3), custom_call_target="tpu_custom_call" | custom-call | flops 1677721600 | bytes 6553600 | tf_op jit(solution)/shard_map/pallas_call | solution.py:98
  27.1 3.0 %collective-permute-done.1 = bf16[10,128,128]{2,1,0:T(8,128)(2,1)S(1)} collective-permute-done((bf16[10,128,128]{2,1,0:T(8,128)(2,1)S(1)}, bf16[10,128,128]{2,1,0:T(8,128)(2,1)S(1)}, u32[]{:S(2)}, u32[]{:S(2)}) %collective-permute-start.1) | collective-permute-done | bytes 327712 | tf_op jit(solution)/shard_map/ppermute | solution.py:204
  30.3 0.6 reshape.3.gain_ref
  30.9 3.8 %shard_map.67.scale_ref = bf16[1024,1280]{1,0:T(8,128)(2,1)} custom-call(bf16[1024,1280]{1,0:T(8,128)(2,1)} %g_ref, f32[1,1280]{1,0:T(1,128)} %reshape.3.gain_ref), custom_call_target="tpu_custom_call" | custom-call | flops 5242880 | bytes 5242880 | tf_op jit(solution)/shard_map/pallas_call | solution.py:119
  34.7 10.3 %collective-permute-done.2 = bf16[10,128,128]{2,1,0:T(8,128)(2,1)S(1)} collective-permute-done((bf16[10,128,128]{2,1,0:T(8,128)(2,1)S(1)}, bf16[10,128,128]{2,1,0:T(8,128)(2,1)S(1)}, u32[]{:S(2)}, u32[]{:S(2)}) %collective-permute-start.2) | collective-permute-done | bytes 327712 | tf_op jit(solution)/shard_map/ppermute | solution.py:204
  45.0 1.0 fusion.19.prefix_ref
  46.0 6.4 %shard_map.68 = bf16[1024,1280]{1,0:T(8,128)(2,1)} custom-call(bf16[1024,640]{1,0:T(8,128)(2,1)} %get-tuple-element.37.local_a_ref, bf16[1024,640]{1,0:T(8,128)(2,1)} %get-tuple-element.45.local_b_ref, bf16[1024,640]{1,0:T(8,128)(2,1)} %get-tuple-element.46.qa_a_ref, bf16[1024,640]{1,0:T(8,128)(2,1)} %get-tuple-element.47.qa_b_ref, ...), custom_call_target="tpu_custom_call" | custom-call | flops 671088640 | bytes 15728640 | tf_op jit(solution)/shard_map/pallas_call | solution.py:160
  52.4 5.9 %fusion.12 = bf16[512,2048]{1,0:T(8,128)(2,1)S(1)} fusion(bf16[1280,6144]{1,0:T(8,128)(2,1)} %param.11, bf16[1024,1280]{1,0:T(8,128)(2,1)} %shard_map.68, s32[]{:T(128)S(6)} %select_n.44), kind=kOutput, calls=%fused_computation.11 | convolution fusion | flops 2685403136 | bytes 8650756 | tf_op jit(solution)/shard_map/dot_general | solution.py:253
  58.4 5.8 %fusion.9 = bf16[512,2048]{1,0:T(8,128)(2,1)S(1)} fusion(bf16[1280,6144]{1,0:T(8,128)(2,1)} %param.11, bf16[1024,1280]{1,0:T(8,128)(2,1)S(1)} %copy-done, s32[]{:T(128)S(6)} %select_n.44), kind=kOutput, calls=%fused_computation.10 | convolution fusion | flops 2685403136 | bytes 8650756 | tf_op jit(solution)/shard_map/dot_general | solution.py:253
  65.1 3.1 %fusion.6 = bf16[512,2048]{1,0:T(8,128)(2,1)S(1)} fusion(bf16[1280,6144]{1,0:T(8,128)(2,1)S(1)} %bitcast.3, bf16[1024,1280]{1,0:T(8,128)(2,1)S(1)} %copy-done, s32[]{:T(128)S(6)} %select_n.44), kind=kOutput, calls=%fused_computation.9 | convolution fusion | flops 2685403136 | bytes 8650756 | tf_op jit(solution)/shard_map/dot_general | solution.py:253
  69.5 1.6 %collective-permute-done.3 = bf16[256,2048]{1,0:T(8,128)(2,1)S(1)} collective-permute-done((bf16[256,2048]{1,0:T(8,128)(2,1)S(1)}, bf16[256,2048]{1,0:T(8,128)(2,1)S(1)}, u32[]{:S(2)}, u32[]{:S(2)}) %collective-permute-start.3) | collective-permute-done | bytes 1048608 | tf_op jit(solution)/shard_map/ppermute | solution.py:193
  71.5 4.4 %convolution_convert_fusion = bf16[256,6144]{1,0:T(8,128)(2,1)S(1)} fusion(bf16[1280,6144]{1,0:T(8,128)(2,1)S(1)} %bitcast.3, bf16[512,1280]{1,0:T(8,128)(2,1)S(1)} %constant_dynamic-slice_fusion, s32[]{:T(128)S(6)} %select_n.46), kind=kOutput, calls=%fused_computation | convolution fusion | flops 4028104704 | bytes 19529732 | tf_op jit(solution)/shard_map/dot_general | solution.py:229
  76.2 1.3 collective-permute-start.7
  77.5 0.7 collective-permute-start.8
  78.2 1.3 collective-permute-start.9
  79.5 9.9 %convolution_convert_fusion.1 = bf16[256,6144]{1,0:T(8,128)(2,1)S(1)} fusion(bf16[1280,6144]{1,0:T(8,128)(2,1)} %param.11, bf16[512,1280]{1,0:T(8,128)(2,1)S(1)} %constant_dynamic-slice_fusion, s32[]{:T(128)S(6)} %select_n.45), kind=kOutput, calls=%fused_computation.1 | convolution fusion | flops 4028104704 | bytes 19529732 | tf_op jit(solution)/shard_map/dot_general | solution.py:229
  89.5 12.8 %collective-permute-done.7 = bf16[256,2048]{1,0:T(8,128)(2,1)S(1)} collective-permute-done((bf16[256,2048]{1,0:T(8,128)(2,1)S(1)}, bf16[256,2048]{1,0:T(8,128)(2,1)S(1)}, u32[]{:S(2)}, u32[]{:S(2)}) %collective-permute-start.7) | collective-permute-done | bytes 1048608 | tf_op jit(solution)/shard_map/ppermute | solution.py:193
  102.2 22.5 %collective-permute-done.8 = bf16[256,2048]{1,0:T(8,128)(2,1)S(1)} collective-permute-done((bf16[256,2048]{1,0:T(8,128)(2,1)S(1)}, bf16[256,2048]{1,0:T(8,128)(2,1)S(1)}, u32[]{:S(2)}, u32[]{:S(2)}) %collective-permute-start.8) | collective-permute-done | bytes 1048608 | tf_op jit(solution)/shard_map/ppermute | solution.py:193
  124.7 21.9 %collective-permute-done.9 = bf16[256,2048]{1,0:T(8,128)(2,1)S(1)} collective-permute-done((bf16[256,2048]{1,0:T(8,128)(2,1)S(1)}, bf16[256,2048]{1,0:T(8,128)(2,1)S(1)}, u32[]{:S(2)}, u32[]{:S(2)}) %collective-permute-start.9) | collective-permute-done | bytes 1048608 | tf_op jit(solution)/shard_map/ppermute | solution.py:193
  146.6 2.6 %add_convert_fusion = bf16[256,6144]{1,0:T(8,128)(2,1)} fusion(bf16[256,6144]{1,0:T(8,128)(2,1)S(1)} %collective-permute-done.6, bf16[256,6144]{1,0:T(8,128)(2,1)S(1)} %convolution_convert_fusion.1, bf16[256,2048]{1,0:T(8,128)(2,1)S(1)} %collective-permute-done.9, bf16[256,2048]{1,0:T(8,128)(2,1)S(1)} %collective-permute-done.8, ...), kind=kLoop, calls=%fused_computation.2 | loop fusion | flops 17301504 | bytes 12582912 | tf_op jit(solution)/shard_map/convert_element_type | solution.py:265
  (36 shorter events, 3.3 us)
Async XLA Ops:
  5.1 13.9 %collective-permute-start = (bf16[10,128,128]{2,1,0:T(8,128)(2,1)}, bf16[10,128,128]{2,1,0:T(8,128)(2,1)S(1)}, u32[]{:S(2)}, u32[]{:S(2)}) collective-permute-start(bf16[10,128,128]{2,1,0:T(8,128)(2,1)} %get-tuple-element.31), channel_id=1, source_target_pairs={{0,4},{4,8},{8,12},{12,16},{16,20},{20,24},{24,28},{28,0},{1,5},{5... | collective-permute-start | bytes 983048 | tf_op jit(solution)/shard_map/ppermute | solution.py:204
  8.1 11.0 %copy-start.1 = (f32[10,128,128]{2,1,0:T(8,128)S(1)}, f32[10,128,128]{2,1,0:T(8,128)}, u32[]{:S(2)}) copy-start(f32[10,128,128]{2,1,0:T(8,128)} %get-tuple-element.38) | copy-start | bytes 1966084
  19.2 10.9 %collective-permute-start.1 = (bf16[10,128,128]{2,1,0:T(8,128)(2,1)S(1)}, bf16[10,128,128]{2,1,0:T(8,128)(2,1)S(1)}, u32[]{:S(2)}, u32[]{:S(2)}) collective-permute-start(bf16[10,128,128]{2,1,0:T(8,128)(2,1)S(1)} %fusion.22), channel_id=1, source_target_pairs={{0,8},{4,12},{8,16},{12,20},{16,24},{20,28},{24,0},{28,4},{1,9},{5... | collective-permute-start | bytes 983048 | tf_op jit(solution)/shard_map/ppermute | solution.py:204
  19.4 10.9 %copy-start.2 = (f32[1280]{0:T(1024)S(1)}, f32[1280]{0:T(1024)}, u32[]{:S(2)}) copy-start(f32[1280]{0:T(1024)} %param.10) | copy-start | bytes 15364
  30.2 14.7 %collective-permute-start.2 = (bf16[10,128,128]{2,1,0:T(8,128)(2,1)S(1)}, bf16[10,128,128]{2,1,0:T(8,128)(2,1)S(1)}, u32[]{:S(2)}, u32[]{:S(2)}) collective-permute-start(bf16[10,128,128]{2,1,0:T(8,128)(2,1)S(1)} %fusion.18), channel_id=1, source_target_pairs={{0,16},{4,20},{8,24},{12,28},{16,0},{20,4},{24,8},{28,12},{1,17},{... | collective-permute-start | bytes 983048 | tf_op jit(solution)/shard_map/ppermute | solution.py:204
  52.4 5.9 %copy-start = (bf16[1024,1280]{1,0:T(8,128)(2,1)S(1)}, bf16[1024,1280]{1,0:T(8,128)(2,1)}, u32[]{:S(2)}) copy-start(bf16[1024,1280]{1,0:T(8,128)(2,1)} %shard_map.68) | copy-start | bytes 7864324
  52.4 12.7 %slice-start = ((s8[15728640]{0:T(1024)(128)(4,1)}), s8[4194304]{0:T(1024)(128)(4,1)S(1)}, s32[]{:S(2)}) async-start(s8[15728640]{0:T(1024)(128)(4,1)} %bitcast.2), calls=%async_computation | async-start | bytes 8388608
  52.4 12.7 %slice-start.1 = ((s8[15728640]{0:T(1024)(128)(4,1)}), s8[4194304]{0:T(1024)(128)(4,1)S(1)}, s32[]{:S(2)}) async-start(s8[15728640]{0:T(1024)(128)(4,1)} %bitcast.2), calls=%async_computation.1 | async-start | bytes 8388608
  58.4 6.7 %slice-start.2 = ((s8[15728640]{0:T(1024)(128)(4,1)}), s8[4194304]{0:T(1024)(128)(4,1)S(1)}, s32[]{:S(2)}) async-start(s8[15728640]{0:T(1024)(128)(4,1)} %bitcast.2), calls=%async_computation.2 | async-start | bytes 8388608
  58.4 6.7 %slice-start.3 = ((s8[15728640]{0:T(1024)(128)(4,1)}), s8[3145728]{0:T(1024)(128)(4,1)S(1)}, s32[]{:S(2)}) async-start(s8[15728640]{0:T(1024)(128)(4,1)} %bitcast.2), calls=%async_computation.3 | async-start | bytes 6291456
  64.3 4.2 %collective-permute-start.5 = (bf16[256,2048]{1,0:T(8,128)(2,1)S(1)}, bf16[256,2048]{1,0:T(8,128)(2,1)S(1)}, u32[]{:S(2)}, u32[]{:S(2)}) collective-permute-start(bf16[256,2048]{1,0:T(8,128)(2,1)S(1)} %constant_dynamic-slice_fusion.1), channel_id=1, source_target_pairs={{0,1},{1,0},{2,3},{3,2},{4,5},{5,4},{6,7},{7,6},{8,9},{9,8},{10,11... | collective-permute-start | bytes 3145736 | tf_op jit(solution)/shard_map/ppermute | solution.py:193
  64.5 4.5 %collective-permute-start.4 = (bf16[256,2048]{1,0:T(8,128)(2,1)S(1)}, bf16[256,2048]{1,0:T(8,128)(2,1)S(1)}, u32[]{:S(2)}, u32[]{:S(2)}) collective-permute-start(bf16[256,2048]{1,0:T(8,128)(2,1)S(1)} %constant_dynamic-slice_fusion.2), channel_id=1, source_target_pairs={{0,1},{1,0},{2,3},{3,2},{4,5},{5,4},{6,7},{7,6},{8,9},{9,8},{10,11... | collective-permute-start | bytes 3145736 | tf_op jit(solution)/shard_map/ppermute | solution.py:193
  68.3 2.7 %collective-permute-start.3 = (bf16[256,2048]{1,0:T(8,128)(2,1)S(1)}, bf16[256,2048]{1,0:T(8,128)(2,1)S(1)}, u32[]{:S(2)}, u32[]{:S(2)}) collective-permute-start(bf16[256,2048]{1,0:T(8,128)(2,1)S(1)} %constant_dynamic-slice_fusion.3), channel_id=1, source_target_pairs={{0,1},{1,0},{2,3},{3,2},{4,5},{5,4},{6,7},{7,6},{8,9},{9,8},{10,11... | collective-permute-start | bytes 3145736 | tf_op jit(solution)/shard_map/ppermute | solution.py:193
  76.0 70.6 %collective-permute-start.6 = (bf16[256,6144]{1,0:T(8,128)(2,1)S(1)}, bf16[256,6144]{1,0:T(8,128)(2,1)S(1)}, u32[]{:S(2)}, u32[]{:S(2)}) collective-permute-start(bf16[256,6144]{1,0:T(8,128)(2,1)S(1)} %convolution_convert_fusion), channel_id=1, source_target_pairs={{0,1},{1,0},{2,3},{3,2},{4,5},{5,4},{6,7},{7,6},{8,9},{9,8},{10,11... | collective-permute-start | bytes 9437192 | tf_op jit(solution)/shard_map/ppermute | solution.py:193
  76.2 26.0 %collective-permute-start.7 = (bf16[256,2048]{1,0:T(8,128)(2,1)S(1)}, bf16[256,2048]{1,0:T(8,128)(2,1)S(1)}, u32[]{:S(2)}, u32[]{:S(2)}) collective-permute-start(bf16[256,2048]{1,0:T(8,128)(2,1)S(1)} %add_convert_fusion.3), channel_id=1, source_target_pairs={{0,2},{2,0},{1,3},{3,1},{4,6},{6,4},{5,7},{7,5},{8,10},{10,8},{9,1... | collective-permute-start | bytes 3145736 | tf_op jit(solution)/shard_map/ppermute | solution.py:193
  77.5 47.2 %collective-permute-start.8 = (bf16[256,2048]{1,0:T(8,128)(2,1)S(1)}, bf16[256,2048]{1,0:T(8,128)(2,1)S(1)}, u32[]{:S(2)}, u32[]{:S(2)}) collective-permute-start(bf16[256,2048]{1,0:T(8,128)(2,1)S(1)} %add_convert_fusion.2), channel_id=1, source_target_pairs={{0,2},{2,0},{1,3},{3,1},{4,6},{6,4},{5,7},{7,5},{8,10},{10,8},{9,1... | collective-permute-start | bytes 3145736 | tf_op jit(solution)/shard_map/ppermute | solution.py:193
  78.2 68.4 %collective-permute-start.9 = (bf16[256,2048]{1,0:T(8,128)(2,1)S(1)}, bf16[256,2048]{1,0:T(8,128)(2,1)S(1)}, u32[]{:S(2)}, u32[]{:S(2)}) collective-permute-start(bf16[256,2048]{1,0:T(8,128)(2,1)S(1)} %add_convert_fusion.1), channel_id=1, source_target_pairs={{0,2},{2,0},{1,3},{3,1},{4,6},{6,4},{5,7},{7,5},{8,10},{10,8},{9,1... | collective-permute-start | bytes 3145736 | tf_op jit(solution)/shard_map/ppermute | solution.py:193

commit v21 on v20

--- a/solution.py
+++ b/solution.py
@@ -261,8 +261,10 @@
     near = swap(product(block_of(near_rows, 1 - tc)), "tc")
     mine = lax.optimization_barrier(product(block_of(near_rows, tc)))
     far = jnp.concatenate(across, axis=1)
-    total = mine.astype(jnp.float32) + near.astype(jnp.float32) + far.astype(jnp.float32)
-    return total.astype(jnp.bfloat16)
+    own_chip = lax.optimization_barrier(
+        (mine.astype(jnp.float32) + near.astype(jnp.float32)).astype(jnp.bfloat16)
+    )
+    return (own_chip + far.astype(jnp.float32)).astype(jnp.bfloat16)
 
 
 def on_device(queries, keys, values, gates, gain, out_weight):

time: 150 us -> 159 us (1.060)
  the two profiles are of different devices: /device:TPU:0 before, /device:TPU:24 now
where the time goes in v21:
time: 159 us; the launch traced here: 156 us
  waiting for transfers between devices  80.8 us (51%)
  Pallas kernels  30.6 us (19%)
  matrix products  29.3 us (18%)
  starting transfers between devices  8.15 us (5%)
  other arithmetic  5.86 us (4%)
    ppermute x7, waiting for transfers between devices, swap(): return lax.ppermute(block, axis, [(0, 1), (1, 0)])  67.5 us
    pallas_call x2, Pallas kernels, local_attention(): pl.pallas_call(local_kernel, grid=(heads,), in_specs=[picked] * 3, out_sp...  15.3 us
    dot_general x3, matrix products, project_and_reduce(): jnp.dot(far_rows, out_weight[:, c * chunk:(c + 1) * chunk], preferred_ele...  14.8 us
    dot_general x2, matrix products, product(): jnp.dot(rows, out_weight, preferred_element_type=jnp.float32)  14.5 us
    ppermute x3, waiting for transfers between devices, exclusive_prefix(): lax.ppermute(sent, axis, [(i, (i + distance) % size) for i in range(size)])  13.3 us
    pallas_call x1, Pallas kernels, mix(): pl.pallas_call(mix_kernel, grid=(tokens // ROW_TILE,), in_specs=[row_bloc...  6.41 us
    pallas_call x1, Pallas kernels, key_value_states(): pl.pallas_call(state_kernel, grid=(tokens // ROW_TILE,), in_specs=[row_bl...  5.11 us
    ppermute x7, starting transfers between devices, swap(): return lax.ppermute(block, axis, [(0, 1), (1, 0)])  4.17 us
  transfers between devices with their start and end apart: 10, of which 6 were waited for; matrix products, arithmetic and copies ran while one was open for 10% of the time, Pallas kernels for 12%

profile of v21, /device:TPU:24, one launch (start us, length us, event | category | flops | bytes accessed | tf_op | source)
XLA Modules:
  0.0 156.0 jit_solution(11334732436173573166)
XLA Ops:
  0.0 5.1 %shard_map.64 = (f32[10,128,128]{2,1,0:T(8,128)}, bf16[10,128,128]{2,1,0:T(8,128)(2,1)}) custom-call(bf16[1024,1280]{1,0:T(8,128)(2,1)} %k_ref.3, bf16[1024,1280]{1,0:T(8,128)(2,1)} %v_ref.3), custom_call_target="tpu_custom_call" | custom-call | flops 335544320 | bytes 5898240 | tf_op jit(solution)/shard_map/pallas_call | solution.py:54
  5.1 1.5 collective-permute-start
  6.6 7.7 %shard_map.65 = (bf16[1024,640]{1,0:T(8,128)(2,1)}, bf16[1024,640]{1,0:T(8,128)(2,1)}) custom-call(bf16[1024,1280]{1,0:T(8,128)(2,1)} %q_ref.1, bf16[1024,1280]{1,0:T(8,128)(2,1)} %k_ref.3, bf16[1024,1280]{1,0:T(8,128)(2,1)} %v_ref.3), custom_call_target="tpu_custom_call" | custom-call | flops 1677721600 | bytes 6553600 | tf_op jit(solution)/shard_map/pallas_call | solution.py:98
  14.3 1.4 collective-permute-done
  15.8 2.3 %collective-permute-start.1 = (bf16[10,128,128]{2,1,0:T(8,128)(2,1)S(1)}, bf16[10,128,128]{2,1,0:T(8,128)(2,1)S(1)}, u32[]{:S(2)}, u32[]{:S(2)}) collective-permute-start(bf16[10,128,128]{2,1,0:T(8,128)(2,1)S(1)} %fusion.22), channel_id=1, source_target_pairs={{0,8},{4,12},{8,16},{12,20},{16,24},{20,28},{24,0},{28,4},{1,9},{5... | collective-permute-start | bytes 983048 | tf_op jit(solution)/shard_map/ppermute | solution.py:204
  18.2 7.6 %shard_map.66 = (bf16[1024,640]{1,0:T(8,128)(2,1)}, bf16[1024,640]{1,0:T(8,128)(2,1)}) custom-call(bf16[1024,1280]{1,0:T(8,128)(2,1)} %q_ref.1, bf16[1024,1280]{1,0:T(8,128)(2,1)} %k_ref.3, bf16[1024,1280]{1,0:T(8,128)(2,1)} %v_ref.3), custom_call_target="tpu_custom_call" | custom-call | flops 1677721600 | bytes 6553600 | tf_op jit(solution)/shard_map/pallas_call | solution.py:98
  26.7 3.8 %shard_map.67.scale_ref = bf16[1024,1280]{1,0:T(8,128)(2,1)} custom-call(bf16[1024,1280]{1,0:T(8,128)(2,1)} %g_ref, f32[1,1280]{1,0:T(1,128)} %reshape.3.gain_ref), custom_call_target="tpu_custom_call" | custom-call | flops 5242880 | bytes 5242880 | tf_op jit(solution)/shard_map/pallas_call | solution.py:119
  30.4 11.9 %collective-permute-done.2 = bf16[10,128,128]{2,1,0:T(8,128)(2,1)S(1)} collective-permute-done((bf16[10,128,128]{2,1,0:T(8,128)(2,1)S(1)}, bf16[10,128,128]{2,1,0:T(8,128)(2,1)S(1)}, u32[]{:S(2)}, u32[]{:S(2)}) %collective-permute-start.2) | collective-permute-done | bytes 327712 | tf_op jit(solution)/shard_map/ppermute | solution.py:204
  42.4 1.0 fusion.19.prefix_ref
  43.4 6.4 %shard_map.68 = bf16[1024,1280]{1,0:T(8,128)(2,1)} custom-call(bf16[1024,640]{1,0:T(8,128)(2,1)} %get-tuple-element.37.local_a_ref, bf16[1024,640]{1,0:T(8,128)(2,1)} %get-tuple-element.45.local_b_ref, bf16[1024,640]{1,0:T(8,128)(2,1)} %get-tuple-element.46.qa_a_ref, bf16[1024,640]{1,0:T(8,128)(2,1)} %get-tuple-element.47.qa_b_ref, ...), custom_call_target="tpu_custom_call" | custom-call | flops 671088640 | bytes 15728640 | tf_op jit(solution)/shard_map/pallas_call | solution.py:160
  49.8 5.9 %fusion.12 = bf16[512,2048]{1,0:T(8,128)(2,1)S(1)} fusion(bf16[1280,6144]{1,0:T(8,128)(2,1)} %param.11, bf16[1024,1280]{1,0:T(8,128)(2,1)} %shard_map.68, s32[]{:T(128)S(6)} %select_n.44), kind=kOutput, calls=%fused_computation.12 | convolution fusion | flops 2685403136 | bytes 8650756 | tf_op jit(solution)/shard_map/dot_general | solution.py:253
  55.8 5.8 %fusion.9 = bf16[512,2048]{1,0:T(8,128)(2,1)S(1)} fusion(bf16[1280,6144]{1,0:T(8,128)(2,1)} %param.11, bf16[1024,1280]{1,0:T(8,128)(2,1)S(1)} %copy-done, s32[]{:T(128)S(6)} %select_n.44), kind=kOutput, calls=%fused_computation.11 | convolution fusion | flops 2685403136 | bytes 8650756 | tf_op jit(solution)/shard_map/dot_general | solution.py:253
  62.5 3.1 %fusion.6 = bf16[512,2048]{1,0:T(8,128)(2,1)S(1)} fusion(bf16[1280,6144]{1,0:T(8,128)(2,1)S(1)} %bitcast.3, bf16[1024,1280]{1,0:T(8,128)(2,1)S(1)} %copy-done, s32[]{:T(128)S(6)} %select_n.44), kind=kOutput, calls=%fused_computation.10 | convolution fusion | flops 2685403136 | bytes 8650756 | tf_op jit(solution)/shard_map/dot_general | solution.py:253
  66.8 1.6 %collective-permute-done.3 = bf16[256,2048]{1,0:T(8,128)(2,1)S(1)} collective-permute-done((bf16[256,2048]{1,0:T(8,128)(2,1)S(1)}, bf16[256,2048]{1,0:T(8,128)(2,1)S(1)}, u32[]{:S(2)}, u32[]{:S(2)}) %collective-permute-start.3) | collective-permute-done | bytes 1048608 | tf_op jit(solution)/shard_map/ppermute | solution.py:193
  68.9 4.4 %convolution_convert_fusion = bf16[256,6144]{1,0:T(8,128)(2,1)S(1)} fusion(bf16[1280,6144]{1,0:T(8,128)(2,1)S(1)} %bitcast.3, bf16[512,1280]{1,0:T(8,128)(2,1)S(1)} %constant_dynamic-slice_fusion, s32[]{:T(128)S(6)} %select_n.46), kind=kOutput, calls=%fused_computation | convolution fusion | flops 4028104704 | bytes 19529732 | tf_op jit(solution)/shard_map/dot_general | solution.py:229
  73.6 10.0 %convolution_convert_fusion.1 = bf16[256,6144]{1,0:T(8,128)(2,1)S(1)} fusion(bf16[1280,6144]{1,0:T(8,128)(2,1)} %param.11, bf16[512,1280]{1,0:T(8,128)(2,1)S(1)} %constant_dynamic-slice_fusion, s32[]{:T(128)S(6)} %select_n.45), kind=kOutput, calls=%fused_computation.1 | convolution fusion | flops 4028104704 | bytes 19529732 | tf_op jit(solution)/shard_map/dot_general | solution.py:229
  83.6 1.2 collective-permute-start.7
  84.8 0.9 collective-permute-start.8
  85.7 1.1 collective-permute-start.9
  86.9 1.2 add_convert_fusion.1
  88.0 21.7 %collective-permute-done.7 = bf16[256,2048]{1,0:T(8,128)(2,1)S(1)} collective-permute-done((bf16[256,2048]{1,0:T(8,128)(2,1)S(1)}, bf16[256,2048]{1,0:T(8,128)(2,1)S(1)}, u32[]{:S(2)}, u32[]{:S(2)}) %collective-permute-start.7) | collective-permute-done | bytes 1048608 | tf_op jit(solution)/shard_map/ppermute | solution.py:193
  109.7 22.5 %collective-permute-done.8 = bf16[256,2048]{1,0:T(8,128)(2,1)S(1)} collective-permute-done((bf16[256,2048]{1,0:T(8,128)(2,1)S(1)}, bf16[256,2048]{1,0:T(8,128)(2,1)S(1)}, u32[]{:S(2)}, u32[]{:S(2)}) %collective-permute-start.8) | collective-permute-done | bytes 1048608 | tf_op jit(solution)/shard_map/ppermute | solution.py:193
  132.2 21.8 %collective-permute-done.9 = bf16[256,2048]{1,0:T(8,128)(2,1)S(1)} collective-permute-done((bf16[256,2048]{1,0:T(8,128)(2,1)S(1)}, bf16[256,2048]{1,0:T(8,128)(2,1)S(1)}, u32[]{:S(2)}, u32[]{:S(2)}) %collective-permute-start.9) | collective-permute-done | bytes 1048608 | tf_op jit(solution)/shard_map/ppermute | solution.py:193
  154.0 2.0 %add_convert_fusion = bf16[256,6144]{1,0:T(8,128)(2,1)} fusion(bf16[256,6144]{1,0:T(8,128)(2,1)S(1)} %add_convert_fusion.1, bf16[256,2048]{1,0:T(8,128)(2,1)S(1)} %collective-permute-done.9, bf16[256,2048]{1,0:T(8,128)(2,1)S(1)} %collective-permute-done.8, bf16[256,2048]{1,0:T(8,128)(2,1)S(1)} %collective-permute-done.7), kind=kLoop, calls=%fused_computation.2 | loop fusion | flops 14155776 | bytes 9437184 | tf_op jit(solution)/shard_map/convert_element_type | solution.py:267
  (37 shorter events, 3.8 us)
Async XLA Ops:
  5.1 10.6 %collective-permute-start = (bf16[10,128,128]{2,1,0:T(8,128)(2,1)}, bf16[10,128,128]{2,1,0:T(8,128)(2,1)S(1)}, u32[]{:S(2)}, u32[]{:S(2)}) collective-permute-start(bf16[10,128,128]{2,1,0:T(8,128)(2,1)} %get-tuple-element.31), channel_id=1, source_target_pairs={{0,4},{4,8},{8,12},{12,16},{16,20},{20,24},{24,28},{28,0},{1,5},{5... | collective-permute-start | bytes 983048 | tf_op jit(solution)/shard_map/ppermute | solution.py:204
  6.6 9.1 %copy-start.1 = (f32[10,128,128]{2,1,0:T(8,128)S(1)}, f32[10,128,128]{2,1,0:T(8,128)}, u32[]{:S(2)}) copy-start(f32[10,128,128]{2,1,0:T(8,128)} %get-tuple-element.38) | copy-start | bytes 1966084
  15.8 10.0 %collective-permute-start.1 = (bf16[10,128,128]{2,1,0:T(8,128)(2,1)S(1)}, bf16[10,128,128]{2,1,0:T(8,128)(2,1)S(1)}, u32[]{:S(2)}, u32[]{:S(2)}) collective-permute-start(bf16[10,128,128]{2,1,0:T(8,128)(2,1)S(1)} %fusion.22), channel_id=1, source_target_pairs={{0,8},{4,12},{8,16},{12,20},{16,24},{20,28},{24,0},{28,4},{1,9},{5... | collective-permute-start | bytes 983048 | tf_op jit(solution)/shard_map/ppermute | solution.py:204
  18.2 7.9 %copy-start.2 = (f32[1280]{0:T(1024)S(1)}, f32[1280]{0:T(1024)}, u32[]{:S(2)}) copy-start(f32[1280]{0:T(1024)} %param.10) | copy-start | bytes 15364
  25.9 16.4 %collective-permute-start.2 = (bf16[10,128,128]{2,1,0:T(8,128)(2,1)S(1)}, bf16[10,128,128]{2,1,0:T(8,128)(2,1)S(1)}, u32[]{:S(2)}, u32[]{:S(2)}) collective-permute-start(bf16[10,128,128]{2,1,0:T(8,128)(2,1)S(1)} %fusion.18), channel_id=1, source_target_pairs={{0,16},{4,20},{8,24},{12,28},{16,0},{20,4},{24,8},{28,12},{1,17},{... | collective-permute-start | bytes 983048 | tf_op jit(solution)/shard_map/ppermute | solution.py:204
  49.8 5.9 %copy-start = (bf16[1024,1280]{1,0:T(8,128)(2,1)S(1)}, bf16[1024,1280]{1,0:T(8,128)(2,1)}, u32[]{:S(2)}) copy-start(bf16[1024,1280]{1,0:T(8,128)(2,1)} %shard_map.68) | copy-start | bytes 7864324
  49.8 12.7 %slice-start = ((s8[15728640]{0:T(1024)(128)(4,1)}), s8[4194304]{0:T(1024)(128)(4,1)S(1)}, s32[]{:S(2)}) async-start(s8[15728640]{0:T(1024)(128)(4,1)} %bitcast.2), calls=%async_computation | async-start | bytes 8388608
  49.8 12.7 %slice-start.1 = ((s8[15728640]{0:T(1024)(128)(4,1)}), s8[4194304]{0:T(1024)(128)(4,1)S(1)}, s32[]{:S(2)}) async-start(s8[15728640]{0:T(1024)(128)(4,1)} %bitcast.2), calls=%async_computation.1 | async-start | bytes 8388608
  55.8 6.7 %slice-start.2 = ((s8[15728640]{0:T(1024)(128)(4,1)}), s8[4194304]{0:T(1024)(128)(4,1)S(1)}, s32[]{:S(2)}) async-start(s8[15728640]{0:T(1024)(128)(4,1)} %bitcast.2), calls=%async_computation.2 | async-start | bytes 8388608
  55.8 6.7 %slice-start.3 = ((s8[15728640]{0:T(1024)(128)(4,1)}), s8[3145728]{0:T(1024)(128)(4,1)S(1)}, s32[]{:S(2)}) async-start(s8[15728640]{0:T(1024)(128)(4,1)} %bitcast.2), calls=%async_computation.3 | async-start | bytes 6291456
  61.7 4.2 %collective-permute-start.5 = (bf16[256,2048]{1,0:T(8,128)(2,1)S(1)}, bf16[256,2048]{1,0:T(8,128)(2,1)S(1)}, u32[]{:S(2)}, u32[]{:S(2)}) collective-permute-start(bf16[256,2048]{1,0:T(8,128)(2,1)S(1)} %constant_dynamic-slice_fusion.1), channel_id=1, source_target_pairs={{0,1},{1,0},{2,3},{3,2},{4,5},{5,4},{6,7},{7,6},{8,9},{9,8},{10,11... | collective-permute-start | bytes 3145736 | tf_op jit(solution)/shard_map/ppermute | solution.py:193
  61.9 4.5 %collective-permute-start.4 = (bf16[256,2048]{1,0:T(8,128)(2,1)S(1)}, bf16[256,2048]{1,0:T(8,128)(2,1)S(1)}, u32[]{:S(2)}, u32[]{:S(2)}) collective-permute-start(bf16[256,2048]{1,0:T(8,128)(2,1)S(1)} %constant_dynamic-slice_fusion.2), channel_id=1, source_target_pairs={{0,1},{1,0},{2,3},{3,2},{4,5},{5,4},{6,7},{7,6},{8,9},{9,8},{10,11... | collective-permute-start | bytes 3145736 | tf_op jit(solution)/shard_map/ppermute | solution.py:193
  65.7 2.7 %collective-permute-start.3 = (bf16[256,2048]{1,0:T(8,128)(2,1)S(1)}, bf16[256,2048]{1,0:T(8,128)(2,1)S(1)}, u32[]{:S(2)}, u32[]{:S(2)}) collective-permute-start(bf16[256,2048]{1,0:T(8,128)(2,1)S(1)} %constant_dynamic-slice_fusion.3), channel_id=1, source_target_pairs={{0,1},{1,0},{2,3},{3,2},{4,5},{5,4},{6,7},{7,6},{8,9},{9,8},{10,11... | collective-permute-start | bytes 3145736 | tf_op jit(solution)/shard_map/ppermute | solution.py:193
  73.4 13.5 %collective-permute-start.6 = (bf16[256,6144]{1,0:T(8,128)(2,1)S(1)}, bf16[256,6144]{1,0:T(8,128)(2,1)S(1)}, u32[]{:S(2)}, u32[]{:S(2)}) collective-permute-start(bf16[256,6144]{1,0:T(8,128)(2,1)S(1)} %convolution_convert_fusion), channel_id=1, source_target_pairs={{0,1},{1,0},{2,3},{3,2},{4,5},{5,4},{6,7},{7,6},{8,9},{9,8},{10,11... | collective-permute-start | bytes 9437192 | tf_op jit(solution)/shard_map/ppermute | solution.py:193
  83.6 26.1 %collective-permute-start.7 = (bf16[256,2048]{1,0:T(8,128)(2,1)S(1)}, bf16[256,2048]{1,0:T(8,128)(2,1)S(1)}, u32[]{:S(2)}, u32[]{:S(2)}) collective-permute-start(bf16[256,2048]{1,0:T(8,128)(2,1)S(1)} %add_convert_fusion.4), channel_id=1, source_target_pairs={{0,2},{2,0},{1,3},{3,1},{4,6},{6,4},{5,7},{7,5},{8,10},{10,8},{9,1... | collective-permute-start | bytes 3145736 | tf_op jit(solution)/shard_map/ppermute | solution.py:193
  84.8 47.4 %collective-permute-start.8 = (bf16[256,2048]{1,0:T(8,128)(2,1)S(1)}, bf16[256,2048]{1,0:T(8,128)(2,1)S(1)}, u32[]{:S(2)}, u32[]{:S(2)}) collective-permute-start(bf16[256,2048]{1,0:T(8,128)(2,1)S(1)} %add_convert_fusion.3), channel_id=1, source_target_pairs={{0,2},{2,0},{1,3},{3,1},{4,6},{6,4},{5,7},{7,5},{8,10},{10,8},{9,1... | collective-permute-start | bytes 3145736 | tf_op jit(solution)/shard_map/ppermute | solution.py:193
  85.7 68.2 %collective-permute-start.9 = (bf16[256,2048]{1,0:T(8,128)(2,1)S(1)}, bf16[256,2048]{1,0:T(8,128)(2,1)S(1)}, u32[]{:S(2)}, u32[]{:S(2)}) collective-permute-start(bf16[256,2048]{1,0:T(8,128)(2,1)S(1)} %add_convert_fusion.2), channel_id=1, source_target_pairs={{0,2},{2,0},{1,3},{3,1},{4,6},{6,4},{5,7},{7,5},{8,10},{10,8},{9,1... | collective-permute-start | bytes 3145736 | tf_op jit(solution)/shard_map/ppermute | solution.py:193

commit v22 on v20

--- a/solution.py
+++ b/solution.py
@@ -10,7 +10,7 @@
 HD = 128
 COLUMN_CHUNKS = 3
 QUERY_TILE = 256
-ROW_TILE = 512
+ROW_TILE = 1024
 
 
 epsilon = 1e-05

time: 150 us -> 151 us (level)
  Pallas kernels: 30.6 us -> 32.3 us
where the time goes in v22:
time: 151 us; the launch traced here: 150 us
  waiting for transfers between devices  74.4 us (49%)
  Pallas kernels  32.3 us (21%)
  matrix products  29.4 us (19%)
  starting transfers between devices  7.56 us (5%)
  other arithmetic  5.24 us (3%)
    ppermute x7, waiting for transfers between devices, swap(): return lax.ppermute(block, axis, [(0, 1), (1, 0)])  58.7 us
    ppermute x3, waiting for transfers between devices, exclusive_prefix(): lax.ppermute(sent, axis, [(i, (i + distance) % size) for i in range(size)])  15.7 us
    pallas_call x2, Pallas kernels, local_attention(): pl.pallas_call(local_kernel, grid=(heads,), in_specs=[picked] * 3, out_sp...  15.3 us
    dot_general x3, matrix products, project_and_reduce(): jnp.dot(far_rows, out_weight[:, c * chunk:(c + 1) * chunk], preferred_ele...  14.8 us
    dot_general x2, matrix products, product(): jnp.dot(rows, out_weight, preferred_element_type=jnp.float32)  14.6 us
    pallas_call x1, Pallas kernels, mix(): pl.pallas_call(mix_kernel, grid=(tokens // ROW_TILE,), in_specs=[row_bloc...  7.15 us
    pallas_call x1, Pallas kernels, key_value_states(): pl.pallas_call(state_kernel, grid=(tokens // ROW_TILE,), in_specs=[row_bl...  5.28 us
    pallas_call x1, Pallas kernels, gate_scale(): pl.pallas_call(gate_kernel, grid=(tokens // ROW_TILE,), in_specs=[row_blo...  4.6 us
  transfers between devices with their start and end apart: 10, of which 7 were waited for; matrix products, arithmetic and copies ran while one was open for 10% of the time, Pallas kernels for 13%

profile of v22, /device:TPU:0, one launch (start us, length us, event | category | flops | bytes accessed | tf_op | source)
XLA Modules:
  0.0 150.3 jit_solution(12284877781862663631)
XLA Ops:
  0.0 5.3 %shard_map.64 = (f32[10,128,128]{2,1,0:T(8,128)}, bf16[10,128,128]{2,1,0:T(8,128)(2,1)}) custom-call(bf16[1024,1280]{1,0:T(8,128)(2,1)} %k_ref.3, bf16[1024,1280]{1,0:T(8,128)(2,1)} %v_ref.3), custom_call_target="tpu_custom_call" | custom-call | flops 335544320 | bytes 5898240 | tf_op jit(solution)/shard_map/pallas_call | solution.py:54
  5.3 3.0 %collective-permute-start = (bf16[10,128,128]{2,1,0:T(8,128)(2,1)}, bf16[10,128,128]{2,1,0:T(8,128)(2,1)S(1)}, u32[]{:S(2)}, u32[]{:S(2)}) collective-permute-start(bf16[10,128,128]{2,1,0:T(8,128)(2,1)} %get-tuple-element.31), channel_id=1, source_target_pairs={{0,4},{4,8},{8,12},{12,16},{16,20},{20,24},{24,28},{28,0},{1,5},{5... | collective-permute-start | bytes 983048 | tf_op jit(solution)/shard_map/ppermute | solution.py:204
  8.3 7.7 %shard_map.65 = (bf16[1024,640]{1,0:T(8,128)(2,1)}, bf16[1024,640]{1,0:T(8,128)(2,1)}) custom-call(bf16[1024,1280]{1,0:T(8,128)(2,1)} %q_ref.1, bf16[1024,1280]{1,0:T(8,128)(2,1)} %k_ref.3, bf16[1024,1280]{1,0:T(8,128)(2,1)} %v_ref.3), custom_call_target="tpu_custom_call" | custom-call | flops 1677721600 | bytes 6553600 | tf_op jit(solution)/shard_map/pallas_call | solution.py:98
  15.9 3.3 %collective-permute-done = bf16[10,128,128]{2,1,0:T(8,128)(2,1)S(1)} collective-permute-done((bf16[10,128,128]{2,1,0:T(8,128)(2,1)}, bf16[10,128,128]{2,1,0:T(8,128)(2,1)S(1)}, u32[]{:S(2)}, u32[]{:S(2)}) %collective-permute-start) | collective-permute-done | bytes 327712 | tf_op jit(solution)/shard_map/ppermute | solution.py:204
  19.6 7.6 %shard_map.66 = (bf16[1024,640]{1,0:T(8,128)(2,1)}, bf16[1024,640]{1,0:T(8,128)(2,1)}) custom-call(bf16[1024,1280]{1,0:T(8,128)(2,1)} %q_ref.1, bf16[1024,1280]{1,0:T(8,128)(2,1)} %k_ref.3, bf16[1024,1280]{1,0:T(8,128)(2,1)} %v_ref.3), custom_call_target="tpu_custom_call" | custom-call | flops 1677721600 | bytes 6553600 | tf_op jit(solution)/shard_map/pallas_call | solution.py:98
  27.2 3.0 %collective-permute-done.1 = bf16[10,128,128]{2,1,0:T(8,128)(2,1)S(1)} collective-permute-done((bf16[10,128,128]{2,1,0:T(8,128)(2,1)S(1)}, bf16[10,128,128]{2,1,0:T(8,128)(2,1)S(1)}, u32[]{:S(2)}, u32[]{:S(2)}) %collective-permute-start.1) | collective-permute-done | bytes 327712 | tf_op jit(solution)/shard_map/ppermute | solution.py:204
  30.5 0.6 reshape.3.gain_ref
  31.1 4.6 %shard_map.67.scale_ref = bf16[1024,1280]{1,0:T(8,128)(2,1)} custom-call(bf16[1024,1280]{1,0:T(8,128)(2,1)} %g_ref, f32[1,1280]{1,0:T(1,128)} %reshape.3.gain_ref), custom_call_target="tpu_custom_call" | custom-call | flops 5242880 | bytes 5242880 | tf_op jit(solution)/shard_map/pallas_call | solution.py:119
  35.7 9.4 %collective-permute-done.2 = bf16[10,128,128]{2,1,0:T(8,128)(2,1)S(1)} collective-permute-done((bf16[10,128,128]{2,1,0:T(8,128)(2,1)S(1)}, bf16[10,128,128]{2,1,0:T(8,128)(2,1)S(1)}, u32[]{:S(2)}, u32[]{:S(2)}) %collective-permute-start.2) | collective-permute-done | bytes 327712 | tf_op jit(solution)/shard_map/ppermute | solution.py:204
  45.2 1.0 fusion.19.prefix_ref
  46.2 7.1 %shard_map.68 = bf16[1024,1280]{1,0:T(8,128)(2,1)} custom-call(bf16[1024,640]{1,0:T(8,128)(2,1)} %get-tuple-element.37.local_a_ref, bf16[1024,640]{1,0:T(8,128)(2,1)} %get-tuple-element.45.local_b_ref, bf16[1024,640]{1,0:T(8,128)(2,1)} %get-tuple-element.46.qa_a_ref, bf16[1024,640]{1,0:T(8,128)(2,1)} %get-tuple-element.47.qa_b_ref, ...), custom_call_target="tpu_custom_call" | custom-call | flops 671088640 | bytes 15728640 | tf_op jit(solution)/shard_map/pallas_call | solution.py:160
  53.3 5.9 %fusion.12 = bf16[512,2048]{1,0:T(8,128)(2,1)S(1)} fusion(bf16[1280,6144]{1,0:T(8,128)(2,1)} %param.11, bf16[1024,1280]{1,0:T(8,128)(2,1)} %shard_map.68, s32[]{:T(128)S(6)} %select_n.44), kind=kOutput, calls=%fused_computation.11 | convolution fusion | flops 2685403136 | bytes 8650756 | tf_op jit(solution)/shard_map/dot_general | solution.py:253
  59.3 5.8 %fusion.9 = bf16[512,2048]{1,0:T(8,128)(2,1)S(1)} fusion(bf16[1280,6144]{1,0:T(8,128)(2,1)} %param.11, bf16[1024,1280]{1,0:T(8,128)(2,1)S(1)} %copy-done, s32[]{:T(128)S(6)} %select_n.44), kind=kOutput, calls=%fused_computation.10 | convolution fusion | flops 2685403136 | bytes 8650756 | tf_op jit(solution)/shard_map/dot_general | solution.py:253
  66.0 3.1 %fusion.6 = bf16[512,2048]{1,0:T(8,128)(2,1)S(1)} fusion(bf16[1280,6144]{1,0:T(8,128)(2,1)S(1)} %bitcast.3, bf16[1024,1280]{1,0:T(8,128)(2,1)S(1)} %copy-done, s32[]{:T(128)S(6)} %select_n.44), kind=kOutput, calls=%fused_computation.9 | convolution fusion | flops 2685403136 | bytes 8650756 | tf_op jit(solution)/shard_map/dot_general | solution.py:253
  70.3 1.6 %collective-permute-done.3 = bf16[256,2048]{1,0:T(8,128)(2,1)S(1)} collective-permute-done((bf16[256,2048]{1,0:T(8,128)(2,1)S(1)}, bf16[256,2048]{1,0:T(8,128)(2,1)S(1)}, u32[]{:S(2)}, u32[]{:S(2)}) %collective-permute-start.3) | collective-permute-done | bytes 1048608 | tf_op jit(solution)/shard_map/ppermute | solution.py:193
  72.4 4.7 %convolution_convert_fusion = bf16[256,6144]{1,0:T(8,128)(2,1)S(1)} fusion(bf16[1280,6144]{1,0:T(8,128)(2,1)S(1)} %bitcast.3, bf16[512,1280]{1,0:T(8,128)(2,1)S(1)} %constant_dynamic-slice_fusion, s32[]{:T(128)S(6)} %select_n.46), kind=kOutput, calls=%fused_computation | convolution fusion | flops 4028104704 | bytes 19529732 | tf_op jit(solution)/shard_map/dot_general | solution.py:229
  77.3 1.3 collective-permute-start.7
  78.6 0.7 collective-permute-start.8
  79.3 1.3 collective-permute-start.9
  80.7 9.9 %convolution_convert_fusion.1 = bf16[256,6144]{1,0:T(8,128)(2,1)S(1)} fusion(bf16[1280,6144]{1,0:T(8,128)(2,1)} %param.11, bf16[512,1280]{1,0:T(8,128)(2,1)S(1)} %constant_dynamic-slice_fusion, s32[]{:T(128)S(6)} %select_n.45), kind=kOutput, calls=%fused_computation.1 | convolution fusion | flops 4028104704 | bytes 19529732 | tf_op jit(solution)/shard_map/dot_general | solution.py:229
  90.6 12.7 %collective-permute-done.7 = bf16[256,2048]{1,0:T(8,128)(2,1)S(1)} collective-permute-done((bf16[256,2048]{1,0:T(8,128)(2,1)S(1)}, bf16[256,2048]{1,0:T(8,128)(2,1)S(1)}, u32[]{:S(2)}, u32[]{:S(2)}) %collective-permute-start.7) | collective-permute-done | bytes 1048608 | tf_op jit(solution)/shard_map/ppermute | solution.py:193
  103.3 22.5 %collective-permute-done.8 = bf16[256,2048]{1,0:T(8,128)(2,1)S(1)} collective-permute-done((bf16[256,2048]{1,0:T(8,128)(2,1)S(1)}, bf16[256,2048]{1,0:T(8,128)(2,1)S(1)}, u32[]{:S(2)}, u32[]{:S(2)}) %collective-permute-start.8) | collective-permute-done | bytes 1048608 | tf_op jit(solution)/shard_map/ppermute | solution.py:193
  125.8 21.9 %collective-permute-done.9 = bf16[256,2048]{1,0:T(8,128)(2,1)S(1)} collective-permute-done((bf16[256,2048]{1,0:T(8,128)(2,1)S(1)}, bf16[256,2048]{1,0:T(8,128)(2,1)S(1)}, u32[]{:S(2)}, u32[]{:S(2)}) %collective-permute-start.9) | collective-permute-done | bytes 1048608 | tf_op jit(solution)/shard_map/ppermute | solution.py:193
  147.7 2.6 %add_convert_fusion = bf16[256,6144]{1,0:T(8,128)(2,1)} fusion(bf16[256,6144]{1,0:T(8,128)(2,1)S(1)} %collective-permute-done.6, bf16[256,6144]{1,0:T(8,128)(2,1)S(1)} %convolution_convert_fusion.1, bf16[256,2048]{1,0:T(8,128)(2,1)S(1)} %collective-permute-done.9, bf16[256,2048]{1,0:T(8,128)(2,1)S(1)} %collective-permute-done.8, ...), kind=kLoop, calls=%fused_computation.2 | loop fusion | flops 17301504 | bytes 12582912 | tf_op jit(solution)/shard_map/convert_element_type | solution.py:265
  (36 shorter events, 3.3 us)
Async XLA Ops:
  5.3 13.9 %collective-permute-start = (bf16[10,128,128]{2,1,0:T(8,128)(2,1)}, bf16[10,128,128]{2,1,0:T(8,128)(2,1)S(1)}, u32[]{:S(2)}, u32[]{:S(2)}) collective-permute-start(bf16[10,128,128]{2,1,0:T(8,128)(2,1)} %get-tuple-element.31), channel_id=1, source_target_pairs={{0,4},{4,8},{8,12},{12,16},{16,20},{20,24},{24,28},{28,0},{1,5},{5... | collective-permute-start | bytes 983048 | tf_op jit(solution)/shard_map/ppermute | solution.py:204
  8.3 11.0 %copy-start.1 = (f32[10,128,128]{2,1,0:T(8,128)S(1)}, f32[10,128,128]{2,1,0:T(8,128)}, u32[]{:S(2)}) copy-start(f32[10,128,128]{2,1,0:T(8,128)} %get-tuple-element.38) | copy-start | bytes 1966084
  19.3 10.9 %collective-permute-start.1 = (bf16[10,128,128]{2,1,0:T(8,128)(2,1)S(1)}, bf16[10,128,128]{2,1,0:T(8,128)(2,1)S(1)}, u32[]{:S(2)}, u32[]{:S(2)}) collective-permute-start(bf16[10,128,128]{2,1,0:T(8,128)(2,1)S(1)} %fusion.22), channel_id=1, source_target_pairs={{0,8},{4,12},{8,16},{12,20},{16,24},{20,28},{24,0},{28,4},{1,9},{5... | collective-permute-start | bytes 983048 | tf_op jit(solution)/shard_map/ppermute | solution.py:204
  19.6 10.9 %copy-start.2 = (f32[1280]{0:T(1024)S(1)}, f32[1280]{0:T(1024)}, u32[]{:S(2)}) copy-start(f32[1280]{0:T(1024)} %param.10) | copy-start | bytes 15364
  30.4 14.7 %collective-permute-start.2 = (bf16[10,128,128]{2,1,0:T(8,128)(2,1)S(1)}, bf16[10,128,128]{2,1,0:T(8,128)(2,1)S(1)}, u32[]{:S(2)}, u32[]{:S(2)}) collective-permute-start(bf16[10,128,128]{2,1,0:T(8,128)(2,1)S(1)} %fusion.18), channel_id=1, source_target_pairs={{0,16},{4,20},{8,24},{12,28},{16,0},{20,4},{24,8},{28,12},{1,17},{... | collective-permute-start | bytes 983048 | tf_op jit(solution)/shard_map/ppermute | solution.py:204
  53.3 5.9 %copy-start = (bf16[1024,1280]{1,0:T(8,128)(2,1)S(1)}, bf16[1024,1280]{1,0:T(8,128)(2,1)}, u32[]{:S(2)}) copy-start(bf16[1024,1280]{1,0:T(8,128)(2,1)} %shard_map.68) | copy-start | bytes 7864324
  53.3 12.6 %slice-start = ((s8[15728640]{0:T(1024)(128)(4,1)}), s8[4194304]{0:T(1024)(128)(4,1)S(1)}, s32[]{:S(2)}) async-start(s8[15728640]{0:T(1024)(128)(4,1)} %bitcast.2), calls=%async_computation | async-start | bytes 8388608
  53.3 12.6 %slice-start.1 = ((s8[15728640]{0:T(1024)(128)(4,1)}), s8[4194304]{0:T(1024)(128)(4,1)S(1)}, s32[]{:S(2)}) async-start(s8[15728640]{0:T(1024)(128)(4,1)} %bitcast.2), calls=%async_computation.1 | async-start | bytes 8388608
  59.3 6.7 %slice-start.2 = ((s8[15728640]{0:T(1024)(128)(4,1)}), s8[4194304]{0:T(1024)(128)(4,1)S(1)}, s32[]{:S(2)}) async-start(s8[15728640]{0:T(1024)(128)(4,1)} %bitcast.2), calls=%async_computation.2 | async-start | bytes 8388608
  59.3 6.7 %slice-start.3 = ((s8[15728640]{0:T(1024)(128)(4,1)}), s8[3145728]{0:T(1024)(128)(4,1)S(1)}, s32[]{:S(2)}) async-start(s8[15728640]{0:T(1024)(128)(4,1)} %bitcast.2), calls=%async_computation.3 | async-start | bytes 6291456
  65.2 4.2 %collective-permute-start.5 = (bf16[256,2048]{1,0:T(8,128)(2,1)S(1)}, bf16[256,2048]{1,0:T(8,128)(2,1)S(1)}, u32[]{:S(2)}, u32[]{:S(2)}) collective-permute-start(bf16[256,2048]{1,0:T(8,128)(2,1)S(1)} %constant_dynamic-slice_fusion.1), channel_id=1, source_target_pairs={{0,1},{1,0},{2,3},{3,2},{4,5},{5,4},{6,7},{7,6},{8,9},{9,8},{10,11... | collective-permute-start | bytes 3145736 | tf_op jit(solution)/shard_map/ppermute | solution.py:193
  65.4 4.5 %collective-permute-start.4 = (bf16[256,2048]{1,0:T(8,128)(2,1)S(1)}, bf16[256,2048]{1,0:T(8,128)(2,1)S(1)}, u32[]{:S(2)}, u32[]{:S(2)}) collective-permute-start(bf16[256,2048]{1,0:T(8,128)(2,1)S(1)} %constant_dynamic-slice_fusion.2), channel_id=1, source_target_pairs={{0,1},{1,0},{2,3},{3,2},{4,5},{5,4},{6,7},{7,6},{8,9},{9,8},{10,11... | collective-permute-start | bytes 3145736 | tf_op jit(solution)/shard_map/ppermute | solution.py:193
  69.2 2.7 %collective-permute-start.3 = (bf16[256,2048]{1,0:T(8,128)(2,1)S(1)}, bf16[256,2048]{1,0:T(8,128)(2,1)S(1)}, u32[]{:S(2)}, u32[]{:S(2)}) collective-permute-start(bf16[256,2048]{1,0:T(8,128)(2,1)S(1)} %constant_dynamic-slice_fusion.3), channel_id=1, source_target_pairs={{0,1},{1,0},{2,3},{3,2},{4,5},{5,4},{6,7},{7,6},{8,9},{9,8},{10,11... | collective-permute-start | bytes 3145736 | tf_op jit(solution)/shard_map/ppermute | solution.py:193
  77.1 70.6 %collective-permute-start.6 = (bf16[256,6144]{1,0:T(8,128)(2,1)S(1)}, bf16[256,6144]{1,0:T(8,128)(2,1)S(1)}, u32[]{:S(2)}, u32[]{:S(2)}) collective-permute-start(bf16[256,6144]{1,0:T(8,128)(2,1)S(1)} %convolution_convert_fusion), channel_id=1, source_target_pairs={{0,1},{1,0},{2,3},{3,2},{4,5},{5,4},{6,7},{7,6},{8,9},{9,8},{10,11... | collective-permute-start | bytes 9437192 | tf_op jit(solution)/shard_map/ppermute | solution.py:193
  77.3 26.0 %collective-permute-start.7 = (bf16[256,2048]{1,0:T(8,128)(2,1)S(1)}, bf16[256,2048]{1,0:T(8,128)(2,1)S(1)}, u32[]{:S(2)}, u32[]{:S(2)}) collective-permute-start(bf16[256,2048]{1,0:T(8,128)(2,1)S(1)} %add_convert_fusion.3), channel_id=1, source_target_pairs={{0,2},{2,0},{1,3},{3,1},{4,6},{6,4},{5,7},{7,5},{8,10},{10,8},{9,1... | collective-permute-start | bytes 3145736 | tf_op jit(solution)/shard_map/ppermute | solution.py:193
  78.6 47.2 %collective-permute-start.8 = (bf16[256,2048]{1,0:T(8,128)(2,1)S(1)}, bf16[256,2048]{1,0:T(8,128)(2,1)S(1)}, u32[]{:S(2)}, u32[]{:S(2)}) collective-permute-start(bf16[256,2048]{1,0:T(8,128)(2,1)S(1)} %add_convert_fusion.2), channel_id=1, source_target_pairs={{0,2},{2,0},{1,3},{3,1},{4,6},{6,4},{5,7},{7,5},{8,10},{10,8},{9,1... | collective-permute-start | bytes 3145736 | tf_op jit(solution)/shard_map/ppermute | solution.py:193
  79.3 68.4 %collective-permute-start.9 = (bf16[256,2048]{1,0:T(8,128)(2,1)S(1)}, bf16[256,2048]{1,0:T(8,128)(2,1)S(1)}, u32[]{:S(2)}, u32[]{:S(2)}) collective-permute-start(bf16[256,2048]{1,0:T(8,128)(2,1)S(1)} %add_convert_fusion.1), channel_id=1, source_target_pairs={{0,2},{2,0},{1,3},{3,1},{4,6},{6,4},{5,7},{7,5},{8,10},{10,8},{9,1... | collective-permute-start | bytes 3145736 | tf_op jit(solution)/shard_map/ppermute | solution.py:193

commit v23 on v20

--- a/solution.py
+++ b/solution.py
@@ -53,8 +53,8 @@
     heads = columns // HD
     return pl.pallas_call(
         state_kernel,
-        grid=(tokens // ROW_TILE,),
-        in_specs=[row_block(columns), row_block(columns)],
+        grid=(1,),
+        in_specs=[pl.BlockSpec((tokens, columns), lambda i: (0, 0))] * 2,
         out_specs=[pl.BlockSpec((heads, HD, HD), lambda i: (0, 0, 0))] * 2,
         out_shape=[
             jax.ShapeDtypeStruct((heads, HD, HD), jnp.float32),

time: 150 us -> 150 us (level)
  the two profiles are of different devices: /device:TPU:0 before, /device:TPU:24 now
where the time goes in v23:
time: 150 us; the launch traced here: 147 us
  waiting for transfers between devices  72.2 us (48%)
  Pallas kernels  30.8 us (21%)
  matrix products  29.2 us (19%)
  starting transfers between devices  8.06 us (5%)
  other arithmetic  5.24 us (3%)
    ppermute x7, waiting for transfers between devices, swap(): return lax.ppermute(block, axis, [(0, 1), (1, 0)])  58.9 us
    pallas_call x2, Pallas kernels, local_attention(): pl.pallas_call(local_kernel, grid=(heads,), in_specs=[picked] * 3, out_sp...  15.3 us
    dot_general x3, matrix products, project_and_reduce(): jnp.dot(far_rows, out_weight[:, c * chunk:(c + 1) * chunk], preferred_ele...  14.8 us
    dot_general x2, matrix products, product(): jnp.dot(rows, out_weight, preferred_element_type=jnp.float32)  14.4 us
    ppermute x3, waiting for transfers between devices, exclusive_prefix(): lax.ppermute(sent, axis, [(i, (i + distance) % size) for i in range(size)])  13.3 us
    pallas_call x1, Pallas kernels, mix(): pl.pallas_call(mix_kernel, grid=(tokens // ROW_TILE,), in_specs=[row_bloc...  6.41 us
    pallas_call x1, Pallas kernels, key_value_states(): pl.pallas_call(state_kernel, grid=(1,), in_specs=[pl.BlockSpec((tokens, c...  5.28 us
    ppermute x7, starting transfers between devices, swap(): return lax.ppermute(block, axis, [(0, 1), (1, 0)])  4.09 us
  transfers between devices with their start and end apart: 10, of which 6 were waited for; matrix products, arithmetic and copies ran while one was open for 10% of the time, Pallas kernels for 13%

profile of v23, /device:TPU:24, one launch (start us, length us, event | category | flops | bytes accessed | tf_op | source)
XLA Modules:
  0.0 146.7 jit_solution(8613056450258045029)
XLA Ops:
  0.0 5.3 %shard_map.64 = (f32[10,128,128]{2,1,0:T(8,128)}, bf16[10,128,128]{2,1,0:T(8,128)(2,1)}) custom-call(bf16[1024,1280]{1,0:T(8,128)(2,1)} %k_ref.3, bf16[1024,1280]{1,0:T(8,128)(2,1)} %v_ref.3), custom_call_target="tpu_custom_call" | custom-call | flops 335544320 | bytes 5898240 | tf_op jit(solution)/shard_map/pallas_call | solution.py:54
  5.3 1.5 %collective-permute-start = (bf16[10,128,128]{2,1,0:T(8,128)(2,1)}, bf16[10,128,128]{2,1,0:T(8,128)(2,1)S(1)}, u32[]{:S(2)}, u32[]{:S(2)}) collective-permute-start(bf16[10,128,128]{2,1,0:T(8,128)(2,1)} %get-tuple-element.31), channel_id=1, source_target_pairs={{0,4},{4,8},{8,12},{12,16},{16,20},{20,24},{24,28},{28,0},{1,5},{5... | collective-permute-start | bytes 983048 | tf_op jit(solution)/shard_map/ppermute | solution.py:204
  6.8 7.7 %shard_map.65 = (bf16[1024,640]{1,0:T(8,128)(2,1)}, bf16[1024,640]{1,0:T(8,128)(2,1)}) custom-call(bf16[1024,1280]{1,0:T(8,128)(2,1)} %q_ref.1, bf16[1024,1280]{1,0:T(8,128)(2,1)} %k_ref.3, bf16[1024,1280]{1,0:T(8,128)(2,1)} %v_ref.3), custom_call_target="tpu_custom_call" | custom-call | flops 1677721600 | bytes 6553600 | tf_op jit(solution)/shard_map/pallas_call | solution.py:98
  14.5 1.4 collective-permute-done
  16.0 2.3 %collective-permute-start.1 = (bf16[10,128,128]{2,1,0:T(8,128)(2,1)S(1)}, bf16[10,128,128]{2,1,0:T(8,128)(2,1)S(1)}, u32[]{:S(2)}, u32[]{:S(2)}) collective-permute-start(bf16[10,128,128]{2,1,0:T(8,128)(2,1)S(1)} %fusion.22), channel_id=1, source_target_pairs={{0,8},{4,12},{8,16},{12,20},{16,24},{20,28},{24,0},{28,4},{1,9},{5... | collective-permute-start | bytes 983048 | tf_op jit(solution)/shard_map/ppermute | solution.py:204
  18.3 7.6 %shard_map.66 = (bf16[1024,640]{1,0:T(8,128)(2,1)}, bf16[1024,640]{1,0:T(8,128)(2,1)}) custom-call(bf16[1024,1280]{1,0:T(8,128)(2,1)} %q_ref.1, bf16[1024,1280]{1,0:T(8,128)(2,1)} %k_ref.3, bf16[1024,1280]{1,0:T(8,128)(2,1)} %v_ref.3), custom_call_target="tpu_custom_call" | custom-call | flops 1677721600 | bytes 6553600 | tf_op jit(solution)/shard_map/pallas_call | solution.py:98
  26.3 0.6 reshape.3.gain_ref
  26.8 3.8 %shard_map.67.scale_ref = bf16[1024,1280]{1,0:T(8,128)(2,1)} custom-call(bf16[1024,1280]{1,0:T(8,128)(2,1)} %g_ref, f32[1,1280]{1,0:T(1,128)} %reshape.3.gain_ref), custom_call_target="tpu_custom_call" | custom-call | flops 5242880 | bytes 5242880 | tf_op jit(solution)/shard_map/pallas_call | solution.py:119
  30.6 11.9 %collective-permute-done.2 = bf16[10,128,128]{2,1,0:T(8,128)(2,1)S(1)} collective-permute-done((bf16[10,128,128]{2,1,0:T(8,128)(2,1)S(1)}, bf16[10,128,128]{2,1,0:T(8,128)(2,1)S(1)}, u32[]{:S(2)}, u32[]{:S(2)}) %collective-permute-start.2) | collective-permute-done | bytes 327712 | tf_op jit(solution)/shard_map/ppermute | solution.py:204
  42.6 1.0 fusion.19.prefix_ref
  43.6 6.4 %shard_map.68 = bf16[1024,1280]{1,0:T(8,128)(2,1)} custom-call(bf16[1024,640]{1,0:T(8,128)(2,1)} %get-tuple-element.37.local_a_ref, bf16[1024,640]{1,0:T(8,128)(2,1)} %get-tuple-element.45.local_b_ref, bf16[1024,640]{1,0:T(8,128)(2,1)} %get-tuple-element.46.qa_a_ref, bf16[1024,640]{1,0:T(8,128)(2,1)} %get-tuple-element.47.qa_b_ref, ...), custom_call_target="tpu_custom_call" | custom-call | flops 671088640 | bytes 15728640 | tf_op jit(solution)/shard_map/pallas_call | solution.py:160
  50.0 5.9 %fusion.12 = bf16[512,2048]{1,0:T(8,128)(2,1)S(1)} fusion(bf16[1280,6144]{1,0:T(8,128)(2,1)} %param.11, bf16[1024,1280]{1,0:T(8,128)(2,1)} %shard_map.68, s32[]{:T(128)S(6)} %select_n.44), kind=kOutput, calls=%fused_computation.11 | convolution fusion | flops 2685403136 | bytes 8650756 | tf_op jit(solution)/shard_map/dot_general | solution.py:253
  56.0 5.8 %fusion.9 = bf16[512,2048]{1,0:T(8,128)(2,1)S(1)} fusion(bf16[1280,6144]{1,0:T(8,128)(2,1)} %param.11, bf16[1024,1280]{1,0:T(8,128)(2,1)S(1)} %copy-done, s32[]{:T(128)S(6)} %select_n.44), kind=kOutput, calls=%fused_computation.10 | convolution fusion | flops 2685403136 | bytes 8650756 | tf_op jit(solution)/shard_map/dot_general | solution.py:253
  62.7 3.1 %fusion.6 = bf16[512,2048]{1,0:T(8,128)(2,1)S(1)} fusion(bf16[1280,6144]{1,0:T(8,128)(2,1)S(1)} %bitcast.3, bf16[1024,1280]{1,0:T(8,128)(2,1)S(1)} %copy-done, s32[]{:T(128)S(6)} %select_n.44), kind=kOutput, calls=%fused_computation.9 | convolution fusion | flops 2685403136 | bytes 8650756 | tf_op jit(solution)/shard_map/dot_general | solution.py:253
  67.0 1.6 %collective-permute-done.3 = bf16[256,2048]{1,0:T(8,128)(2,1)S(1)} collective-permute-done((bf16[256,2048]{1,0:T(8,128)(2,1)S(1)}, bf16[256,2048]{1,0:T(8,128)(2,1)S(1)}, u32[]{:S(2)}, u32[]{:S(2)}) %collective-permute-start.3) | collective-permute-done | bytes 1048608 | tf_op jit(solution)/shard_map/ppermute | solution.py:193
  69.1 4.4 %convolution_convert_fusion = bf16[256,6144]{1,0:T(8,128)(2,1)S(1)} fusion(bf16[1280,6144]{1,0:T(8,128)(2,1)S(1)} %bitcast.3, bf16[512,1280]{1,0:T(8,128)(2,1)S(1)} %constant_dynamic-slice_fusion, s32[]{:T(128)S(6)} %select_n.46), kind=kOutput, calls=%fused_computation | convolution fusion | flops 4028104704 | bytes 19529732 | tf_op jit(solution)/shard_map/dot_general | solution.py:229
  73.8 1.1 collective-permute-start.7
  74.9 0.9 collective-permute-start.8
  75.8 1.1 collective-permute-start.9
  76.9 9.9 %convolution_convert_fusion.1 = bf16[256,6144]{1,0:T(8,128)(2,1)S(1)} fusion(bf16[1280,6144]{1,0:T(8,128)(2,1)} %param.11, bf16[512,1280]{1,0:T(8,128)(2,1)S(1)} %constant_dynamic-slice_fusion, s32[]{:T(128)S(6)} %select_n.45), kind=kOutput, calls=%fused_computation.1 | convolution fusion | flops 4028104704 | bytes 19529732 | tf_op jit(solution)/shard_map/dot_general | solution.py:229
  86.8 12.9 %collective-permute-done.7 = bf16[256,2048]{1,0:T(8,128)(2,1)S(1)} collective-permute-done((bf16[256,2048]{1,0:T(8,128)(2,1)S(1)}, bf16[256,2048]{1,0:T(8,128)(2,1)S(1)}, u32[]{:S(2)}, u32[]{:S(2)}) %collective-permute-start.7) | collective-permute-done | bytes 1048608 | tf_op jit(solution)/shard_map/ppermute | solution.py:193
  99.8 22.5 %collective-permute-done.8 = bf16[256,2048]{1,0:T(8,128)(2,1)S(1)} collective-permute-done((bf16[256,2048]{1,0:T(8,128)(2,1)S(1)}, bf16[256,2048]{1,0:T(8,128)(2,1)S(1)}, u32[]{:S(2)}, u32[]{:S(2)}) %collective-permute-start.8) | collective-permute-done | bytes 1048608 | tf_op jit(solution)/shard_map/ppermute | solution.py:193
  122.3 21.9 %collective-permute-done.9 = bf16[256,2048]{1,0:T(8,128)(2,1)S(1)} collective-permute-done((bf16[256,2048]{1,0:T(8,128)(2,1)S(1)}, bf16[256,2048]{1,0:T(8,128)(2,1)S(1)}, u32[]{:S(2)}, u32[]{:S(2)}) %collective-permute-start.9) | collective-permute-done | bytes 1048608 | tf_op jit(solution)/shard_map/ppermute | solution.py:193
  144.1 2.6 %add_convert_fusion = bf16[256,6144]{1,0:T(8,128)(2,1)} fusion(bf16[256,6144]{1,0:T(8,128)(2,1)S(1)} %collective-permute-done.6, bf16[256,6144]{1,0:T(8,128)(2,1)S(1)} %convolution_convert_fusion.1, bf16[256,2048]{1,0:T(8,128)(2,1)S(1)} %collective-permute-done.9, bf16[256,2048]{1,0:T(8,128)(2,1)S(1)} %collective-permute-done.8, ...), kind=kLoop, calls=%fused_computation.2 | loop fusion | flops 17301504 | bytes 12582912 | tf_op jit(solution)/shard_map/convert_element_type | solution.py:265
  (36 shorter events, 3.2 us)
Async XLA Ops:
  5.3 10.6 %collective-permute-start = (bf16[10,128,128]{2,1,0:T(8,128)(2,1)}, bf16[10,128,128]{2,1,0:T(8,128)(2,1)S(1)}, u32[]{:S(2)}, u32[]{:S(2)}) collective-permute-start(bf16[10,128,128]{2,1,0:T(8,128)(2,1)} %get-tuple-element.31), channel_id=1, source_target_pairs={{0,4},{4,8},{8,12},{12,16},{16,20},{20,24},{24,28},{28,0},{1,5},{5... | collective-permute-start | bytes 983048 | tf_op jit(solution)/shard_map/ppermute | solution.py:204
  6.8 9.1 %copy-start.1 = (f32[10,128,128]{2,1,0:T(8,128)S(1)}, f32[10,128,128]{2,1,0:T(8,128)}, u32[]{:S(2)}) copy-start(f32[10,128,128]{2,1,0:T(8,128)} %get-tuple-element.38) | copy-start | bytes 1966084
  16.0 10.0 %collective-permute-start.1 = (bf16[10,128,128]{2,1,0:T(8,128)(2,1)S(1)}, bf16[10,128,128]{2,1,0:T(8,128)(2,1)S(1)}, u32[]{:S(2)}, u32[]{:S(2)}) collective-permute-start(bf16[10,128,128]{2,1,0:T(8,128)(2,1)S(1)} %fusion.22), channel_id=1, source_target_pairs={{0,8},{4,12},{8,16},{12,20},{16,24},{20,28},{24,0},{28,4},{1,9},{5... | collective-permute-start | bytes 983048 | tf_op jit(solution)/shard_map/ppermute | solution.py:204
  18.3 7.9 %copy-start.2 = (f32[1280]{0:T(1024)S(1)}, f32[1280]{0:T(1024)}, u32[]{:S(2)}) copy-start(f32[1280]{0:T(1024)} %param.10) | copy-start | bytes 15364
  26.1 16.4 %collective-permute-start.2 = (bf16[10,128,128]{2,1,0:T(8,128)(2,1)S(1)}, bf16[10,128,128]{2,1,0:T(8,128)(2,1)S(1)}, u32[]{:S(2)}, u32[]{:S(2)}) collective-permute-start(bf16[10,128,128]{2,1,0:T(8,128)(2,1)S(1)} %fusion.18), channel_id=1, source_target_pairs={{0,16},{4,20},{8,24},{12,28},{16,0},{20,4},{24,8},{28,12},{1,17},{... | collective-permute-start | bytes 983048 | tf_op jit(solution)/shard_map/ppermute | solution.py:204
  50.0 5.9 %copy-start = (bf16[1024,1280]{1,0:T(8,128)(2,1)S(1)}, bf16[1024,1280]{1,0:T(8,128)(2,1)}, u32[]{:S(2)}) copy-start(bf16[1024,1280]{1,0:T(8,128)(2,1)} %shard_map.68) | copy-start | bytes 7864324
  50.0 12.7 %slice-start = ((s8[15728640]{0:T(1024)(128)(4,1)}), s8[4194304]{0:T(1024)(128)(4,1)S(1)}, s32[]{:S(2)}) async-start(s8[15728640]{0:T(1024)(128)(4,1)} %bitcast.2), calls=%async_computation | async-start | bytes 8388608
  50.0 12.7 %slice-start.1 = ((s8[15728640]{0:T(1024)(128)(4,1)}), s8[4194304]{0:T(1024)(128)(4,1)S(1)}, s32[]{:S(2)}) async-start(s8[15728640]{0:T(1024)(128)(4,1)} %bitcast.2), calls=%async_computation.1 | async-start | bytes 8388608
  55.9 6.7 %slice-start.2 = ((s8[15728640]{0:T(1024)(128)(4,1)}), s8[4194304]{0:T(1024)(128)(4,1)S(1)}, s32[]{:S(2)}) async-start(s8[15728640]{0:T(1024)(128)(4,1)} %bitcast.2), calls=%async_computation.2 | async-start | bytes 8388608
  55.9 6.7 %slice-start.3 = ((s8[15728640]{0:T(1024)(128)(4,1)}), s8[3145728]{0:T(1024)(128)(4,1)S(1)}, s32[]{:S(2)}) async-start(s8[15728640]{0:T(1024)(128)(4,1)} %bitcast.2), calls=%async_computation.3 | async-start | bytes 6291456
  61.9 4.2 %collective-permute-start.5 = (bf16[256,2048]{1,0:T(8,128)(2,1)S(1)}, bf16[256,2048]{1,0:T(8,128)(2,1)S(1)}, u32[]{:S(2)}, u32[]{:S(2)}) collective-permute-start(bf16[256,2048]{1,0:T(8,128)(2,1)S(1)} %constant_dynamic-slice_fusion.1), channel_id=1, source_target_pairs={{0,1},{1,0},{2,3},{3,2},{4,5},{5,4},{6,7},{7,6},{8,9},{9,8},{10,11... | collective-permute-start | bytes 3145736 | tf_op jit(solution)/shard_map/ppermute | solution.py:193
  62.1 4.5 %collective-permute-start.4 = (bf16[256,2048]{1,0:T(8,128)(2,1)S(1)}, bf16[256,2048]{1,0:T(8,128)(2,1)S(1)}, u32[]{:S(2)}, u32[]{:S(2)}) collective-permute-start(bf16[256,2048]{1,0:T(8,128)(2,1)S(1)} %constant_dynamic-slice_fusion.2), channel_id=1, source_target_pairs={{0,1},{1,0},{2,3},{3,2},{4,5},{5,4},{6,7},{7,6},{8,9},{9,8},{10,11... | collective-permute-start | bytes 3145736 | tf_op jit(solution)/shard_map/ppermute | solution.py:193
  65.9 2.7 %collective-permute-start.3 = (bf16[256,2048]{1,0:T(8,128)(2,1)S(1)}, bf16[256,2048]{1,0:T(8,128)(2,1)S(1)}, u32[]{:S(2)}, u32[]{:S(2)}) collective-permute-start(bf16[256,2048]{1,0:T(8,128)(2,1)S(1)} %constant_dynamic-slice_fusion.3), channel_id=1, source_target_pairs={{0,1},{1,0},{2,3},{3,2},{4,5},{5,4},{6,7},{7,6},{8,9},{9,8},{10,11... | collective-permute-start | bytes 3145736 | tf_op jit(solution)/shard_map/ppermute | solution.py:193
  73.6 70.6 %collective-permute-start.6 = (bf16[256,6144]{1,0:T(8,128)(2,1)S(1)}, bf16[256,6144]{1,0:T(8,128)(2,1)S(1)}, u32[]{:S(2)}, u32[]{:S(2)}) collective-permute-start(bf16[256,6144]{1,0:T(8,128)(2,1)S(1)} %convolution_convert_fusion), channel_id=1, source_target_pairs={{0,1},{1,0},{2,3},{3,2},{4,5},{5,4},{6,7},{7,6},{8,9},{9,8},{10,11... | collective-permute-start | bytes 9437192 | tf_op jit(solution)/shard_map/ppermute | solution.py:193
  73.8 26.0 %collective-permute-start.7 = (bf16[256,2048]{1,0:T(8,128)(2,1)S(1)}, bf16[256,2048]{1,0:T(8,128)(2,1)S(1)}, u32[]{:S(2)}, u32[]{:S(2)}) collective-permute-start(bf16[256,2048]{1,0:T(8,128)(2,1)S(1)} %add_convert_fusion.3), channel_id=1, source_target_pairs={{0,2},{2,0},{1,3},{3,1},{4,6},{6,4},{5,7},{7,5},{8,10},{10,8},{9,1... | collective-permute-start | bytes 3145736 | tf_op jit(solution)/shard_map/ppermute | solution.py:193
  74.9 47.4 %collective-permute-start.8 = (bf16[256,2048]{1,0:T(8,128)(2,1)S(1)}, bf16[256,2048]{1,0:T(8,128)(2,1)S(1)}, u32[]{:S(2)}, u32[]{:S(2)}) collective-permute-start(bf16[256,2048]{1,0:T(8,128)(2,1)S(1)} %add_convert_fusion.2), channel_id=1, source_target_pairs={{0,2},{2,0},{1,3},{3,1},{4,6},{6,4},{5,7},{7,5},{8,10},{10,8},{9,1... | collective-permute-start | bytes 3145736 | tf_op jit(solution)/shard_map/ppermute | solution.py:193
  75.8 68.4 %collective-permute-start.9 = (bf16[256,2048]{1,0:T(8,128)(2,1)S(1)}, bf16[256,2048]{1,0:T(8,128)(2,1)S(1)}, u32[]{:S(2)}, u32[]{:S(2)}) collective-permute-start(bf16[256,2048]{1,0:T(8,128)(2,1)S(1)} %add_convert_fusion.1), channel_id=1, source_target_pairs={{0,2},{2,0},{1,3},{3,1},{4,6},{6,4},{5,7},{7,5},{8,10},{10,8},{9,1... | collective-permute-start | bytes 3145736 | tf_op jit(solution)/shard_map/ppermute | solution.py:193
